TPU v7x, 32 devices: a whole 2x2x4 slice. The times are simulated.
32 devices in a mesh: groups: 2 (over y), row: 4 (over x, core), col: 4 (over z).
Axes of the slice: x: 2, y: 2, z: 4, core: 2. Of those that a mesh axis runs over, the one named last changes fastest.
Arguments:
- tokens: float32 [256, 8192], P(('groups', 'row', 'col')), parts along dimension 0, may hold values from -36 to 36
- modulation: float32 [3, 2, 8192], P(None, 'groups'), parts along dimension 1, may hold values from -4 to 4
- up_weight: float32 [8192, 16384], P('row', 'col'), may hold values from -0.0625 to 0.0625
- up_bias: float32 [16384], P('col'), may hold values from -3 to 3
- down_weight: float32 [16384, 8192], P('col', 'row'), may hold values from -0.046875 to 0.046875
- down_bias: float32 [8192], replicated, may hold values from -3 to 3
Outputs:
- result: float32 [256, 8192], P(('groups', 'row', 'col')), parts along dimension 0
There are 2 independent parts, one for each index of `groups`. A program takes and returns all parts, laid end to end along the dimension named above; an argument that names none is the same for every part. Nothing has to cross between parts.
All inputs are finite; a program needn't handle non-finite values.
Results may differ from a plain program's by a relative error of at most 0.00005.
Values sent between devices are 32-bit elements; how exact they have to be, the bound alone decides.
No kernel may reach another device: no remote copies, remote signals or barrier semaphores. Data moves between devices by JAX's collectives and lax.ppermute only.
A program may use at most 128 MiB of HBM per device.

v0:
```python
import jax
import jax.numpy as jnp
from jax import lax
from jax.sharding import PartitionSpec as P

SEQ = 256


layer_eps = 1e-06


def local(tokens, modulation, up_weight, up_bias, down_weight, down_bias):
    tok_dev = tokens.shape[0]
    first_tok = (lax.axis_index("row") * lax.axis_size("col") + lax.axis_index("col")) * tok_dev
    sample = first_tok // SEQ
    own_mods = lax.dynamic_slice_in_dim(modulation, sample, 1, 1)[:, 0]
    shift_vec = own_mods[0]
    scale_vec = own_mods[1]
    gate_vec = own_mods[2]
    average = jnp.mean(tokens, axis=1, keepdims=True)
    centred = tokens - average
    spread_sq = jnp.mean(centred * centred, axis=1, keepdims=True)
    normed = centred * lax.rsqrt(spread_sq + layer_eps)
    mixed = normed * (1.0 + scale_vec) + shift_vec
    columns = lax.all_to_all(mixed, "row", split_axis=1, concat_axis=0, tiled=True)
    partial_value = jnp.dot(
        lax.all_gather(columns, "col", axis=0, tiled=True),
        up_weight,
        precision=lax.Precision.HIGHEST,
        preferred_element_type=jnp.float32,
    )
    own_share = lax.psum_scatter(partial_value, "row", scatter_dimension=0, tiled=True)
    activated_share = jax.nn.gelu(own_share + up_bias, approximate=True)
    activated = lax.all_gather(activated_share, "row", axis=0, tiled=True)
    out_share = lax.psum_scatter(
        jnp.dot(
            activated,
            down_weight,
            precision=lax.Precision.HIGHEST,
            preferred_element_type=jnp.float32,
        ),
        "col",
        scatter_dimension=0,
        tiled=True,
    )
    returned = lax.all_to_all(out_share, "row", split_axis=0, concat_axis=1, tiled=True)
    return tokens + gate_vec * (returned + down_bias)


def solution(mesh):
    in_specs = (
        P(("groups", "row", "col"), None),
        P(None, "groups", None),
        P("row", "col"),
        P("col"),
        P("col", "row"),
        P(),
    )
    out_specs = P(("groups", "row", "col"), None)
    return jax.shard_map(local, mesh=mesh, in_specs=in_specs, out_specs=out_specs, check_vma=False)
```

profile of v0, /device:TPU:0, one launch (start us, length us, event | category | flops | bytes accessed | tf_op | source)
XLA Modules:
  0.0 196.5 jit_solution(8773014007138817047)
XLA Ops:
  6.5 0.0 copy-start.2
  6.5 0.0 all-gather.3.cloned.1.call-start
  6.5 1.1 reduce_sum.18
  7.7 1.2 multiply_reduce_fusion
  8.9 0.8 fusion.7
  9.7 1.1 multiply_add_fusion.1
  10.8 10.2 %all_to_all.38 = f32[8,4,2048]{2,0,1:T(8,128)} all-to-all(f32[8,4,2048]{2,0,1:T(8,128)S(1)} %bitcast.16), channel_id=1, replica_groups=mesh['groups'=2,'row'=4,'col'=4] {'row'}, dimensions={1} | all-to-all | bytes 524288 | tf_op jit(solution)/shard_map/all_to_all | solution.py:25
  20.9 0.0 all-gather.3.cloned.1.call-update
  21.0 0.0 copy-start
  21.0 0.0 copy-start.1
  21.0 0.0 reduce-scatter.3.cloned.1.call-start
  21.0 28.7 %all-gather.3.cloned.1.call-done = f32[128,2048]{1,0:T(8,128)} async-done(((f32[32,2048]{1,0:T(8,128)}), f32[128,2048]{1,0:T(8,128)}) %all-gather.3.cloned.1.call-update) | async-done | bytes 1048592 | tf_op jit(solution)/shard_map/all_gather | solution.py:27
  49.8 23.1 %fusion.8 = f32[128,4096]{1,0:T(8,128)} fusion(f32[128,2048]{1,0:T(8,128)} %all-gather.3.cloned.1.call-done, f32[2048,4096]{1,0:T(8,128)} %param.8), kind=kOutput, calls=%fused_computation.15 | convolution fusion | flops 12884901888 | bytes 36700160 | tf_op jit(solution)/shard_map/dot_general | solution.py:26
  72.9 0.0 reduce-scatter.3.cloned.1.call-update
  72.9 0.0 all-gather.5.cloned.1.call-start
  72.9 31.0 %reduce-scatter.3.cloned.1.call-done = f32[32,4096]{1,0:T(8,128)} async-done(((f32[128,4096]{1,0:T(8,128)}), f32[32,4096]{1,0:T(8,128)}) %reduce-scatter.3.cloned.1.call-update) | async-done | bytes 524304 | tf_op jit(solution)/shard_map/reduce_scatter | solution.py:32
  104.0 0.0 copy-done.2
  104.0 2.0 %fusion.6 = f32[32,4096]{1,0:T(8,128)} fusion(f32[32,4096]{1,0:T(8,128)} %reduce-scatter.3.cloned.1.call-done, f32[4096]{0:T(1024)S(1)} %copy-done.2), kind=kLoop, calls=%fused_computation.7 | loop fusion | flops 1179648 | bytes 1064960 | tf_op jit(solution)/shard_map/mul | solution.py:33
  106.0 0.0 all-gather.5.cloned.1.call-update
  106.0 0.0 reduce-scatter.5.cloned.1.call-start
  106.1 22.7 %all-gather.5.cloned.1.call-done = f32[128,4096]{1,0:T(8,128)} async-done(((f32[32,4096]{1,0:T(8,128)}), f32[128,4096]{1,0:T(8,128)}) %all-gather.5.cloned.1.call-update) | async-done | bytes 2097168 | tf_op jit(solution)/shard_map/all_gather | solution.py:34
  128.8 23.7 %fusion.9 = f32[128,2048]{1,0:T(8,128)} fusion(f32[128,4096]{1,0:T(8,128)} %all-gather.5.cloned.1.call-done, f32[4096,2048]{1,0:T(8,128)} %param.10), kind=kOutput, calls=%fused_computation.16 | convolution fusion | flops 12884901888 | bytes 36700160 | tf_op jit(solution)/shard_map/dot_general | solution.py:36
  152.5 0.0 reduce-scatter.5.cloned.1.call-update
  152.5 27.3 %reduce-scatter.5.cloned.1.call-done = f32[32,2048]{1,0:T(8,128)} async-done(((f32[128,2048]{1,0:T(8,128)}), f32[32,2048]{1,0:T(8,128)}) %reduce-scatter.5.cloned.1.call-update) | async-done | bytes 262160 | tf_op jit(solution)/shard_map/reduce_scatter | solution.py:35
  179.8 9.4 %all_to_all.39 = f32[4,8,2048]{2,1,0:T(8,128)S(1)} all-to-all(f32[4,8,2048]{2,1,0:T(8,128)} %bitcast.18), channel_id=1, replica_groups=mesh['groups'=2,'row'=4,'col'=4] {'row'}, dimensions={0} | all-to-all | bytes 524288 | tf_op jit(solution)/shard_map/all_to_all | solution.py:46
  189.2 0.0 copy-done
  189.2 0.0 copy-done.1
  189.2 0.8 multiply_add_fusion
  (2 shorter events, 0.0 us)
Async XLA Ops:
  6.5 97.4 %copy-start.2 = (f32[4096]{0:T(1024)S(1)}, f32[4096]{0:T(1024)}, u32[]{:S(2)}) copy-start(f32[4096]{0:T(1024)} %param.9) | copy-start | bytes 49156
  6.5 43.2 %all-gather.3.cloned.1.call-start = ((), (), s32[]{:S(2)}) async-start(), calls=%async_computation.4 | async-start | bytes 1310720 | tf_op jit(solution)/shard_map/all_gather | solution.py:27
  21.0 168.2 %copy-start = (f32[8,8192]{1,0:T(8,128)S(1)}, f32[8,8192]{1,0:T(8,128)}, u32[]{:S(2)}) copy-start(f32[8,8192]{1,0:T(8,128)} %param.6) | copy-start | bytes 786436
  21.0 168.2 %copy-start.1 = (f32[8192]{0:T(1024)S(1)}, f32[8192]{0:T(1024)}, u32[]{:S(2)}) copy-start(f32[8192]{0:T(1024)} %param.11) | copy-start | bytes 98308
  21.0 83.0 %reduce-scatter.3.cloned.1.call-start = ((), (), s32[]{:S(2)}) async-start(), calls=%async_computation.5 | async-start | bytes 2621440 | tf_op jit(solution)/shard_map/reduce_scatter | solution.py:32
  72.9 55.9 %all-gather.5.cloned.1.call-start = ((), (), s32[]{:S(2)}) async-start(), calls=%async_computation.6 | async-start | bytes 2621440 | tf_op jit(solution)/shard_map/all_gather | solution.py:34
  106.0 73.8 %reduce-scatter.5.cloned.1.call-start = ((), (), s32[]{:S(2)}) async-start(), calls=%async_computation.7 | async-start | bytes 1310720 | tf_op jit(solution)/shard_map/reduce_scatter | solution.py:35
Sparse Core Ops, SparseCore 0:
  21.1 28.6 all-gather.2
  73.0 30.9 reduce-scatter.2
  106.1 22.5 all-gather.4
  152.6 27.1 reduce-scatter.4
where the time goes:
time: 197 us
  waiting for transfers between devices  110 us (56%)
  matrix products  46.8 us (24%)
  blocking collectives  19.6 us (10%)
  between operations  13.2 us (7%)
  other arithmetic  7.04 us (4%)
    reduce_scatter x1, waiting for transfers between devices, local(): lax.psum_scatter(partial_value, 'row', scatter_dimension=0, tiled=True)  31 us
    all_gather x1, waiting for transfers between devices, local(): lax.all_gather(columns, 'col', axis=0, tiled=True)  28.7 us
    reduce_scatter x1, waiting for transfers between devices, local(): lax.psum_scatter(jnp.dot(activated, down_weight, precision=lax.Precision....  27.3 us
    dot_general x1, matrix products, local(): jnp.dot(activated, down_weight, precision=lax.Precision.HIGHEST, preferre...  23.7 us
    dot_general x1, matrix products, local(): jnp.dot(lax.all_gather(columns, 'col', axis=0, tiled=True), up_weight, pr...  23.1 us
    all_gather x1, waiting for transfers between devices, local(): activated = lax.all_gather(activated_share, 'row', axis=0, tiled=True)  22.7 us
    all_to_all x1, blocking collectives, local(): lax.all_to_all(mixed, 'row', split_axis=1, concat_axis=0, tiled=True)  10.2 us
    all_to_all x1, blocking collectives, local(): lax.all_to_all(out_share, 'row', split_axis=0, concat_axis=1, tiled=True)  9.41 us
  transfers between devices with their start and end apart: 4, of which 4 were waited for; matrix products, arithmetic and copies ran while one was open for 0% of the time, Pallas kernels for 0%

commit v1 on v0

--- a/solution.py
+++ b/solution.py
@@ -26,7 +26,7 @@
     partial_value = jnp.dot(
         lax.all_gather(columns, "col", axis=0, tiled=True),
         up_weight,
-        precision=lax.Precision.HIGHEST,
+        precision=lax.Precision.HIGH,
         preferred_element_type=jnp.float32,
     )
     own_share = lax.psum_scatter(partial_value, "row", scatter_dimension=0, tiled=True)
@@ -36,7 +36,7 @@
         jnp.dot(
             activated,
             down_weight,
-            precision=lax.Precision.HIGHEST,
+            precision=lax.Precision.HIGH,
             preferred_element_type=jnp.float32,
         ),
         "col",

time: 197 us -> 184 us (0.934)
  matrix products: 46.8 us -> 33.5 us
    dot_general x1, matrix products: 23.7 us -> 15.8 us  [local(): jnp.dot(activated, down_weight, precision=lax.Precision.HIGH, preferred_e...]
    dot_general x1, matrix products: 23.1 us -> 17.7 us  [local(): jnp.dot(lax.all_gather(columns, 'col', axis=0, tiled=True), up_weight, pr...]
where the time goes in v1:
time: 184 us; the launch traced here: 183 us
  waiting for transfers between devices  110 us (60%)
  matrix products  33.5 us (18%)
  blocking collectives  19.6 us (11%)
  between operations  13.2 us (7%)
  other arithmetic  7.04 us (4%)
    reduce_scatter x1, waiting for transfers between devices, local(): lax.psum_scatter(partial_value, 'row', scatter_dimension=0, tiled=True)  31 us
    all_gather x1, waiting for transfers between devices, local(): lax.all_gather(columns, 'col', axis=0, tiled=True)  28.7 us
    reduce_scatter x1, waiting for transfers between devices, local(): lax.psum_scatter(jnp.dot(activated, down_weight, precision=lax.Precision....  27.3 us
    all_gather x1, waiting for transfers between devices, local(): activated = lax.all_gather(activated_share, 'row', axis=0, tiled=True)  22.7 us
    dot_general x1, matrix products, local(): jnp.dot(lax.all_gather(columns, 'col', axis=0, tiled=True), up_weight, pr...  17.7 us
    dot_general x1, matrix products, local(): jnp.dot(activated, down_weight, precision=lax.Precision.HIGH, preferred_e...  15.8 us
    all_to_all x1, blocking collectives, local(): lax.all_to_all(mixed, 'row', split_axis=1, concat_axis=0, tiled=True)  10.2 us
    all_to_all x1, blocking collectives, local(): lax.all_to_all(out_share, 'row', split_axis=0, concat_axis=1, tiled=True)  9.41 us
  transfers between devices with their start and end apart: 4, of which 4 were waited for; matrix products, arithmetic and copies ran while one was open for 0% of the time, Pallas kernels for 0%

profile of v1, /device:TPU:0, one launch (start us, length us, event | category | flops | bytes accessed | tf_op | source)
XLA Modules:
  0.0 183.2 jit_solution(12808481648443348210)
XLA Ops:
  6.5 0.0 copy-start.2
  6.5 0.0 all-gather.3.cloned.1.call-start
  6.5 1.1 reduce_sum.18
  7.7 1.2 multiply_reduce_fusion
  8.9 0.8 fusion.7
  9.7 1.1 multiply_add_fusion.1
  10.8 10.2 %all_to_all.38 = f32[8,4,2048]{2,0,1:T(8,128)} all-to-all(f32[8,4,2048]{2,0,1:T(8,128)S(1)} %bitcast.16), channel_id=1, replica_groups=mesh['groups'=2,'row'=4,'col'=4] {'row'}, dimensions={1} | all-to-all | bytes 524288 | tf_op jit(solution)/shard_map/all_to_all | solution.py:25
  20.9 0.0 all-gather.3.cloned.1.call-update
  21.0 0.0 copy-start
  21.0 0.0 copy-start.1
  21.0 0.0 reduce-scatter.3.cloned.1.call-start
  21.0 28.7 %all-gather.3.cloned.1.call-done = f32[128,2048]{1,0:T(8,128)} async-done(((f32[32,2048]{1,0:T(8,128)}), f32[128,2048]{1,0:T(8,128)}) %all-gather.3.cloned.1.call-update) | async-done | bytes 1048592 | tf_op jit(solution)/shard_map/all_gather | solution.py:27
  49.8 17.7 %fusion.8 = f32[128,4096]{1,0:T(8,128)} fusion(f32[128,2048]{1,0:T(8,128)} %all-gather.3.cloned.1.call-done, f32[2048,4096]{1,0:T(8,128)} %param.8), kind=kOutput, calls=%fused_computation.15 | convolution fusion | flops 6442450944 | bytes 36700160 | tf_op jit(solution)/shard_map/dot_general | solution.py:26
  67.5 0.0 reduce-scatter.3.cloned.1.call-update
  67.5 0.0 all-gather.5.cloned.1.call-start
  67.6 31.0 %reduce-scatter.3.cloned.1.call-done = f32[32,4096]{1,0:T(8,128)} async-done(((f32[128,4096]{1,0:T(8,128)}), f32[32,4096]{1,0:T(8,128)}) %reduce-scatter.3.cloned.1.call-update) | async-done | bytes 524304 | tf_op jit(solution)/shard_map/reduce_scatter | solution.py:32
  98.6 0.0 copy-done.2
  98.6 2.0 %fusion.6 = f32[32,4096]{1,0:T(8,128)} fusion(f32[32,4096]{1,0:T(8,128)} %reduce-scatter.3.cloned.1.call-done, f32[4096]{0:T(1024)S(1)} %copy-done.2), kind=kLoop, calls=%fused_computation.7 | loop fusion | flops 1179648 | bytes 1064960 | tf_op jit(solution)/shard_map/mul | solution.py:33
  100.6 0.0 all-gather.5.cloned.1.call-update
  100.7 0.0 reduce-scatter.5.cloned.1.call-start
  100.7 22.7 %all-gather.5.cloned.1.call-done = f32[128,4096]{1,0:T(8,128)} async-done(((f32[32,4096]{1,0:T(8,128)}), f32[128,4096]{1,0:T(8,128)}) %all-gather.5.cloned.1.call-update) | async-done | bytes 2097168 | tf_op jit(solution)/shard_map/all_gather | solution.py:34
  123.4 15.8 %fusion.9 = f32[128,2048]{1,0:T(8,128)} fusion(f32[128,4096]{1,0:T(8,128)} %all-gather.5.cloned.1.call-done, f32[4096,2048]{1,0:T(8,128)} %param.10), kind=kOutput, calls=%fused_computation.16 | convolution fusion | flops 6442450944 | bytes 36700160 | tf_op jit(solution)/shard_map/dot_general | solution.py:36
  139.2 0.0 reduce-scatter.5.cloned.1.call-update
  139.2 27.3 %reduce-scatter.5.cloned.1.call-done = f32[32,2048]{1,0:T(8,128)} async-done(((f32[128,2048]{1,0:T(8,128)}), f32[32,2048]{1,0:T(8,128)}) %reduce-scatter.5.cloned.1.call-update) | async-done | bytes 262160 | tf_op jit(solution)/shard_map/reduce_scatter | solution.py:35
  166.5 9.4 %all_to_all.39 = f32[4,8,2048]{2,1,0:T(8,128)S(1)} all-to-all(f32[4,8,2048]{2,1,0:T(8,128)} %bitcast.18), channel_id=1, replica_groups=mesh['groups'=2,'row'=4,'col'=4] {'row'}, dimensions={0} | all-to-all | bytes 524288 | tf_op jit(solution)/shard_map/all_to_all | solution.py:46
  175.9 0.0 copy-done
  175.9 0.0 copy-done.1
  175.9 0.8 multiply_add_fusion
  (2 shorter events, 0.0 us)
Async XLA Ops:
  6.5 92.1 %copy-start.2 = (f32[4096]{0:T(1024)S(1)}, f32[4096]{0:T(1024)}, u32[]{:S(2)}) copy-start(f32[4096]{0:T(1024)} %param.9) | copy-start | bytes 49156
  6.5 43.2 %all-gather.3.cloned.1.call-start = ((), (), s32[]{:S(2)}) async-start(), calls=%async_computation.4 | async-start | bytes 1310720 | tf_op jit(solution)/shard_map/all_gather | solution.py:27
  21.0 154.9 %copy-start = (f32[8,8192]{1,0:T(8,128)S(1)}, f32[8,8192]{1,0:T(8,128)}, u32[]{:S(2)}) copy-start(f32[8,8192]{1,0:T(8,128)} %param.6) | copy-start | bytes 786436
  21.0 154.9 %copy-start.1 = (f32[8192]{0:T(1024)S(1)}, f32[8192]{0:T(1024)}, u32[]{:S(2)}) copy-start(f32[8192]{0:T(1024)} %param.11) | copy-start | bytes 98308
  21.0 77.6 %reduce-scatter.3.cloned.1.call-start = ((), (), s32[]{:S(2)}) async-start(), calls=%async_computation.5 | async-start | bytes 2621440 | tf_op jit(solution)/shard_map/reduce_scatter | solution.py:32
  67.5 55.9 %all-gather.5.cloned.1.call-start = ((), (), s32[]{:S(2)}) async-start(), calls=%async_computation.6 | async-start | bytes 2621440 | tf_op jit(solution)/shard_map/all_gather | solution.py:34
  100.7 65.9 %reduce-scatter.5.cloned.1.call-start = ((), (), s32[]{:S(2)}) async-start(), calls=%async_computation.7 | async-start | bytes 1310720 | tf_op jit(solution)/shard_map/reduce_scatter | solution.py:35
Sparse Core Ops, SparseCore 0:
  21.1 28.6 all-gather.2
  67.6 30.9 reduce-scatter.2
  100.8 22.5 all-gather.4
  139.3 27.1 reduce-scatter.4

commit v2 on v1

v2 whole, which is shorter than its diff:
```python
import jax
import jax.numpy as jnp
from jax import lax
from jax.sharding import PartitionSpec as P

SEQ = 256


layer_eps = 1e-06


def _pairs(n, flip):
    return [(i, i ^ flip) for i in range(n)]


def local(tokens, modulation, up_weight, up_bias, down_weight, down_bias):
    n_row = lax.axis_size("row")
    tok_dev = tokens.shape[0]
    first_tok = (lax.axis_index("row") * lax.axis_size("col") + lax.axis_index("col")) * tok_dev
    sample = first_tok // SEQ
    own_mods = lax.dynamic_slice_in_dim(modulation, sample, 1, 1)[:, 0]
    shift_vec = own_mods[0]
    scale_vec = own_mods[1]
    gate_vec = own_mods[2]
    average = jnp.mean(tokens, axis=1, keepdims=True)
    centred = tokens - average
    spread_sq = jnp.mean(centred * centred, axis=1, keepdims=True)
    normed = centred * lax.rsqrt(spread_sq + layer_eps)
    mixed = normed * (1.0 + scale_vec) + shift_vec
    columns = lax.all_to_all(mixed, "row", split_axis=1, concat_axis=0, tiled=True)
    gathered = lax.all_gather(columns, "col", axis=0, tiled=True)
    hidden = jnp.dot(gathered, up_weight, precision=lax.Precision.HIGH,
                     preferred_element_type=jnp.float32)
    n_pos, ff_blk = hidden.shape
    quarter = ff_blk // n_row
    r = lax.axis_index("row")
    buf = hidden.reshape(n_pos, n_row, quarter)
    flip = 1
    while flip < n_row:
        bit = (r // flip) % 2
        pairs = buf.reshape(n_pos, buf.shape[1] // 2, 2, quarter)
        keep = jnp.where(bit == 0, pairs[:, :, 0], pairs[:, :, 1])
        send = jnp.where(bit == 0, pairs[:, :, 1], pairs[:, :, 0])
        buf = keep + lax.ppermute(send, "row", _pairs(n_row, flip))
        flip *= 2
    bias_q = lax.dynamic_slice_in_dim(up_bias, r * quarter, quarter)
    act = jax.nn.gelu(buf + bias_q[None, None, :], approximate=True)
    flip = n_row // 2
    while flip >= 1:
        bit = (r // flip) % 2
        other = lax.ppermute(act, "row", _pairs(n_row, flip))
        act = jnp.where(bit == 0, jnp.stack([act, other], axis=2), jnp.stack([other, act], axis=2))
        act = act.reshape(n_pos, act.shape[1] * 2, quarter)
        flip //= 2
    act = act.reshape(n_pos, ff_blk)
    partial_out = jnp.dot(act, down_weight, precision=lax.Precision.HIGH,
                          preferred_element_type=jnp.float32)
    out_share = lax.psum_scatter(partial_out, "col", scatter_dimension=0, tiled=True)
    returned = lax.all_to_all(out_share, "row", split_axis=0, concat_axis=1, tiled=True)
    return tokens + gate_vec * (returned + down_bias)


def solution(mesh):
    in_specs = (
        P(("groups", "row", "col"), None),
        P(None, "groups", None),
        P("row", "col"),
        P("col"),
        P("col", "row"),
        P(),
    )
    out_specs = P(("groups", "row", "col"), None)
    return jax.shard_map(local, mesh=mesh, in_specs=in_specs, out_specs=out_specs, check_vma=False)
```

time: 184 us -> 171 us (0.929)
  waiting for transfers between devices: 110 us -> 84.4 us
  local copies, waits for them, and re-layouts: 0.02 us -> 9.42 us
  starting transfers between devices: 0.13 us -> 3.26 us
    reduce_scatter x2 -> x1, waiting for transfers between devices: 58.3 us -> 26.8 us  [local(): lax.psum_scatter(partial_out, 'col', scatter_dimension=0, tiled=True)]
    ppermute x0 -> x4, waiting for transfers between devices: none -> 28.8 us  [the longest x2 14.6 us: local(): buf = keep + lax.ppermute(send, 'row', _pairs(n_row, flip))]
    all_gather x2 -> x1, waiting for transfers between devices: 51.4 us -> 28.7 us  [local(): gathered = lax.all_gather(columns, 'col', axis=0, tiled=True)]
    slice x0 -> x1, local copies, waits for them, and re-layouts: none -> 4.37 us  [local(): keep = jnp.where(bit == 0, pairs[:, :, 0], pairs[:, :, 1])]
    ppermute x0 -> x4, starting transfers between devices: none -> 3.21 us  [the longest x2 1.61 us: local(): buf = keep + lax.ppermute(send, 'row', _pairs(n_row, flip))]
    another operation x0 -> x1, local copies, waits for them, and re-layouts: none -> 2.83 us  [local(): pairs = buf.reshape(n_pos, buf.shape[1] // 2, 2, quarter)]
  transfers between devices with their start and end apart: 4 -> 6, of which waited for: 4 -> 6; matrix products, arithmetic and copies ran while one was open for 0% -> 0% of each run, Pallas kernels for 0% -> 0%
where the time goes in v2:
time: 171 us; the launch traced here: 170 us
  waiting for transfers between devices  84.4 us (49%)
  matrix products  33 us (19%)
  blocking collectives  19.6 us (11%)
  between operations  13.6 us (8%)
  local copies, waits for them, and re-layouts  9.42 us (6%)
  other arithmetic  7.07 us (4%)
  starting transfers between devices  3.26 us (2%)
    all_gather x1, waiting for transfers between devices, local(): gathered = lax.all_gather(columns, 'col', axis=0, tiled=True)  28.7 us
    reduce_scatter x1, waiting for transfers between devices, local(): lax.psum_scatter(partial_out, 'col', scatter_dimension=0, tiled=True)  26.8 us
    dot_general x1, matrix products, local(): jnp.dot(gathered, up_weight, precision=lax.Precision.HIGH, preferred_elem...  16.7 us
    dot_general x1, matrix products, local(): jnp.dot(act, down_weight, precision=lax.Precision.HIGH, preferred_element...  16.3 us
    ppermute x2, waiting for transfers between devices, local(): buf = keep + lax.ppermute(send, 'row', _pairs(n_row, flip))  14.6 us
    ppermute x2, waiting for transfers between devices, local(): other = lax.ppermute(act, 'row', _pairs(n_row, flip))  14.2 us
    all_to_all x1, blocking collectives, local(): lax.all_to_all(mixed, 'row', split_axis=1, concat_axis=0, tiled=True)  10.2 us
    all_to_all x1, blocking collectives, local(): lax.all_to_all(out_share, 'row', split_axis=0, concat_axis=1, tiled=True)  9.41 us
  transfers between devices with their start and end apart: 6, of which 6 were waited for; matrix products, arithmetic and copies ran while one was open for 0% of the time, Pallas kernels for 0%

profile of v2, /device:TPU:0, one launch (start us, length us, event | category | flops | bytes accessed | tf_op | source)
XLA Modules:
  0.0 170.2 jit_solution(618338506341184580)
XLA Ops:
  6.5 0.0 all-gather.2.cloned.1.call-start
  6.5 0.8 fusion.10
  7.4 1.1 reduce_sum.18
  8.5 1.2 multiply_reduce_fusion
  9.7 1.1 multiply_add_fusion.1
  10.8 10.2 %all_to_all.38 = f32[8,4,2048]{2,0,1:T(8,128)} all-to-all(f32[8,4,2048]{2,0,1:T(8,128)S(1)} %bitcast.40), channel_id=1, replica_groups=mesh['groups'=2,'row'=4,'col'=4] {'row'}, dimensions={1} | all-to-all | bytes 524288 | tf_op jit(solution)/shard_map/all_to_all | solution.py:30
  20.9 0.0 all-gather.2.cloned.1.call-update
  21.0 0.0 reduce-scatter.2.cloned.1.call-start
  21.0 28.7 %all-gather.2.cloned.1.call-done = f32[128,2048]{1,0:T(8,128)} async-done(((f32[32,2048]{1,0:T(8,128)}), f32[128,2048]{1,0:T(8,128)}) %all-gather.2.cloned.1.call-update) | async-done | bytes 1048592 | tf_op jit(solution)/shard_map/all_gather | solution.py:31
  49.8 16.7 %fusion.11 = f32[128,4096]{1,0:T(8,128)S(1)} fusion(f32[128,2048]{1,0:T(8,128)} %all-gather.2.cloned.1.call-done, f32[2048,4096]{1,0:T(8,128)} %param.8), kind=kOutput, calls=%fused_computation.25 | convolution fusion | flops 6442450944 | bytes 36700160 | tf_op jit(solution)/shard_map/dot_general | solution.py:32
  66.5 2.8 %reshape_reshape.4 = f32[128,2,2,1024]{3,2,1,0:T(2,128)} reshape(f32[128,4096]{1,0:T(8,128)S(1)} %fusion.11) | data formatting | bytes 4194304 | tf_op jit(solution)/shard_map/reshape;reshape | solution.py:41
  69.3 4.4 %fusion.9 = (f32[128,2,1,1024]{3,2,1,0:T(1,128)S(1)}, f32[128,2,1,1024]{3,2,1,0:T(1,128)S(1)}) fusion(f32[128,2,2,1024]{3,2,1,0:T(2,128)} %reshape_reshape.4), kind=kLoop, calls=%fused_computation.23 | loop fusion | bytes 4194304 | tf_op jit(solution)/shard_map/slice | solution.py:42
  73.7 0.8 copy.17
  74.5 0.8 copy.18
  75.2 0.1 select_bitcast_fusion
  75.3 0.1 collective-permute-start
  75.4 2.7 %collective-permute-done = f32[128,2,1024]{0,2,1:T(8,128)} collective-permute-done((f32[128,2,1024]{0,2,1:T(8,128)S(1)}, f32[128,2,1024]{0,2,1:T(8,128)}, u32[]{:S(2)}, u32[]{:S(2)}) %collective-permute-start) | collective-permute-done | bytes 1048608 | tf_op jit(solution)/shard_map/ppermute | solution.py:44
  78.2 1.4 fusion
  79.6 0.1 select_bitcast_fusion.1
  79.6 1.5 collective-permute-start.1
  81.2 0.7 dynamic_slice.4
  81.8 11.8 %collective-permute-done.1 = f32[128,1,1024]{0,2,1:T(8,128)S(1)} collective-permute-done((f32[128,1,1024]{0,2,1:T(8,128)S(1)}, f32[128,1,1024]{0,2,1:T(8,128)S(1)}, u32[]{:S(2)}, u32[]{:S(2)}) %collective-permute-start.1) | collective-permute-done | bytes 524320 | tf_op jit(solution)/shard_map/ppermute | solution.py:44
  93.7 0.3 fusion.7
  93.9 1.5 collective-permute-start.2
  95.5 11.7 %collective-permute-done.2 = f32[128,1,1024]{0,2,1:T(8,128)S(1)} collective-permute-done((f32[128,1,1024]{0,2,1:T(8,128)S(1)}, f32[128,1,1024]{0,2,1:T(8,128)S(1)}, u32[]{:S(2)}, u32[]{:S(2)}) %collective-permute-start.2) | collective-permute-done | bytes 524320 | tf_op jit(solution)/shard_map/ppermute | solution.py:51
  107.1 0.1 maximum_select_fusion.2
  107.2 0.1 collective-permute-start.3
  107.3 0.1 maximum_select_fusion.1
  107.4 2.6 %collective-permute-done.3 = f32[128,2,1024]{0,2,1:T(8,128)S(1)} collective-permute-done((f32[128,2,1024]{0,2,1:T(8,128)S(1)}, f32[128,2,1024]{0,2,1:T(8,128)S(1)}, u32[]{:S(2)}, u32[]{:S(2)}) %collective-permute-start.3) | collective-permute-done | bytes 1048608 | tf_op jit(solution)/shard_map/ppermute | solution.py:51
  109.9 0.1 maximum_select_fusion
  110.1 0.0 copy-start
  110.1 0.0 copy-start.1
  110.1 16.3 %fusion.12 = f32[128,2048]{1,0:T(8,128)} fusion(f32[128,4096]{0,1:T(8,128)S(1)} %bitcast.35, f32[4096,2048]{1,0:T(8,128)} %param.10), kind=kOutput, calls=%fused_computation.26 | convolution fusion | flops 6442450944 | bytes 36700160 | tf_op jit(solution)/shard_map/dot_general | solution.py:56
  126.4 0.0 reduce-scatter.2.cloned.1.call-update
  126.4 26.8 %reduce-scatter.2.cloned.1.call-done = f32[32,2048]{1,0:T(8,128)} async-done(((f32[128,2048]{1,0:T(8,128)}), f32[32,2048]{1,0:T(8,128)}) %reduce-scatter.2.cloned.1.call-update) | async-done | bytes 262160 | tf_op jit(solution)/shard_map/reduce_scatter | solution.py:58
  153.2 9.4 %all_to_all.39 = f32[4,8,2048]{2,1,0:T(8,128)S(1)} all-to-all(f32[4,8,2048]{2,1,0:T(8,128)} %bitcast.42), channel_id=1, replica_groups=mesh['groups'=2,'row'=4,'col'=4] {'row'}, dimensions={0} | all-to-all | bytes 524288 | tf_op jit(solution)/shard_map/all_to_all | solution.py:59
  162.6 0.0 copy-done
  162.6 0.0 copy-done.1
  162.6 0.8 multiply_add_fusion
  (2 shorter events, 0.0 us)
Async XLA Ops:
  6.5 43.2 %all-gather.2.cloned.1.call-start = ((), (), s32[]{:S(2)}) async-start(), calls=%async_computation.3 | async-start | bytes 1310720 | tf_op jit(solution)/shard_map/all_gather | solution.py:31
  21.0 132.2 %reduce-scatter.2.cloned.1.call-start = ((), (), s32[]{:S(2)}) async-start(), calls=%async_computation.4 | async-start | bytes 1310720 | tf_op jit(solution)/shard_map/reduce_scatter | solution.py:58
  75.3 2.9 %collective-permute-start = (f32[128,2,1024]{0,2,1:T(8,128)S(1)}, f32[128,2,1024]{0,2,1:T(8,128)}, u32[]{:S(2)}, u32[]{:S(2)}) collective-permute-start(f32[128,2,1024]{0,2,1:T(8,128)S(1)} %select_bitcast_fusion), channel_id=1, source_target_pairs={{0,4},{4,0},{8,12},{12,8},{1,5},{5,1},{9,13},{13,9},{2,6},{6,2},{1... | collective-permute-start | bytes 3145736 | tf_op jit(solution)/shard_map/ppermute | solution.py:44
  79.6 14.0 %collective-permute-start.1 = (f32[128,1,1024]{0,2,1:T(8,128)S(1)}, f32[128,1,1024]{0,2,1:T(8,128)S(1)}, u32[]{:S(2)}, u32[]{:S(2)}) collective-permute-start(f32[128,1,1024]{0,2,1:T(8,128)S(1)} %select_bitcast_fusion.1), channel_id=1, source_target_pairs={{0,8},{4,12},{8,0},{12,4},{1,9},{5,13},{9,1},{13,5},{2,10},{6,14},... | collective-permute-start | bytes 1572872 | tf_op jit(solution)/shard_map/ppermute | solution.py:44
  93.9 13.2 %collective-permute-start.2 = (f32[128,1,1024]{0,2,1:T(8,128)S(1)}, f32[128,1,1024]{0,2,1:T(8,128)S(1)}, u32[]{:S(2)}, u32[]{:S(2)}) collective-permute-start(f32[128,1,1024]{0,2,1:T(8,128)S(1)} %fusion.7), channel_id=1, source_target_pairs={{0,8},{4,12},{8,0},{12,4},{1,9},{5,13},{9,1},{13,5},{2,10},{6,14},... | collective-permute-start | bytes 1572872 | tf_op jit(solution)/shard_map/ppermute | solution.py:51
  107.2 2.7 %collective-permute-start.3 = (f32[128,2,1024]{0,2,1:T(8,128)S(1)}, f32[128,2,1024]{0,2,1:T(8,128)S(1)}, u32[]{:S(2)}, u32[]{:S(2)}) collective-permute-start(f32[128,2,1024]{0,2,1:T(8,128)S(1)} %maximum_select_fusion.2), channel_id=1, source_target_pairs={{0,4},{4,0},{8,12},{12,8},{1,5},{5,1},{9,13},{13,9},{2,6},{6,2},{1... | collective-permute-start | bytes 3145736 | tf_op jit(solution)/shard_map/ppermute | solution.py:51
  110.1 52.5 %copy-start = (f32[8,8192]{1,0:T(8,128)S(1)}, f32[8,8192]{1,0:T(8,128)}, u32[]{:S(2)}) copy-start(f32[8,8192]{1,0:T(8,128)} %param.6) | copy-start | bytes 786436
  110.1 52.5 %copy-start.1 = (f32[8192]{0:T(1024)S(1)}, f32[8192]{0:T(1024)}, u32[]{:S(2)}) copy-start(f32[8192]{0:T(1024)} %param.11) | copy-start | bytes 98308
Sparse Core Ops, SparseCore 0:
  21.1 28.6 all-gather.1
  126.5 26.6 reduce-scatter.1

commit v3 on v2

v3 whole, which is shorter than its diff:
```python
import jax
import jax.numpy as jnp
from jax import lax
from jax.sharding import PartitionSpec as P

SEQ = 256


layer_eps = 1e-06


def _pairs(n, flip):
    return [(i, i ^ flip) for i in range(n)]


def local(tokens, modulation, up_weight, up_bias, down_weight, down_bias):
    n_row = lax.axis_size("row")
    tok_dev = tokens.shape[0]
    first_tok = (lax.axis_index("row") * lax.axis_size("col") + lax.axis_index("col")) * tok_dev
    sample = first_tok // SEQ
    own_mods = lax.dynamic_slice_in_dim(modulation, sample, 1, 1)[:, 0]
    shift_vec = own_mods[0]
    scale_vec = own_mods[1]
    gate_vec = own_mods[2]
    average = jnp.mean(tokens, axis=1, keepdims=True)
    centred = tokens - average
    spread_sq = jnp.mean(centred * centred, axis=1, keepdims=True)
    normed = centred * lax.rsqrt(spread_sq + layer_eps)
    mixed = normed * (1.0 + scale_vec) + shift_vec
    columns = lax.all_to_all(mixed, "row", split_axis=1, concat_axis=0, tiled=True)
    gathered = lax.all_gather(columns, "col", axis=0, tiled=True)
    n_pos = gathered.shape[0]
    ff_blk = up_weight.shape[1]
    quarter = ff_blk // n_row
    r = lax.axis_index("row")

    def up_block(d):
        w = lax.dynamic_slice_in_dim(up_weight, (r ^ d) * quarter, quarter, 1)
        return jnp.dot(gathered, w, precision=lax.Precision.HIGH,
                       preferred_element_type=jnp.float32)

    held = {d: lax.optimization_barrier(up_block(d)) for d in range(n_row)}
    flip = 1
    while flip < n_row:
        sent = [d for d in sorted(held) if d & flip]
        got = lax.ppermute(jnp.stack([held[d] for d in sent]), "row", _pairs(n_row, flip))
        held = {d ^ flip: held[d ^ flip] + got[i] for i, d in enumerate(sent)}
        flip *= 2
    bias_q = lax.dynamic_slice_in_dim(up_bias, r * quarter, quarter)
    acts = {0: jax.nn.gelu(held[0] + bias_q[None, :], approximate=True)}
    acts[1] = lax.ppermute(acts[0], "row", _pairs(n_row, 1))
    flip = 2
    while flip < n_row:
        mine = sorted(d for d in acts if d % 2 == 0)
        got = lax.ppermute(jnp.stack([acts[d] for d in mine]), "row", _pairs(n_row, flip))
        for i, d in enumerate(mine):
            acts[d ^ flip] = got[i]
        flip *= 2
    def down_term(d):
        w = lax.dynamic_slice_in_dim(down_weight, (r ^ d) * quarter, quarter, 0)
        return jnp.dot(acts[d], w, precision=lax.Precision.HIGH,
                       preferred_element_type=jnp.float32)

    partial_out = down_term(0) + down_term(1)
    far = sorted(d for d in acts if d % 2 == 0 and d != 0)
    if far:
        stacked, partial_out = lax.optimization_barrier(
            (jnp.stack([acts[d] for d in far]), partial_out))
        got = lax.ppermute(stacked, "row", _pairs(n_row, 1))
        for i, d in enumerate(far):
            acts[d ^ 1] = got[i]
        for d in far:
            partial_out = partial_out + down_term(d)
        for d in far:
            partial_out = partial_out + down_term(d ^ 1)
    out_share = lax.psum_scatter(partial_out, "col", scatter_dimension=0, tiled=True)
    returned = lax.all_to_all(out_share, "row", split_axis=0, concat_axis=1, tiled=True)
    return tokens + gate_vec * (returned + down_bias)


def solution(mesh):
    in_specs = (
        P(("groups", "row", "col"), None),
        P(None, "groups", None),
        P("row", "col"),
        P("col"),
        P("col", "row"),
        P(),
    )
    out_specs = P(("groups", "row", "col"), None)
    return jax.shard_map(local, mesh=mesh, in_specs=in_specs, out_specs=out_specs, check_vma=False)
```

time: 171 us -> 156 us (0.912)
  waiting for transfers between devices: 84.4 us -> 62.3 us
  matrix products: 33 us -> 50.4 us
  local copies, waits for them, and re-layouts: 9.42 us -> 0.7 us
    ppermute x4 -> x5, waiting for transfers between devices: 28.8 us -> 6.66 us  [the longest x2 6.19 us: local(): lax.ppermute(jnp.stack([held[d] for d in sent]), 'row', _pairs(n_row, flip))]
    dot_general x2 -> x8, matrix products: 33 us -> 50.4 us  [the longest x4 25.5 us: down_term(): jnp.dot(acts[d], w, precision=lax.Precision.HIGH, preferred_element_type=...]
    slice x1 -> x0, local copies, waits for them, and re-layouts: 4.37 us -> none  [local(): keep = jnp.where(bit == 0, pairs[:, :, 0], pairs[:, :, 1])]
    another operation x1 -> x0, local copies, waits for them, and re-layouts: 2.83 us -> none  [local(): pairs = buf.reshape(n_pos, buf.shape[1] // 2, 2, quarter)]
  transfers between devices with their start and end apart: 6 -> 7, of which waited for: 6 -> 5; matrix products, arithmetic and copies ran while one was open for 0% -> 20% of each run, Pallas kernels for 0% -> 0%
where the time goes in v3:
time: 156 us; the launch traced here: 155 us
  waiting for transfers between devices  62.3 us (40%)
  matrix products  50.4 us (32%)
  blocking collectives  19.6 us (13%)
  between operations  13.6 us (9%)
  other arithmetic  5.41 us (3%)
  starting transfers between devices  3.35 us (2%)
    all_gather x1, waiting for transfers between devices, local(): gathered = lax.all_gather(columns, 'col', axis=0, tiled=True)  28.7 us
    reduce_scatter x1, waiting for transfers between devices, local(): lax.psum_scatter(partial_out, 'col', scatter_dimension=0, tiled=True)  26.9 us
    dot_general x4, matrix products, down_term(): jnp.dot(acts[d], w, precision=lax.Precision.HIGH, preferred_element_type=...  25.5 us
    dot_general x4, matrix products, up_block(): jnp.dot(gathered, w, precision=lax.Precision.HIGH, preferred_element_type...  24.9 us
    all_to_all x1, blocking collectives, local(): lax.all_to_all(mixed, 'row', split_axis=1, concat_axis=0, tiled=True)  10.2 us
    all_to_all x1, blocking collectives, local(): lax.all_to_all(out_share, 'row', split_axis=0, concat_axis=1, tiled=True)  9.41 us
    ppermute x2, waiting for transfers between devices, local(): lax.ppermute(jnp.stack([held[d] for d in sent]), 'row', _pairs(n_row, flip))  6.19 us
  transfers between devices with their start and end apart: 7, of which 5 were waited for; matrix products, arithmetic and copies ran while one was open for 20% of the time, Pallas kernels for 0%

profile of v3, /device:TPU:0, one launch (start us, length us, event | category | flops | bytes accessed | tf_op | source)
XLA Modules:
  0.0 155.3 jit_solution(5297609197484573728)
XLA Ops:
  6.5 0.0 all-gather.2.cloned.1.call-start
  6.5 0.8 fusion.45
  7.4 1.1 reduce_sum.18
  8.5 1.2 multiply_reduce_fusion
  9.7 1.1 multiply_add_fusion.1
  10.8 10.2 %all_to_all.38 = f32[8,4,2048]{2,0,1:T(8,128)} all-to-all(f32[8,4,2048]{2,0,1:T(8,128)S(1)} %bitcast.52), channel_id=1, replica_groups=mesh['groups'=2,'row'=4,'col'=4] {'row'}, dimensions={1} | all-to-all | bytes 524288 | tf_op jit(solution)/shard_map/all_to_all | solution.py:30
  20.9 0.0 all-gather.2.cloned.1.call-update
  21.0 0.0 reduce-scatter.2.cloned.1.call-start
  21.0 28.7 %all-gather.2.cloned.1.call-done = f32[128,2048]{1,0:T(8,128)} async-done(((f32[32,2048]{1,0:T(8,128)}), f32[128,2048]{1,0:T(8,128)}) %all-gather.2.cloned.1.call-update) | async-done | bytes 1048592 | tf_op jit(solution)/shard_map/all_gather | solution.py:31
  49.8 0.0 copy-start
  49.8 6.3 %fusion.12 = f32[128,1024]{1,0:T(8,128)S(1)} fusion(f32[128,2048]{1,0:T(8,128)} %all-gather.2.cloned.1.call-done, f32[2048,4096]{1,0:T(8,128)} %param.8, s32[]{:T(128)S(6)} %select_n.22), kind=kOutput, calls=%fused_computation.12 | convolution fusion | flops 1610612736 | bytes 9961476 | tf_op jit(solution)/shard_map/dot_general | solution.py:39
  56.1 6.3 %fusion.10 = f32[128,1024]{1,0:T(8,128)S(1)} fusion(f32[128,2048]{1,0:T(8,128)} %all-gather.2.cloned.1.call-done, f32[2048,4096]{1,0:T(8,128)} %param.8, s32[]{:T(128)S(6)} %select_n.23), kind=kOutput, calls=%fused_computation.10 | convolution fusion | flops 1610612736 | bytes 9961476 | tf_op jit(solution)/shard_map/dot_general | solution.py:39
  62.4 0.1 pad_maximum_fusion
  62.5 0.1 collective-permute-start
  62.6 0.0 copy-start.1
  62.6 0.0 copy-start.2
  62.6 6.3 %fusion.8 = f32[128,1024]{1,0:T(8,128)S(1)} fusion(f32[128,2048]{1,0:T(8,128)} %all-gather.2.cloned.1.call-done, f32[2048,4096]{1,0:T(8,128)} %param.8, s32[]{:T(128)S(6)} %select_n.24), kind=kOutput, calls=%fused_computation.8 | convolution fusion | flops 1610612736 | bytes 9961476 | tf_op jit(solution)/shard_map/dot_general | solution.py:39
  69.0 0.0 collective-permute-done
  69.0 0.1 fusion.27
  69.0 1.5 collective-permute-start.1
  70.6 0.7 dynamic_slice.32
  71.3 0.0 copy-done
  71.3 5.9 %fusion.14 = f32[128,1024]{1,0:T(8,128)S(1)} fusion(f32[128,2048]{1,0:T(8,128)S(1)} %copy-done, f32[2048,4096]{1,0:T(8,128)} %param.8, s32[]{:T(128)S(6)} %select_n.11), kind=kOutput, calls=%fused_computation.14 | convolution fusion | flops 1610612736 | bytes 9961476 | tf_op jit(solution)/shard_map/dot_general | solution.py:39
  77.2 6.2 %collective-permute-done.1 = f32[1,128,1024]{2,1,0:T(8,128)S(1)} collective-permute-done((f32[1,128,1024]{2,1,0:T(8,128)S(1)}, f32[1,128,1024]{2,1,0:T(8,128)S(1)}, u32[]{:S(2)}, u32[]{:S(2)}) %collective-permute-start.1) | collective-permute-done | bytes 524320 | tf_op jit(solution)/shard_map/ppermute | solution.py:46
  83.4 0.2 fusion.25
  83.6 0.1 collective-permute-start.3
  83.7 1.5 collective-permute-start.2
  85.2 0.4 collective-permute-done.3
  85.6 6.2 %fusion.4 = f32[128,2048]{1,0:T(8,128)S(1)} fusion(f32[128,1024]{1,0:T(8,128)S(1)} %collective-permute-done.3, f32[4096,2048]{1,0:T(8,128)} %param.10, s32[]{:T(128)S(6)} %select_n.22), kind=kOutput, calls=%fused_computation.4 | convolution fusion | flops 1610612736 | bytes 9961476 | tf_op jit(solution)/shard_map/dot_general | solution.py:61
  91.8 6.1 %fusion.16 = f32[128,2048]{1,0:T(8,128)S(1)} fusion(f32[128,2048]{1,0:T(8,128)S(1)} %fusion.4, f32[128,1024]{1,0:T(8,128)S(1)} %fusion.25, f32[4096,2048]{1,0:T(8,128)} %param.10, s32[]{:T(128)S(6)} %select_n.11), kind=kOutput, calls=%fused_computation.16 | convolution fusion | flops 1610874880 | bytes 11010052 | tf_op jit(solution)/shard_map/dot_general | solution.py:61
  97.9 0.1 collective-permute-done.2
  98.1 0.1 collective-permute-start.4
  98.1 6.1 %fusion.2 = f32[128,2048]{1,0:T(8,128)S(1)} fusion(f32[4096,2048]{1,0:T(8,128)} %param.10, s32[]{:T(128)S(6)} %select_n.24, f32[1,128,1024]{2,1,0:T(8,128)S(1)} %collective-permute-done.2), kind=kOutput, calls=%fused_computation.2 | convolution fusion | flops 1610612736 | bytes 9961476 | tf_op jit(solution)/shard_map/dot_general | solution.py:61
  104.2 0.0 collective-permute-done.4
  104.2 7.1 %add_add_fusion = f32[128,2048]{1,0:T(8,128)} fusion(f32[128,2048]{1,0:T(8,128)S(1)} %fusion.16, f32[128,2048]{1,0:T(8,128)S(1)} %fusion.2, f32[4096,2048]{1,0:T(8,128)} %param.10, s32[]{:T(128)S(6)} %select_n.23, f32[1,128,1024]{2,1,0:T(8,128)S(1)} %collective-permute-done.4), kind=kOutput, calls=%fused_computation.18 | convolution fusion | flops 1611137024 | bytes 12058628 | tf_op jit(solution)/shard_map/dot_general | solution.py:61
  111.4 0.0 reduce-scatter.2.cloned.1.call-update
  111.4 26.9 %reduce-scatter.2.cloned.1.call-done = f32[32,2048]{1,0:T(8,128)} async-done(((f32[128,2048]{1,0:T(8,128)}), f32[32,2048]{1,0:T(8,128)}) %reduce-scatter.2.cloned.1.call-update) | async-done | bytes 262160 | tf_op jit(solution)/shard_map/reduce_scatter | solution.py:76
  138.2 9.4 %all_to_all.39 = f32[4,8,2048]{2,1,0:T(8,128)S(1)} all-to-all(f32[4,8,2048]{2,1,0:T(8,128)} %bitcast.54), channel_id=1, replica_groups=mesh['groups'=2,'row'=4,'col'=4] {'row'}, dimensions={0} | all-to-all | bytes 524288 | tf_op jit(solution)/shard_map/all_to_all | solution.py:77
  147.6 0.0 copy-done.1
  147.6 0.0 copy-done.2
  147.6 0.8 multiply_add_fusion
  (2 shorter events, 0.0 us)
Async XLA Ops:
  6.5 43.2 %all-gather.2.cloned.1.call-start = ((), (), s32[]{:S(2)}) async-start(), calls=%async_computation.3 | async-start | bytes 1310720 | tf_op jit(solution)/shard_map/all_gather | solution.py:31
  21.0 117.3 %reduce-scatter.2.cloned.1.call-start = ((), (), s32[]{:S(2)}) async-start(), calls=%async_computation.4 | async-start | bytes 1310720 | tf_op jit(solution)/shard_map/reduce_scatter | solution.py:76
  49.8 21.5 %copy-start = (f32[128,2048]{1,0:T(8,128)S(1)}, f32[128,2048]{1,0:T(8,128)}, u32[]{:S(2)}) copy-start(f32[128,2048]{1,0:T(8,128)} %all-gather.2.cloned.1.call-done) | copy-start | bytes 3145732
  62.5 6.4 %collective-permute-start = (f32[2,128,1024]{2,1,0:T(8,128)S(1)}, f32[2,128,1024]{2,1,0:T(8,128)S(1)}, u32[]{:S(2)}, u32[]{:S(2)}) collective-permute-start(f32[2,128,1024]{2,1,0:T(8,128)S(1)} %pad_maximum_fusion), channel_id=1, source_target_pairs={{0,4},{4,0},{8,12},{12,8},{1,5},{5,1},{9,13},{13,9},{2,6},{6,2},{1... | collective-permute-start | bytes 3145736 | tf_op jit(solution)/shard_map/ppermute | solution.py:46
  62.6 85.0 %copy-start.1 = (f32[8,8192]{1,0:T(8,128)S(1)}, f32[8,8192]{1,0:T(8,128)}, u32[]{:S(2)}) copy-start(f32[8,8192]{1,0:T(8,128)} %param.6) | copy-start | bytes 786436
  62.6 85.0 %copy-start.2 = (f32[8192]{0:T(1024)S(1)}, f32[8192]{0:T(1024)}, u32[]{:S(2)}) copy-start(f32[8192]{0:T(1024)} %param.11) | copy-start | bytes 98308
  69.0 14.4 %collective-permute-start.1 = (f32[1,128,1024]{2,1,0:T(8,128)S(1)}, f32[1,128,1024]{2,1,0:T(8,128)S(1)}, u32[]{:S(2)}, u32[]{:S(2)}) collective-permute-start(f32[1,128,1024]{2,1,0:T(8,128)S(1)} %fusion.27), channel_id=1, source_target_pairs={{0,8},{4,12},{8,0},{12,4},{1,9},{5,13},{9,1},{13,5},{2,10},{6,14},... | collective-permute-start | bytes 1572872 | tf_op jit(solution)/shard_map/ppermute | solution.py:46
  83.6 2.0 %collective-permute-start.3 = (f32[128,1024]{1,0:T(8,128)S(1)}, f32[128,1024]{1,0:T(8,128)S(1)}, u32[]{:S(2)}, u32[]{:S(2)}) collective-permute-start(f32[128,1024]{1,0:T(8,128)S(1)} %fusion.25), channel_id=1, source_target_pairs={{0,4},{4,0},{8,12},{12,8},{1,5},{5,1},{9,13},{13,9},{2,6},{6,2},{1... | collective-permute-start | bytes 1572872 | tf_op jit(solution)/shard_map/ppermute | solution.py:51
  83.7 14.3 %collective-permute-start.2 = (f32[1,128,1024]{2,1,0:T(8,128)S(1)}, f32[1,128,1024]{2,1,0:T(8,128)S(1)}, u32[]{:S(2)}, u32[]{:S(2)}) collective-permute-start(f32[1,128,1024]{2,1,0:T(8,128)S(1)} %bitcast.48), channel_id=1, source_target_pairs={{0,8},{4,12},{8,0},{12,4},{1,9},{5,13},{9,1},{13,5},{2,10},{6,14},... | collective-permute-start | bytes 1572872 | tf_op jit(solution)/shard_map/ppermute | solution.py:55
  98.1 6.2 %collective-permute-start.4 = (f32[1,128,1024]{2,1,0:T(8,128)S(1)}, f32[1,128,1024]{2,1,0:T(8,128)S(1)}, u32[]{:S(2)}, u32[]{:S(2)}) collective-permute-start(f32[1,128,1024]{2,1,0:T(8,128)S(1)} %collective-permute-done.2), channel_id=1, source_target_pairs={{0,4},{4,0},{8,12},{12,8},{1,5},{5,1},{9,13},{13,9},{2,6},{6,2},{1... | collective-permute-start | bytes 1572872 | tf_op jit(solution)/shard_map/ppermute | solution.py:69
Sparse Core Ops, SparseCore 0:
  21.1 28.6 all-gather.1
  111.5 26.6 reduce-scatter.1

commit v4 on v3

--- a/solution.py
+++ b/solution.py
@@ -11,6 +11,30 @@
 
 def _pairs(n, flip):
     return [(i, i ^ flip) for i in range(n)]
+
+
+def _gather_rel(x, axis, n):
+    held = {0: x}
+    flip = n // 2
+    while flip >= 1:
+        keys = sorted(held)
+        got = lax.ppermute(jnp.stack([held[k] for k in keys]), axis, _pairs(n, flip))
+        for i, k in enumerate(keys):
+            held[k ^ flip] = got[i]
+        flip //= 2
+    return jnp.concatenate([held[d] for d in range(n)], axis=0)
+
+
+def _scatter_rel(x, axis, n):
+    blk = x.shape[0] // n
+    held = {d: x[d * blk:(d + 1) * blk] for d in range(n)}
+    flip = 1
+    while flip < n:
+        sent = [d for d in sorted(held) if d & flip]
+        got = lax.ppermute(jnp.stack([held[d] for d in sent]), axis, _pairs(n, flip))
+        held = {d ^ flip: held[d ^ flip] + got[i] for i, d in enumerate(sent)}
+        flip *= 2
+    return held[0]
 
 
 def local(tokens, modulation, up_weight, up_bias, down_weight, down_bias):
@@ -28,7 +52,8 @@
     normed = centred * lax.rsqrt(spread_sq + layer_eps)
     mixed = normed * (1.0 + scale_vec) + shift_vec
     columns = lax.all_to_all(mixed, "row", split_axis=1, concat_axis=0, tiled=True)
-    gathered = lax.all_gather(columns, "col", axis=0, tiled=True)
+    n_col = lax.axis_size("col")
+    gathered = _gather_rel(columns, "col", n_col)
     n_pos = gathered.shape[0]
     ff_blk = up_weight.shape[1]
     quarter = ff_blk // n_row
@@ -73,7 +98,7 @@
             partial_out = partial_out + down_term(d)
         for d in far:
             partial_out = partial_out + down_term(d ^ 1)
-    out_share = lax.psum_scatter(partial_out, "col", scatter_dimension=0, tiled=True)
+    out_share = _scatter_rel(partial_out, "col", n_col)
     returned = lax.all_to_all(out_share, "row", split_axis=0, concat_axis=1, tiled=True)
     return tokens + gate_vec * (returned + down_bias)
 

time: 156 us -> 140 us (0.90)
  between operations: 13.6 us -> 0.18 us
  starting transfers between devices: 3.35 us -> 10.9 us
  waiting for transfers between devices: 62.3 us -> 55.5 us
  matrix products: 50.4 us -> 48.4 us
    ppermute x0 -> x4, waiting for transfers between devices: none -> 47.8 us  [the longest x2 24.1 us: _scatter_rel(): lax.ppermute(jnp.stack([held[d] for d in sent]), axis, _pairs(n, flip))]
    all_gather x1 -> x0, waiting for transfers between devices: 28.7 us -> none  [local(): gathered = lax.all_gather(columns, 'col', axis=0, tiled=True)]
    reduce_scatter x1 -> x0, waiting for transfers between devices: 26.9 us -> none  [local(): lax.psum_scatter(partial_out, 'col', scatter_dimension=0, tiled=True)]
    ppermute x0 -> x4, starting transfers between devices: none -> 8.58 us  [the longest x2 5.25 us: _scatter_rel(): lax.ppermute(jnp.stack([held[d] for d in sent]), axis, _pairs(n, flip))]
  transfers between devices with their start and end apart: 7 -> 9, of which waited for: 5 -> 7; matrix products, arithmetic and copies ran while one was open for 20% -> 22% of each run, Pallas kernels for 0% -> 0%
where the time goes in v4:
time: 140 us
  waiting for transfers between devices  55.5 us (40%)
  matrix products  48.4 us (35%)
  blocking collectives  18.5 us (13%)
  starting transfers between devices  10.9 us (8%)
  other arithmetic  5.53 us (4%)
    dot_general x4, matrix products, down_term(): jnp.dot(acts[d], w, precision=lax.Precision.HIGH, preferred_element_type=...  24.5 us
    ppermute x2, waiting for transfers between devices, _scatter_rel(): lax.ppermute(jnp.stack([held[d] for d in sent]), axis, _pairs(n, flip))  24.1 us
    dot_general x4, matrix products, up_block(): jnp.dot(gathered, w, precision=lax.Precision.HIGH, preferred_element_type...  23.8 us
    ppermute x2, waiting for transfers between devices, _gather_rel(): lax.ppermute(jnp.stack([held[k] for k in keys]), axis, _pairs(n, flip))  23.7 us
    all_to_all x1, blocking collectives, local(): lax.all_to_all(mixed, 'row', split_axis=1, concat_axis=0, tiled=True)  10 us
    all_to_all x1, blocking collectives, local(): lax.all_to_all(out_share, 'row', split_axis=0, concat_axis=1, tiled=True)  8.42 us
    ppermute x2, waiting for transfers between devices, local(): lax.ppermute(jnp.stack([held[d] for d in sent]), 'row', _pairs(n_row, flip))  6.71 us
    ppermute x2, starting transfers between devices, _scatter_rel(): lax.ppermute(jnp.stack([held[d] for d in sent]), axis, _pairs(n, flip))  5.25 us
  transfers between devices with their start and end apart: 9, of which 7 were waited for; matrix products, arithmetic and copies ran while one was open for 22% of the time, Pallas kernels for 0%

profile of v4, /device:TPU:0, one launch (start us, length us, event | category | flops | bytes accessed | tf_op | source)
XLA Modules:
  0.0 139.7 jit_solution(10967757291133520586)
XLA Ops:
  0.0 0.8 fusion.50
  0.8 1.1 reduce_sum.18
  2.0 1.2 multiply_reduce_fusion
  3.2 1.1 multiply_add_fusion.1
  4.2 10.0 %all_to_all.38 = f32[8,4,2048]{2,0,1:T(8,128)S(1)} all-to-all(f32[8,4,2048]{2,0,1:T(8,128)S(1)} %bitcast.87), channel_id=1, replica_groups=mesh['groups'=2,'row'=4,'col'=4] {'row'}, dimensions={1} | all-to-all | bytes 524288 | tf_op jit(solution)/shard_map/all_to_all | solution.py:54
  14.3 2.6 %collective-permute-start = (f32[1,32,2048]{2,1,0:T(8,128)S(1)}, f32[1,32,2048]{2,1,0:T(8,128)S(1)}, u32[]{:S(2)}, u32[]{:S(2)}) collective-permute-start(f32[1,32,2048]{2,1,0:T(8,128)S(1)} %bitcast.74), channel_id=1, source_target_pairs={{0,2},{1,3},{2,0},{3,1},{4,6},{5,7},{6,4},{7,5},{8,10},{9,11},{10,... | collective-permute-start | bytes 786440 | tf_op jit(solution)/shard_map/ppermute | solution.py:21
  16.9 11.6 %collective-permute-done = f32[1,32,2048]{2,1,0:T(8,128)S(1)} collective-permute-done((f32[1,32,2048]{2,1,0:T(8,128)S(1)}, f32[1,32,2048]{2,1,0:T(8,128)S(1)}, u32[]{:S(2)}, u32[]{:S(2)}) %collective-permute-start) | collective-permute-done | bytes 262176 | tf_op jit(solution)/shard_map/ppermute | solution.py:21
  28.5 0.7 collective-permute-start.1
  29.3 12.1 %collective-permute-done.1 = f32[2,32,2048]{2,1,0:T(8,128)S(1)} collective-permute-done((f32[2,32,2048]{2,1,0:T(8,128)S(1)}, f32[2,32,2048]{2,1,0:T(8,128)S(1)}, u32[]{:S(2)}, u32[]{:S(2)}) %collective-permute-start.1) | collective-permute-done | bytes 524320 | tf_op jit(solution)/shard_map/ppermute | solution.py:21
  41.4 6.0 %fusion.12 = f32[128,1024]{1,0:T(8,128)S(1)} fusion(f32[2048,4096]{1,0:T(8,128)} %param.8, s32[]{:T(128)S(6)} %select_n.22, f32[32,2048]{1,0:T(8,128)S(1)} %get-tuple-element.12, f32[32,2048]{1,0:T(8,128)S(1)} %bitcast.80, f32[32,2048]{1,0:T(8,128)S(1)} %get-tuple-element.11, f32[32,2048]{1,0:T(8,128)S(1)} %bitcast.76), kind=kOutput, calls=%fused_computation.12 | convolution fusion | flops 1611399168 | bytes 9961476 | tf_op jit(solution)/shard_map/dot_general | solution.py:64
  47.4 6.0 %fusion.10 = f32[128,1024]{1,0:T(8,128)S(1)} fusion(f32[2048,4096]{1,0:T(8,128)} %param.8, s32[]{:T(128)S(6)} %select_n.23, f32[32,2048]{1,0:T(8,128)S(1)} %get-tuple-element.12, f32[32,2048]{1,0:T(8,128)S(1)} %bitcast.81, f32[32,2048]{1,0:T(8,128)S(1)} %get-tuple-element.11, f32[32,2048]{1,0:T(8,128)S(1)} %bitcast.77), kind=kOutput, calls=%fused_computation.10 | convolution fusion | flops 1611399168 | bytes 9961476 | tf_op jit(solution)/shard_map/dot_general | solution.py:64
  53.3 0.1 pad_maximum_fusion.1
  53.4 0.1 collective-permute-start.2
  53.5 0.0 copy-start
  53.5 0.0 copy-start.1
  53.5 6.0 %fusion.8 = f32[128,1024]{1,0:T(8,128)S(1)} fusion(f32[2048,4096]{1,0:T(8,128)} %param.8, s32[]{:T(128)S(6)} %select_n.24, f32[32,2048]{1,0:T(8,128)S(1)} %get-tuple-element.12, f32[32,2048]{1,0:T(8,128)S(1)} %bitcast.82, f32[32,2048]{1,0:T(8,128)S(1)} %get-tuple-element.11, f32[32,2048]{1,0:T(8,128)S(1)} %bitcast.78), kind=kOutput, calls=%fused_computation.8 | convolution fusion | flops 1611399168 | bytes 9961476 | tf_op jit(solution)/shard_map/dot_general | solution.py:64
  59.5 0.0 collective-permute-done.2
  59.5 0.1 fusion.27
  59.6 1.0 collective-permute-start.3
  60.6 0.7 dynamic_slice.32
  61.3 5.9 %fusion.14 = f32[128,1024]{1,0:T(8,128)S(1)} fusion(f32[2048,4096]{1,0:T(8,128)} %param.8, s32[]{:T(128)S(6)} %select_n.11, f32[32,2048]{1,0:T(8,128)S(1)} %get-tuple-element.12, f32[32,2048]{1,0:T(8,128)S(1)} %bitcast.83, f32[32,2048]{1,0:T(8,128)S(1)} %get-tuple-element.11, f32[32,2048]{1,0:T(8,128)S(1)} %bitcast.79), kind=kOutput, calls=%fused_computation.14 | convolution fusion | flops 1611399168 | bytes 9961476 | tf_op jit(solution)/shard_map/dot_general | solution.py:64
  67.2 6.7 %collective-permute-done.3 = f32[1,128,1024]{2,1,0:T(8,128)S(1)} collective-permute-done((f32[1,128,1024]{2,1,0:T(8,128)S(1)}, f32[1,128,1024]{2,1,0:T(8,128)S(1)}, u32[]{:S(2)}, u32[]{:S(2)}) %collective-permute-start.3) | collective-permute-done | bytes 524320 | tf_op jit(solution)/shard_map/ppermute | solution.py:71
  74.0 0.2 fusion.25
  74.2 0.1 collective-permute-start.5
  74.3 1.0 collective-permute-start.4
  75.3 0.9 collective-permute-done.5
  76.2 6.2 %fusion.4 = f32[128,2048]{1,0:T(8,128)S(1)} fusion(f32[128,1024]{1,0:T(8,128)S(1)} %collective-permute-done.5, f32[4096,2048]{1,0:T(8,128)} %param.10, s32[]{:T(128)S(6)} %select_n.22), kind=kOutput, calls=%fused_computation.4 | convolution fusion | flops 1610612736 | bytes 9961476 | tf_op jit(solution)/shard_map/dot_general | solution.py:86
  82.4 6.1 %fusion.16 = f32[128,2048]{1,0:T(8,128)S(1)} fusion(f32[128,2048]{1,0:T(8,128)S(1)} %fusion.4, f32[128,1024]{1,0:T(8,128)S(1)} %fusion.25, f32[4096,2048]{1,0:T(8,128)} %param.10, s32[]{:T(128)S(6)} %select_n.11), kind=kOutput, calls=%fused_computation.16 | convolution fusion | flops 1610874880 | bytes 11010052 | tf_op jit(solution)/shard_map/dot_general | solution.py:86
  88.5 0.1 collective-permute-done.4
  88.6 0.1 collective-permute-start.6
  88.7 6.1 %fusion.2 = f32[128,2048]{1,0:T(8,128)S(1)} fusion(f32[4096,2048]{1,0:T(8,128)} %param.10, s32[]{:T(128)S(6)} %select_n.24, f32[1,128,1024]{2,1,0:T(8,128)S(1)} %collective-permute-done.4), kind=kOutput, calls=%fused_computation.2 | convolution fusion | flops 1610612736 | bytes 9961476 | tf_op jit(solution)/shard_map/dot_general | solution.py:86
  94.8 0.0 collective-permute-done.6
  94.8 6.1 %add_add_fusion = f32[128,2048]{1,0:T(8,128)S(1)} fusion(f32[128,2048]{1,0:T(8,128)S(1)} %fusion.16, f32[128,2048]{1,0:T(8,128)S(1)} %fusion.2, f32[4096,2048]{1,0:T(8,128)} %param.10, s32[]{:T(128)S(6)} %select_n.23, f32[1,128,1024]{2,1,0:T(8,128)S(1)} %collective-permute-done.6), kind=kOutput, calls=%fused_computation.19 | convolution fusion | flops 1611137024 | bytes 12058628 | tf_op jit(solution)/shard_map/dot_general | solution.py:86
  101.0 1.8 %collective-permute-start.7 = (f32[2,32,2048]{2,1,0:T(8,128)S(1)}, f32[2,32,2048]{2,1,0:T(8,128)S(1)}, u32[]{:S(2)}, u32[]{:S(2)}) collective-permute-start(f32[2,32,2048]{2,1,0:T(8,128)S(1)} %pad_maximum_fusion.3), channel_id=1, source_target_pairs={{0,1},{1,0},{2,3},{3,2},{4,5},{5,4},{6,7},{7,6},{8,9},{9,8},{10,11... | collective-permute-start | bytes 1572872 | tf_op jit(solution)/shard_map/ppermute | solution.py:34
  102.9 12.5 %collective-permute-done.7 = f32[2,32,2048]{2,1,0:T(8,128)S(1)} collective-permute-done((f32[2,32,2048]{2,1,0:T(8,128)S(1)}, f32[2,32,2048]{2,1,0:T(8,128)S(1)}, u32[]{:S(2)}, u32[]{:S(2)}) %collective-permute-start.7) | collective-permute-done | bytes 524320 | tf_op jit(solution)/shard_map/ppermute | solution.py:34
  115.4 3.4 %collective-permute-start.8 = (f32[1,32,2048]{2,1,0:T(8,128)S(1)}, f32[1,32,2048]{2,1,0:T(8,128)S(1)}, u32[]{:S(2)}, u32[]{:S(2)}) collective-permute-start(f32[1,32,2048]{2,1,0:T(8,128)S(1)} %fusion.38), channel_id=1, source_target_pairs={{0,2},{1,3},{2,0},{3,1},{4,6},{5,7},{6,4},{7,5},{8,10},{9,11},{10,... | collective-permute-start | bytes 786440 | tf_op jit(solution)/shard_map/ppermute | solution.py:34
  118.8 11.6 %collective-permute-done.8 = f32[1,32,2048]{2,1,0:T(8,128)S(1)} collective-permute-done((f32[1,32,2048]{2,1,0:T(8,128)S(1)}, f32[1,32,2048]{2,1,0:T(8,128)S(1)}, u32[]{:S(2)}, u32[]{:S(2)}) %collective-permute-start.8) | collective-permute-done | bytes 262176 | tf_op jit(solution)/shard_map/ppermute | solution.py:34
  130.4 0.1 fusion.41
  130.5 8.4 %all_to_all.39 = f32[4,8,2048]{2,1,0:T(8,128)S(1)} all-to-all(f32[4,8,2048]{2,1,0:T(8,128)S(1)} %fusion.41), channel_id=1, replica_groups=mesh['groups'=2,'row'=4,'col'=4] {'row'}, dimensions={0} | all-to-all | bytes 524288 | tf_op jit(solution)/shard_map/all_to_all | solution.py:102
  138.9 0.0 copy-done
  138.9 0.0 copy-done.1
  138.9 0.8 multiply_add_fusion
  (7 shorter events, 0.2 us)
Async XLA Ops:
  14.3 14.2 %collective-permute-start = (f32[1,32,2048]{2,1,0:T(8,128)S(1)}, f32[1,32,2048]{2,1,0:T(8,128)S(1)}, u32[]{:S(2)}, u32[]{:S(2)}) collective-permute-start(f32[1,32,2048]{2,1,0:T(8,128)S(1)} %bitcast.74), channel_id=1, source_target_pairs={{0,2},{1,3},{2,0},{3,1},{4,6},{5,7},{6,4},{7,5},{8,10},{9,11},{10,... | collective-permute-start | bytes 786440 | tf_op jit(solution)/shard_map/ppermute | solution.py:21
  28.5 12.8 %collective-permute-start.1 = (f32[2,32,2048]{2,1,0:T(8,128)S(1)}, f32[2,32,2048]{2,1,0:T(8,128)S(1)}, u32[]{:S(2)}, u32[]{:S(2)}) collective-permute-start(f32[2,32,2048]{2,1,0:T(8,128)S(1)} %pad_maximum_fusion.2), channel_id=1, source_target_pairs={{0,1},{1,0},{2,3},{3,2},{4,5},{5,4},{6,7},{7,6},{8,9},{9,8},{10,11... | collective-permute-start | bytes 1572872 | tf_op jit(solution)/shard_map/ppermute | solution.py:21
  53.4 6.1 %collective-permute-start.2 = (f32[2,128,1024]{2,1,0:T(8,128)S(1)}, f32[2,128,1024]{2,1,0:T(8,128)S(1)}, u32[]{:S(2)}, u32[]{:S(2)}) collective-permute-start(f32[2,128,1024]{2,1,0:T(8,128)S(1)} %pad_maximum_fusion.1), channel_id=1, source_target_pairs={{0,4},{4,0},{8,12},{12,8},{1,5},{5,1},{9,13},{13,9},{2,6},{6,2},{1... | collective-permute-start | bytes 3145736 | tf_op jit(solution)/shard_map/ppermute | solution.py:71
  53.5 85.4 %copy-start = (f32[8,8192]{1,0:T(8,128)S(1)}, f32[8,8192]{1,0:T(8,128)}, u32[]{:S(2)}) copy-start(f32[8,8192]{1,0:T(8,128)} %param.6) | copy-start | bytes 786436
  53.5 85.4 %copy-start.1 = (f32[8192]{0:T(1024)S(1)}, f32[8192]{0:T(1024)}, u32[]{:S(2)}) copy-start(f32[8192]{0:T(1024)} %param.11) | copy-start | bytes 98308
  59.6 14.4 %collective-permute-start.3 = (f32[1,128,1024]{2,1,0:T(8,128)S(1)}, f32[1,128,1024]{2,1,0:T(8,128)S(1)}, u32[]{:S(2)}, u32[]{:S(2)}) collective-permute-start(f32[1,128,1024]{2,1,0:T(8,128)S(1)} %fusion.27), channel_id=1, source_target_pairs={{0,8},{4,12},{8,0},{12,4},{1,9},{5,13},{9,1},{13,5},{2,10},{6,14},... | collective-permute-start | bytes 1572872 | tf_op jit(solution)/shard_map/ppermute | solution.py:71
  74.2 2.0 %collective-permute-start.5 = (f32[128,1024]{1,0:T(8,128)S(1)}, f32[128,1024]{1,0:T(8,128)S(1)}, u32[]{:S(2)}, u32[]{:S(2)}) collective-permute-start(f32[128,1024]{1,0:T(8,128)S(1)} %fusion.25), channel_id=1, source_target_pairs={{0,4},{4,0},{8,12},{12,8},{1,5},{5,1},{9,13},{13,9},{2,6},{6,2},{1... | collective-permute-start | bytes 1572872 | tf_op jit(solution)/shard_map/ppermute | solution.py:76
  74.3 14.3 %collective-permute-start.4 = (f32[1,128,1024]{2,1,0:T(8,128)S(1)}, f32[1,128,1024]{2,1,0:T(8,128)S(1)}, u32[]{:S(2)}, u32[]{:S(2)}) collective-permute-start(f32[1,128,1024]{2,1,0:T(8,128)S(1)} %bitcast.84), channel_id=1, source_target_pairs={{0,8},{4,12},{8,0},{12,4},{1,9},{5,13},{9,1},{13,5},{2,10},{6,14},... | collective-permute-start | bytes 1572872 | tf_op jit(solution)/shard_map/ppermute | solution.py:80
  88.6 6.2 %collective-permute-start.6 = (f32[1,128,1024]{2,1,0:T(8,128)S(1)}, f32[1,128,1024]{2,1,0:T(8,128)S(1)}, u32[]{:S(2)}, u32[]{:S(2)}) collective-permute-start(f32[1,128,1024]{2,1,0:T(8,128)S(1)} %collective-permute-done.4), channel_id=1, source_target_pairs={{0,4},{4,0},{8,12},{12,8},{1,5},{5,1},{9,13},{13,9},{2,6},{6,2},{1... | collective-permute-start | bytes 1572872 | tf_op jit(solution)/shard_map/ppermute | solution.py:94
  101.0 14.3 %collective-permute-start.7 = (f32[2,32,2048]{2,1,0:T(8,128)S(1)}, f32[2,32,2048]{2,1,0:T(8,128)S(1)}, u32[]{:S(2)}, u32[]{:S(2)}) collective-permute-start(f32[2,32,2048]{2,1,0:T(8,128)S(1)} %pad_maximum_fusion.3), channel_id=1, source_target_pairs={{0,1},{1,0},{2,3},{3,2},{4,5},{5,4},{6,7},{7,6},{8,9},{9,8},{10,11... | collective-permute-start | bytes 1572872 | tf_op jit(solution)/shard_map/ppermute | solution.py:34
  115.4 15.1 %collective-permute-start.8 = (f32[1,32,2048]{2,1,0:T(8,128)S(1)}, f32[1,32,2048]{2,1,0:T(8,128)S(1)}, u32[]{:S(2)}, u32[]{:S(2)}) collective-permute-start(f32[1,32,2048]{2,1,0:T(8,128)S(1)} %fusion.38), channel_id=1, source_target_pairs={{0,2},{1,3},{2,0},{3,1},{4,6},{5,7},{6,4},{7,5},{8,10},{9,11},{10,... | collective-permute-start | bytes 786440 | tf_op jit(solution)/shard_map/ppermute | solution.py:34

commit v5 on v4

--- a/solution.py
+++ b/solution.py
@@ -37,6 +37,14 @@
     return held[0]
 
 
+def _exchange_abs(blocks, axis, n, idx):
+    got = [blocks[idx]]
+    for d in range(1, n):
+        got.append(lax.ppermute(blocks[idx ^ d], axis, _pairs(n, d)))
+    rel = jnp.stack(got)
+    return jnp.stack([rel[s ^ idx] for s in range(n)])
+
+
 def local(tokens, modulation, up_weight, up_bias, down_weight, down_bias):
     n_row = lax.axis_size("row")
     tok_dev = tokens.shape[0]
@@ -51,13 +59,15 @@
     spread_sq = jnp.mean(centred * centred, axis=1, keepdims=True)
     normed = centred * lax.rsqrt(spread_sq + layer_eps)
     mixed = normed * (1.0 + scale_vec) + shift_vec
-    columns = lax.all_to_all(mixed, "row", split_axis=1, concat_axis=0, tiled=True)
+    r = lax.axis_index("row")
+    d_blk = mixed.shape[1] // n_row
+    sent_in = mixed.reshape(tok_dev, n_row, d_blk).swapaxes(0, 1)
+    columns = _exchange_abs(sent_in, "row", n_row, r).reshape(n_row * tok_dev, d_blk)
     n_col = lax.axis_size("col")
     gathered = _gather_rel(columns, "col", n_col)
     n_pos = gathered.shape[0]
     ff_blk = up_weight.shape[1]
     quarter = ff_blk // n_row
-    r = lax.axis_index("row")
 
     def up_block(d):
         w = lax.dynamic_slice_in_dim(up_weight, (r ^ d) * quarter, quarter, 1)
@@ -99,7 +109,8 @@
         for d in far:
             partial_out = partial_out + down_term(d ^ 1)
     out_share = _scatter_rel(partial_out, "col", n_col)
-    returned = lax.all_to_all(out_share, "row", split_axis=0, concat_axis=1, tiled=True)
+    back = _exchange_abs(out_share.reshape(n_row, tok_dev, d_blk), "row", n_row, r)
+    returned = back.swapaxes(0, 1).reshape(tok_dev, n_row * d_blk)
     return tokens + gate_vec * (returned + down_bias)
 
 

time: 140 us -> 136 us (0.971)
  blocking collectives: 18.5 us -> 0 us
  waiting for transfers between devices: 55.5 us -> 63.1 us
  starting transfers between devices: 10.9 us -> 17.3 us
    all_to_all x2 -> x0, blocking collectives: 18.5 us -> none  [the longest x1 10 us: local(): lax.all_to_all(mixed, 'row', split_axis=1, concat_axis=0, tiled=True)]
    ppermute x0 -> x6, waiting for transfers between devices: none -> 7.91 us  [_exchange_abs(): got.append(lax.ppermute(blocks[idx ^ d], axis, _pairs(n, d)))]
    ppermute x0 -> x6, starting transfers between devices: none -> 5.07 us  [_exchange_abs(): got.append(lax.ppermute(blocks[idx ^ d], axis, _pairs(n, d)))]
  transfers between devices with their start and end apart: 9 -> 15, of which waited for: 7 -> 10; matrix products, arithmetic and copies ran while one was open for 22% -> 23% of each run, Pallas kernels for 0% -> 0%
where the time goes in v5:
time: 136 us; the launch traced here: 135 us
  waiting for transfers between devices  63.1 us (46%)
  matrix products  48.1 us (35%)
  starting transfers between devices  17.3 us (13%)
  other arithmetic  5.64 us (4%)
    ppermute x2, waiting for transfers between devices, _scatter_rel(): lax.ppermute(jnp.stack([held[d] for d in sent]), axis, _pairs(n, flip))  24.7 us
    ppermute x2, waiting for transfers between devices, _gather_rel(): lax.ppermute(jnp.stack([held[k] for k in keys]), axis, _pairs(n, flip))  24.4 us
    dot_general x4, matrix products, down_term(): jnp.dot(acts[d], w, precision=lax.Precision.HIGH, preferred_element_type=...  24.3 us
    dot_general x4, matrix products, up_block(): jnp.dot(gathered, w, precision=lax.Precision.HIGH, preferred_element_type...  23.8 us
    ppermute x6, waiting for transfers between devices, _exchange_abs(): got.append(lax.ppermute(blocks[idx ^ d], axis, _pairs(n, d)))  7.91 us
    ppermute x2, waiting for transfers between devices, local(): lax.ppermute(jnp.stack([held[d] for d in sent]), 'row', _pairs(n_row, flip))  5.96 us
    ppermute x6, starting transfers between devices, _exchange_abs(): got.append(lax.ppermute(blocks[idx ^ d], axis, _pairs(n, d)))  5.07 us
    ppermute x2, starting transfers between devices, _scatter_rel(): lax.ppermute(jnp.stack([held[d] for d in sent]), axis, _pairs(n, flip))  4.75 us
  transfers between devices with their start and end apart: 15, of which 10 were waited for; matrix products, arithmetic and copies ran while one was open for 23% of the time, Pallas kernels for 0%

profile of v5, /device:TPU:0, one launch (start us, length us, event | category | flops | bytes accessed | tf_op | source)
XLA Modules:
  0.0 135.4 jit_solution(17336838062585038889)
XLA Ops:
  0.0 1.1 reduce_sum.18
  1.1 1.2 multiply_reduce_fusion
  2.3 0.8 fusion.52
  3.2 1.1 multiply_add_fusion.1
  4.3 2.4 %collective-permute-start.2 = (f32[8,2048]{1,0:T(8,128)S(1)}, f32[8,2048]{1,0:T(8,128)S(1)}, u32[]{:S(2)}, u32[]{:S(2)}) collective-permute-start(f32[8,2048]{1,0:T(8,128)S(1)} %get-tuple-element.28), channel_id=1, source_target_pairs={{0,12},{4,8},{8,4},{12,0},{1,13},{5,9},{9,5},{13,1},{2,14},{6,10},... | collective-permute-start | bytes 196616 | tf_op jit(solution)/shard_map/ppermute | solution.py:43
  6.7 0.6 collective-permute-start.1
  7.4 0.0 collective-permute-start
  7.4 1.8 %collective-permute-done.2 = f32[8,2048]{1,0:T(8,128)S(1)} collective-permute-done((f32[8,2048]{1,0:T(8,128)S(1)}, f32[8,2048]{1,0:T(8,128)S(1)}, u32[]{:S(2)}, u32[]{:S(2)}) %collective-permute-start.2) | collective-permute-done | bytes 65568 | tf_op jit(solution)/shard_map/ppermute | solution.py:43
  9.2 2.2 %collective-permute-done.1 = f32[8,2048]{1,0:T(8,128)S(1)} collective-permute-done((f32[8,2048]{1,0:T(8,128)S(1)}, f32[8,2048]{1,0:T(8,128)S(1)}, u32[]{:S(2)}, u32[]{:S(2)}) %collective-permute-start.1) | collective-permute-done | bytes 65568 | tf_op jit(solution)/shard_map/ppermute | solution.py:43
  11.4 0.0 collective-permute-done
  11.5 2.8 %collective-permute-start.3 = (f32[1,32,2048]{2,1,0:T(8,128)S(1)}, f32[1,32,2048]{2,1,0:T(8,128)S(1)}, u32[]{:S(2)}, u32[]{:S(2)}) collective-permute-start(f32[1,32,2048]{2,1,0:T(8,128)S(1)} %get-tuple-element.22), channel_id=1, source_target_pairs={{0,2},{1,3},{2,0},{3,1},{4,6},{5,7},{6,4},{7,5},{8,10},{9,11},{10,... | collective-permute-start | bytes 786440 | tf_op jit(solution)/shard_map/ppermute | solution.py:21
  14.4 12.0 %collective-permute-done.3 = f32[1,32,2048]{2,1,0:T(8,128)S(1)} collective-permute-done((f32[1,32,2048]{2,1,0:T(8,128)S(1)}, f32[1,32,2048]{2,1,0:T(8,128)S(1)}, u32[]{:S(2)}, u32[]{:S(2)}) %collective-permute-start.3) | collective-permute-done | bytes 262176 | tf_op jit(solution)/shard_map/ppermute | solution.py:21
  26.5 0.8 collective-permute-start.4
  27.2 12.4 %collective-permute-done.4 = f32[2,32,2048]{2,1,0:T(8,128)S(1)} collective-permute-done((f32[2,32,2048]{2,1,0:T(8,128)S(1)}, f32[2,32,2048]{2,1,0:T(8,128)S(1)}, u32[]{:S(2)}, u32[]{:S(2)}) %collective-permute-start.4) | collective-permute-done | bytes 524320 | tf_op jit(solution)/shard_map/ppermute | solution.py:21
  39.6 6.0 %fusion.12 = f32[128,1024]{1,0:T(8,128)S(1)} fusion(f32[2048,4096]{1,0:T(8,128)} %param.8, s32[]{:T(128)S(6)} %select_n.24, f32[32,2048]{1,0:T(8,128)S(1)} %get-tuple-element.12, f32[32,2048]{1,0:T(8,128)S(1)} %bitcast.93, f32[32,2048]{1,0:T(8,128)S(1)} %get-tuple-element.11, f32[32,2048]{1,0:T(8,128)S(1)} %get-tuple-element.21), kind=kOutput, calls=%fused_computation.12 | convolution fusion | flops 1611399168 | bytes 9961476 | tf_op jit(solution)/shard_map/dot_general | solution.py:74
  45.6 6.0 %fusion.10 = f32[128,1024]{1,0:T(8,128)S(1)} fusion(f32[2048,4096]{1,0:T(8,128)} %param.8, s32[]{:T(128)S(6)} %select_n.25, f32[32,2048]{1,0:T(8,128)S(1)} %get-tuple-element.12, f32[32,2048]{1,0:T(8,128)S(1)} %bitcast.94, f32[32,2048]{1,0:T(8,128)S(1)} %get-tuple-element.11, f32[32,2048]{1,0:T(8,128)S(1)} %get-tuple-element.21), kind=kOutput, calls=%fused_computation.10 | convolution fusion | flops 1611399168 | bytes 9961476 | tf_op jit(solution)/shard_map/dot_general | solution.py:74
  51.6 0.1 pad_maximum_fusion.1
  51.6 0.1 collective-permute-start.5
  51.7 6.0 %fusion.8 = f32[128,1024]{1,0:T(8,128)S(1)} fusion(f32[2048,4096]{1,0:T(8,128)} %param.8, s32[]{:T(128)S(6)} %select_n.26, f32[32,2048]{1,0:T(8,128)S(1)} %get-tuple-element.12, f32[32,2048]{1,0:T(8,128)S(1)} %bitcast.95, f32[32,2048]{1,0:T(8,128)S(1)} %get-tuple-element.11, f32[32,2048]{1,0:T(8,128)S(1)} %get-tuple-element.21), kind=kOutput, calls=%fused_computation.8 | convolution fusion | flops 1611399168 | bytes 9961476 | tf_op jit(solution)/shard_map/dot_general | solution.py:74
  57.7 0.0 copy-start
  57.7 0.0 copy-start.1
  57.7 0.0 collective-permute-done.5
  57.7 0.1 fusion.27
  57.8 1.8 %collective-permute-start.6 = (f32[1,128,1024]{2,1,0:T(8,128)S(1)}, f32[1,128,1024]{2,1,0:T(8,128)S(1)}, u32[]{:S(2)}, u32[]{:S(2)}) collective-permute-start(f32[1,128,1024]{2,1,0:T(8,128)S(1)} %fusion.27), channel_id=1, source_target_pairs={{0,8},{4,12},{8,0},{12,4},{1,9},{5,13},{9,1},{13,5},{2,10},{6,14},... | collective-permute-start | bytes 1572872 | tf_op jit(solution)/shard_map/ppermute | solution.py:81
  59.6 0.7 dynamic_slice.79
  60.3 5.9 %fusion.14 = f32[128,1024]{1,0:T(8,128)S(1)} fusion(f32[2048,4096]{1,0:T(8,128)} %param.8, s32[]{:T(128)S(6)} %select_n.23, f32[32,2048]{1,0:T(8,128)S(1)} %get-tuple-element.12, f32[32,2048]{1,0:T(8,128)S(1)} %bitcast.96, f32[32,2048]{1,0:T(8,128)S(1)} %get-tuple-element.11, f32[32,2048]{1,0:T(8,128)S(1)} %get-tuple-element.21), kind=kOutput, calls=%fused_computation.14 | convolution fusion | flops 1611399168 | bytes 9961476 | tf_op jit(solution)/shard_map/dot_general | solution.py:74
  66.2 6.0 %collective-permute-done.6 = f32[1,128,1024]{2,1,0:T(8,128)S(1)} collective-permute-done((f32[1,128,1024]{2,1,0:T(8,128)S(1)}, f32[1,128,1024]{2,1,0:T(8,128)S(1)}, u32[]{:S(2)}, u32[]{:S(2)}) %collective-permute-start.6) | collective-permute-done | bytes 524320 | tf_op jit(solution)/shard_map/ppermute | solution.py:81
  72.2 0.2 fusion.25
  72.4 0.1 collective-permute-start.8
  72.5 2.0 %collective-permute-start.7 = (f32[1,128,1024]{2,1,0:T(8,128)S(1)}, f32[1,128,1024]{2,1,0:T(8,128)S(1)}, u32[]{:S(2)}, u32[]{:S(2)}) collective-permute-start(f32[1,128,1024]{2,1,0:T(8,128)S(1)} %bitcast.97), channel_id=1, source_target_pairs={{0,8},{4,12},{8,0},{12,4},{1,9},{5,13},{9,1},{13,5},{2,10},{6,14},... | collective-permute-start | bytes 1572872 | tf_op jit(solution)/shard_map/ppermute | solution.py:90
  74.4 6.1 %fusion.4 = f32[128,2048]{1,0:T(8,128)S(1)} fusion(f32[128,1024]{1,0:T(8,128)S(1)} %collective-permute-done.8, f32[4096,2048]{1,0:T(8,128)} %param.10, s32[]{:T(128)S(6)} %select_n.24), kind=kOutput, calls=%fused_computation.4 | convolution fusion | flops 1610612736 | bytes 9961476 | tf_op jit(solution)/shard_map/dot_general | solution.py:96
  80.5 6.1 %fusion.16 = f32[128,2048]{1,0:T(8,128)S(1)} fusion(f32[128,2048]{1,0:T(8,128)S(1)} %fusion.4, f32[128,1024]{1,0:T(8,128)S(1)} %fusion.25, f32[4096,2048]{1,0:T(8,128)} %param.10, s32[]{:T(128)S(6)} %select_n.23), kind=kOutput, calls=%fused_computation.16 | convolution fusion | flops 1610874880 | bytes 11010052 | tf_op jit(solution)/shard_map/dot_general | solution.py:96
  86.6 0.2 collective-permute-done.7
  86.8 6.1 %fusion.2 = f32[128,2048]{1,0:T(8,128)S(1)} fusion(f32[4096,2048]{1,0:T(8,128)} %param.10, s32[]{:T(128)S(6)} %select_n.26, f32[1,128,1024]{2,1,0:T(8,128)S(1)} %collective-permute-done.7), kind=kOutput, calls=%fused_computation.2 | convolution fusion | flops 1610612736 | bytes 9961476 | tf_op jit(solution)/shard_map/dot_general | solution.py:96
  92.9 0.0 collective-permute-done.9
  92.9 6.1 %add_add_fusion = f32[128,2048]{1,0:T(8,128)S(1)} fusion(f32[128,2048]{1,0:T(8,128)S(1)} %fusion.16, f32[128,2048]{1,0:T(8,128)S(1)} %fusion.2, f32[4096,2048]{1,0:T(8,128)} %param.10, s32[]{:T(128)S(6)} %select_n.25, f32[1,128,1024]{2,1,0:T(8,128)S(1)} %collective-permute-done.9), kind=kOutput, calls=%fused_computation.19 | convolution fusion | flops 1611137024 | bytes 12058628 | tf_op jit(solution)/shard_map/dot_general | solution.py:96
  99.1 1.6 %collective-permute-start.10 = (f32[2,32,2048]{2,1,0:T(8,128)S(1)}, f32[2,32,2048]{2,1,0:T(8,128)S(1)}, u32[]{:S(2)}, u32[]{:S(2)}) collective-permute-start(f32[2,32,2048]{2,1,0:T(8,128)S(1)} %pad_maximum_fusion.3), channel_id=1, source_target_pairs={{0,1},{1,0},{2,3},{3,2},{4,5},{5,4},{6,7},{7,6},{8,9},{9,8},{10,11... | collective-permute-start | bytes 1572872 | tf_op jit(solution)/shard_map/ppermute | solution.py:34
  100.7 12.8 %collective-permute-done.10 = f32[2,32,2048]{2,1,0:T(8,128)S(1)} collective-permute-done((f32[2,32,2048]{2,1,0:T(8,128)S(1)}, f32[2,32,2048]{2,1,0:T(8,128)S(1)}, u32[]{:S(2)}, u32[]{:S(2)}) %collective-permute-start.10) | collective-permute-done | bytes 524320 | tf_op jit(solution)/shard_map/ppermute | solution.py:34
  113.5 3.2 %collective-permute-start.11 = (f32[1,32,2048]{2,1,0:T(8,128)S(1)}, f32[1,32,2048]{2,1,0:T(8,128)S(1)}, u32[]{:S(2)}, u32[]{:S(2)}) collective-permute-start(f32[1,32,2048]{2,1,0:T(8,128)S(1)} %fusion.38), channel_id=1, source_target_pairs={{0,2},{1,3},{2,0},{3,1},{4,6},{5,7},{6,4},{7,5},{8,10},{9,11},{10,... | collective-permute-start | bytes 786440 | tf_op jit(solution)/shard_map/ppermute | solution.py:34
  116.7 11.8 %collective-permute-done.11 = f32[1,32,2048]{2,1,0:T(8,128)S(1)} collective-permute-done((f32[1,32,2048]{2,1,0:T(8,128)S(1)}, f32[1,32,2048]{2,1,0:T(8,128)S(1)}, u32[]{:S(2)}, u32[]{:S(2)}) %collective-permute-start.11) | collective-permute-done | bytes 262176 | tf_op jit(solution)/shard_map/ppermute | solution.py:34
  128.6 0.1 fusion.41
  128.6 0.5 collective-permute-start.14
  129.1 1.3 collective-permute-start.13
  130.4 0.1 collective-permute-start.12
  130.6 2.3 %collective-permute-done.14 = f32[8,2048]{1,0:T(8,128)S(1)} collective-permute-done((f32[8,2048]{1,0:T(8,128)S(1)}, f32[8,2048]{1,0:T(8,128)S(1)}, u32[]{:S(2)}, u32[]{:S(2)}) %collective-permute-start.14) | collective-permute-done | bytes 65568 | tf_op jit(solution)/shard_map/ppermute | solution.py:43
  132.9 1.6 %collective-permute-done.13 = f32[8,2048]{1,0:T(8,128)S(1)} collective-permute-done((f32[8,2048]{1,0:T(8,128)S(1)}, f32[8,2048]{1,0:T(8,128)S(1)}, u32[]{:S(2)}, u32[]{:S(2)}) %collective-permute-start.13) | collective-permute-done | bytes 65568 | tf_op jit(solution)/shard_map/ppermute | solution.py:43
  134.5 0.0 collective-permute-done.12
  134.6 0.8 multiply_add_fusion
  (19 shorter events, 0.4 us)
Async XLA Ops:
  4.3 4.9 %collective-permute-start.2 = (f32[8,2048]{1,0:T(8,128)S(1)}, f32[8,2048]{1,0:T(8,128)S(1)}, u32[]{:S(2)}, u32[]{:S(2)}) collective-permute-start(f32[8,2048]{1,0:T(8,128)S(1)} %get-tuple-element.28), channel_id=1, source_target_pairs={{0,12},{4,8},{8,4},{12,0},{1,13},{5,9},{9,5},{13,1},{2,14},{6,10},... | collective-permute-start | bytes 196616 | tf_op jit(solution)/shard_map/ppermute | solution.py:43
  6.7 4.7 %collective-permute-start.1 = (f32[8,2048]{1,0:T(8,128)S(1)}, f32[8,2048]{1,0:T(8,128)S(1)}, u32[]{:S(2)}, u32[]{:S(2)}) collective-permute-start(f32[8,2048]{1,0:T(8,128)S(1)} %get-tuple-element.29), channel_id=1, source_target_pairs={{0,8},{4,12},{8,0},{12,4},{1,9},{5,13},{9,1},{13,5},{2,10},{6,14},... | collective-permute-start | bytes 196616 | tf_op jit(solution)/shard_map/ppermute | solution.py:43
  7.4 4.0 %collective-permute-start = (f32[8,2048]{1,0:T(8,128)S(1)}, f32[8,2048]{1,0:T(8,128)S(1)}, u32[]{:S(2)}, u32[]{:S(2)}) collective-permute-start(f32[8,2048]{1,0:T(8,128)S(1)} %get-tuple-element.30), channel_id=1, source_target_pairs={{0,4},{4,0},{8,12},{12,8},{1,5},{5,1},{9,13},{13,9},{2,6},{6,2},{1... | collective-permute-start | bytes 196616 | tf_op jit(solution)/shard_map/ppermute | solution.py:43
  11.5 14.9 %collective-permute-start.3 = (f32[1,32,2048]{2,1,0:T(8,128)S(1)}, f32[1,32,2048]{2,1,0:T(8,128)S(1)}, u32[]{:S(2)}, u32[]{:S(2)}) collective-permute-start(f32[1,32,2048]{2,1,0:T(8,128)S(1)} %get-tuple-element.22), channel_id=1, source_target_pairs={{0,2},{1,3},{2,0},{3,1},{4,6},{5,7},{6,4},{7,5},{8,10},{9,11},{10,... | collective-permute-start | bytes 786440 | tf_op jit(solution)/shard_map/ppermute | solution.py:21
  26.5 13.1 %collective-permute-start.4 = (f32[2,32,2048]{2,1,0:T(8,128)S(1)}, f32[2,32,2048]{2,1,0:T(8,128)S(1)}, u32[]{:S(2)}, u32[]{:S(2)}) collective-permute-start(f32[2,32,2048]{2,1,0:T(8,128)S(1)} %pad_maximum_fusion.2), channel_id=1, source_target_pairs={{0,1},{1,0},{2,3},{3,2},{4,5},{5,4},{6,7},{7,6},{8,9},{9,8},{10,11... | collective-permute-start | bytes 1572872 | tf_op jit(solution)/shard_map/ppermute | solution.py:21
  51.6 6.1 %collective-permute-start.5 = (f32[2,128,1024]{2,1,0:T(8,128)S(1)}, f32[2,128,1024]{2,1,0:T(8,128)S(1)}, u32[]{:S(2)}, u32[]{:S(2)}) collective-permute-start(f32[2,128,1024]{2,1,0:T(8,128)S(1)} %pad_maximum_fusion.1), channel_id=1, source_target_pairs={{0,4},{4,0},{8,12},{12,8},{1,5},{5,1},{9,13},{13,9},{2,6},{6,2},{1... | collective-permute-start | bytes 3145736 | tf_op jit(solution)/shard_map/ppermute | solution.py:81
  57.7 76.9 %copy-start = (f32[8,8192]{1,0:T(8,128)S(1)}, f32[8,8192]{1,0:T(8,128)}, u32[]{:S(2)}) copy-start(f32[8,8192]{1,0:T(8,128)} %param.6) | copy-start | bytes 786436
  57.7 76.9 %copy-start.1 = (f32[8192]{0:T(1024)S(1)}, f32[8192]{0:T(1024)}, u32[]{:S(2)}) copy-start(f32[8192]{0:T(1024)} %param.11) | copy-start | bytes 98308
  57.8 14.4 %collective-permute-start.6 = (f32[1,128,1024]{2,1,0:T(8,128)S(1)}, f32[1,128,1024]{2,1,0:T(8,128)S(1)}, u32[]{:S(2)}, u32[]{:S(2)}) collective-permute-start(f32[1,128,1024]{2,1,0:T(8,128)S(1)} %fusion.27), channel_id=1, source_target_pairs={{0,8},{4,12},{8,0},{12,4},{1,9},{5,13},{9,1},{13,5},{2,10},{6,14},... | collective-permute-start | bytes 1572872 | tf_op jit(solution)/shard_map/ppermute | solution.py:81
  72.4 2.0 %collective-permute-start.8 = (f32[128,1024]{1,0:T(8,128)S(1)}, f32[128,1024]{1,0:T(8,128)S(1)}, u32[]{:S(2)}, u32[]{:S(2)}) collective-permute-start(f32[128,1024]{1,0:T(8,128)S(1)} %fusion.25), channel_id=1, source_target_pairs={{0,4},{4,0},{8,12},{12,8},{1,5},{5,1},{9,13},{13,9},{2,6},{6,2},{1... | collective-permute-start | bytes 1572872 | tf_op jit(solution)/shard_map/ppermute | solution.py:86
  72.5 14.3 %collective-permute-start.7 = (f32[1,128,1024]{2,1,0:T(8,128)S(1)}, f32[1,128,1024]{2,1,0:T(8,128)S(1)}, u32[]{:S(2)}, u32[]{:S(2)}) collective-permute-start(f32[1,128,1024]{2,1,0:T(8,128)S(1)} %bitcast.97), channel_id=1, source_target_pairs={{0,8},{4,12},{8,0},{12,4},{1,9},{5,13},{9,1},{13,5},{2,10},{6,14},... | collective-permute-start | bytes 1572872 | tf_op jit(solution)/shard_map/ppermute | solution.py:90
  86.8 6.1 %collective-permute-start.9 = (f32[1,128,1024]{2,1,0:T(8,128)S(1)}, f32[1,128,1024]{2,1,0:T(8,128)S(1)}, u32[]{:S(2)}, u32[]{:S(2)}) collective-permute-start(f32[1,128,1024]{2,1,0:T(8,128)S(1)} %collective-permute-done.7), channel_id=1, source_target_pairs={{0,4},{4,0},{8,12},{12,8},{1,5},{5,1},{9,13},{13,9},{2,6},{6,2},{1... | collective-permute-start | bytes 1572872 | tf_op jit(solution)/shard_map/ppermute | solution.py:104
  99.1 14.4 %collective-permute-start.10 = (f32[2,32,2048]{2,1,0:T(8,128)S(1)}, f32[2,32,2048]{2,1,0:T(8,128)S(1)}, u32[]{:S(2)}, u32[]{:S(2)}) collective-permute-start(f32[2,32,2048]{2,1,0:T(8,128)S(1)} %pad_maximum_fusion.3), channel_id=1, source_target_pairs={{0,1},{1,0},{2,3},{3,2},{4,5},{5,4},{6,7},{7,6},{8,9},{9,8},{10,11... | collective-permute-start | bytes 1572872 | tf_op jit(solution)/shard_map/ppermute | solution.py:34
  113.5 15.0 %collective-permute-start.11 = (f32[1,32,2048]{2,1,0:T(8,128)S(1)}, f32[1,32,2048]{2,1,0:T(8,128)S(1)}, u32[]{:S(2)}, u32[]{:S(2)}) collective-permute-start(f32[1,32,2048]{2,1,0:T(8,128)S(1)} %fusion.38), channel_id=1, source_target_pairs={{0,2},{1,3},{2,0},{3,1},{4,6},{5,7},{6,4},{7,5},{8,10},{9,11},{10,... | collective-permute-start | bytes 786440 | tf_op jit(solution)/shard_map/ppermute | solution.py:34
  128.6 4.2 %collective-permute-start.14 = (f32[8,2048]{1,0:T(8,128)S(1)}, f32[8,2048]{1,0:T(8,128)S(1)}, u32[]{:S(2)}, u32[]{:S(2)}) collective-permute-start(f32[8,2048]{1,0:T(8,128)S(1)} %get-tuple-element.18), channel_id=1, source_target_pairs={{0,12},{4,8},{8,4},{12,0},{1,13},{5,9},{9,5},{13,1},{2,14},{6,10},... | collective-permute-start | bytes 196616 | tf_op jit(solution)/shard_map/ppermute | solution.py:43
  129.1 5.4 %collective-permute-start.13 = (f32[8,2048]{1,0:T(8,128)S(1)}, f32[8,2048]{1,0:T(8,128)S(1)}, u32[]{:S(2)}, u32[]{:S(2)}) collective-permute-start(f32[8,2048]{1,0:T(8,128)S(1)} %get-tuple-element.19), channel_id=1, source_target_pairs={{0,8},{4,12},{8,0},{12,4},{1,9},{5,13},{9,1},{13,5},{2,10},{6,14},... | collective-permute-start | bytes 196616 | tf_op jit(solution)/shard_map/ppermute | solution.py:43
  130.4 4.1 %collective-permute-start.12 = (f32[8,2048]{1,0:T(8,128)S(1)}, f32[8,2048]{1,0:T(8,128)S(1)}, u32[]{:S(2)}, u32[]{:S(2)}) collective-permute-start(f32[8,2048]{1,0:T(8,128)S(1)} %get-tuple-element.20), channel_id=1, source_target_pairs={{0,4},{4,0},{8,12},{12,8},{1,5},{5,1},{9,13},{13,9},{2,6},{6,2},{1... | collective-permute-start | bytes 196616 | tf_op jit(solution)/shard_map/ppermute | solution.py:43

commit v6 on v5

--- a/solution.py
+++ b/solution.py
@@ -4,6 +4,7 @@
 from jax.sharding import PartitionSpec as P
 
 SEQ = 256
+N_CHUNK = 2
 
 
 layer_eps = 1e-06
@@ -64,7 +65,10 @@
     sent_in = mixed.reshape(tok_dev, n_row, d_blk).swapaxes(0, 1)
     columns = _exchange_abs(sent_in, "row", n_row, r).reshape(n_row * tok_dev, d_blk)
     n_col = lax.axis_size("col")
-    gathered = _gather_rel(columns, "col", n_col)
+    chunk = columns.shape[0] // N_CHUNK
+    gathered = jnp.concatenate(
+        [_gather_rel(columns[i * chunk:(i + 1) * chunk], "col", n_col) for i in range(N_CHUNK)],
+        axis=0)
     n_pos = gathered.shape[0]
     ff_blk = up_weight.shape[1]
     quarter = ff_blk // n_row
@@ -108,7 +112,10 @@
             partial_out = partial_out + down_term(d)
         for d in far:
             partial_out = partial_out + down_term(d ^ 1)
-    out_share = _scatter_rel(partial_out, "col", n_col)
+    per_chunk = partial_out.shape[0] // N_CHUNK
+    out_share = jnp.concatenate(
+        [_scatter_rel(partial_out[i * per_chunk:(i + 1) * per_chunk], "col", n_col)
+         for i in range(N_CHUNK)], axis=0)
     back = _exchange_abs(out_share.reshape(n_row, tok_dev, d_blk), "row", n_row, r)
     returned = back.swapaxes(0, 1).reshape(tok_dev, n_row * d_blk)
     return tokens + gate_vec * (returned + down_bias)

time: 136 us -> 133 us (0.978)
  waiting for transfers between devices: 63.1 us -> 57.5 us
  starting transfers between devices: 17.3 us -> 19.8 us
    ppermute x2 -> x4, waiting for transfers between devices: 24.4 us -> 21.1 us  [_gather_rel(): lax.ppermute(jnp.stack([held[k] for k in keys]), axis, _pairs(n, flip))]
    ppermute x2 -> x4, waiting for transfers between devices: 24.7 us -> 21.8 us  [_scatter_rel(): lax.ppermute(jnp.stack([held[d] for d in sent]), axis, _pairs(n, flip))]
    ppermute x2 -> x4, starting transfers between devices: 4.75 us -> 6.39 us  [_scatter_rel(): lax.ppermute(jnp.stack([held[d] for d in sent]), axis, _pairs(n, flip))]
    ppermute x2 -> x4, starting transfers between devices: 3.63 us -> 3.77 us  [_gather_rel(): lax.ppermute(jnp.stack([held[k] for k in keys]), axis, _pairs(n, flip))]
  transfers between devices with their start and end apart: 15 -> 19, of which waited for: 10 -> 15; matrix products, arithmetic and copies ran while one was open for 23% -> 23% of each run, Pallas kernels for 0% -> 0%
where the time goes in v6:
time: 133 us; the launch traced here: 132 us
  waiting for transfers between devices  57.5 us (43%)
  matrix products  48.1 us (36%)
  starting transfers between devices  19.8 us (15%)
  other arithmetic  5.88 us (4%)
    dot_general x4, matrix products, down_term(): jnp.dot(acts[d], w, precision=lax.Precision.HIGH, preferred_element_type=...  24.3 us
    dot_general x4, matrix products, up_block(): jnp.dot(gathered, w, precision=lax.Precision.HIGH, preferred_element_type...  23.8 us
    ppermute x4, waiting for transfers between devices, _scatter_rel(): lax.ppermute(jnp.stack([held[d] for d in sent]), axis, _pairs(n, flip))  21.8 us
    ppermute x4, waiting for transfers between devices, _gather_rel(): lax.ppermute(jnp.stack([held[k] for k in keys]), axis, _pairs(n, flip))  21.1 us
    ppermute x6, waiting for transfers between devices, _exchange_abs(): got.append(lax.ppermute(blocks[idx ^ d], axis, _pairs(n, d)))  8.2 us
    ppermute x4, starting transfers between devices, _scatter_rel(): lax.ppermute(jnp.stack([held[d] for d in sent]), axis, _pairs(n, flip))  6.39 us
    ppermute x2, waiting for transfers between devices, local(): lax.ppermute(jnp.stack([held[d] for d in sent]), 'row', _pairs(n_row, flip))  5.93 us
    ppermute x6, starting transfers between devices, _exchange_abs(): got.append(lax.ppermute(blocks[idx ^ d], axis, _pairs(n, d)))  5.11 us
  transfers between devices with their start and end apart: 19, of which 15 were waited for; matrix products, arithmetic and copies ran while one was open for 23% of the time, Pallas kernels for 0%

profile of v6, /device:TPU:0, one launch (start us, length us, event | category | flops | bytes accessed | tf_op | source)
XLA Modules:
  0.0 132.5 jit_solution(5245826740107194648)
XLA Ops:
  0.0 0.8 fusion.59
  0.8 1.1 reduce_sum.18
  2.0 1.2 multiply_reduce_fusion
  3.2 1.1 multiply_add_fusion.1
  4.3 2.4 %collective-permute-start.2 = (f32[8,2048]{1,0:T(8,128)S(1)}, f32[8,2048]{1,0:T(8,128)S(1)}, u32[]{:S(2)}, u32[]{:S(2)}) collective-permute-start(f32[8,2048]{1,0:T(8,128)S(1)} %get-tuple-element.29), channel_id=1, source_target_pairs={{0,12},{4,8},{8,4},{12,0},{1,13},{5,9},{9,5},{13,1},{2,14},{6,10},... | collective-permute-start | bytes 196616 | tf_op jit(solution)/shard_map/ppermute | solution.py:44
  6.7 0.7 collective-permute-start
  7.5 1.8 %collective-permute-done.2 = f32[8,2048]{1,0:T(8,128)S(1)} collective-permute-done((f32[8,2048]{1,0:T(8,128)S(1)}, f32[8,2048]{1,0:T(8,128)S(1)}, u32[]{:S(2)}, u32[]{:S(2)}) %collective-permute-start.2) | collective-permute-done | bytes 65568 | tf_op jit(solution)/shard_map/ppermute | solution.py:44
  9.2 2.5 %collective-permute-done.1 = f32[8,2048]{1,0:T(8,128)S(1)} collective-permute-done((f32[8,2048]{1,0:T(8,128)S(1)}, f32[8,2048]{1,0:T(8,128)S(1)}, u32[]{:S(2)}, u32[]{:S(2)}) %collective-permute-start.1) | collective-permute-done | bytes 65568 | tf_op jit(solution)/shard_map/ppermute | solution.py:44
  11.8 2.7 %collective-permute-start.3 = (f32[1,16,2048]{2,1,0:T(8,128)S(1)}, f32[1,16,2048]{2,1,0:T(8,128)S(1)}, u32[]{:S(2)}, u32[]{:S(2)}) collective-permute-start(f32[1,16,2048]{2,1,0:T(8,128)S(1)} %fusion.50), channel_id=1, source_target_pairs={{0,2},{1,3},{2,0},{3,1},{4,6},{5,7},{6,4},{7,5},{8,10},{9,11},{10,... | collective-permute-start | bytes 393224 | tf_op jit(solution)/shard_map/ppermute | solution.py:22
  14.4 0.4 collective-permute-start.5
  14.8 9.1 %collective-permute-done.3 = f32[1,16,2048]{2,1,0:T(8,128)S(1)} collective-permute-done((f32[1,16,2048]{2,1,0:T(8,128)S(1)}, f32[1,16,2048]{2,1,0:T(8,128)S(1)}, u32[]{:S(2)}, u32[]{:S(2)}) %collective-permute-start.3) | collective-permute-done | bytes 131104 | tf_op jit(solution)/shard_map/ppermute | solution.py:22
  24.0 0.1 collective-permute-start.4
  24.1 1.6 %collective-permute-done.5 = f32[1,16,2048]{2,1,0:T(8,128)S(1)} collective-permute-done((f32[1,16,2048]{2,1,0:T(8,128)S(1)}, f32[1,16,2048]{2,1,0:T(8,128)S(1)}, u32[]{:S(2)}, u32[]{:S(2)}) %collective-permute-start.5) | collective-permute-done | bytes 131104 | tf_op jit(solution)/shard_map/ppermute | solution.py:22
  25.7 0.6 collective-permute-start.6
  26.3 6.9 %collective-permute-done.4 = f32[2,16,2048]{2,1,0:T(8,128)S(1)} collective-permute-done((f32[2,16,2048]{2,1,0:T(8,128)S(1)}, f32[2,16,2048]{2,1,0:T(8,128)S(1)}, u32[]{:S(2)}, u32[]{:S(2)}) %collective-permute-start.4) | collective-permute-done | bytes 262176 | tf_op jit(solution)/shard_map/ppermute | solution.py:22
  33.4 3.5 %collective-permute-done.6 = f32[2,16,2048]{2,1,0:T(8,128)S(1)} collective-permute-done((f32[2,16,2048]{2,1,0:T(8,128)S(1)}, f32[2,16,2048]{2,1,0:T(8,128)S(1)}, u32[]{:S(2)}, u32[]{:S(2)}) %collective-permute-start.6) | collective-permute-done | bytes 262176 | tf_op jit(solution)/shard_map/ppermute | solution.py:22
  36.9 6.0 %fusion.12 = f32[128,1024]{1,0:T(8,128)S(1)} fusion(f32[128,2048]{1,0:T(8,128)S(1)} %fusion.45, f32[2048,4096]{1,0:T(8,128)} %param.8, s32[]{:T(128)S(6)} %select_n.24), kind=kOutput, calls=%fused_computation.12 | convolution fusion | flops 1610612736 | bytes 9961476 | tf_op jit(solution)/shard_map/dot_general | solution.py:78
  42.8 6.0 %fusion.10 = f32[128,1024]{1,0:T(8,128)S(1)} fusion(f32[128,2048]{1,0:T(8,128)S(1)} %fusion.45, f32[2048,4096]{1,0:T(8,128)} %param.8, s32[]{:T(128)S(6)} %select_n.25), kind=kOutput, calls=%fused_computation.10 | convolution fusion | flops 1610612736 | bytes 9961476 | tf_op jit(solution)/shard_map/dot_general | solution.py:78
  48.8 0.1 pad_maximum_fusion
  48.9 0.1 collective-permute-start.7
  49.0 5.9 %fusion.8 = f32[128,1024]{1,0:T(8,128)S(1)} fusion(f32[128,2048]{1,0:T(8,128)S(1)} %fusion.45, f32[2048,4096]{1,0:T(8,128)} %param.8, s32[]{:T(128)S(6)} %select_n.26), kind=kOutput, calls=%fused_computation.8 | convolution fusion | flops 1610612736 | bytes 9961476 | tf_op jit(solution)/shard_map/dot_general | solution.py:78
  55.0 0.1 fusion.27
  55.1 2.5 %collective-permute-start.8 = (f32[1,128,1024]{2,1,0:T(8,128)S(1)}, f32[1,128,1024]{2,1,0:T(8,128)S(1)}, u32[]{:S(2)}, u32[]{:S(2)}) collective-permute-start(f32[1,128,1024]{2,1,0:T(8,128)S(1)} %fusion.27), channel_id=1, source_target_pairs={{0,8},{4,12},{8,0},{12,4},{1,9},{5,13},{9,1},{13,5},{2,10},{6,14},... | collective-permute-start | bytes 1572872 | tf_op jit(solution)/shard_map/ppermute | solution.py:85
  57.6 0.7 dynamic_slice.79
  58.3 5.9 %fusion.14 = f32[128,1024]{1,0:T(8,128)S(1)} fusion(f32[128,2048]{1,0:T(8,128)S(1)} %fusion.45, f32[2048,4096]{1,0:T(8,128)} %param.8, s32[]{:T(128)S(6)} %select_n.23), kind=kOutput, calls=%fused_computation.14 | convolution fusion | flops 1610612736 | bytes 9961476 | tf_op jit(solution)/shard_map/dot_general | solution.py:78
  64.2 5.9 %collective-permute-done.8 = f32[1,128,1024]{2,1,0:T(8,128)S(1)} collective-permute-done((f32[1,128,1024]{2,1,0:T(8,128)S(1)}, f32[1,128,1024]{2,1,0:T(8,128)S(1)}, u32[]{:S(2)}, u32[]{:S(2)}) %collective-permute-start.8) | collective-permute-done | bytes 524320 | tf_op jit(solution)/shard_map/ppermute | solution.py:85
  70.2 0.4 fusion.25
  70.6 0.1 collective-permute-start.10
  70.7 1.8 %collective-permute-start.9 = (f32[1,128,1024]{2,1,0:T(8,128)S(1)}, f32[1,128,1024]{2,1,0:T(8,128)S(1)}, u32[]{:S(2)}, u32[]{:S(2)}) collective-permute-start(f32[1,128,1024]{2,1,0:T(8,128)S(1)} %bitcast.134), channel_id=1, source_target_pairs={{0,8},{4,12},{8,0},{12,4},{1,9},{5,13},{9,1},{13,5},{2,10},{6,14},... | collective-permute-start | bytes 1572872 | tf_op jit(solution)/shard_map/ppermute | solution.py:94
  72.5 0.1 collective-permute-done.10
  72.6 6.0 %fusion.4 = f32[128,2048]{1,0:T(8,128)S(1)} fusion(f32[128,1024]{1,0:T(8,128)S(1)} %collective-permute-done.10, f32[4096,2048]{1,0:T(8,128)} %param.10, s32[]{:T(128)S(6)} %select_n.24), kind=kOutput, calls=%fused_computation.4 | convolution fusion | flops 1610612736 | bytes 9961476 | tf_op jit(solution)/shard_map/dot_general | solution.py:100
  78.6 6.1 %fusion.16 = f32[128,2048]{1,0:T(8,128)S(1)} fusion(f32[128,2048]{1,0:T(8,128)S(1)} %fusion.4, f32[128,1024]{1,0:T(8,128)S(1)} %fusion.25, f32[4096,2048]{1,0:T(8,128)} %param.10, s32[]{:T(128)S(6)} %select_n.23), kind=kOutput, calls=%fused_computation.16 | convolution fusion | flops 1610874880 | bytes 11010052 | tf_op jit(solution)/shard_map/dot_general | solution.py:100
  84.7 0.3 collective-permute-done.9
  85.0 6.1 %fusion.2 = f32[128,2048]{1,0:T(8,128)S(1)} fusion(f32[4096,2048]{1,0:T(8,128)} %param.10, s32[]{:T(128)S(6)} %select_n.26, f32[1,128,1024]{2,1,0:T(8,128)S(1)} %collective-permute-done.9), kind=kOutput, calls=%fused_computation.2 | convolution fusion | flops 1610612736 | bytes 9961476 | tf_op jit(solution)/shard_map/dot_general | solution.py:100
  91.1 6.1 %add_add_fusion = f32[128,2048]{1,0:T(8,128)S(1)} fusion(f32[128,2048]{1,0:T(8,128)S(1)} %fusion.16, f32[128,2048]{1,0:T(8,128)S(1)} %fusion.2, f32[4096,2048]{1,0:T(8,128)} %param.10, s32[]{:T(128)S(6)} %select_n.25, f32[1,128,1024]{2,1,0:T(8,128)S(1)} %collective-permute-done.11), kind=kOutput, calls=%fused_computation.18 | convolution fusion | flops 1611137024 | bytes 12058628 | tf_op jit(solution)/shard_map/dot_general | solution.py:100
  97.3 0.6 collective-permute-start.12
  97.9 8.1 %collective-permute-done.12 = f32[2,16,2048]{2,1,0:T(8,128)S(1)} collective-permute-done((f32[2,16,2048]{2,1,0:T(8,128)S(1)}, f32[2,16,2048]{2,1,0:T(8,128)S(1)}, u32[]{:S(2)}, u32[]{:S(2)}) %collective-permute-start.12) | collective-permute-done | bytes 262176 | tf_op jit(solution)/shard_map/ppermute | solution.py:35
  106.1 0.6 collective-permute-start.14
  106.8 3.5 %collective-permute-start.13 = (f32[1,16,2048]{2,1,0:T(8,128)S(1)}, f32[1,16,2048]{2,1,0:T(8,128)S(1)}, u32[]{:S(2)}, u32[]{:S(2)}) collective-permute-start(f32[1,16,2048]{2,1,0:T(8,128)S(1)} %get-tuple-element.11), channel_id=1, source_target_pairs={{0,2},{1,3},{2,0},{3,1},{4,6},{5,7},{6,4},{7,5},{8,10},{9,11},{10,... | collective-permute-start | bytes 393224 | tf_op jit(solution)/shard_map/ppermute | solution.py:35
  110.2 4.8 %collective-permute-done.13 = f32[1,16,2048]{2,1,0:T(8,128)S(1)} collective-permute-done((f32[1,16,2048]{2,1,0:T(8,128)S(1)}, f32[1,16,2048]{2,1,0:T(8,128)S(1)}, u32[]{:S(2)}, u32[]{:S(2)}) %collective-permute-start.13) | collective-permute-done | bytes 131104 | tf_op jit(solution)/shard_map/ppermute | solution.py:35
  115.0 1.9 %collective-permute-done.14 = f32[2,16,2048]{2,1,0:T(8,128)S(1)} collective-permute-done((f32[2,16,2048]{2,1,0:T(8,128)S(1)}, f32[2,16,2048]{2,1,0:T(8,128)S(1)}, u32[]{:S(2)}, u32[]{:S(2)}) %collective-permute-start.14) | collective-permute-done | bytes 262176 | tf_op jit(solution)/shard_map/ppermute | solution.py:35
  117.0 1.6 %collective-permute-start.15 = (f32[1,16,2048]{2,1,0:T(8,128)S(1)}, f32[1,16,2048]{2,1,0:T(8,128)S(1)}, u32[]{:S(2)}, u32[]{:S(2)}) collective-permute-start(f32[1,16,2048]{2,1,0:T(8,128)S(1)} %get-tuple-element.10), channel_id=1, source_target_pairs={{0,2},{1,3},{2,0},{3,1},{4,6},{5,7},{6,4},{7,5},{8,10},{9,11},{10,... | collective-permute-start | bytes 393224 | tf_op jit(solution)/shard_map/ppermute | solution.py:35
  118.6 7.0 %collective-permute-done.15 = f32[1,16,2048]{2,1,0:T(8,128)S(1)} collective-permute-done((f32[1,16,2048]{2,1,0:T(8,128)S(1)}, f32[1,16,2048]{2,1,0:T(8,128)S(1)}, u32[]{:S(2)}, u32[]{:S(2)}) %collective-permute-start.15) | collective-permute-done | bytes 131104 | tf_op jit(solution)/shard_map/ppermute | solution.py:35
  125.7 0.1 collective-permute-start.16
  125.7 1.8 %collective-permute-start.17 = (f32[8,2048]{1,0:T(8,128)S(1)}, f32[8,2048]{1,0:T(8,128)S(1)}, u32[]{:S(2)}, u32[]{:S(2)}) collective-permute-start(f32[8,2048]{1,0:T(8,128)S(1)} %get-tuple-element.22), channel_id=1, source_target_pairs={{0,8},{4,12},{8,0},{12,4},{1,9},{5,13},{9,1},{13,5},{2,10},{6,14},... | collective-permute-start | bytes 196616 | tf_op jit(solution)/shard_map/ppermute | solution.py:44
  127.6 2.6 %collective-permute-done.17 = f32[8,2048]{1,0:T(8,128)S(1)} collective-permute-done((f32[8,2048]{1,0:T(8,128)S(1)}, f32[8,2048]{1,0:T(8,128)S(1)}, u32[]{:S(2)}, u32[]{:S(2)}) %collective-permute-start.17) | collective-permute-done | bytes 65568 | tf_op jit(solution)/shard_map/ppermute | solution.py:44
  130.3 1.3 %collective-permute-done.18 = f32[8,2048]{1,0:T(8,128)S(1)} collective-permute-done((f32[8,2048]{1,0:T(8,128)S(1)}, f32[8,2048]{1,0:T(8,128)S(1)}, u32[]{:S(2)}, u32[]{:S(2)}) %collective-permute-start.18) | collective-permute-done | bytes 65568 | tf_op jit(solution)/shard_map/ppermute | solution.py:44
  131.7 0.8 multiply_add_fusion
  (39 shorter events, 0.7 us)
Async XLA Ops:
  4.3 4.9 %collective-permute-start.2 = (f32[8,2048]{1,0:T(8,128)S(1)}, f32[8,2048]{1,0:T(8,128)S(1)}, u32[]{:S(2)}, u32[]{:S(2)}) collective-permute-start(f32[8,2048]{1,0:T(8,128)S(1)} %get-tuple-element.29), channel_id=1, source_target_pairs={{0,12},{4,8},{8,4},{12,0},{1,13},{5,9},{9,5},{13,1},{2,14},{6,10},... | collective-permute-start | bytes 196616 | tf_op jit(solution)/shard_map/ppermute | solution.py:44
  6.7 2.5 %collective-permute-start = (f32[8,2048]{1,0:T(8,128)S(1)}, f32[8,2048]{1,0:T(8,128)S(1)}, u32[]{:S(2)}, u32[]{:S(2)}) collective-permute-start(f32[8,2048]{1,0:T(8,128)S(1)} %get-tuple-element.31), channel_id=1, source_target_pairs={{0,4},{4,0},{8,12},{12,8},{1,5},{5,1},{9,13},{13,9},{2,6},{6,2},{1... | collective-permute-start | bytes 196616 | tf_op jit(solution)/shard_map/ppermute | solution.py:44
  7.4 4.3 %collective-permute-start.1 = (f32[8,2048]{1,0:T(8,128)S(1)}, f32[8,2048]{1,0:T(8,128)S(1)}, u32[]{:S(2)}, u32[]{:S(2)}) collective-permute-start(f32[8,2048]{1,0:T(8,128)S(1)} %get-tuple-element.30), channel_id=1, source_target_pairs={{0,8},{4,12},{8,0},{12,4},{1,9},{5,13},{9,1},{13,5},{2,10},{6,14},... | collective-permute-start | bytes 196616 | tf_op jit(solution)/shard_map/ppermute | solution.py:44
  11.8 12.2 %collective-permute-start.3 = (f32[1,16,2048]{2,1,0:T(8,128)S(1)}, f32[1,16,2048]{2,1,0:T(8,128)S(1)}, u32[]{:S(2)}, u32[]{:S(2)}) collective-permute-start(f32[1,16,2048]{2,1,0:T(8,128)S(1)} %fusion.50), channel_id=1, source_target_pairs={{0,2},{1,3},{2,0},{3,1},{4,6},{5,7},{6,4},{7,5},{8,10},{9,11},{10,... | collective-permute-start | bytes 393224 | tf_op jit(solution)/shard_map/ppermute | solution.py:22
  14.4 11.3 %collective-permute-start.5 = (f32[1,16,2048]{2,1,0:T(8,128)S(1)}, f32[1,16,2048]{2,1,0:T(8,128)S(1)}, u32[]{:S(2)}, u32[]{:S(2)}) collective-permute-start(f32[1,16,2048]{2,1,0:T(8,128)S(1)} %fusion.49), channel_id=1, source_target_pairs={{0,2},{1,3},{2,0},{3,1},{4,6},{5,7},{6,4},{7,5},{8,10},{9,11},{10,... | collective-permute-start | bytes 393224 | tf_op jit(solution)/shard_map/ppermute | solution.py:22
  24.0 9.3 %collective-permute-start.4 = (f32[2,16,2048]{2,1,0:T(8,128)S(1)}, f32[2,16,2048]{2,1,0:T(8,128)S(1)}, u32[]{:S(2)}, u32[]{:S(2)}) collective-permute-start(f32[2,16,2048]{2,1,0:T(8,128)S(1)} %pad_maximum_fusion.2), channel_id=1, source_target_pairs={{0,1},{1,0},{2,3},{3,2},{4,5},{5,4},{6,7},{7,6},{8,9},{9,8},{10,11... | collective-permute-start | bytes 786440 | tf_op jit(solution)/shard_map/ppermute | solution.py:22
  25.7 11.1 %collective-permute-start.6 = (f32[2,16,2048]{2,1,0:T(8,128)S(1)}, f32[2,16,2048]{2,1,0:T(8,128)S(1)}, u32[]{:S(2)}, u32[]{:S(2)}) collective-permute-start(f32[2,16,2048]{2,1,0:T(8,128)S(1)} %pad_maximum_fusion.3), channel_id=1, source_target_pairs={{0,1},{1,0},{2,3},{3,2},{4,5},{5,4},{6,7},{7,6},{8,9},{9,8},{10,11... | collective-permute-start | bytes 786440 | tf_op jit(solution)/shard_map/ppermute | solution.py:22
  48.9 6.1 %collective-permute-start.7 = (f32[2,128,1024]{2,1,0:T(8,128)S(1)}, f32[2,128,1024]{2,1,0:T(8,128)S(1)}, u32[]{:S(2)}, u32[]{:S(2)}) collective-permute-start(f32[2,128,1024]{2,1,0:T(8,128)S(1)} %pad_maximum_fusion), channel_id=1, source_target_pairs={{0,4},{4,0},{8,12},{12,8},{1,5},{5,1},{9,13},{13,9},{2,6},{6,2},{1... | collective-permute-start | bytes 3145736 | tf_op jit(solution)/shard_map/ppermute | solution.py:85
  54.9 76.7 %copy-start = (f32[8,8192]{1,0:T(8,128)S(1)}, f32[8,8192]{1,0:T(8,128)}, u32[]{:S(2)}) copy-start(f32[8,8192]{1,0:T(8,128)} %param.6) | copy-start | bytes 786436
  55.0 76.7 %copy-start.1 = (f32[8192]{0:T(1024)S(1)}, f32[8192]{0:T(1024)}, u32[]{:S(2)}) copy-start(f32[8192]{0:T(1024)} %param.11) | copy-start | bytes 98308
  55.1 15.1 %collective-permute-start.8 = (f32[1,128,1024]{2,1,0:T(8,128)S(1)}, f32[1,128,1024]{2,1,0:T(8,128)S(1)}, u32[]{:S(2)}, u32[]{:S(2)}) collective-permute-start(f32[1,128,1024]{2,1,0:T(8,128)S(1)} %fusion.27), channel_id=1, source_target_pairs={{0,8},{4,12},{8,0},{12,4},{1,9},{5,13},{9,1},{13,5},{2,10},{6,14},... | collective-permute-start | bytes 1572872 | tf_op jit(solution)/shard_map/ppermute | solution.py:85
  70.6 2.0 %collective-permute-start.10 = (f32[128,1024]{1,0:T(8,128)S(1)}, f32[128,1024]{1,0:T(8,128)S(1)}, u32[]{:S(2)}, u32[]{:S(2)}) collective-permute-start(f32[128,1024]{1,0:T(8,128)S(1)} %fusion.25), channel_id=1, source_target_pairs={{0,4},{4,0},{8,12},{12,8},{1,5},{5,1},{9,13},{13,9},{2,6},{6,2},{1... | collective-permute-start | bytes 1572872 | tf_op jit(solution)/shard_map/ppermute | solution.py:90
  70.7 14.3 %collective-permute-start.9 = (f32[1,128,1024]{2,1,0:T(8,128)S(1)}, f32[1,128,1024]{2,1,0:T(8,128)S(1)}, u32[]{:S(2)}, u32[]{:S(2)}) collective-permute-start(f32[1,128,1024]{2,1,0:T(8,128)S(1)} %bitcast.134), channel_id=1, source_target_pairs={{0,8},{4,12},{8,0},{12,4},{1,9},{5,13},{9,1},{13,5},{2,10},{6,14},... | collective-permute-start | bytes 1572872 | tf_op jit(solution)/shard_map/ppermute | solution.py:94
  85.0 6.1 %collective-permute-start.11 = (f32[1,128,1024]{2,1,0:T(8,128)S(1)}, f32[1,128,1024]{2,1,0:T(8,128)S(1)}, u32[]{:S(2)}, u32[]{:S(2)}) collective-permute-start(f32[1,128,1024]{2,1,0:T(8,128)S(1)} %collective-permute-done.9), channel_id=1, source_target_pairs={{0,4},{4,0},{8,12},{12,8},{1,5},{5,1},{9,13},{13,9},{2,6},{6,2},{1... | collective-permute-start | bytes 1572872 | tf_op jit(solution)/shard_map/ppermute | solution.py:108
  97.3 8.8 %collective-permute-start.12 = (f32[2,16,2048]{2,1,0:T(8,128)S(1)}, f32[2,16,2048]{2,1,0:T(8,128)S(1)}, u32[]{:S(2)}, u32[]{:S(2)}) collective-permute-start(f32[2,16,2048]{2,1,0:T(8,128)S(1)} %pad_maximum_fusion.4), channel_id=1, source_target_pairs={{0,1},{1,0},{2,3},{3,2},{4,5},{5,4},{6,7},{7,6},{8,9},{9,8},{10,11... | collective-permute-start | bytes 786440 | tf_op jit(solution)/shard_map/ppermute | solution.py:35
  106.1 10.8 %collective-permute-start.14 = (f32[2,16,2048]{2,1,0:T(8,128)S(1)}, f32[2,16,2048]{2,1,0:T(8,128)S(1)}, u32[]{:S(2)}, u32[]{:S(2)}) collective-permute-start(f32[2,16,2048]{2,1,0:T(8,128)S(1)} %pad_maximum_fusion.5), channel_id=1, source_target_pairs={{0,1},{1,0},{2,3},{3,2},{4,5},{5,4},{6,7},{7,6},{8,9},{9,8},{10,11... | collective-permute-start | bytes 786440 | tf_op jit(solution)/shard_map/ppermute | solution.py:35
  106.8 8.3 %collective-permute-start.13 = (f32[1,16,2048]{2,1,0:T(8,128)S(1)}, f32[1,16,2048]{2,1,0:T(8,128)S(1)}, u32[]{:S(2)}, u32[]{:S(2)}) collective-permute-start(f32[1,16,2048]{2,1,0:T(8,128)S(1)} %get-tuple-element.11), channel_id=1, source_target_pairs={{0,2},{1,3},{2,0},{3,1},{4,6},{5,7},{6,4},{7,5},{8,10},{9,11},{10,... | collective-permute-start | bytes 393224 | tf_op jit(solution)/shard_map/ppermute | solution.py:35
  117.0 8.6 %collective-permute-start.15 = (f32[1,16,2048]{2,1,0:T(8,128)S(1)}, f32[1,16,2048]{2,1,0:T(8,128)S(1)}, u32[]{:S(2)}, u32[]{:S(2)}) collective-permute-start(f32[1,16,2048]{2,1,0:T(8,128)S(1)} %get-tuple-element.10), channel_id=1, source_target_pairs={{0,2},{1,3},{2,0},{3,1},{4,6},{5,7},{6,4},{7,5},{8,10},{9,11},{10,... | collective-permute-start | bytes 393224 | tf_op jit(solution)/shard_map/ppermute | solution.py:35
  125.7 2.0 %collective-permute-start.16 = (f32[8,2048]{1,0:T(8,128)S(1)}, f32[8,2048]{1,0:T(8,128)S(1)}, u32[]{:S(2)}, u32[]{:S(2)}) collective-permute-start(f32[8,2048]{1,0:T(8,128)S(1)} %get-tuple-element.23), channel_id=1, source_target_pairs={{0,4},{4,0},{8,12},{12,8},{1,5},{5,1},{9,13},{13,9},{2,6},{6,2},{1... | collective-permute-start | bytes 196616 | tf_op jit(solution)/shard_map/ppermute | solution.py:44
  125.7 4.5 %collective-permute-start.17 = (f32[8,2048]{1,0:T(8,128)S(1)}, f32[8,2048]{1,0:T(8,128)S(1)}, u32[]{:S(2)}, u32[]{:S(2)}) collective-permute-start(f32[8,2048]{1,0:T(8,128)S(1)} %get-tuple-element.22), channel_id=1, source_target_pairs={{0,8},{4,12},{8,0},{12,4},{1,9},{5,13},{9,1},{13,5},{2,10},{6,14},... | collective-permute-start | bytes 196616 | tf_op jit(solution)/shard_map/ppermute | solution.py:44
  127.6 4.0 %collective-permute-start.18 = (f32[8,2048]{1,0:T(8,128)S(1)}, f32[8,2048]{1,0:T(8,128)S(1)}, u32[]{:S(2)}, u32[]{:S(2)}) collective-permute-start(f32[8,2048]{1,0:T(8,128)S(1)} %get-tuple-element.21), channel_id=1, source_target_pairs={{0,12},{4,8},{8,4},{12,0},{1,13},{5,9},{9,5},{13,1},{2,14},{6,10},... | collective-permute-start | bytes 196616 | tf_op jit(solution)/shard_map/ppermute | solution.py:44

commit v7 on v6

--- a/solution.py
+++ b/solution.py
@@ -95,12 +95,17 @@
         for i, d in enumerate(mine):
             acts[d ^ flip] = got[i]
         flip *= 2
-    def down_term(d):
-        w = lax.dynamic_slice_in_dim(down_weight, (r ^ d) * quarter, quarter, 0)
-        return jnp.dot(acts[d], w, precision=lax.Precision.HIGH,
+    core = r % 2
+
+    def down_pair(d):
+        lo, hi = acts[d], acts[d ^ 1]
+        pair = jnp.where(core == 0, jnp.concatenate([lo, hi], axis=1),
+                         jnp.concatenate([hi, lo], axis=1))
+        w = lax.dynamic_slice_in_dim(down_weight, ((r ^ d) // 2) * 2 * quarter, 2 * quarter, 0)
+        return jnp.dot(pair, w, precision=lax.Precision.HIGH,
                        preferred_element_type=jnp.float32)
 
-    partial_out = down_term(0) + down_term(1)
+    partial_out = down_pair(0)
     far = sorted(d for d in acts if d % 2 == 0 and d != 0)
     if far:
         stacked, partial_out = lax.optimization_barrier(
@@ -109,9 +114,7 @@
         for i, d in enumerate(far):
             acts[d ^ 1] = got[i]
         for d in far:
-            partial_out = partial_out + down_term(d)
-        for d in far:
-            partial_out = partial_out + down_term(d ^ 1)
+            partial_out = partial_out + down_pair(d)
     per_chunk = partial_out.shape[0] // N_CHUNK
     out_share = jnp.concatenate(
         [_scatter_rel(partial_out[i * per_chunk:(i + 1) * per_chunk], "col", n_col)

time: 133 us -> 129 us (0.970)
  matrix products: 48.1 us -> 41.2 us
  waiting for transfers between devices: 57.5 us -> 59.9 us
    dot_general x4 -> x2, matrix products: 24.3 us -> 17.4 us  [down_pair(): jnp.dot(pair, w, precision=lax.Precision.HIGH, preferred_element_type=jnp...]
    ppermute x1, waiting for transfers between devices: 0.29 us -> 3.76 us  [local(): lax.ppermute(jnp.stack([acts[d] for d in mine]), 'row', _pairs(n_row, flip))]
    ppermute x4, waiting for transfers between devices: 21.8 us -> 18.8 us  [_scatter_rel(): lax.ppermute(jnp.stack([held[d] for d in sent]), axis, _pairs(n, flip))]
    ppermute x1, waiting for transfers between devices: 0.01 us -> 1.91 us  [local(): got = lax.ppermute(stacked, 'row', _pairs(n_row, 1))]
  transfers between devices with their start and end apart: 19 -> 19, of which waited for: 15 -> 16; matrix products, arithmetic and copies ran while one was open for 23% -> 17% of each run, Pallas kernels for 0% -> 0%
where the time goes in v7:
time: 129 us
  waiting for transfers between devices  59.9 us (46%)
  matrix products  41.2 us (32%)
  starting transfers between devices  19.7 us (15%)
  other arithmetic  7 us (5%)
    dot_general x4, matrix products, up_block(): jnp.dot(gathered, w, precision=lax.Precision.HIGH, preferred_element_type...  23.8 us
    ppermute x4, waiting for transfers between devices, _gather_rel(): lax.ppermute(jnp.stack([held[k] for k in keys]), axis, _pairs(n, flip))  21.1 us
    ppermute x4, waiting for transfers between devices, _scatter_rel(): lax.ppermute(jnp.stack([held[d] for d in sent]), axis, _pairs(n, flip))  18.8 us
    dot_general x2, matrix products, down_pair(): jnp.dot(pair, w, precision=lax.Precision.HIGH, preferred_element_type=jnp...  17.4 us
    ppermute x6, waiting for transfers between devices, _exchange_abs(): got.append(lax.ppermute(blocks[idx ^ d], axis, _pairs(n, d)))  8.2 us
    ppermute x4, starting transfers between devices, _scatter_rel(): lax.ppermute(jnp.stack([held[d] for d in sent]), axis, _pairs(n, flip))  6.39 us
    ppermute x2, waiting for transfers between devices, local(): lax.ppermute(jnp.stack([held[d] for d in sent]), 'row', _pairs(n_row, flip))  5.96 us
    ppermute x6, starting transfers between devices, _exchange_abs(): got.append(lax.ppermute(blocks[idx ^ d], axis, _pairs(n, d)))  5.11 us
  transfers between devices with their start and end apart: 19, of which 16 were waited for; matrix products, arithmetic and copies ran while one was open for 17% of the time, Pallas kernels for 0%

profile of v7, /device:TPU:0, one launch (start us, length us, event | category | flops | bytes accessed | tf_op | source)
XLA Modules:
  0.0 129.0 jit_solution(16484987231114755371)
XLA Ops:
  0.0 0.8 fusion.58
  0.8 1.1 reduce_sum.18
  2.0 1.2 multiply_reduce_fusion
  3.2 1.1 multiply_add_fusion.1
  4.3 2.4 %collective-permute-start.2 = (f32[8,2048]{1,0:T(8,128)S(1)}, f32[8,2048]{1,0:T(8,128)S(1)}, u32[]{:S(2)}, u32[]{:S(2)}) collective-permute-start(f32[8,2048]{1,0:T(8,128)S(1)} %get-tuple-element.29), channel_id=1, source_target_pairs={{0,12},{4,8},{8,4},{12,0},{1,13},{5,9},{9,5},{13,1},{2,14},{6,10},... | collective-permute-start | bytes 196616 | tf_op jit(solution)/shard_map/ppermute | solution.py:44
  6.7 0.7 collective-permute-start
  7.5 1.8 %collective-permute-done.2 = f32[8,2048]{1,0:T(8,128)S(1)} collective-permute-done((f32[8,2048]{1,0:T(8,128)S(1)}, f32[8,2048]{1,0:T(8,128)S(1)}, u32[]{:S(2)}, u32[]{:S(2)}) %collective-permute-start.2) | collective-permute-done | bytes 65568 | tf_op jit(solution)/shard_map/ppermute | solution.py:44
  9.2 2.5 %collective-permute-done.1 = f32[8,2048]{1,0:T(8,128)S(1)} collective-permute-done((f32[8,2048]{1,0:T(8,128)S(1)}, f32[8,2048]{1,0:T(8,128)S(1)}, u32[]{:S(2)}, u32[]{:S(2)}) %collective-permute-start.1) | collective-permute-done | bytes 65568 | tf_op jit(solution)/shard_map/ppermute | solution.py:44
  11.8 2.7 %collective-permute-start.3 = (f32[1,16,2048]{2,1,0:T(8,128)S(1)}, f32[1,16,2048]{2,1,0:T(8,128)S(1)}, u32[]{:S(2)}, u32[]{:S(2)}) collective-permute-start(f32[1,16,2048]{2,1,0:T(8,128)S(1)} %fusion.49), channel_id=1, source_target_pairs={{0,2},{1,3},{2,0},{3,1},{4,6},{5,7},{6,4},{7,5},{8,10},{9,11},{10,... | collective-permute-start | bytes 393224 | tf_op jit(solution)/shard_map/ppermute | solution.py:22
  14.4 0.4 collective-permute-start.5
  14.8 9.1 %collective-permute-done.3 = f32[1,16,2048]{2,1,0:T(8,128)S(1)} collective-permute-done((f32[1,16,2048]{2,1,0:T(8,128)S(1)}, f32[1,16,2048]{2,1,0:T(8,128)S(1)}, u32[]{:S(2)}, u32[]{:S(2)}) %collective-permute-start.3) | collective-permute-done | bytes 131104 | tf_op jit(solution)/shard_map/ppermute | solution.py:22
  24.0 0.1 collective-permute-start.4
  24.1 1.6 %collective-permute-done.5 = f32[1,16,2048]{2,1,0:T(8,128)S(1)} collective-permute-done((f32[1,16,2048]{2,1,0:T(8,128)S(1)}, f32[1,16,2048]{2,1,0:T(8,128)S(1)}, u32[]{:S(2)}, u32[]{:S(2)}) %collective-permute-start.5) | collective-permute-done | bytes 131104 | tf_op jit(solution)/shard_map/ppermute | solution.py:22
  25.7 0.6 collective-permute-start.6
  26.3 6.9 %collective-permute-done.4 = f32[2,16,2048]{2,1,0:T(8,128)S(1)} collective-permute-done((f32[2,16,2048]{2,1,0:T(8,128)S(1)}, f32[2,16,2048]{2,1,0:T(8,128)S(1)}, u32[]{:S(2)}, u32[]{:S(2)}) %collective-permute-start.4) | collective-permute-done | bytes 262176 | tf_op jit(solution)/shard_map/ppermute | solution.py:22
  33.4 3.5 %collective-permute-done.6 = f32[2,16,2048]{2,1,0:T(8,128)S(1)} collective-permute-done((f32[2,16,2048]{2,1,0:T(8,128)S(1)}, f32[2,16,2048]{2,1,0:T(8,128)S(1)}, u32[]{:S(2)}, u32[]{:S(2)}) %collective-permute-start.6) | collective-permute-done | bytes 262176 | tf_op jit(solution)/shard_map/ppermute | solution.py:22
  36.9 6.0 %fusion.8 = f32[128,1024]{1,0:T(8,128)S(1)} fusion(f32[128,2048]{1,0:T(8,128)S(1)} %fusion.44, f32[2048,4096]{1,0:T(8,128)} %param.8, s32[]{:T(128)S(6)} %select_n.76), kind=kOutput, calls=%fused_computation.8 | convolution fusion | flops 1610612736 | bytes 9961476 | tf_op jit(solution)/shard_map/dot_general | solution.py:78
  42.8 6.0 %fusion.6 = f32[128,1024]{1,0:T(8,128)S(1)} fusion(f32[128,2048]{1,0:T(8,128)S(1)} %fusion.44, f32[2048,4096]{1,0:T(8,128)} %param.8, s32[]{:T(128)S(6)} %select_n.77), kind=kOutput, calls=%fused_computation.6 | convolution fusion | flops 1610612736 | bytes 9961476 | tf_op jit(solution)/shard_map/dot_general | solution.py:78
  48.8 1.1 pad_maximum_fusion
  49.9 6.0 %fusion.4 = f32[128,1024]{1,0:T(8,128)S(1)} fusion(f32[128,2048]{1,0:T(8,128)S(1)} %fusion.44, f32[2048,4096]{1,0:T(8,128)} %param.8, s32[]{:T(128)S(6)} %select_n.78), kind=kOutput, calls=%fused_computation.4 | convolution fusion | flops 1610612736 | bytes 9961476 | tf_op jit(solution)/shard_map/dot_general | solution.py:78
  55.9 0.1 fusion.30
  55.9 2.5 %collective-permute-start.8 = (f32[1,128,1024]{2,1,0:T(8,128)S(1)}, f32[1,128,1024]{2,1,0:T(8,128)S(1)}, u32[]{:S(2)}, u32[]{:S(2)}) collective-permute-start(f32[1,128,1024]{2,1,0:T(8,128)S(1)} %fusion.30), channel_id=1, source_target_pairs={{0,8},{4,12},{8,0},{12,4},{1,9},{5,13},{9,1},{13,5},{2,10},{6,14},... | collective-permute-start | bytes 1572872 | tf_op jit(solution)/shard_map/ppermute | solution.py:85
  58.5 0.7 dynamic_slice.73
  59.2 5.9 %fusion.10 = f32[128,1024]{1,0:T(8,128)S(1)} fusion(f32[128,2048]{1,0:T(8,128)S(1)} %fusion.44, f32[2048,4096]{1,0:T(8,128)} %param.8, s32[]{:T(128)S(6)} %select_n.75), kind=kOutput, calls=%fused_computation.10 | convolution fusion | flops 1610612736 | bytes 9961476 | tf_op jit(solution)/shard_map/dot_general | solution.py:78
  65.1 6.0 %collective-permute-done.8 = f32[1,128,1024]{2,1,0:T(8,128)S(1)} collective-permute-done((f32[1,128,1024]{2,1,0:T(8,128)S(1)}, f32[1,128,1024]{2,1,0:T(8,128)S(1)}, u32[]{:S(2)}, u32[]{:S(2)}) %collective-permute-start.8) | collective-permute-done | bytes 524320 | tf_op jit(solution)/shard_map/ppermute | solution.py:85
  71.1 0.4 fusion.28
  71.5 0.1 collective-permute-start.10
  71.6 1.8 %collective-permute-start.9 = (f32[1,128,1024]{2,1,0:T(8,128)S(1)}, f32[1,128,1024]{2,1,0:T(8,128)S(1)}, u32[]{:S(2)}, u32[]{:S(2)}) collective-permute-start(f32[1,128,1024]{2,1,0:T(8,128)S(1)} %bitcast.126), channel_id=1, source_target_pairs={{0,8},{4,12},{8,0},{12,4},{1,9},{5,13},{9,1},{13,5},{2,10},{6,14},... | collective-permute-start | bytes 1572872 | tf_op jit(solution)/shard_map/ppermute | solution.py:94
  73.4 0.1 collective-permute-done.10
  73.5 8.7 %fusion.2 = f32[128,2048]{1,0:T(8,128)S(1)} fusion(f32[4096,2048]{1,0:T(8,128)} %param.10, s32[]{:T(128)S(6)} %select_n.83, f32[128,1024]{1,0:T(8,128)S(1)} %collective-permute-done.10, f32[128,1024]{1,0:T(8,128)S(1)} %fusion.28, pred[]{:T(512)S(6)} %eq.6), kind=kOutput, calls=%fused_computation.2 | convolution fusion | flops 3222011904 | bytes 18874372 | tf_op jit(solution)/shard_map/dot_general | solution.py:105
  82.1 3.8 %collective-permute-done.9 = f32[1,128,1024]{2,1,0:T(8,128)S(1)} collective-permute-done((f32[1,128,1024]{2,1,0:T(8,128)S(1)}, f32[1,128,1024]{2,1,0:T(8,128)S(1)}, u32[]{:S(2)}, u32[]{:S(2)}) %collective-permute-start.9) | collective-permute-done | bytes 524320 | tf_op jit(solution)/shard_map/ppermute | solution.py:94
  85.9 1.9 %collective-permute-done.11 = f32[1,128,1024]{2,1,0:T(8,128)S(1)} collective-permute-done((f32[1,128,1024]{2,1,0:T(8,128)S(1)}, f32[1,128,1024]{2,1,0:T(8,128)S(1)}, u32[]{:S(2)}, u32[]{:S(2)}) %collective-permute-start.11) | collective-permute-done | bytes 524320 | tf_op jit(solution)/shard_map/ppermute | solution.py:113
  87.8 8.7 %fusion = f32[128,2048]{1,0:T(8,128)S(1)} fusion(f32[4096,2048]{1,0:T(8,128)} %param.10, s32[]{:T(128)S(6)} %select_n.86, f32[128,1024]{1,0:T(8,128)S(1)} %bitcast.132, f32[128,1024]{1,0:T(8,128)S(1)} %bitcast.131, pred[]{:T(512)S(6)} %eq.6), kind=kOutput, calls=%fused_computation | convolution fusion | flops 3222011904 | bytes 18874372 | tf_op jit(solution)/shard_map/dot_general | solution.py:105
  96.5 0.2 add.167
  96.7 0.6 collective-permute-start.12
  97.4 7.8 %collective-permute-done.12 = f32[2,16,2048]{2,1,0:T(8,128)S(1)} collective-permute-done((f32[2,16,2048]{2,1,0:T(8,128)S(1)}, f32[2,16,2048]{2,1,0:T(8,128)S(1)}, u32[]{:S(2)}, u32[]{:S(2)}) %collective-permute-start.12) | collective-permute-done | bytes 262176 | tf_op jit(solution)/shard_map/ppermute | solution.py:35
  105.2 0.6 collective-permute-start.14
  105.9 3.5 %collective-permute-start.13 = (f32[1,16,2048]{2,1,0:T(8,128)S(1)}, f32[1,16,2048]{2,1,0:T(8,128)S(1)}, u32[]{:S(2)}, u32[]{:S(2)}) collective-permute-start(f32[1,16,2048]{2,1,0:T(8,128)S(1)} %get-tuple-element.11), channel_id=1, source_target_pairs={{0,2},{1,3},{2,0},{3,1},{4,6},{5,7},{6,4},{7,5},{8,10},{9,11},{10,... | collective-permute-start | bytes 393224 | tf_op jit(solution)/shard_map/ppermute | solution.py:35
  109.3 4.4 %collective-permute-done.13 = f32[1,16,2048]{2,1,0:T(8,128)S(1)} collective-permute-done((f32[1,16,2048]{2,1,0:T(8,128)S(1)}, f32[1,16,2048]{2,1,0:T(8,128)S(1)}, u32[]{:S(2)}, u32[]{:S(2)}) %collective-permute-start.13) | collective-permute-done | bytes 131104 | tf_op jit(solution)/shard_map/ppermute | solution.py:35
  113.7 1.9 %collective-permute-done.14 = f32[2,16,2048]{2,1,0:T(8,128)S(1)} collective-permute-done((f32[2,16,2048]{2,1,0:T(8,128)S(1)}, f32[2,16,2048]{2,1,0:T(8,128)S(1)}, u32[]{:S(2)}, u32[]{:S(2)}) %collective-permute-start.14) | collective-permute-done | bytes 262176 | tf_op jit(solution)/shard_map/ppermute | solution.py:35
  115.7 1.6 %collective-permute-start.15 = (f32[1,16,2048]{2,1,0:T(8,128)S(1)}, f32[1,16,2048]{2,1,0:T(8,128)S(1)}, u32[]{:S(2)}, u32[]{:S(2)}) collective-permute-start(f32[1,16,2048]{2,1,0:T(8,128)S(1)} %get-tuple-element.10), channel_id=1, source_target_pairs={{0,2},{1,3},{2,0},{3,1},{4,6},{5,7},{6,4},{7,5},{8,10},{9,11},{10,... | collective-permute-start | bytes 393224 | tf_op jit(solution)/shard_map/ppermute | solution.py:35
  117.3 4.8 %collective-permute-done.15 = f32[1,16,2048]{2,1,0:T(8,128)S(1)} collective-permute-done((f32[1,16,2048]{2,1,0:T(8,128)S(1)}, f32[1,16,2048]{2,1,0:T(8,128)S(1)}, u32[]{:S(2)}, u32[]{:S(2)}) %collective-permute-start.15) | collective-permute-done | bytes 131104 | tf_op jit(solution)/shard_map/ppermute | solution.py:35
  122.2 0.1 collective-permute-start.16
  122.3 1.8 %collective-permute-start.17 = (f32[8,2048]{1,0:T(8,128)S(1)}, f32[8,2048]{1,0:T(8,128)S(1)}, u32[]{:S(2)}, u32[]{:S(2)}) collective-permute-start(f32[8,2048]{1,0:T(8,128)S(1)} %get-tuple-element.22), channel_id=1, source_target_pairs={{0,8},{4,12},{8,0},{12,4},{1,9},{5,13},{9,1},{13,5},{2,10},{6,14},... | collective-permute-start | bytes 196616 | tf_op jit(solution)/shard_map/ppermute | solution.py:44
  124.1 0.1 collective-permute-start.18
  124.1 2.6 %collective-permute-done.17 = f32[8,2048]{1,0:T(8,128)S(1)} collective-permute-done((f32[8,2048]{1,0:T(8,128)S(1)}, f32[8,2048]{1,0:T(8,128)S(1)}, u32[]{:S(2)}, u32[]{:S(2)}) %collective-permute-start.17) | collective-permute-done | bytes 65568 | tf_op jit(solution)/shard_map/ppermute | solution.py:44
  126.8 1.3 %collective-permute-done.18 = f32[8,2048]{1,0:T(8,128)S(1)} collective-permute-done((f32[8,2048]{1,0:T(8,128)S(1)}, f32[8,2048]{1,0:T(8,128)S(1)}, u32[]{:S(2)}, u32[]{:S(2)}) %collective-permute-start.18) | collective-permute-done | bytes 65568 | tf_op jit(solution)/shard_map/ppermute | solution.py:44
  128.2 0.8 multiply_add_fusion
  (38 shorter events, 0.6 us)
Async XLA Ops:
  4.3 4.9 %collective-permute-start.2 = (f32[8,2048]{1,0:T(8,128)S(1)}, f32[8,2048]{1,0:T(8,128)S(1)}, u32[]{:S(2)}, u32[]{:S(2)}) collective-permute-start(f32[8,2048]{1,0:T(8,128)S(1)} %get-tuple-element.29), channel_id=1, source_target_pairs={{0,12},{4,8},{8,4},{12,0},{1,13},{5,9},{9,5},{13,1},{2,14},{6,10},... | collective-permute-start | bytes 196616 | tf_op jit(solution)/shard_map/ppermute | solution.py:44
  6.7 2.5 %collective-permute-start = (f32[8,2048]{1,0:T(8,128)S(1)}, f32[8,2048]{1,0:T(8,128)S(1)}, u32[]{:S(2)}, u32[]{:S(2)}) collective-permute-start(f32[8,2048]{1,0:T(8,128)S(1)} %get-tuple-element.31), channel_id=1, source_target_pairs={{0,4},{4,0},{8,12},{12,8},{1,5},{5,1},{9,13},{13,9},{2,6},{6,2},{1... | collective-permute-start | bytes 196616 | tf_op jit(solution)/shard_map/ppermute | solution.py:44
  7.4 4.3 %collective-permute-start.1 = (f32[8,2048]{1,0:T(8,128)S(1)}, f32[8,2048]{1,0:T(8,128)S(1)}, u32[]{:S(2)}, u32[]{:S(2)}) collective-permute-start(f32[8,2048]{1,0:T(8,128)S(1)} %get-tuple-element.30), channel_id=1, source_target_pairs={{0,8},{4,12},{8,0},{12,4},{1,9},{5,13},{9,1},{13,5},{2,10},{6,14},... | collective-permute-start | bytes 196616 | tf_op jit(solution)/shard_map/ppermute | solution.py:44
  11.8 12.2 %collective-permute-start.3 = (f32[1,16,2048]{2,1,0:T(8,128)S(1)}, f32[1,16,2048]{2,1,0:T(8,128)S(1)}, u32[]{:S(2)}, u32[]{:S(2)}) collective-permute-start(f32[1,16,2048]{2,1,0:T(8,128)S(1)} %fusion.49), channel_id=1, source_target_pairs={{0,2},{1,3},{2,0},{3,1},{4,6},{5,7},{6,4},{7,5},{8,10},{9,11},{10,... | collective-permute-start | bytes 393224 | tf_op jit(solution)/shard_map/ppermute | solution.py:22
  14.4 11.3 %collective-permute-start.5 = (f32[1,16,2048]{2,1,0:T(8,128)S(1)}, f32[1,16,2048]{2,1,0:T(8,128)S(1)}, u32[]{:S(2)}, u32[]{:S(2)}) collective-permute-start(f32[1,16,2048]{2,1,0:T(8,128)S(1)} %fusion.48), channel_id=1, source_target_pairs={{0,2},{1,3},{2,0},{3,1},{4,6},{5,7},{6,4},{7,5},{8,10},{9,11},{10,... | collective-permute-start | bytes 393224 | tf_op jit(solution)/shard_map/ppermute | solution.py:22
  24.0 9.3 %collective-permute-start.4 = (f32[2,16,2048]{2,1,0:T(8,128)S(1)}, f32[2,16,2048]{2,1,0:T(8,128)S(1)}, u32[]{:S(2)}, u32[]{:S(2)}) collective-permute-start(f32[2,16,2048]{2,1,0:T(8,128)S(1)} %pad_maximum_fusion.2), channel_id=1, source_target_pairs={{0,1},{1,0},{2,3},{3,2},{4,5},{5,4},{6,7},{7,6},{8,9},{9,8},{10,11... | collective-permute-start | bytes 786440 | tf_op jit(solution)/shard_map/ppermute | solution.py:22
  25.7 11.1 %collective-permute-start.6 = (f32[2,16,2048]{2,1,0:T(8,128)S(1)}, f32[2,16,2048]{2,1,0:T(8,128)S(1)}, u32[]{:S(2)}, u32[]{:S(2)}) collective-permute-start(f32[2,16,2048]{2,1,0:T(8,128)S(1)} %pad_maximum_fusion.3), channel_id=1, source_target_pairs={{0,1},{1,0},{2,3},{3,2},{4,5},{5,4},{6,7},{7,6},{8,9},{9,8},{10,11... | collective-permute-start | bytes 786440 | tf_op jit(solution)/shard_map/ppermute | solution.py:22
  49.9 6.0 %collective-permute-start.7 = (f32[2,128,1024]{2,1,0:T(8,128)}, f32[2,128,1024]{2,1,0:T(8,128)S(1)}, u32[]{:S(2)}, u32[]{:S(2)}) collective-permute-start(f32[2,128,1024]{2,1,0:T(8,128)} %pad_maximum_fusion), channel_id=1, source_target_pairs={{0,4},{4,0},{8,12},{12,8},{1,5},{5,1},{9,13},{13,9},{2,6},{6,2},{1... | collective-permute-start | bytes 3145736 | tf_op jit(solution)/shard_map/ppermute | solution.py:85
  49.9 78.3 %copy-start = (f32[8,8192]{1,0:T(8,128)S(1)}, f32[8,8192]{1,0:T(8,128)}, u32[]{:S(2)}) copy-start(f32[8,8192]{1,0:T(8,128)} %param.6) | copy-start | bytes 786436
  49.9 78.4 %copy-start.1 = (f32[8192]{0:T(1024)S(1)}, f32[8192]{0:T(1024)}, u32[]{:S(2)}) copy-start(f32[8192]{0:T(1024)} %param.11) | copy-start | bytes 98308
  55.9 15.1 %collective-permute-start.8 = (f32[1,128,1024]{2,1,0:T(8,128)S(1)}, f32[1,128,1024]{2,1,0:T(8,128)S(1)}, u32[]{:S(2)}, u32[]{:S(2)}) collective-permute-start(f32[1,128,1024]{2,1,0:T(8,128)S(1)} %fusion.30), channel_id=1, source_target_pairs={{0,8},{4,12},{8,0},{12,4},{1,9},{5,13},{9,1},{13,5},{2,10},{6,14},... | collective-permute-start | bytes 1572872 | tf_op jit(solution)/shard_map/ppermute | solution.py:85
  71.5 2.0 %collective-permute-start.10 = (f32[128,1024]{1,0:T(8,128)S(1)}, f32[128,1024]{1,0:T(8,128)S(1)}, u32[]{:S(2)}, u32[]{:S(2)}) collective-permute-start(f32[128,1024]{1,0:T(8,128)S(1)} %fusion.28), channel_id=1, source_target_pairs={{0,4},{4,0},{8,12},{12,8},{1,5},{5,1},{9,13},{13,9},{2,6},{6,2},{1... | collective-permute-start | bytes 1572872 | tf_op jit(solution)/shard_map/ppermute | solution.py:90
  71.6 14.3 %collective-permute-start.9 = (f32[1,128,1024]{2,1,0:T(8,128)S(1)}, f32[1,128,1024]{2,1,0:T(8,128)S(1)}, u32[]{:S(2)}, u32[]{:S(2)}) collective-permute-start(f32[1,128,1024]{2,1,0:T(8,128)S(1)} %bitcast.126), channel_id=1, source_target_pairs={{0,8},{4,12},{8,0},{12,4},{1,9},{5,13},{9,1},{13,5},{2,10},{6,14},... | collective-permute-start | bytes 1572872 | tf_op jit(solution)/shard_map/ppermute | solution.py:94
  85.9 1.9 %collective-permute-start.11 = (f32[1,128,1024]{2,1,0:T(8,128)S(1)}, f32[1,128,1024]{2,1,0:T(8,128)S(1)}, u32[]{:S(2)}, u32[]{:S(2)}) collective-permute-start(f32[1,128,1024]{2,1,0:T(8,128)S(1)} %collective-permute-done.9), channel_id=1, source_target_pairs={{0,4},{4,0},{8,12},{12,8},{1,5},{5,1},{9,13},{13,9},{2,6},{6,2},{1... | collective-permute-start | bytes 1572872 | tf_op jit(solution)/shard_map/ppermute | solution.py:113
  96.7 8.4 %collective-permute-start.12 = (f32[2,16,2048]{2,1,0:T(8,128)S(1)}, f32[2,16,2048]{2,1,0:T(8,128)S(1)}, u32[]{:S(2)}, u32[]{:S(2)}) collective-permute-start(f32[2,16,2048]{2,1,0:T(8,128)S(1)} %pad_maximum_fusion.4), channel_id=1, source_target_pairs={{0,1},{1,0},{2,3},{3,2},{4,5},{5,4},{6,7},{7,6},{8,9},{9,8},{10,11... | collective-permute-start | bytes 786440 | tf_op jit(solution)/shard_map/ppermute | solution.py:35
  105.2 10.4 %collective-permute-start.14 = (f32[2,16,2048]{2,1,0:T(8,128)S(1)}, f32[2,16,2048]{2,1,0:T(8,128)S(1)}, u32[]{:S(2)}, u32[]{:S(2)}) collective-permute-start(f32[2,16,2048]{2,1,0:T(8,128)S(1)} %pad_maximum_fusion.5), channel_id=1, source_target_pairs={{0,1},{1,0},{2,3},{3,2},{4,5},{5,4},{6,7},{7,6},{8,9},{9,8},{10,11... | collective-permute-start | bytes 786440 | tf_op jit(solution)/shard_map/ppermute | solution.py:35
  105.9 7.8 %collective-permute-start.13 = (f32[1,16,2048]{2,1,0:T(8,128)S(1)}, f32[1,16,2048]{2,1,0:T(8,128)S(1)}, u32[]{:S(2)}, u32[]{:S(2)}) collective-permute-start(f32[1,16,2048]{2,1,0:T(8,128)S(1)} %get-tuple-element.11), channel_id=1, source_target_pairs={{0,2},{1,3},{2,0},{3,1},{4,6},{5,7},{6,4},{7,5},{8,10},{9,11},{10,... | collective-permute-start | bytes 393224 | tf_op jit(solution)/shard_map/ppermute | solution.py:35
  115.7 6.4 %collective-permute-start.15 = (f32[1,16,2048]{2,1,0:T(8,128)S(1)}, f32[1,16,2048]{2,1,0:T(8,128)S(1)}, u32[]{:S(2)}, u32[]{:S(2)}) collective-permute-start(f32[1,16,2048]{2,1,0:T(8,128)S(1)} %get-tuple-element.10), channel_id=1, source_target_pairs={{0,2},{1,3},{2,0},{3,1},{4,6},{5,7},{6,4},{7,5},{8,10},{9,11},{10,... | collective-permute-start | bytes 393224 | tf_op jit(solution)/shard_map/ppermute | solution.py:35
  122.2 2.0 %collective-permute-start.16 = (f32[8,2048]{1,0:T(8,128)S(1)}, f32[8,2048]{1,0:T(8,128)S(1)}, u32[]{:S(2)}, u32[]{:S(2)}) collective-permute-start(f32[8,2048]{1,0:T(8,128)S(1)} %get-tuple-element.23), channel_id=1, source_target_pairs={{0,4},{4,0},{8,12},{12,8},{1,5},{5,1},{9,13},{13,9},{2,6},{6,2},{1... | collective-permute-start | bytes 196616 | tf_op jit(solution)/shard_map/ppermute | solution.py:44
  122.3 4.5 %collective-permute-start.17 = (f32[8,2048]{1,0:T(8,128)S(1)}, f32[8,2048]{1,0:T(8,128)S(1)}, u32[]{:S(2)}, u32[]{:S(2)}) collective-permute-start(f32[8,2048]{1,0:T(8,128)S(1)} %get-tuple-element.22), channel_id=1, source_target_pairs={{0,8},{4,12},{8,0},{12,4},{1,9},{5,13},{9,1},{13,5},{2,10},{6,14},... | collective-permute-start | bytes 196616 | tf_op jit(solution)/shard_map/ppermute | solution.py:44
  124.1 4.0 %collective-permute-start.18 = (f32[8,2048]{1,0:T(8,128)S(1)}, f32[8,2048]{1,0:T(8,128)S(1)}, u32[]{:S(2)}, u32[]{:S(2)}) collective-permute-start(f32[8,2048]{1,0:T(8,128)S(1)} %get-tuple-element.21), channel_id=1, source_target_pairs={{0,12},{4,8},{8,4},{12,0},{1,13},{5,9},{9,5},{13,1},{2,14},{6,10},... | collective-permute-start | bytes 196616 | tf_op jit(solution)/shard_map/ppermute | solution.py:44

commit v8 on v7

--- a/solution.py
+++ b/solution.py
@@ -97,15 +97,17 @@
         flip *= 2
     core = r % 2
 
-    def down_pair(d):
+    def down_pair(d, col0, cols):
         lo, hi = acts[d], acts[d ^ 1]
         pair = jnp.where(core == 0, jnp.concatenate([lo, hi], axis=1),
                          jnp.concatenate([hi, lo], axis=1))
-        w = lax.dynamic_slice_in_dim(down_weight, ((r ^ d) // 2) * 2 * quarter, 2 * quarter, 0)
+        w = lax.dynamic_slice(down_weight, (((r ^ d) // 2) * 2 * quarter, col0),
+                              (2 * quarter, cols))
         return jnp.dot(pair, w, precision=lax.Precision.HIGH,
                        preferred_element_type=jnp.float32)
 
-    partial_out = down_pair(0)
+    d_cols = down_weight.shape[1]
+    partial_out = down_pair(0, 0, d_cols)
     far = sorted(d for d in acts if d % 2 == 0 and d != 0)
     if far:
         stacked, partial_out = lax.optimization_barrier(
@@ -113,11 +115,17 @@
         got = lax.ppermute(stacked, "row", _pairs(n_row, 1))
         for i, d in enumerate(far):
             acts[d ^ 1] = got[i]
+    half = d_cols // 2
+    halves = []
+    for h in range(2):
+        part = partial_out[:, h * half:(h + 1) * half]
         for d in far:
-            partial_out = partial_out + down_pair(d)
-    per_chunk = partial_out.shape[0] // N_CHUNK
+            part = part + down_pair(d, h * half, half)
+        halves.append(part)
+    per_chunk = n_pos // N_CHUNK
     out_share = jnp.concatenate(
-        [_scatter_rel(partial_out[i * per_chunk:(i + 1) * per_chunk], "col", n_col)
+        [jnp.concatenate([_scatter_rel(hv[i * per_chunk:(i + 1) * per_chunk], "col", n_col)
+                          for hv in halves], axis=1)
          for i in range(N_CHUNK)], axis=0)
     back = _exchange_abs(out_share.reshape(n_row, tok_dev, d_blk), "row", n_row, r)
     returned = back.swapaxes(0, 1).reshape(tok_dev, n_row * d_blk)

time: 129 us -> 131 us (1.016)
  waiting for transfers between devices: 59.9 us -> 50.7 us
  starting transfers between devices: 19.7 us -> 26.9 us
  matrix products: 41.2 us -> 44.6 us
    ppermute x4 -> x8, waiting for transfers between devices: 18.8 us -> 9.61 us  [_scatter_rel(): lax.ppermute(jnp.stack([held[d] for d in sent]), axis, _pairs(n, flip))]
    ppermute x4 -> x8, starting transfers between devices: 6.39 us -> 13.6 us  [_scatter_rel(): lax.ppermute(jnp.stack([held[d] for d in sent]), axis, _pairs(n, flip))]
    dot_general x2 -> x3, matrix products: 17.4 us -> 20.8 us  [down_pair(): jnp.dot(pair, w, precision=lax.Precision.HIGH, preferred_element_type=jnp...]
  transfers between devices with their start and end apart: 19 -> 23, of which waited for: 16 -> 16; matrix products, arithmetic and copies ran while one was open for 17% -> 17% of each run, Pallas kernels for 0% -> 0%
where the time goes in v8:
time: 131 us; the launch traced here: 130 us
  waiting for transfers between devices  50.7 us (39%)
  matrix products  44.6 us (34%)
  starting transfers between devices  26.9 us (21%)
  other arithmetic  6.85 us (5%)
    dot_general x4, matrix products, up_block(): jnp.dot(gathered, w, precision=lax.Precision.HIGH, preferred_element_type...  23.8 us
    ppermute x4, waiting for transfers between devices, _gather_rel(): lax.ppermute(jnp.stack([held[k] for k in keys]), axis, _pairs(n, flip))  21.1 us
    dot_general x3, matrix products, down_pair(): jnp.dot(pair, w, precision=lax.Precision.HIGH, preferred_element_type=jnp...  20.8 us
    ppermute x8, starting transfers between devices, _scatter_rel(): lax.ppermute(jnp.stack([held[d] for d in sent]), axis, _pairs(n, flip))  13.6 us
    ppermute x8, waiting for transfers between devices, _scatter_rel(): lax.ppermute(jnp.stack([held[d] for d in sent]), axis, _pairs(n, flip))  9.61 us
    ppermute x6, waiting for transfers between devices, _exchange_abs(): got.append(lax.ppermute(blocks[idx ^ d], axis, _pairs(n, d)))  8.19 us
    ppermute x2, waiting for transfers between devices, local(): lax.ppermute(jnp.stack([held[d] for d in sent]), 'row', _pairs(n_row, flip))  5.96 us
    ppermute x6, starting transfers between devices, _exchange_abs(): got.append(lax.ppermute(blocks[idx ^ d], axis, _pairs(n, d)))  5.11 us
  transfers between devices with their start and end apart: 23, of which 16 were waited for; matrix products, arithmetic and copies ran while one was open for 17% of the time, Pallas kernels for 0%

profile of v8, /device:TPU:0, one launch (start us, length us, event | category | flops | bytes accessed | tf_op | source)
XLA Modules:
  0.0 130.3 jit_solution(5347638419544049749)
XLA Ops:
  0.0 0.8 fusion.70
  0.8 1.1 reduce_sum.18
  2.0 1.2 multiply_reduce_fusion
  3.2 1.1 multiply_add_fusion.1
  4.3 2.4 %collective-permute-start.2 = (f32[8,2048]{1,0:T(8,128)S(1)}, f32[8,2048]{1,0:T(8,128)S(1)}, u32[]{:S(2)}, u32[]{:S(2)}) collective-permute-start(f32[8,2048]{1,0:T(8,128)S(1)} %get-tuple-element.36), channel_id=1, source_target_pairs={{0,12},{4,8},{8,4},{12,0},{1,13},{5,9},{9,5},{13,1},{2,14},{6,10},... | collective-permute-start | bytes 196616 | tf_op jit(solution)/shard_map/ppermute | solution.py:44
  6.7 0.7 collective-permute-start
  7.5 1.8 %collective-permute-done.2 = f32[8,2048]{1,0:T(8,128)S(1)} collective-permute-done((f32[8,2048]{1,0:T(8,128)S(1)}, f32[8,2048]{1,0:T(8,128)S(1)}, u32[]{:S(2)}, u32[]{:S(2)}) %collective-permute-start.2) | collective-permute-done | bytes 65568 | tf_op jit(solution)/shard_map/ppermute | solution.py:44
  9.2 2.5 %collective-permute-done.1 = f32[8,2048]{1,0:T(8,128)S(1)} collective-permute-done((f32[8,2048]{1,0:T(8,128)S(1)}, f32[8,2048]{1,0:T(8,128)S(1)}, u32[]{:S(2)}, u32[]{:S(2)}) %collective-permute-start.1) | collective-permute-done | bytes 65568 | tf_op jit(solution)/shard_map/ppermute | solution.py:44
  11.8 2.7 %collective-permute-start.3 = (f32[1,16,2048]{2,1,0:T(8,128)S(1)}, f32[1,16,2048]{2,1,0:T(8,128)S(1)}, u32[]{:S(2)}, u32[]{:S(2)}) collective-permute-start(f32[1,16,2048]{2,1,0:T(8,128)S(1)} %fusion.43), channel_id=1, source_target_pairs={{0,2},{1,3},{2,0},{3,1},{4,6},{5,7},{6,4},{7,5},{8,10},{9,11},{10,... | collective-permute-start | bytes 393224 | tf_op jit(solution)/shard_map/ppermute | solution.py:22
  14.4 0.4 collective-permute-start.5
  14.8 9.1 %collective-permute-done.3 = f32[1,16,2048]{2,1,0:T(8,128)S(1)} collective-permute-done((f32[1,16,2048]{2,1,0:T(8,128)S(1)}, f32[1,16,2048]{2,1,0:T(8,128)S(1)}, u32[]{:S(2)}, u32[]{:S(2)}) %collective-permute-start.3) | collective-permute-done | bytes 131104 | tf_op jit(solution)/shard_map/ppermute | solution.py:22
  24.1 1.6 %collective-permute-done.5 = f32[1,16,2048]{2,1,0:T(8,128)S(1)} collective-permute-done((f32[1,16,2048]{2,1,0:T(8,128)S(1)}, f32[1,16,2048]{2,1,0:T(8,128)S(1)}, u32[]{:S(2)}, u32[]{:S(2)}) %collective-permute-start.5) | collective-permute-done | bytes 131104 | tf_op jit(solution)/shard_map/ppermute | solution.py:22
  25.7 0.6 collective-permute-start.6
  26.3 6.9 %collective-permute-done.4 = f32[2,16,2048]{2,1,0:T(8,128)S(1)} collective-permute-done((f32[2,16,2048]{2,1,0:T(8,128)S(1)}, f32[2,16,2048]{2,1,0:T(8,128)S(1)}, u32[]{:S(2)}, u32[]{:S(2)}) %collective-permute-start.4) | collective-permute-done | bytes 262176 | tf_op jit(solution)/shard_map/ppermute | solution.py:22
  33.4 3.5 %collective-permute-done.6 = f32[2,16,2048]{2,1,0:T(8,128)S(1)} collective-permute-done((f32[2,16,2048]{2,1,0:T(8,128)S(1)}, f32[2,16,2048]{2,1,0:T(8,128)S(1)}, u32[]{:S(2)}, u32[]{:S(2)}) %collective-permute-start.6) | collective-permute-done | bytes 262176 | tf_op jit(solution)/shard_map/ppermute | solution.py:22
  36.9 6.0 %fusion.10 = f32[128,1024]{1,0:T(8,128)S(1)} fusion(f32[128,2048]{1,0:T(8,128)S(1)} %fusion.38, f32[2048,4096]{1,0:T(8,128)} %param.8, s32[]{:T(128)S(6)} %select_n.80), kind=kOutput, calls=%fused_computation.10 | convolution fusion | flops 1610612736 | bytes 9961476 | tf_op jit(solution)/shard_map/dot_general | solution.py:78
  42.8 6.0 %fusion.8 = f32[128,1024]{1,0:T(8,128)S(1)} fusion(f32[128,2048]{1,0:T(8,128)S(1)} %fusion.38, f32[2048,4096]{1,0:T(8,128)} %param.8, s32[]{:T(128)S(6)} %select_n.81), kind=kOutput, calls=%fused_computation.8 | convolution fusion | flops 1610612736 | bytes 9961476 | tf_op jit(solution)/shard_map/dot_general | solution.py:78
  48.8 1.1 pad_maximum_fusion
  49.9 6.0 %fusion.6 = f32[128,1024]{1,0:T(8,128)S(1)} fusion(f32[128,2048]{1,0:T(8,128)S(1)} %fusion.38, f32[2048,4096]{1,0:T(8,128)} %param.8, s32[]{:T(128)S(6)} %select_n.82), kind=kOutput, calls=%fused_computation.6 | convolution fusion | flops 1610612736 | bytes 9961476 | tf_op jit(solution)/shard_map/dot_general | solution.py:78
  55.9 0.1 fusion.27
  55.9 2.5 %collective-permute-start.8 = (f32[1,128,1024]{2,1,0:T(8,128)S(1)}, f32[1,128,1024]{2,1,0:T(8,128)S(1)}, u32[]{:S(2)}, u32[]{:S(2)}) collective-permute-start(f32[1,128,1024]{2,1,0:T(8,128)S(1)} %fusion.27), channel_id=1, source_target_pairs={{0,8},{4,12},{8,0},{12,4},{1,9},{5,13},{9,1},{13,5},{2,10},{6,14},... | collective-permute-start | bytes 1572872 | tf_op jit(solution)/shard_map/ppermute | solution.py:85
  58.5 0.7 dynamic_slice.76
  59.2 5.9 %fusion.12 = f32[128,1024]{1,0:T(8,128)S(1)} fusion(f32[128,2048]{1,0:T(8,128)S(1)} %fusion.38, f32[2048,4096]{1,0:T(8,128)} %param.8, s32[]{:T(128)S(6)} %select_n.79), kind=kOutput, calls=%fused_computation.12 | convolution fusion | flops 1610612736 | bytes 9961476 | tf_op jit(solution)/shard_map/dot_general | solution.py:78
  65.1 6.0 %collective-permute-done.8 = f32[1,128,1024]{2,1,0:T(8,128)S(1)} collective-permute-done((f32[1,128,1024]{2,1,0:T(8,128)S(1)}, f32[1,128,1024]{2,1,0:T(8,128)S(1)}, u32[]{:S(2)}, u32[]{:S(2)}) %collective-permute-start.8) | collective-permute-done | bytes 524320 | tf_op jit(solution)/shard_map/ppermute | solution.py:85
  71.1 0.4 fusion.25
  71.6 1.8 %collective-permute-start.9 = (f32[1,128,1024]{2,1,0:T(8,128)S(1)}, f32[1,128,1024]{2,1,0:T(8,128)S(1)}, u32[]{:S(2)}, u32[]{:S(2)}) collective-permute-start(f32[1,128,1024]{2,1,0:T(8,128)S(1)} %bitcast.166), channel_id=1, source_target_pairs={{0,8},{4,12},{8,0},{12,4},{1,9},{5,13},{9,1},{13,5},{2,10},{6,14},... | collective-permute-start | bytes 1572872 | tf_op jit(solution)/shard_map/ppermute | solution.py:94
  73.4 0.1 collective-permute-done.10
  73.5 8.7 %fusion = f32[128,2048]{1,0:T(8,128)S(1)} fusion(f32[4096,2048]{1,0:T(8,128)} %param.10, s32[]{:T(128)S(6)} %select_n.87, f32[128,1024]{1,0:T(8,128)S(1)} %collective-permute-done.10, f32[128,1024]{1,0:T(8,128)S(1)} %fusion.25, pred[]{:T(512)S(6)} %eq.4), kind=kOutput, calls=%fused_computation | convolution fusion | flops 3222011904 | bytes 18874372 | tf_op jit(solution)/shard_map/dot_general | solution.py:106
  82.1 3.8 %collective-permute-done.9 = f32[1,128,1024]{2,1,0:T(8,128)S(1)} collective-permute-done((f32[1,128,1024]{2,1,0:T(8,128)S(1)}, f32[1,128,1024]{2,1,0:T(8,128)S(1)}, u32[]{:S(2)}, u32[]{:S(2)}) %collective-permute-start.9) | collective-permute-done | bytes 524320 | tf_op jit(solution)/shard_map/ppermute | solution.py:94
  85.9 1.9 %collective-permute-done.11 = f32[1,128,1024]{2,1,0:T(8,128)S(1)} collective-permute-done((f32[1,128,1024]{2,1,0:T(8,128)S(1)}, f32[1,128,1024]{2,1,0:T(8,128)S(1)}, u32[]{:S(2)}, u32[]{:S(2)}) %collective-permute-start.11) | collective-permute-done | bytes 524320 | tf_op jit(solution)/shard_map/ppermute | solution.py:115
  87.8 6.0 %slice_add_fusion.1 = f32[128,1024]{1,0:T(8,128)S(1)} fusion(f32[128,2048]{1,0:T(8,128)S(1)} %fusion, f32[4096,2048]{1,0:T(8,128)} %param.10, s32[]{:T(128)S(6)} %select_n.90, f32[128,1024]{1,0:T(8,128)S(1)} %bitcast.171, f32[128,1024]{1,0:T(8,128)S(1)} %bitcast.169, pred[]{:T(512)S(6)} %eq.4), kind=kOutput, calls=%fused_computation.38 | convolution fusion | flops 1611530240 | bytes 10485765 | tf_op jit(solution)/shard_map/dot_general | solution.py:106
  93.9 6.1 %slice_add_fusion = f32[128,1024]{1,0:T(8,128)S(1)} fusion(f32[128,2048]{1,0:T(8,128)S(1)} %fusion, f32[4096,2048]{1,0:T(8,128)} %param.10, s32[]{:T(128)S(6)} %select_n.90, f32[128,1024]{1,0:T(8,128)S(1)} %bitcast.172, f32[128,1024]{1,0:T(8,128)S(1)} %bitcast.170, pred[]{:T(512)S(6)} %eq.4), kind=kOutput, calls=%fused_computation.37 | convolution fusion | flops 1611530240 | bytes 10485765 | tf_op jit(solution)/shard_map/dot_general | solution.py:106
  100.0 0.6 collective-permute-start.12
  100.6 1.5 %collective-permute-start.14 = (f32[2,16,1024]{2,1,0:T(8,128)S(1)}, f32[2,16,1024]{2,1,0:T(8,128)S(1)}, u32[]{:S(2)}, u32[]{:S(2)}) collective-permute-start(f32[2,16,1024]{2,1,0:T(8,128)S(1)} %pad_maximum_fusion.9), channel_id=1, source_target_pairs={{0,1},{1,0},{2,3},{3,2},{4,5},{5,4},{6,7},{7,6},{8,9},{9,8},{10,11... | collective-permute-start | bytes 393224 | tf_op jit(solution)/shard_map/ppermute | solution.py:35
  102.2 4.2 %collective-permute-done.12 = f32[2,16,1024]{2,1,0:T(8,128)S(1)} collective-permute-done((f32[2,16,1024]{2,1,0:T(8,128)S(1)}, f32[2,16,1024]{2,1,0:T(8,128)S(1)}, u32[]{:S(2)}, u32[]{:S(2)}) %collective-permute-start.12) | collective-permute-done | bytes 131104 | tf_op jit(solution)/shard_map/ppermute | solution.py:35
  106.4 0.6 collective-permute-start.16
  107.1 3.5 %collective-permute-start.13 = (f32[1,16,1024]{2,1,0:T(8,128)S(1)}, f32[1,16,1024]{2,1,0:T(8,128)S(1)}, u32[]{:S(2)}, u32[]{:S(2)}) collective-permute-start(f32[1,16,1024]{2,1,0:T(8,128)S(1)} %get-tuple-element.11), channel_id=1, source_target_pairs={{0,2},{1,3},{2,0},{3,1},{4,6},{5,7},{6,4},{7,5},{8,10},{9,11},{10,... | collective-permute-start | bytes 196616 | tf_op jit(solution)/shard_map/ppermute | solution.py:35
  110.6 0.2 collective-permute-start.18
  110.8 3.2 %collective-permute-start.15 = (f32[1,16,1024]{2,1,0:T(8,128)S(1)}, f32[1,16,1024]{2,1,0:T(8,128)S(1)}, u32[]{:S(2)}, u32[]{:S(2)}) collective-permute-start(f32[1,16,1024]{2,1,0:T(8,128)S(1)} %get-tuple-element.18), channel_id=1, source_target_pairs={{0,2},{1,3},{2,0},{3,1},{4,6},{5,7},{6,4},{7,5},{8,10},{9,11},{10,... | collective-permute-start | bytes 196616 | tf_op jit(solution)/shard_map/ppermute | solution.py:35
  114.0 2.6 %collective-permute-start.17 = (f32[1,16,1024]{2,1,0:T(8,128)S(1)}, f32[1,16,1024]{2,1,0:T(8,128)S(1)}, u32[]{:S(2)}, u32[]{:S(2)}) collective-permute-start(f32[1,16,1024]{2,1,0:T(8,128)S(1)} %get-tuple-element.10), channel_id=1, source_target_pairs={{0,2},{1,3},{2,0},{3,1},{4,6},{5,7},{6,4},{7,5},{8,10},{9,11},{10,... | collective-permute-start | bytes 196616 | tf_op jit(solution)/shard_map/ppermute | solution.py:35
  116.6 1.5 %collective-permute-done.15 = f32[1,16,1024]{2,1,0:T(8,128)S(1)} collective-permute-done((f32[1,16,1024]{2,1,0:T(8,128)S(1)}, f32[1,16,1024]{2,1,0:T(8,128)S(1)}, u32[]{:S(2)}, u32[]{:S(2)}) %collective-permute-start.15) | collective-permute-done | bytes 65568 | tf_op jit(solution)/shard_map/ppermute | solution.py:35
  118.1 1.3 %collective-permute-start.19 = (f32[1,16,1024]{2,1,0:T(8,128)S(1)}, f32[1,16,1024]{2,1,0:T(8,128)S(1)}, u32[]{:S(2)}, u32[]{:S(2)}) collective-permute-start(f32[1,16,1024]{2,1,0:T(8,128)S(1)} %get-tuple-element.17), channel_id=1, source_target_pairs={{0,2},{1,3},{2,0},{3,1},{4,6},{5,7},{6,4},{7,5},{8,10},{9,11},{10,... | collective-permute-start | bytes 196616 | tf_op jit(solution)/shard_map/ppermute | solution.py:35
  119.5 2.5 %collective-permute-done.17 = f32[1,16,1024]{2,1,0:T(8,128)S(1)} collective-permute-done((f32[1,16,1024]{2,1,0:T(8,128)S(1)}, f32[1,16,1024]{2,1,0:T(8,128)S(1)}, u32[]{:S(2)}, u32[]{:S(2)}) %collective-permute-start.17) | collective-permute-done | bytes 65568 | tf_op jit(solution)/shard_map/ppermute | solution.py:35
  122.0 1.3 %collective-permute-done.19 = f32[1,16,1024]{2,1,0:T(8,128)S(1)} collective-permute-done((f32[1,16,1024]{2,1,0:T(8,128)S(1)}, f32[1,16,1024]{2,1,0:T(8,128)S(1)}, u32[]{:S(2)}, u32[]{:S(2)}) %collective-permute-start.19) | collective-permute-done | bytes 65568 | tf_op jit(solution)/shard_map/ppermute | solution.py:35
  123.5 1.8 %collective-permute-start.21 = (f32[8,2048]{1,0:T(8,128)S(1)}, f32[8,2048]{1,0:T(8,128)S(1)}, u32[]{:S(2)}, u32[]{:S(2)}) collective-permute-start(f32[8,2048]{1,0:T(8,128)S(1)} %get-tuple-element.29), channel_id=1, source_target_pairs={{0,8},{4,12},{8,0},{12,4},{1,9},{5,13},{9,1},{13,5},{2,10},{6,14},... | collective-permute-start | bytes 196616 | tf_op jit(solution)/shard_map/ppermute | solution.py:44
  125.4 2.6 %collective-permute-done.21 = f32[8,2048]{1,0:T(8,128)S(1)} collective-permute-done((f32[8,2048]{1,0:T(8,128)S(1)}, f32[8,2048]{1,0:T(8,128)S(1)}, u32[]{:S(2)}, u32[]{:S(2)}) %collective-permute-start.21) | collective-permute-done | bytes 65568 | tf_op jit(solution)/shard_map/ppermute | solution.py:44
  128.0 1.3 %collective-permute-done.22 = f32[8,2048]{1,0:T(8,128)S(1)} collective-permute-done((f32[8,2048]{1,0:T(8,128)S(1)}, f32[8,2048]{1,0:T(8,128)S(1)}, u32[]{:S(2)}, u32[]{:S(2)}) %collective-permute-start.22) | collective-permute-done | bytes 65568 | tf_op jit(solution)/shard_map/ppermute | solution.py:44
  129.5 0.8 multiply_add_fusion
  (52 shorter events, 0.9 us)
Async XLA Ops:
  4.3 4.9 %collective-permute-start.2 = (f32[8,2048]{1,0:T(8,128)S(1)}, f32[8,2048]{1,0:T(8,128)S(1)}, u32[]{:S(2)}, u32[]{:S(2)}) collective-permute-start(f32[8,2048]{1,0:T(8,128)S(1)} %get-tuple-element.36), channel_id=1, source_target_pairs={{0,12},{4,8},{8,4},{12,0},{1,13},{5,9},{9,5},{13,1},{2,14},{6,10},... | collective-permute-start | bytes 196616 | tf_op jit(solution)/shard_map/ppermute | solution.py:44
  6.7 2.5 %collective-permute-start = (f32[8,2048]{1,0:T(8,128)S(1)}, f32[8,2048]{1,0:T(8,128)S(1)}, u32[]{:S(2)}, u32[]{:S(2)}) collective-permute-start(f32[8,2048]{1,0:T(8,128)S(1)} %get-tuple-element.38), channel_id=1, source_target_pairs={{0,4},{4,0},{8,12},{12,8},{1,5},{5,1},{9,13},{13,9},{2,6},{6,2},{1... | collective-permute-start | bytes 196616 | tf_op jit(solution)/shard_map/ppermute | solution.py:44
  7.4 4.3 %collective-permute-start.1 = (f32[8,2048]{1,0:T(8,128)S(1)}, f32[8,2048]{1,0:T(8,128)S(1)}, u32[]{:S(2)}, u32[]{:S(2)}) collective-permute-start(f32[8,2048]{1,0:T(8,128)S(1)} %get-tuple-element.37), channel_id=1, source_target_pairs={{0,8},{4,12},{8,0},{12,4},{1,9},{5,13},{9,1},{13,5},{2,10},{6,14},... | collective-permute-start | bytes 196616 | tf_op jit(solution)/shard_map/ppermute | solution.py:44
  11.8 12.2 %collective-permute-start.3 = (f32[1,16,2048]{2,1,0:T(8,128)S(1)}, f32[1,16,2048]{2,1,0:T(8,128)S(1)}, u32[]{:S(2)}, u32[]{:S(2)}) collective-permute-start(f32[1,16,2048]{2,1,0:T(8,128)S(1)} %fusion.43), channel_id=1, source_target_pairs={{0,2},{1,3},{2,0},{3,1},{4,6},{5,7},{6,4},{7,5},{8,10},{9,11},{10,... | collective-permute-start | bytes 393224 | tf_op jit(solution)/shard_map/ppermute | solution.py:22
  14.4 11.3 %collective-permute-start.5 = (f32[1,16,2048]{2,1,0:T(8,128)S(1)}, f32[1,16,2048]{2,1,0:T(8,128)S(1)}, u32[]{:S(2)}, u32[]{:S(2)}) collective-permute-start(f32[1,16,2048]{2,1,0:T(8,128)S(1)} %fusion.42), channel_id=1, source_target_pairs={{0,2},{1,3},{2,0},{3,1},{4,6},{5,7},{6,4},{7,5},{8,10},{9,11},{10,... | collective-permute-start | bytes 393224 | tf_op jit(solution)/shard_map/ppermute | solution.py:22
  24.0 9.3 %collective-permute-start.4 = (f32[2,16,2048]{2,1,0:T(8,128)S(1)}, f32[2,16,2048]{2,1,0:T(8,128)S(1)}, u32[]{:S(2)}, u32[]{:S(2)}) collective-permute-start(f32[2,16,2048]{2,1,0:T(8,128)S(1)} %pad_maximum_fusion.2), channel_id=1, source_target_pairs={{0,1},{1,0},{2,3},{3,2},{4,5},{5,4},{6,7},{7,6},{8,9},{9,8},{10,11... | collective-permute-start | bytes 786440 | tf_op jit(solution)/shard_map/ppermute | solution.py:22
  25.7 11.1 %collective-permute-start.6 = (f32[2,16,2048]{2,1,0:T(8,128)S(1)}, f32[2,16,2048]{2,1,0:T(8,128)S(1)}, u32[]{:S(2)}, u32[]{:S(2)}) collective-permute-start(f32[2,16,2048]{2,1,0:T(8,128)S(1)} %pad_maximum_fusion.3), channel_id=1, source_target_pairs={{0,1},{1,0},{2,3},{3,2},{4,5},{5,4},{6,7},{7,6},{8,9},{9,8},{10,11... | collective-permute-start | bytes 786440 | tf_op jit(solution)/shard_map/ppermute | solution.py:22
  49.8 6.0 %collective-permute-start.7 = (f32[2,128,1024]{2,1,0:T(8,128)}, f32[2,128,1024]{2,1,0:T(8,128)S(1)}, u32[]{:S(2)}, u32[]{:S(2)}) collective-permute-start(f32[2,128,1024]{2,1,0:T(8,128)} %pad_maximum_fusion), channel_id=1, source_target_pairs={{0,4},{4,0},{8,12},{12,8},{1,5},{5,1},{9,13},{13,9},{2,6},{6,2},{1... | collective-permute-start | bytes 3145736 | tf_op jit(solution)/shard_map/ppermute | solution.py:85
  49.9 79.6 %copy-start = (f32[8,8192]{1,0:T(8,128)S(1)}, f32[8,8192]{1,0:T(8,128)}, u32[]{:S(2)}) copy-start(f32[8,8192]{1,0:T(8,128)} %param.6) | copy-start | bytes 786436
  49.9 79.6 %copy-start.1 = (f32[8192]{0:T(1024)S(1)}, f32[8192]{0:T(1024)}, u32[]{:S(2)}) copy-start(f32[8192]{0:T(1024)} %param.11) | copy-start | bytes 98308
  55.9 15.1 %collective-permute-start.8 = (f32[1,128,1024]{2,1,0:T(8,128)S(1)}, f32[1,128,1024]{2,1,0:T(8,128)S(1)}, u32[]{:S(2)}, u32[]{:S(2)}) collective-permute-start(f32[1,128,1024]{2,1,0:T(8,128)S(1)} %fusion.27), channel_id=1, source_target_pairs={{0,8},{4,12},{8,0},{12,4},{1,9},{5,13},{9,1},{13,5},{2,10},{6,14},... | collective-permute-start | bytes 1572872 | tf_op jit(solution)/shard_map/ppermute | solution.py:85
  71.5 2.0 %collective-permute-start.10 = (f32[128,1024]{1,0:T(8,128)S(1)}, f32[128,1024]{1,0:T(8,128)S(1)}, u32[]{:S(2)}, u32[]{:S(2)}) collective-permute-start(f32[128,1024]{1,0:T(8,128)S(1)} %fusion.25), channel_id=1, source_target_pairs={{0,4},{4,0},{8,12},{12,8},{1,5},{5,1},{9,13},{13,9},{2,6},{6,2},{1... | collective-permute-start | bytes 1572872 | tf_op jit(solution)/shard_map/ppermute | solution.py:90
  71.6 14.3 %collective-permute-start.9 = (f32[1,128,1024]{2,1,0:T(8,128)S(1)}, f32[1,128,1024]{2,1,0:T(8,128)S(1)}, u32[]{:S(2)}, u32[]{:S(2)}) collective-permute-start(f32[1,128,1024]{2,1,0:T(8,128)S(1)} %bitcast.166), channel_id=1, source_target_pairs={{0,8},{4,12},{8,0},{12,4},{1,9},{5,13},{9,1},{13,5},{2,10},{6,14},... | collective-permute-start | bytes 1572872 | tf_op jit(solution)/shard_map/ppermute | solution.py:94
  85.9 1.9 %collective-permute-start.11 = (f32[1,128,1024]{2,1,0:T(8,128)S(1)}, f32[1,128,1024]{2,1,0:T(8,128)S(1)}, u32[]{:S(2)}, u32[]{:S(2)}) collective-permute-start(f32[1,128,1024]{2,1,0:T(8,128)S(1)} %collective-permute-done.9), channel_id=1, source_target_pairs={{0,4},{4,0},{8,12},{12,8},{1,5},{5,1},{9,13},{13,9},{2,6},{6,2},{1... | collective-permute-start | bytes 1572872 | tf_op jit(solution)/shard_map/ppermute | solution.py:115
  100.0 6.4 %collective-permute-start.12 = (f32[2,16,1024]{2,1,0:T(8,128)S(1)}, f32[2,16,1024]{2,1,0:T(8,128)S(1)}, u32[]{:S(2)}, u32[]{:S(2)}) collective-permute-start(f32[2,16,1024]{2,1,0:T(8,128)S(1)} %pad_maximum_fusion.8), channel_id=1, source_target_pairs={{0,1},{1,0},{2,3},{3,2},{4,5},{5,4},{6,7},{7,6},{8,9},{9,8},{10,11... | collective-permute-start | bytes 393224 | tf_op jit(solution)/shard_map/ppermute | solution.py:35
  100.6 9.9 %collective-permute-start.14 = (f32[2,16,1024]{2,1,0:T(8,128)S(1)}, f32[2,16,1024]{2,1,0:T(8,128)S(1)}, u32[]{:S(2)}, u32[]{:S(2)}) collective-permute-start(f32[2,16,1024]{2,1,0:T(8,128)S(1)} %pad_maximum_fusion.9), channel_id=1, source_target_pairs={{0,1},{1,0},{2,3},{3,2},{4,5},{5,4},{6,7},{7,6},{8,9},{9,8},{10,11... | collective-permute-start | bytes 393224 | tf_op jit(solution)/shard_map/ppermute | solution.py:35
  106.4 7.6 %collective-permute-start.16 = (f32[2,16,1024]{2,1,0:T(8,128)S(1)}, f32[2,16,1024]{2,1,0:T(8,128)S(1)}, u32[]{:S(2)}, u32[]{:S(2)}) collective-permute-start(f32[2,16,1024]{2,1,0:T(8,128)S(1)} %pad_maximum_fusion.10), channel_id=1, source_target_pairs={{0,1},{1,0},{2,3},{3,2},{4,5},{5,4},{6,7},{7,6},{8,9},{9,8},{10,11... | collective-permute-start | bytes 393224 | tf_op jit(solution)/shard_map/ppermute | solution.py:35
  107.1 6.9 %collective-permute-start.13 = (f32[1,16,1024]{2,1,0:T(8,128)S(1)}, f32[1,16,1024]{2,1,0:T(8,128)S(1)}, u32[]{:S(2)}, u32[]{:S(2)}) collective-permute-start(f32[1,16,1024]{2,1,0:T(8,128)S(1)} %get-tuple-element.11), channel_id=1, source_target_pairs={{0,2},{1,3},{2,0},{3,1},{4,6},{5,7},{6,4},{7,5},{8,10},{9,11},{10,... | collective-permute-start | bytes 196616 | tf_op jit(solution)/shard_map/ppermute | solution.py:35
  110.6 7.5 %collective-permute-start.18 = (f32[2,16,1024]{2,1,0:T(8,128)S(1)}, f32[2,16,1024]{2,1,0:T(8,128)S(1)}, u32[]{:S(2)}, u32[]{:S(2)}) collective-permute-start(f32[2,16,1024]{2,1,0:T(8,128)S(1)} %pad_maximum_fusion.11), channel_id=1, source_target_pairs={{0,1},{1,0},{2,3},{3,2},{4,5},{5,4},{6,7},{7,6},{8,9},{9,8},{10,11... | collective-permute-start | bytes 393224 | tf_op jit(solution)/shard_map/ppermute | solution.py:35
  110.8 7.3 %collective-permute-start.15 = (f32[1,16,1024]{2,1,0:T(8,128)S(1)}, f32[1,16,1024]{2,1,0:T(8,128)S(1)}, u32[]{:S(2)}, u32[]{:S(2)}) collective-permute-start(f32[1,16,1024]{2,1,0:T(8,128)S(1)} %get-tuple-element.18), channel_id=1, source_target_pairs={{0,2},{1,3},{2,0},{3,1},{4,6},{5,7},{6,4},{7,5},{8,10},{9,11},{10,... | collective-permute-start | bytes 196616 | tf_op jit(solution)/shard_map/ppermute | solution.py:35
  114.0 8.0 %collective-permute-start.17 = (f32[1,16,1024]{2,1,0:T(8,128)S(1)}, f32[1,16,1024]{2,1,0:T(8,128)S(1)}, u32[]{:S(2)}, u32[]{:S(2)}) collective-permute-start(f32[1,16,1024]{2,1,0:T(8,128)S(1)} %get-tuple-element.10), channel_id=1, source_target_pairs={{0,2},{1,3},{2,0},{3,1},{4,6},{5,7},{6,4},{7,5},{8,10},{9,11},{10,... | collective-permute-start | bytes 196616 | tf_op jit(solution)/shard_map/ppermute | solution.py:35
  118.1 5.2 %collective-permute-start.19 = (f32[1,16,1024]{2,1,0:T(8,128)S(1)}, f32[1,16,1024]{2,1,0:T(8,128)S(1)}, u32[]{:S(2)}, u32[]{:S(2)}) collective-permute-start(f32[1,16,1024]{2,1,0:T(8,128)S(1)} %get-tuple-element.17), channel_id=1, source_target_pairs={{0,2},{1,3},{2,0},{3,1},{4,6},{5,7},{6,4},{7,5},{8,10},{9,11},{10,... | collective-permute-start | bytes 196616 | tf_op jit(solution)/shard_map/ppermute | solution.py:35
  123.5 2.0 %collective-permute-start.20 = (f32[8,2048]{1,0:T(8,128)S(1)}, f32[8,2048]{1,0:T(8,128)S(1)}, u32[]{:S(2)}, u32[]{:S(2)}) collective-permute-start(f32[8,2048]{1,0:T(8,128)S(1)} %get-tuple-element.30), channel_id=1, source_target_pairs={{0,4},{4,0},{8,12},{12,8},{1,5},{5,1},{9,13},{13,9},{2,6},{6,2},{1... | collective-permute-start | bytes 196616 | tf_op jit(solution)/shard_map/ppermute | solution.py:44
  123.5 4.5 %collective-permute-start.21 = (f32[8,2048]{1,0:T(8,128)S(1)}, f32[8,2048]{1,0:T(8,128)S(1)}, u32[]{:S(2)}, u32[]{:S(2)}) collective-permute-start(f32[8,2048]{1,0:T(8,128)S(1)} %get-tuple-element.29), channel_id=1, source_target_pairs={{0,8},{4,12},{8,0},{12,4},{1,9},{5,13},{9,1},{13,5},{2,10},{6,14},... | collective-permute-start | bytes 196616 | tf_op jit(solution)/shard_map/ppermute | solution.py:44
  125.3 4.0 %collective-permute-start.22 = (f32[8,2048]{1,0:T(8,128)S(1)}, f32[8,2048]{1,0:T(8,128)S(1)}, u32[]{:S(2)}, u32[]{:S(2)}) collective-permute-start(f32[8,2048]{1,0:T(8,128)S(1)} %get-tuple-element.28), channel_id=1, source_target_pairs={{0,12},{4,8},{8,4},{12,0},{1,13},{5,9},{9,5},{13,1},{2,14},{6,10},... | collective-permute-start | bytes 196616 | tf_op jit(solution)/shard_map/ppermute | solution.py:44

commit v9 on v7

--- a/solution.py
+++ b/solution.py
@@ -2,6 +2,8 @@
 import jax.numpy as jnp
 from jax import lax
 from jax.sharding import PartitionSpec as P
+from jax.experimental import pallas as pl
+from jax.experimental.pallas import tpu as pltpu
 
 SEQ = 256
 N_CHUNK = 2
@@ -46,20 +48,35 @@
     return jnp.stack([rel[s ^ idx] for s in range(n)])
 
 
+def _norm_kernel(x_ref, m_ref, o_ref):
+    x = x_ref[...]
+    average = jnp.mean(x, axis=1, keepdims=True)
+    centred = x - average
+    spread_sq = jnp.mean(centred * centred, axis=1, keepdims=True)
+    normed = centred * lax.rsqrt(spread_sq + layer_eps)
+    o_ref[...] = normed * (1.0 + m_ref[1:2, :]) + m_ref[0:1, :]
+
+
+def _norm_modulate(tokens, mods):
+    rows, width = tokens.shape
+    return pl.pallas_call(
+        _norm_kernel,
+        out_shape=jax.ShapeDtypeStruct(tokens.shape, jnp.float32),
+        in_specs=[pl.BlockSpec(memory_space=pltpu.VMEM)] * 2,
+        out_specs=pl.BlockSpec(memory_space=pltpu.VMEM),
+        cost_estimate=pl.CostEstimate(flops=8 * rows * width, transcendentals=rows,
+                                      bytes_accessed=4 * (2 * rows + 3) * width),
+    )(tokens, mods)
+
+
 def local(tokens, modulation, up_weight, up_bias, down_weight, down_bias):
     n_row = lax.axis_size("row")
     tok_dev = tokens.shape[0]
     first_tok = (lax.axis_index("row") * lax.axis_size("col") + lax.axis_index("col")) * tok_dev
     sample = first_tok // SEQ
     own_mods = lax.dynamic_slice_in_dim(modulation, sample, 1, 1)[:, 0]
-    shift_vec = own_mods[0]
-    scale_vec = own_mods[1]
     gate_vec = own_mods[2]
-    average = jnp.mean(tokens, axis=1, keepdims=True)
-    centred = tokens - average
-    spread_sq = jnp.mean(centred * centred, axis=1, keepdims=True)
-    normed = centred * lax.rsqrt(spread_sq + layer_eps)
-    mixed = normed * (1.0 + scale_vec) + shift_vec
+    mixed = _norm_modulate(tokens, own_mods)
     r = lax.axis_index("row")
     d_blk = mixed.shape[1] // n_row
     sent_in = mixed.reshape(tok_dev, n_row, d_blk).swapaxes(0, 1)

time: 129 us -> 130 us (level)
  other arithmetic: 7 us -> 2.77 us
  local copies, waits for them, and re-layouts: 0.9 us -> 3.44 us
  Pallas kernels: 0 us -> 2.03 us
  starting transfers between devices: 19.7 us -> 18.4 us
    reduce_sum x2 -> x0, other arithmetic: 2.33 us -> none  [the longest x1 1.2 us: local(): spread_sq = jnp.mean(centred * centred, axis=1, keepdims=True)]
    pallas_call x0 -> x1, Pallas kernels: none -> 2.03 us  [_norm_modulate(): pl.pallas_call(_norm_kernel, out_shape=jax.ShapeDtypeStruct(tokens.shape,...]
    unnamed x9 -> x10, local copies, waits for them, and re-layouts: 0.06 us -> 1.67 us
where the time goes in v9:
time: 130 us; the launch traced here: 129 us
  waiting for transfers between devices  61.1 us (47%)
  matrix products  41.2 us (32%)
  starting transfers between devices  18.4 us (14%)
  local copies, waits for them, and re-layouts  3.44 us (3%)
  other arithmetic  2.77 us (2%)
  Pallas kernels  2.03 us (2%)
    dot_general x4, matrix products, up_block(): jnp.dot(gathered, w, precision=lax.Precision.HIGH, preferred_element_type...  23.8 us
    ppermute x4, waiting for transfers between devices, _gather_rel(): lax.ppermute(jnp.stack([held[k] for k in keys]), axis, _pairs(n, flip))  22.2 us
    ppermute x4, waiting for transfers between devices, _scatter_rel(): lax.ppermute(jnp.stack([held[d] for d in sent]), axis, _pairs(n, flip))  18.8 us
    dot_general x2, matrix products, down_pair(): jnp.dot(pair, w, precision=lax.Precision.HIGH, preferred_element_type=jnp...  17.4 us
    ppermute x6, waiting for transfers between devices, _exchange_abs(): got.append(lax.ppermute(blocks[idx ^ d], axis, _pairs(n, d)))  7.7 us
    ppermute x4, starting transfers between devices, _scatter_rel(): lax.ppermute(jnp.stack([held[d] for d in sent]), axis, _pairs(n, flip))  6.4 us
    ppermute x2, waiting for transfers between devices, local(): lax.ppermute(jnp.stack([held[d] for d in sent]), 'row', _pairs(n_row, flip))  6.24 us
    ppermute x6, starting transfers between devices, _exchange_abs(): got.append(lax.ppermute(blocks[idx ^ d], axis, _pairs(n, d)))  5.08 us
  transfers between devices with their start and end apart: 19, of which 16 were waited for; matrix products, arithmetic and copies ran while one was open for 17% of the time, Pallas kernels for 0%

profile of v9, /device:TPU:0, one launch (start us, length us, event | category | flops | bytes accessed | tf_op | source)
XLA Modules:
  0.0 129.2 jit_solution(18417501214944589975)
XLA Ops:
  0.0 1.6 %copy.9 = f32[3,1,8192]{2,0,1:T(4,128)} copy(f32[3,1,8192]{2,1,0:T(1,128)} %param.7) | data formatting | bytes 196608
  1.6 2.0 %shard_map.64 = f32[8,8192]{1,0:T(8,128)} custom-call(f32[8,8192]{1,0:T(8,128)} %x_ref.1, f32[3,8192]{1,0:T(4,128)} %bitcast.134), custom_call_target="tpu_custom_call" | custom-call | flops 524288 | bytes 622592 | tf_op jit(solution)/shard_map/pallas_call | solution.py:62
  3.6 1.0 dynamic-slice_bitcast_fusion.6
  4.6 0.5 collective-permute-start
  5.1 2.6 %collective-permute-start.1 = (f32[8,2048]{1,0:T(8,128)S(1)}, f32[8,2048]{1,0:T(8,128)S(1)}, u32[]{:S(2)}, u32[]{:S(2)}) collective-permute-start(f32[8,2048]{1,0:T(8,128)S(1)} %get-tuple-element.30), channel_id=1, source_target_pairs={{0,8},{4,12},{8,0},{12,4},{1,9},{5,13},{9,1},{13,5},{2,10},{6,14},... | collective-permute-start | bytes 196616 | tf_op jit(solution)/shard_map/ppermute | solution.py:46
  7.7 0.1 collective-permute-start.2
  7.8 2.6 %collective-permute-done.1 = f32[8,2048]{1,0:T(8,128)S(1)} collective-permute-done((f32[8,2048]{1,0:T(8,128)S(1)}, f32[8,2048]{1,0:T(8,128)S(1)}, u32[]{:S(2)}, u32[]{:S(2)}) %collective-permute-start.1) | collective-permute-done | bytes 65568 | tf_op jit(solution)/shard_map/ppermute | solution.py:46
  10.4 1.4 %collective-permute-done.2 = f32[8,2048]{1,0:T(8,128)S(1)} collective-permute-done((f32[8,2048]{1,0:T(8,128)S(1)}, f32[8,2048]{1,0:T(8,128)S(1)}, u32[]{:S(2)}, u32[]{:S(2)}) %collective-permute-start.2) | collective-permute-done | bytes 65568 | tf_op jit(solution)/shard_map/ppermute | solution.py:46
  11.8 2.7 %collective-permute-start.3 = (f32[1,16,2048]{2,1,0:T(8,128)S(1)}, f32[1,16,2048]{2,1,0:T(8,128)S(1)}, u32[]{:S(2)}, u32[]{:S(2)}) collective-permute-start(f32[1,16,2048]{2,1,0:T(8,128)S(1)} %fusion.49), channel_id=1, source_target_pairs={{0,2},{1,3},{2,0},{3,1},{4,6},{5,7},{6,4},{7,5},{8,10},{9,11},{10,... | collective-permute-start | bytes 393224 | tf_op jit(solution)/shard_map/ppermute | solution.py:24
  14.5 0.4 collective-permute-start.5
  14.9 9.9 %collective-permute-done.3 = f32[1,16,2048]{2,1,0:T(8,128)S(1)} collective-permute-done((f32[1,16,2048]{2,1,0:T(8,128)S(1)}, f32[1,16,2048]{2,1,0:T(8,128)S(1)}, u32[]{:S(2)}, u32[]{:S(2)}) %collective-permute-start.3) | collective-permute-done | bytes 131104 | tf_op jit(solution)/shard_map/ppermute | solution.py:24
  24.8 0.1 collective-permute-start.4
  24.9 2.0 %collective-permute-done.5 = f32[1,16,2048]{2,1,0:T(8,128)S(1)} collective-permute-done((f32[1,16,2048]{2,1,0:T(8,128)S(1)}, f32[1,16,2048]{2,1,0:T(8,128)S(1)}, u32[]{:S(2)}, u32[]{:S(2)}) %collective-permute-start.5) | collective-permute-done | bytes 131104 | tf_op jit(solution)/shard_map/ppermute | solution.py:24
  26.9 0.7 collective-permute-start.6
  27.5 6.5 %collective-permute-done.4 = f32[2,16,2048]{2,1,0:T(8,128)S(1)} collective-permute-done((f32[2,16,2048]{2,1,0:T(8,128)S(1)}, f32[2,16,2048]{2,1,0:T(8,128)S(1)}, u32[]{:S(2)}, u32[]{:S(2)}) %collective-permute-start.4) | collective-permute-done | bytes 262176 | tf_op jit(solution)/shard_map/ppermute | solution.py:24
  34.1 3.9 %collective-permute-done.6 = f32[2,16,2048]{2,1,0:T(8,128)S(1)} collective-permute-done((f32[2,16,2048]{2,1,0:T(8,128)S(1)}, f32[2,16,2048]{2,1,0:T(8,128)S(1)}, u32[]{:S(2)}, u32[]{:S(2)}) %collective-permute-start.6) | collective-permute-done | bytes 262176 | tf_op jit(solution)/shard_map/ppermute | solution.py:24
  38.1 6.0 %fusion.8 = f32[128,1024]{1,0:T(8,128)S(1)} fusion(f32[128,2048]{1,0:T(8,128)S(1)} %fusion.44, f32[2048,4096]{1,0:T(8,128)} %param.8, s32[]{:T(128)S(6)} %select_n.76), kind=kOutput, calls=%fused_computation.8 | convolution fusion | flops 1610612736 | bytes 9961476 | tf_op jit(solution)/shard_map/dot_general | solution.py:95
  44.0 6.0 %fusion.6 = f32[128,1024]{1,0:T(8,128)S(1)} fusion(f32[128,2048]{1,0:T(8,128)S(1)} %fusion.44, f32[2048,4096]{1,0:T(8,128)} %param.8, s32[]{:T(128)S(6)} %select_n.77), kind=kOutput, calls=%fused_computation.6 | convolution fusion | flops 1610612736 | bytes 9961476 | tf_op jit(solution)/shard_map/dot_general | solution.py:95
  50.0 1.1 pad_maximum_fusion
  51.0 6.0 %fusion.4 = f32[128,1024]{1,0:T(8,128)S(1)} fusion(f32[128,2048]{1,0:T(8,128)S(1)} %fusion.44, f32[2048,4096]{1,0:T(8,128)} %param.8, s32[]{:T(128)S(6)} %select_n.78), kind=kOutput, calls=%fused_computation.4 | convolution fusion | flops 1610612736 | bytes 9961476 | tf_op jit(solution)/shard_map/dot_general | solution.py:95
  57.1 0.1 fusion.30
  57.1 1.5 %collective-permute-start.8 = (f32[1,128,1024]{2,1,0:T(8,128)S(1)}, f32[1,128,1024]{2,1,0:T(8,128)S(1)}, u32[]{:S(2)}, u32[]{:S(2)}) collective-permute-start(f32[1,128,1024]{2,1,0:T(8,128)S(1)} %fusion.30), channel_id=1, source_target_pairs={{0,8},{4,12},{8,0},{12,4},{1,9},{5,13},{9,1},{13,5},{2,10},{6,14},... | collective-permute-start | bytes 1572872 | tf_op jit(solution)/shard_map/ppermute | solution.py:102
  58.7 0.7 dynamic_slice.73
  59.3 5.9 %fusion.10 = f32[128,1024]{1,0:T(8,128)S(1)} fusion(f32[128,2048]{1,0:T(8,128)S(1)} %fusion.44, f32[2048,4096]{1,0:T(8,128)} %param.8, s32[]{:T(128)S(6)} %select_n.75), kind=kOutput, calls=%fused_computation.10 | convolution fusion | flops 1610612736 | bytes 9961476 | tf_op jit(solution)/shard_map/dot_general | solution.py:95
  65.3 6.2 %collective-permute-done.8 = f32[1,128,1024]{2,1,0:T(8,128)S(1)} collective-permute-done((f32[1,128,1024]{2,1,0:T(8,128)S(1)}, f32[1,128,1024]{2,1,0:T(8,128)S(1)}, u32[]{:S(2)}, u32[]{:S(2)}) %collective-permute-start.8) | collective-permute-done | bytes 524320 | tf_op jit(solution)/shard_map/ppermute | solution.py:102
  71.5 0.4 fusion.28
  71.9 0.1 collective-permute-start.10
  72.0 1.5 %collective-permute-start.9 = (f32[1,128,1024]{2,1,0:T(8,128)S(1)}, f32[1,128,1024]{2,1,0:T(8,128)S(1)}, u32[]{:S(2)}, u32[]{:S(2)}) collective-permute-start(f32[1,128,1024]{2,1,0:T(8,128)S(1)} %bitcast.127), channel_id=1, source_target_pairs={{0,8},{4,12},{8,0},{12,4},{1,9},{5,13},{9,1},{13,5},{2,10},{6,14},... | collective-permute-start | bytes 1572872 | tf_op jit(solution)/shard_map/ppermute | solution.py:111
  73.5 0.4 collective-permute-done.10
  73.9 8.7 %fusion.2 = f32[128,2048]{1,0:T(8,128)S(1)} fusion(f32[4096,2048]{1,0:T(8,128)} %param.10, s32[]{:T(128)S(6)} %select_n.83, f32[128,1024]{1,0:T(8,128)S(1)} %collective-permute-done.10, f32[128,1024]{1,0:T(8,128)S(1)} %fusion.28, pred[]{:T(512)S(6)} %eq.6), kind=kOutput, calls=%fused_computation.2 | convolution fusion | flops 3222011904 | bytes 18874372 | tf_op jit(solution)/shard_map/dot_general | solution.py:122
  82.6 3.8 %collective-permute-done.9 = f32[1,128,1024]{2,1,0:T(8,128)S(1)} collective-permute-done((f32[1,128,1024]{2,1,0:T(8,128)S(1)}, f32[1,128,1024]{2,1,0:T(8,128)S(1)}, u32[]{:S(2)}, u32[]{:S(2)}) %collective-permute-start.9) | collective-permute-done | bytes 524320 | tf_op jit(solution)/shard_map/ppermute | solution.py:111
  86.4 1.9 %collective-permute-done.11 = f32[1,128,1024]{2,1,0:T(8,128)S(1)} collective-permute-done((f32[1,128,1024]{2,1,0:T(8,128)S(1)}, f32[1,128,1024]{2,1,0:T(8,128)S(1)}, u32[]{:S(2)}, u32[]{:S(2)}) %collective-permute-start.11) | collective-permute-done | bytes 524320 | tf_op jit(solution)/shard_map/ppermute | solution.py:130
  88.3 8.7 %fusion = f32[128,2048]{1,0:T(8,128)S(1)} fusion(f32[4096,2048]{1,0:T(8,128)} %param.10, s32[]{:T(128)S(6)} %select_n.86, f32[128,1024]{1,0:T(8,128)S(1)} %bitcast.133, f32[128,1024]{1,0:T(8,128)S(1)} %bitcast.132, pred[]{:T(512)S(6)} %eq.6), kind=kOutput, calls=%fused_computation | convolution fusion | flops 3222011904 | bytes 18874372 | tf_op jit(solution)/shard_map/dot_general | solution.py:122
  97.0 0.2 add.129
  97.2 0.6 collective-permute-start.12
  97.8 7.8 %collective-permute-done.12 = f32[2,16,2048]{2,1,0:T(8,128)S(1)} collective-permute-done((f32[2,16,2048]{2,1,0:T(8,128)S(1)}, f32[2,16,2048]{2,1,0:T(8,128)S(1)}, u32[]{:S(2)}, u32[]{:S(2)}) %collective-permute-start.12) | collective-permute-done | bytes 262176 | tf_op jit(solution)/shard_map/ppermute | solution.py:37
  105.7 0.6 collective-permute-start.14
  106.3 3.5 %collective-permute-start.13 = (f32[1,16,2048]{2,1,0:T(8,128)S(1)}, f32[1,16,2048]{2,1,0:T(8,128)S(1)}, u32[]{:S(2)}, u32[]{:S(2)}) collective-permute-start(f32[1,16,2048]{2,1,0:T(8,128)S(1)} %get-tuple-element.11), channel_id=1, source_target_pairs={{0,2},{1,3},{2,0},{3,1},{4,6},{5,7},{6,4},{7,5},{8,10},{9,11},{10,... | collective-permute-start | bytes 393224 | tf_op jit(solution)/shard_map/ppermute | solution.py:37
  109.8 4.4 %collective-permute-done.13 = f32[1,16,2048]{2,1,0:T(8,128)S(1)} collective-permute-done((f32[1,16,2048]{2,1,0:T(8,128)S(1)}, f32[1,16,2048]{2,1,0:T(8,128)S(1)}, u32[]{:S(2)}, u32[]{:S(2)}) %collective-permute-start.13) | collective-permute-done | bytes 131104 | tf_op jit(solution)/shard_map/ppermute | solution.py:37
  114.2 1.9 %collective-permute-done.14 = f32[2,16,2048]{2,1,0:T(8,128)S(1)} collective-permute-done((f32[2,16,2048]{2,1,0:T(8,128)S(1)}, f32[2,16,2048]{2,1,0:T(8,128)S(1)}, u32[]{:S(2)}, u32[]{:S(2)}) %collective-permute-start.14) | collective-permute-done | bytes 262176 | tf_op jit(solution)/shard_map/ppermute | solution.py:37
  116.1 1.6 %collective-permute-start.15 = (f32[1,16,2048]{2,1,0:T(8,128)S(1)}, f32[1,16,2048]{2,1,0:T(8,128)S(1)}, u32[]{:S(2)}, u32[]{:S(2)}) collective-permute-start(f32[1,16,2048]{2,1,0:T(8,128)S(1)} %get-tuple-element.10), channel_id=1, source_target_pairs={{0,2},{1,3},{2,0},{3,1},{4,6},{5,7},{6,4},{7,5},{8,10},{9,11},{10,... | collective-permute-start | bytes 393224 | tf_op jit(solution)/shard_map/ppermute | solution.py:37
  117.7 4.8 %collective-permute-done.15 = f32[1,16,2048]{2,1,0:T(8,128)S(1)} collective-permute-done((f32[1,16,2048]{2,1,0:T(8,128)S(1)}, f32[1,16,2048]{2,1,0:T(8,128)S(1)}, u32[]{:S(2)}, u32[]{:S(2)}) %collective-permute-start.15) | collective-permute-done | bytes 131104 | tf_op jit(solution)/shard_map/ppermute | solution.py:37
  122.6 0.1 collective-permute-start.16
  122.7 1.5 %collective-permute-start.17 = (f32[8,2048]{1,0:T(8,128)S(1)}, f32[8,2048]{1,0:T(8,128)S(1)}, u32[]{:S(2)}, u32[]{:S(2)}) collective-permute-start(f32[8,2048]{1,0:T(8,128)S(1)} %get-tuple-element.22), channel_id=1, source_target_pairs={{0,8},{4,12},{8,0},{12,4},{1,9},{5,13},{9,1},{13,5},{2,10},{6,14},... | collective-permute-start | bytes 196616 | tf_op jit(solution)/shard_map/ppermute | solution.py:46
  124.2 0.4 collective-permute-start.18
  124.6 2.7 %collective-permute-done.17 = f32[8,2048]{1,0:T(8,128)S(1)} collective-permute-done((f32[8,2048]{1,0:T(8,128)S(1)}, f32[8,2048]{1,0:T(8,128)S(1)}, u32[]{:S(2)}, u32[]{:S(2)}) %collective-permute-start.17) | collective-permute-done | bytes 65568 | tf_op jit(solution)/shard_map/ppermute | solution.py:46
  127.2 1.0 collective-permute-done.18
  128.4 0.8 multiply_add_fusion
  (36 shorter events, 0.5 us)
Async XLA Ops:
  4.6 3.2 %collective-permute-start = (f32[8,2048]{1,0:T(8,128)S(1)}, f32[8,2048]{1,0:T(8,128)S(1)}, u32[]{:S(2)}, u32[]{:S(2)}) collective-permute-start(f32[8,2048]{1,0:T(8,128)S(1)} %get-tuple-element.31), channel_id=1, source_target_pairs={{0,4},{4,0},{8,12},{12,8},{1,5},{5,1},{9,13},{13,9},{2,6},{6,2},{1... | collective-permute-start | bytes 196616 | tf_op jit(solution)/shard_map/ppermute | solution.py:46
  5.1 5.3 %collective-permute-start.1 = (f32[8,2048]{1,0:T(8,128)S(1)}, f32[8,2048]{1,0:T(8,128)S(1)}, u32[]{:S(2)}, u32[]{:S(2)}) collective-permute-start(f32[8,2048]{1,0:T(8,128)S(1)} %get-tuple-element.30), channel_id=1, source_target_pairs={{0,8},{4,12},{8,0},{12,4},{1,9},{5,13},{9,1},{13,5},{2,10},{6,14},... | collective-permute-start | bytes 196616 | tf_op jit(solution)/shard_map/ppermute | solution.py:46
  7.7 4.0 %collective-permute-start.2 = (f32[8,2048]{1,0:T(8,128)S(1)}, f32[8,2048]{1,0:T(8,128)S(1)}, u32[]{:S(2)}, u32[]{:S(2)}) collective-permute-start(f32[8,2048]{1,0:T(8,128)S(1)} %get-tuple-element.29), channel_id=1, source_target_pairs={{0,12},{4,8},{8,4},{12,0},{1,13},{5,9},{9,5},{13,1},{2,14},{6,10},... | collective-permute-start | bytes 196616 | tf_op jit(solution)/shard_map/ppermute | solution.py:46
  11.8 12.9 %collective-permute-start.3 = (f32[1,16,2048]{2,1,0:T(8,128)S(1)}, f32[1,16,2048]{2,1,0:T(8,128)S(1)}, u32[]{:S(2)}, u32[]{:S(2)}) collective-permute-start(f32[1,16,2048]{2,1,0:T(8,128)S(1)} %fusion.49), channel_id=1, source_target_pairs={{0,2},{1,3},{2,0},{3,1},{4,6},{5,7},{6,4},{7,5},{8,10},{9,11},{10,... | collective-permute-start | bytes 393224 | tf_op jit(solution)/shard_map/ppermute | solution.py:24
  14.5 12.4 %collective-permute-start.5 = (f32[1,16,2048]{2,1,0:T(8,128)S(1)}, f32[1,16,2048]{2,1,0:T(8,128)S(1)}, u32[]{:S(2)}, u32[]{:S(2)}) collective-permute-start(f32[1,16,2048]{2,1,0:T(8,128)S(1)} %fusion.48), channel_id=1, source_target_pairs={{0,2},{1,3},{2,0},{3,1},{4,6},{5,7},{6,4},{7,5},{8,10},{9,11},{10,... | collective-permute-start | bytes 393224 | tf_op jit(solution)/shard_map/ppermute | solution.py:24
  24.8 9.3 %collective-permute-start.4 = (f32[2,16,2048]{2,1,0:T(8,128)S(1)}, f32[2,16,2048]{2,1,0:T(8,128)S(1)}, u32[]{:S(2)}, u32[]{:S(2)}) collective-permute-start(f32[2,16,2048]{2,1,0:T(8,128)S(1)} %pad_maximum_fusion.2), channel_id=1, source_target_pairs={{0,1},{1,0},{2,3},{3,2},{4,5},{5,4},{6,7},{7,6},{8,9},{9,8},{10,11... | collective-permute-start | bytes 786440 | tf_op jit(solution)/shard_map/ppermute | solution.py:24
  26.9 11.1 %collective-permute-start.6 = (f32[2,16,2048]{2,1,0:T(8,128)S(1)}, f32[2,16,2048]{2,1,0:T(8,128)S(1)}, u32[]{:S(2)}, u32[]{:S(2)}) collective-permute-start(f32[2,16,2048]{2,1,0:T(8,128)S(1)} %pad_maximum_fusion.3), channel_id=1, source_target_pairs={{0,1},{1,0},{2,3},{3,2},{4,5},{5,4},{6,7},{7,6},{8,9},{9,8},{10,11... | collective-permute-start | bytes 786440 | tf_op jit(solution)/shard_map/ppermute | solution.py:24
  51.0 6.0 %collective-permute-start.7 = (f32[2,128,1024]{2,1,0:T(8,128)}, f32[2,128,1024]{2,1,0:T(8,128)S(1)}, u32[]{:S(2)}, u32[]{:S(2)}) collective-permute-start(f32[2,128,1024]{2,1,0:T(8,128)} %pad_maximum_fusion), channel_id=1, source_target_pairs={{0,4},{4,0},{8,12},{12,8},{1,5},{5,1},{9,13},{13,9},{2,6},{6,2},{1... | collective-permute-start | bytes 3145736 | tf_op jit(solution)/shard_map/ppermute | solution.py:102
  51.0 77.3 %copy-start = (f32[8,8192]{1,0:T(8,128)S(1)}, f32[8,8192]{1,0:T(8,128)}, u32[]{:S(2)}) copy-start(f32[8,8192]{1,0:T(8,128)} %x_ref.1) | copy-start | bytes 786436
  51.0 77.3 %slice-start = ((f32[3,1,8192]{2,1,0:T(1,128)}), f32[1,1,8192]{2,1,0:T(1,128)S(1)}, s32[]{:S(2)}) async-start(f32[3,1,8192]{2,1,0:T(1,128)} %param.7), calls=%async_computation | async-start | bytes 65536 | tf_op jit(solution)/shard_map/slice | solution.py:78
  51.0 77.4 %copy-start.1 = (f32[8192]{0:T(1024)S(1)}, f32[8192]{0:T(1024)}, u32[]{:S(2)}) copy-start(f32[8192]{0:T(1024)} %param.11) | copy-start | bytes 98308
  57.1 14.4 %collective-permute-start.8 = (f32[1,128,1024]{2,1,0:T(8,128)S(1)}, f32[1,128,1024]{2,1,0:T(8,128)S(1)}, u32[]{:S(2)}, u32[]{:S(2)}) collective-permute-start(f32[1,128,1024]{2,1,0:T(8,128)S(1)} %fusion.30), channel_id=1, source_target_pairs={{0,8},{4,12},{8,0},{12,4},{1,9},{5,13},{9,1},{13,5},{2,10},{6,14},... | collective-permute-start | bytes 1572872 | tf_op jit(solution)/shard_map/ppermute | solution.py:102
  71.9 2.0 %collective-permute-start.10 = (f32[128,1024]{1,0:T(8,128)S(1)}, f32[128,1024]{1,0:T(8,128)S(1)}, u32[]{:S(2)}, u32[]{:S(2)}) collective-permute-start(f32[128,1024]{1,0:T(8,128)S(1)} %fusion.28), channel_id=1, source_target_pairs={{0,4},{4,0},{8,12},{12,8},{1,5},{5,1},{9,13},{13,9},{2,6},{6,2},{1... | collective-permute-start | bytes 1572872 | tf_op jit(solution)/shard_map/ppermute | solution.py:107
  72.0 14.3 %collective-permute-start.9 = (f32[1,128,1024]{2,1,0:T(8,128)S(1)}, f32[1,128,1024]{2,1,0:T(8,128)S(1)}, u32[]{:S(2)}, u32[]{:S(2)}) collective-permute-start(f32[1,128,1024]{2,1,0:T(8,128)S(1)} %bitcast.127), channel_id=1, source_target_pairs={{0,8},{4,12},{8,0},{12,4},{1,9},{5,13},{9,1},{13,5},{2,10},{6,14},... | collective-permute-start | bytes 1572872 | tf_op jit(solution)/shard_map/ppermute | solution.py:111
  86.4 1.9 %collective-permute-start.11 = (f32[1,128,1024]{2,1,0:T(8,128)S(1)}, f32[1,128,1024]{2,1,0:T(8,128)S(1)}, u32[]{:S(2)}, u32[]{:S(2)}) collective-permute-start(f32[1,128,1024]{2,1,0:T(8,128)S(1)} %collective-permute-done.9), channel_id=1, source_target_pairs={{0,4},{4,0},{8,12},{12,8},{1,5},{5,1},{9,13},{13,9},{2,6},{6,2},{1... | collective-permute-start | bytes 1572872 | tf_op jit(solution)/shard_map/ppermute | solution.py:130
  97.2 8.4 %collective-permute-start.12 = (f32[2,16,2048]{2,1,0:T(8,128)S(1)}, f32[2,16,2048]{2,1,0:T(8,128)S(1)}, u32[]{:S(2)}, u32[]{:S(2)}) collective-permute-start(f32[2,16,2048]{2,1,0:T(8,128)S(1)} %pad_maximum_fusion.4), channel_id=1, source_target_pairs={{0,1},{1,0},{2,3},{3,2},{4,5},{5,4},{6,7},{7,6},{8,9},{9,8},{10,11... | collective-permute-start | bytes 786440 | tf_op jit(solution)/shard_map/ppermute | solution.py:37
  105.7 10.4 %collective-permute-start.14 = (f32[2,16,2048]{2,1,0:T(8,128)S(1)}, f32[2,16,2048]{2,1,0:T(8,128)S(1)}, u32[]{:S(2)}, u32[]{:S(2)}) collective-permute-start(f32[2,16,2048]{2,1,0:T(8,128)S(1)} %pad_maximum_fusion.5), channel_id=1, source_target_pairs={{0,1},{1,0},{2,3},{3,2},{4,5},{5,4},{6,7},{7,6},{8,9},{9,8},{10,11... | collective-permute-start | bytes 786440 | tf_op jit(solution)/shard_map/ppermute | solution.py:37
  106.3 7.8 %collective-permute-start.13 = (f32[1,16,2048]{2,1,0:T(8,128)S(1)}, f32[1,16,2048]{2,1,0:T(8,128)S(1)}, u32[]{:S(2)}, u32[]{:S(2)}) collective-permute-start(f32[1,16,2048]{2,1,0:T(8,128)S(1)} %get-tuple-element.11), channel_id=1, source_target_pairs={{0,2},{1,3},{2,0},{3,1},{4,6},{5,7},{6,4},{7,5},{8,10},{9,11},{10,... | collective-permute-start | bytes 393224 | tf_op jit(solution)/shard_map/ppermute | solution.py:37
  116.1 6.4 %collective-permute-start.15 = (f32[1,16,2048]{2,1,0:T(8,128)S(1)}, f32[1,16,2048]{2,1,0:T(8,128)S(1)}, u32[]{:S(2)}, u32[]{:S(2)}) collective-permute-start(f32[1,16,2048]{2,1,0:T(8,128)S(1)} %get-tuple-element.10), channel_id=1, source_target_pairs={{0,2},{1,3},{2,0},{3,1},{4,6},{5,7},{6,4},{7,5},{8,10},{9,11},{10,... | collective-permute-start | bytes 393224 | tf_op jit(solution)/shard_map/ppermute | solution.py:37
  122.6 1.9 %collective-permute-start.16 = (f32[8,2048]{1,0:T(8,128)S(1)}, f32[8,2048]{1,0:T(8,128)S(1)}, u32[]{:S(2)}, u32[]{:S(2)}) collective-permute-start(f32[8,2048]{1,0:T(8,128)S(1)} %get-tuple-element.23), channel_id=1, source_target_pairs={{0,4},{4,0},{8,12},{12,8},{1,5},{5,1},{9,13},{13,9},{2,6},{6,2},{1... | collective-permute-start | bytes 196616 | tf_op jit(solution)/shard_map/ppermute | solution.py:46
  122.7 4.6 %collective-permute-start.17 = (f32[8,2048]{1,0:T(8,128)S(1)}, f32[8,2048]{1,0:T(8,128)S(1)}, u32[]{:S(2)}, u32[]{:S(2)}) collective-permute-start(f32[8,2048]{1,0:T(8,128)S(1)} %get-tuple-element.22), channel_id=1, source_target_pairs={{0,8},{4,12},{8,0},{12,4},{1,9},{5,13},{9,1},{13,5},{2,10},{6,14},... | collective-permute-start | bytes 196616 | tf_op jit(solution)/shard_map/ppermute | solution.py:46
  124.2 4.1 %collective-permute-start.18 = (f32[8,2048]{1,0:T(8,128)S(1)}, f32[8,2048]{1,0:T(8,128)S(1)}, u32[]{:S(2)}, u32[]{:S(2)}) collective-permute-start(f32[8,2048]{1,0:T(8,128)S(1)} %get-tuple-element.21), channel_id=1, source_target_pairs={{0,12},{4,8},{8,4},{12,0},{1,13},{5,9},{9,5},{13,1},{2,14},{6,10},... | collective-permute-start | bytes 196616 | tf_op jit(solution)/shard_map/ppermute | solution.py:46

commit v10 on v7

--- a/solution.py
+++ b/solution.py
@@ -73,13 +73,26 @@
     ff_blk = up_weight.shape[1]
     quarter = ff_blk // n_row
 
-    def up_block(d):
+    def up_block(d, lhs):
         w = lax.dynamic_slice_in_dim(up_weight, (r ^ d) * quarter, quarter, 1)
-        return jnp.dot(gathered, w, precision=lax.Precision.HIGH,
+        return jnp.dot(lhs, w, precision=lax.Precision.HIGH,
                        preferred_element_type=jnp.float32)
 
-    held = {d: lax.optimization_barrier(up_block(d)) for d in range(n_row)}
-    flip = 1
+    def low_bit(d):
+        return (d & -d) if d else 2 * n_row
+
+    odd = sorted(range(1, n_row, 2), key=lambda d: low_bit(d ^ 1))
+    even = sorted(range(0, n_row, 2), key=low_bit)
+    recv = {}
+    held = {}
+    lhs = gathered
+    for d_odd, d_even in zip(odd, even):
+        recv[d_odd ^ 1] = lax.ppermute(
+            lax.optimization_barrier(up_block(d_odd, lhs)), "row", _pairs(n_row, 1))
+        held[d_even] = lax.optimization_barrier(up_block(d_even, lhs)) + recv[d_even]
+        if d_even == even[0]:
+            lhs, held[d_even] = lax.optimization_barrier((lhs, held[d_even]))
+    flip = 2
     while flip < n_row:
         sent = [d for d in sorted(held) if d & flip]
         got = lax.ppermute(jnp.stack([held[d] for d in sent]), "row", _pairs(n_row, flip))

time: 129 us -> 129 us (level)
    ppermute x2 -> x1, waiting for transfers between devices: 5.96 us -> 5.56 us  [local(): lax.ppermute(jnp.stack([held[d] for d in sent]), 'row', _pairs(n_row, flip))]
  transfers between devices with their start and end apart: 19 -> 20, of which waited for: 16 -> 16; matrix products, arithmetic and copies ran while one was open for 17% -> 17% of each run, Pallas kernels for 0% -> 0%
where the time goes in v10:
time: 129 us; the launch traced here: 128 us
  waiting for transfers between devices  60.3 us (47%)
  matrix products  41.2 us (32%)
  starting transfers between devices  19.5 us (15%)
  other arithmetic  5.94 us (5%)
    dot_general x4, matrix products, up_block(): jnp.dot(lhs, w, precision=lax.Precision.HIGH, preferred_element_type=jnp....  23.8 us
    ppermute x4, waiting for transfers between devices, _gather_rel(): lax.ppermute(jnp.stack([held[k] for k in keys]), axis, _pairs(n, flip))  22.1 us
    ppermute x4, waiting for transfers between devices, _scatter_rel(): lax.ppermute(jnp.stack([held[d] for d in sent]), axis, _pairs(n, flip))  18.8 us
    dot_general x2, matrix products, down_pair(): jnp.dot(pair, w, precision=lax.Precision.HIGH, preferred_element_type=jnp...  17.4 us
    ppermute x6, waiting for transfers between devices, _exchange_abs(): got.append(lax.ppermute(blocks[idx ^ d], axis, _pairs(n, d)))  7.93 us
    ppermute x4, starting transfers between devices, _scatter_rel(): lax.ppermute(jnp.stack([held[d] for d in sent]), axis, _pairs(n, flip))  6.53 us
    ppermute x1, waiting for transfers between devices, local(): lax.ppermute(jnp.stack([held[d] for d in sent]), 'row', _pairs(n_row, flip))  5.56 us
    ppermute x6, starting transfers between devices, _exchange_abs(): got.append(lax.ppermute(blocks[idx ^ d], axis, _pairs(n, d)))  5.04 us
  transfers between devices with their start and end apart: 20, of which 16 were waited for; matrix products, arithmetic and copies ran while one was open for 17% of the time, Pallas kernels for 0%

profile of v10, /device:TPU:0, one launch (start us, length us, event | category | flops | bytes accessed | tf_op | source)
XLA Modules:
  0.0 128.2 jit_solution(11876050016355448543)
XLA Ops:
  0.0 1.1 reduce_sum.18
  1.1 1.2 multiply_reduce_fusion
  2.3 0.8 fusion.54
  3.2 1.1 multiply_add_fusion.1
  4.3 2.4 %collective-permute-start.2 = (f32[8,2048]{1,0:T(8,128)S(1)}, f32[8,2048]{1,0:T(8,128)S(1)}, u32[]{:S(2)}, u32[]{:S(2)}) collective-permute-start(f32[8,2048]{1,0:T(8,128)S(1)} %get-tuple-element.33), channel_id=1, source_target_pairs={{0,12},{4,8},{8,4},{12,0},{1,13},{5,9},{9,5},{13,1},{2,14},{6,10},... | collective-permute-start | bytes 196616 | tf_op jit(solution)/shard_map/ppermute | solution.py:44
  6.7 0.6 collective-permute-start.1
  7.4 1.8 %collective-permute-done.2 = f32[8,2048]{1,0:T(8,128)S(1)} collective-permute-done((f32[8,2048]{1,0:T(8,128)S(1)}, f32[8,2048]{1,0:T(8,128)S(1)}, u32[]{:S(2)}, u32[]{:S(2)}) %collective-permute-start.2) | collective-permute-done | bytes 65568 | tf_op jit(solution)/shard_map/ppermute | solution.py:44
  9.2 2.2 %collective-permute-done.1 = f32[8,2048]{1,0:T(8,128)S(1)} collective-permute-done((f32[8,2048]{1,0:T(8,128)S(1)}, f32[8,2048]{1,0:T(8,128)S(1)}, u32[]{:S(2)}, u32[]{:S(2)}) %collective-permute-start.1) | collective-permute-done | bytes 65568 | tf_op jit(solution)/shard_map/ppermute | solution.py:44
  11.5 2.8 %collective-permute-start.3 = (f32[1,16,2048]{2,1,0:T(8,128)S(1)}, f32[1,16,2048]{2,1,0:T(8,128)S(1)}, u32[]{:S(2)}, u32[]{:S(2)}) collective-permute-start(f32[1,16,2048]{2,1,0:T(8,128)S(1)} %fusion.45), channel_id=1, source_target_pairs={{0,2},{1,3},{2,0},{3,1},{4,6},{5,7},{6,4},{7,5},{8,10},{9,11},{10,... | collective-permute-start | bytes 393224 | tf_op jit(solution)/shard_map/ppermute | solution.py:22
  14.4 0.2 collective-permute-start.5
  14.6 9.9 %collective-permute-done.3 = f32[1,16,2048]{2,1,0:T(8,128)S(1)} collective-permute-done((f32[1,16,2048]{2,1,0:T(8,128)S(1)}, f32[1,16,2048]{2,1,0:T(8,128)S(1)}, u32[]{:S(2)}, u32[]{:S(2)}) %collective-permute-start.3) | collective-permute-done | bytes 131104 | tf_op jit(solution)/shard_map/ppermute | solution.py:22
  24.5 0.1 collective-permute-start.4
  24.6 1.9 %collective-permute-done.5 = f32[1,16,2048]{2,1,0:T(8,128)S(1)} collective-permute-done((f32[1,16,2048]{2,1,0:T(8,128)S(1)}, f32[1,16,2048]{2,1,0:T(8,128)S(1)}, u32[]{:S(2)}, u32[]{:S(2)}) %collective-permute-start.5) | collective-permute-done | bytes 131104 | tf_op jit(solution)/shard_map/ppermute | solution.py:22
  26.5 0.7 collective-permute-start.6
  27.2 6.6 %collective-permute-done.4 = f32[2,16,2048]{2,1,0:T(8,128)S(1)} collective-permute-done((f32[2,16,2048]{2,1,0:T(8,128)S(1)}, f32[2,16,2048]{2,1,0:T(8,128)S(1)}, u32[]{:S(2)}, u32[]{:S(2)}) %collective-permute-start.4) | collective-permute-done | bytes 262176 | tf_op jit(solution)/shard_map/ppermute | solution.py:22
  33.8 3.8 %collective-permute-done.6 = f32[2,16,2048]{2,1,0:T(8,128)S(1)} collective-permute-done((f32[2,16,2048]{2,1,0:T(8,128)S(1)}, f32[2,16,2048]{2,1,0:T(8,128)S(1)}, u32[]{:S(2)}, u32[]{:S(2)}) %collective-permute-start.6) | collective-permute-done | bytes 262176 | tf_op jit(solution)/shard_map/ppermute | solution.py:22
  37.7 5.9 %fusion.8 = f32[128,1024]{1,0:T(8,128)S(1)} fusion(f32[128,2048]{1,0:T(8,128)S(1)} %fusion.40, f32[2048,4096]{1,0:T(8,128)} %param.8, s32[]{:T(128)S(6)} %select_n.76), kind=kOutput, calls=%fused_computation.8 | convolution fusion | flops 1610612736 | bytes 9961476 | tf_op jit(solution)/shard_map/dot_general | solution.py:78
  43.6 0.1 collective-permute-start.7
  43.7 5.9 %fusion.10 = f32[128,1024]{1,0:T(8,128)S(1)} fusion(f32[128,2048]{1,0:T(8,128)S(1)} %fusion.40, f32[2048,4096]{1,0:T(8,128)} %param.8, s32[]{:T(128)S(6)} %select_n.75), kind=kOutput, calls=%fused_computation.10 | convolution fusion | flops 1610612736 | bytes 9961476 | tf_op jit(solution)/shard_map/dot_general | solution.py:78
  49.7 0.1 add.154
  49.8 6.0 %fusion.4 = f32[128,1024]{1,0:T(8,128)S(1)} fusion(f32[128,2048]{1,0:T(8,128)S(1)} %fusion.40, f32[2048,4096]{1,0:T(8,128)} %param.8, s32[]{:T(128)S(6)} %select_n.78), kind=kOutput, calls=%fused_computation.4 | convolution fusion | flops 1610612736 | bytes 9961476 | tf_op jit(solution)/shard_map/dot_general | solution.py:78
  55.8 0.5 collective-permute-start.8
  56.3 1.7 %collective-permute-start.9 = (f32[1,128,1024]{2,1,0:T(8,128)S(1)}, f32[1,128,1024]{2,1,0:T(8,128)S(1)}, u32[]{:S(2)}, u32[]{:S(2)}) collective-permute-start(f32[1,128,1024]{2,1,0:T(8,128)S(1)} %bitcast.116), channel_id=1, source_target_pairs={{0,8},{4,12},{8,0},{12,4},{1,9},{5,13},{9,1},{13,5},{2,10},{6,14},... | collective-permute-start | bytes 1572872 | tf_op jit(solution)/shard_map/ppermute | solution.py:98
  58.0 0.7 dynamic_slice.73
  58.7 5.9 %fusion.6 = f32[128,1024]{1,0:T(8,128)S(1)} fusion(f32[128,2048]{1,0:T(8,128)S(1)} %fusion.40, f32[2048,4096]{1,0:T(8,128)} %param.8, s32[]{:T(128)S(6)} %select_n.77), kind=kOutput, calls=%fused_computation.6 | convolution fusion | flops 1610612736 | bytes 9961476 | tf_op jit(solution)/shard_map/dot_general | solution.py:78
  64.7 5.6 %collective-permute-done.9 = f32[1,128,1024]{2,1,0:T(8,128)S(1)} collective-permute-done((f32[1,128,1024]{2,1,0:T(8,128)S(1)}, f32[1,128,1024]{2,1,0:T(8,128)S(1)}, u32[]{:S(2)}, u32[]{:S(2)}) %collective-permute-start.9) | collective-permute-done | bytes 524320 | tf_op jit(solution)/shard_map/ppermute | solution.py:98
  70.2 0.4 fusion.28
  70.6 0.1 collective-permute-start.11
  70.7 1.8 %collective-permute-start.10 = (f32[1,128,1024]{2,1,0:T(8,128)S(1)}, f32[1,128,1024]{2,1,0:T(8,128)S(1)}, u32[]{:S(2)}, u32[]{:S(2)}) collective-permute-start(f32[1,128,1024]{2,1,0:T(8,128)S(1)} %bitcast.111), channel_id=1, source_target_pairs={{0,8},{4,12},{8,0},{12,4},{1,9},{5,13},{9,1},{13,5},{2,10},{6,14},... | collective-permute-start | bytes 1572872 | tf_op jit(solution)/shard_map/ppermute | solution.py:107
  72.5 0.1 collective-permute-done.11
  72.6 8.7 %fusion.2 = f32[128,2048]{1,0:T(8,128)S(1)} fusion(f32[4096,2048]{1,0:T(8,128)} %param.10, s32[]{:T(128)S(6)} %select_n.83, f32[128,1024]{1,0:T(8,128)S(1)} %collective-permute-done.11, f32[128,1024]{1,0:T(8,128)S(1)} %fusion.28, pred[]{:T(512)S(6)} %eq.6), kind=kOutput, calls=%fused_computation.2 | convolution fusion | flops 3222011904 | bytes 18874372 | tf_op jit(solution)/shard_map/dot_general | solution.py:118
  81.3 3.8 %collective-permute-done.10 = f32[1,128,1024]{2,1,0:T(8,128)S(1)} collective-permute-done((f32[1,128,1024]{2,1,0:T(8,128)S(1)}, f32[1,128,1024]{2,1,0:T(8,128)S(1)}, u32[]{:S(2)}, u32[]{:S(2)}) %collective-permute-start.10) | collective-permute-done | bytes 524320 | tf_op jit(solution)/shard_map/ppermute | solution.py:107
  85.1 1.9 %collective-permute-done.12 = f32[1,128,1024]{2,1,0:T(8,128)S(1)} collective-permute-done((f32[1,128,1024]{2,1,0:T(8,128)S(1)}, f32[1,128,1024]{2,1,0:T(8,128)S(1)}, u32[]{:S(2)}, u32[]{:S(2)}) %collective-permute-start.12) | collective-permute-done | bytes 524320 | tf_op jit(solution)/shard_map/ppermute | solution.py:126
  87.0 8.7 %fusion = f32[128,2048]{1,0:T(8,128)S(1)} fusion(f32[4096,2048]{1,0:T(8,128)} %param.10, s32[]{:T(128)S(6)} %select_n.86, f32[128,1024]{1,0:T(8,128)S(1)} %bitcast.115, f32[128,1024]{1,0:T(8,128)S(1)} %bitcast.114, pred[]{:T(512)S(6)} %eq.6), kind=kOutput, calls=%fused_computation | convolution fusion | flops 3222011904 | bytes 18874372 | tf_op jit(solution)/shard_map/dot_general | solution.py:118
  95.7 0.2 add.167
  95.9 0.7 collective-permute-start.13
  96.6 7.7 %collective-permute-done.13 = f32[2,16,2048]{2,1,0:T(8,128)S(1)} collective-permute-done((f32[2,16,2048]{2,1,0:T(8,128)S(1)}, f32[2,16,2048]{2,1,0:T(8,128)S(1)}, u32[]{:S(2)}, u32[]{:S(2)}) %collective-permute-start.13) | collective-permute-done | bytes 262176 | tf_op jit(solution)/shard_map/ppermute | solution.py:35
  104.4 0.7 collective-permute-start.15
  105.0 3.5 %collective-permute-start.14 = (f32[1,16,2048]{2,1,0:T(8,128)S(1)}, f32[1,16,2048]{2,1,0:T(8,128)S(1)}, u32[]{:S(2)}, u32[]{:S(2)}) collective-permute-start(f32[1,16,2048]{2,1,0:T(8,128)S(1)} %get-tuple-element.15), channel_id=1, source_target_pairs={{0,2},{1,3},{2,0},{3,1},{4,6},{5,7},{6,4},{7,5},{8,10},{9,11},{10,... | collective-permute-start | bytes 393224 | tf_op jit(solution)/shard_map/ppermute | solution.py:35
  108.5 4.4 %collective-permute-done.14 = f32[1,16,2048]{2,1,0:T(8,128)S(1)} collective-permute-done((f32[1,16,2048]{2,1,0:T(8,128)S(1)}, f32[1,16,2048]{2,1,0:T(8,128)S(1)}, u32[]{:S(2)}, u32[]{:S(2)}) %collective-permute-start.14) | collective-permute-done | bytes 131104 | tf_op jit(solution)/shard_map/ppermute | solution.py:35
  112.9 1.9 %collective-permute-done.15 = f32[2,16,2048]{2,1,0:T(8,128)S(1)} collective-permute-done((f32[2,16,2048]{2,1,0:T(8,128)S(1)}, f32[2,16,2048]{2,1,0:T(8,128)S(1)}, u32[]{:S(2)}, u32[]{:S(2)}) %collective-permute-start.15) | collective-permute-done | bytes 262176 | tf_op jit(solution)/shard_map/ppermute | solution.py:35
  114.8 1.7 %collective-permute-start.16 = (f32[1,16,2048]{2,1,0:T(8,128)S(1)}, f32[1,16,2048]{2,1,0:T(8,128)S(1)}, u32[]{:S(2)}, u32[]{:S(2)}) collective-permute-start(f32[1,16,2048]{2,1,0:T(8,128)S(1)} %get-tuple-element.14), channel_id=1, source_target_pairs={{0,2},{1,3},{2,0},{3,1},{4,6},{5,7},{6,4},{7,5},{8,10},{9,11},{10,... | collective-permute-start | bytes 393224 | tf_op jit(solution)/shard_map/ppermute | solution.py:35
  116.5 4.8 %collective-permute-done.16 = f32[1,16,2048]{2,1,0:T(8,128)S(1)} collective-permute-done((f32[1,16,2048]{2,1,0:T(8,128)S(1)}, f32[1,16,2048]{2,1,0:T(8,128)S(1)}, u32[]{:S(2)}, u32[]{:S(2)}) %collective-permute-start.16) | collective-permute-done | bytes 131104 | tf_op jit(solution)/shard_map/ppermute | solution.py:35
  121.5 1.7 %collective-permute-start.18 = (f32[8,2048]{1,0:T(8,128)S(1)}, f32[8,2048]{1,0:T(8,128)S(1)}, u32[]{:S(2)}, u32[]{:S(2)}) collective-permute-start(f32[8,2048]{1,0:T(8,128)S(1)} %get-tuple-element.26), channel_id=1, source_target_pairs={{0,8},{4,12},{8,0},{12,4},{1,9},{5,13},{9,1},{13,5},{2,10},{6,14},... | collective-permute-start | bytes 196616 | tf_op jit(solution)/shard_map/ppermute | solution.py:44
  123.2 0.2 collective-permute-start.17
  123.3 2.4 %collective-permute-done.19 = f32[8,2048]{1,0:T(8,128)S(1)} collective-permute-done((f32[8,2048]{1,0:T(8,128)S(1)}, f32[8,2048]{1,0:T(8,128)S(1)}, u32[]{:S(2)}, u32[]{:S(2)}) %collective-permute-start.19) | collective-permute-done | bytes 65568 | tf_op jit(solution)/shard_map/ppermute | solution.py:44
  125.7 1.6 %collective-permute-done.18 = f32[8,2048]{1,0:T(8,128)S(1)} collective-permute-done((f32[8,2048]{1,0:T(8,128)S(1)}, f32[8,2048]{1,0:T(8,128)S(1)}, u32[]{:S(2)}, u32[]{:S(2)}) %collective-permute-start.18) | collective-permute-done | bytes 65568 | tf_op jit(solution)/shard_map/ppermute | solution.py:44
  127.4 0.8 multiply_add_fusion
  (39 shorter events, 0.7 us)
Async XLA Ops:
  4.3 4.9 %collective-permute-start.2 = (f32[8,2048]{1,0:T(8,128)S(1)}, f32[8,2048]{1,0:T(8,128)S(1)}, u32[]{:S(2)}, u32[]{:S(2)}) collective-permute-start(f32[8,2048]{1,0:T(8,128)S(1)} %get-tuple-element.33), channel_id=1, source_target_pairs={{0,12},{4,8},{8,4},{12,0},{1,13},{5,9},{9,5},{13,1},{2,14},{6,10},... | collective-permute-start | bytes 196616 | tf_op jit(solution)/shard_map/ppermute | solution.py:44
  6.7 4.7 %collective-permute-start.1 = (f32[8,2048]{1,0:T(8,128)S(1)}, f32[8,2048]{1,0:T(8,128)S(1)}, u32[]{:S(2)}, u32[]{:S(2)}) collective-permute-start(f32[8,2048]{1,0:T(8,128)S(1)} %get-tuple-element.34), channel_id=1, source_target_pairs={{0,8},{4,12},{8,0},{12,4},{1,9},{5,13},{9,1},{13,5},{2,10},{6,14},... | collective-permute-start | bytes 196616 | tf_op jit(solution)/shard_map/ppermute | solution.py:44
  7.4 4.0 %collective-permute-start = (f32[8,2048]{1,0:T(8,128)S(1)}, f32[8,2048]{1,0:T(8,128)S(1)}, u32[]{:S(2)}, u32[]{:S(2)}) collective-permute-start(f32[8,2048]{1,0:T(8,128)S(1)} %get-tuple-element.35), channel_id=1, source_target_pairs={{0,4},{4,0},{8,12},{12,8},{1,5},{5,1},{9,13},{13,9},{2,6},{6,2},{1... | collective-permute-start | bytes 196616 | tf_op jit(solution)/shard_map/ppermute | solution.py:44
  11.5 12.9 %collective-permute-start.3 = (f32[1,16,2048]{2,1,0:T(8,128)S(1)}, f32[1,16,2048]{2,1,0:T(8,128)S(1)}, u32[]{:S(2)}, u32[]{:S(2)}) collective-permute-start(f32[1,16,2048]{2,1,0:T(8,128)S(1)} %fusion.45), channel_id=1, source_target_pairs={{0,2},{1,3},{2,0},{3,1},{4,6},{5,7},{6,4},{7,5},{8,10},{9,11},{10,... | collective-permute-start | bytes 393224 | tf_op jit(solution)/shard_map/ppermute | solution.py:22
  14.4 12.1 %collective-permute-start.5 = (f32[1,16,2048]{2,1,0:T(8,128)S(1)}, f32[1,16,2048]{2,1,0:T(8,128)S(1)}, u32[]{:S(2)}, u32[]{:S(2)}) collective-permute-start(f32[1,16,2048]{2,1,0:T(8,128)S(1)} %fusion.44), channel_id=1, source_target_pairs={{0,2},{1,3},{2,0},{3,1},{4,6},{5,7},{6,4},{7,5},{8,10},{9,11},{10,... | collective-permute-start | bytes 393224 | tf_op jit(solution)/shard_map/ppermute | solution.py:22
  24.5 9.3 %collective-permute-start.4 = (f32[2,16,2048]{2,1,0:T(8,128)S(1)}, f32[2,16,2048]{2,1,0:T(8,128)S(1)}, u32[]{:S(2)}, u32[]{:S(2)}) collective-permute-start(f32[2,16,2048]{2,1,0:T(8,128)S(1)} %pad_maximum_fusion.1), channel_id=1, source_target_pairs={{0,1},{1,0},{2,3},{3,2},{4,5},{5,4},{6,7},{7,6},{8,9},{9,8},{10,11... | collective-permute-start | bytes 786440 | tf_op jit(solution)/shard_map/ppermute | solution.py:22
  26.5 11.1 %collective-permute-start.6 = (f32[2,16,2048]{2,1,0:T(8,128)S(1)}, f32[2,16,2048]{2,1,0:T(8,128)S(1)}, u32[]{:S(2)}, u32[]{:S(2)}) collective-permute-start(f32[2,16,2048]{2,1,0:T(8,128)S(1)} %pad_maximum_fusion.2), channel_id=1, source_target_pairs={{0,1},{1,0},{2,3},{3,2},{4,5},{5,4},{6,7},{7,6},{8,9},{9,8},{10,11... | collective-permute-start | bytes 786440 | tf_op jit(solution)/shard_map/ppermute | solution.py:22
  43.6 6.1 %collective-permute-start.7 = (f32[128,1024]{1,0:T(8,128)S(1)}, f32[128,1024]{1,0:T(8,128)S(1)}, u32[]{:S(2)}, u32[]{:S(2)}) collective-permute-start(f32[128,1024]{1,0:T(8,128)S(1)} %fusion.8), channel_id=1, source_target_pairs={{0,4},{4,0},{8,12},{12,8},{1,5},{5,1},{9,13},{13,9},{2,6},{6,2},{1... | collective-permute-start | bytes 1572872 | tf_op jit(solution)/shard_map/ppermute | solution.py:90
  49.8 77.6 %copy-start = (f32[8,8192]{1,0:T(8,128)S(1)}, f32[8,8192]{1,0:T(8,128)}, u32[]{:S(2)}) copy-start(f32[8,8192]{1,0:T(8,128)} %param.6) | copy-start | bytes 786436
  49.8 77.6 %copy-start.1 = (f32[8192]{0:T(1024)S(1)}, f32[8192]{0:T(1024)}, u32[]{:S(2)}) copy-start(f32[8192]{0:T(1024)} %param.11) | copy-start | bytes 98308
  55.8 8.9 %collective-permute-start.8 = (f32[128,1024]{1,0:T(8,128)S(1)}, f32[128,1024]{1,0:T(8,128)S(1)}, u32[]{:S(2)}, u32[]{:S(2)}) collective-permute-start(f32[128,1024]{1,0:T(8,128)S(1)} %fusion.4), channel_id=1, source_target_pairs={{0,4},{4,0},{8,12},{12,8},{1,5},{5,1},{9,13},{13,9},{2,6},{6,2},{1... | collective-permute-start | bytes 1572872 | tf_op jit(solution)/shard_map/ppermute | solution.py:90
  56.3 13.9 %collective-permute-start.9 = (f32[1,128,1024]{2,1,0:T(8,128)S(1)}, f32[1,128,1024]{2,1,0:T(8,128)S(1)}, u32[]{:S(2)}, u32[]{:S(2)}) collective-permute-start(f32[1,128,1024]{2,1,0:T(8,128)S(1)} %bitcast.116), channel_id=1, source_target_pairs={{0,8},{4,12},{8,0},{12,4},{1,9},{5,13},{9,1},{13,5},{2,10},{6,14},... | collective-permute-start | bytes 1572872 | tf_op jit(solution)/shard_map/ppermute | solution.py:98
  70.6 2.0 %collective-permute-start.11 = (f32[128,1024]{1,0:T(8,128)S(1)}, f32[128,1024]{1,0:T(8,128)S(1)}, u32[]{:S(2)}, u32[]{:S(2)}) collective-permute-start(f32[128,1024]{1,0:T(8,128)S(1)} %fusion.28), channel_id=1, source_target_pairs={{0,4},{4,0},{8,12},{12,8},{1,5},{5,1},{9,13},{13,9},{2,6},{6,2},{1... | collective-permute-start | bytes 1572872 | tf_op jit(solution)/shard_map/ppermute | solution.py:103
  70.7 14.3 %collective-permute-start.10 = (f32[1,128,1024]{2,1,0:T(8,128)S(1)}, f32[1,128,1024]{2,1,0:T(8,128)S(1)}, u32[]{:S(2)}, u32[]{:S(2)}) collective-permute-start(f32[1,128,1024]{2,1,0:T(8,128)S(1)} %bitcast.111), channel_id=1, source_target_pairs={{0,8},{4,12},{8,0},{12,4},{1,9},{5,13},{9,1},{13,5},{2,10},{6,14},... | collective-permute-start | bytes 1572872 | tf_op jit(solution)/shard_map/ppermute | solution.py:107
  85.0 1.9 %collective-permute-start.12 = (f32[1,128,1024]{2,1,0:T(8,128)S(1)}, f32[1,128,1024]{2,1,0:T(8,128)S(1)}, u32[]{:S(2)}, u32[]{:S(2)}) collective-permute-start(f32[1,128,1024]{2,1,0:T(8,128)S(1)} %collective-permute-done.10), channel_id=1, source_target_pairs={{0,4},{4,0},{8,12},{12,8},{1,5},{5,1},{9,13},{13,9},{2,6},{6,2},{1... | collective-permute-start | bytes 1572872 | tf_op jit(solution)/shard_map/ppermute | solution.py:126
  95.9 8.4 %collective-permute-start.13 = (f32[2,16,2048]{2,1,0:T(8,128)S(1)}, f32[2,16,2048]{2,1,0:T(8,128)S(1)}, u32[]{:S(2)}, u32[]{:S(2)}) collective-permute-start(f32[2,16,2048]{2,1,0:T(8,128)S(1)} %pad_maximum_fusion.3), channel_id=1, source_target_pairs={{0,1},{1,0},{2,3},{3,2},{4,5},{5,4},{6,7},{7,6},{8,9},{9,8},{10,11... | collective-permute-start | bytes 786440 | tf_op jit(solution)/shard_map/ppermute | solution.py:35
  104.4 10.4 %collective-permute-start.15 = (f32[2,16,2048]{2,1,0:T(8,128)S(1)}, f32[2,16,2048]{2,1,0:T(8,128)S(1)}, u32[]{:S(2)}, u32[]{:S(2)}) collective-permute-start(f32[2,16,2048]{2,1,0:T(8,128)S(1)} %pad_maximum_fusion.4), channel_id=1, source_target_pairs={{0,1},{1,0},{2,3},{3,2},{4,5},{5,4},{6,7},{7,6},{8,9},{9,8},{10,11... | collective-permute-start | bytes 786440 | tf_op jit(solution)/shard_map/ppermute | solution.py:35
  105.0 7.8 %collective-permute-start.14 = (f32[1,16,2048]{2,1,0:T(8,128)S(1)}, f32[1,16,2048]{2,1,0:T(8,128)S(1)}, u32[]{:S(2)}, u32[]{:S(2)}) collective-permute-start(f32[1,16,2048]{2,1,0:T(8,128)S(1)} %get-tuple-element.15), channel_id=1, source_target_pairs={{0,2},{1,3},{2,0},{3,1},{4,6},{5,7},{6,4},{7,5},{8,10},{9,11},{10,... | collective-permute-start | bytes 393224 | tf_op jit(solution)/shard_map/ppermute | solution.py:35
  114.8 6.5 %collective-permute-start.16 = (f32[1,16,2048]{2,1,0:T(8,128)S(1)}, f32[1,16,2048]{2,1,0:T(8,128)S(1)}, u32[]{:S(2)}, u32[]{:S(2)}) collective-permute-start(f32[1,16,2048]{2,1,0:T(8,128)S(1)} %get-tuple-element.14), channel_id=1, source_target_pairs={{0,2},{1,3},{2,0},{3,1},{4,6},{5,7},{6,4},{7,5},{8,10},{9,11},{10,... | collective-permute-start | bytes 393224 | tf_op jit(solution)/shard_map/ppermute | solution.py:35
  121.4 4.3 %collective-permute-start.19 = (f32[8,2048]{1,0:T(8,128)S(1)}, f32[8,2048]{1,0:T(8,128)S(1)}, u32[]{:S(2)}, u32[]{:S(2)}) collective-permute-start(f32[8,2048]{1,0:T(8,128)S(1)} %get-tuple-element.25), channel_id=1, source_target_pairs={{0,12},{4,8},{8,4},{12,0},{1,13},{5,9},{9,5},{13,1},{2,14},{6,10},... | collective-permute-start | bytes 196616 | tf_op jit(solution)/shard_map/ppermute | solution.py:44
  121.5 5.8 %collective-permute-start.18 = (f32[8,2048]{1,0:T(8,128)S(1)}, f32[8,2048]{1,0:T(8,128)S(1)}, u32[]{:S(2)}, u32[]{:S(2)}) collective-permute-start(f32[8,2048]{1,0:T(8,128)S(1)} %get-tuple-element.26), channel_id=1, source_target_pairs={{0,8},{4,12},{8,0},{12,4},{1,9},{5,13},{9,1},{13,5},{2,10},{6,14},... | collective-permute-start | bytes 196616 | tf_op jit(solution)/shard_map/ppermute | solution.py:44
  123.2 4.1 %collective-permute-start.17 = (f32[8,2048]{1,0:T(8,128)S(1)}, f32[8,2048]{1,0:T(8,128)S(1)}, u32[]{:S(2)}, u32[]{:S(2)}) collective-permute-start(f32[8,2048]{1,0:T(8,128)S(1)} %get-tuple-element.27), channel_id=1, source_target_pairs={{0,4},{4,0},{8,12},{12,8},{1,5},{5,1},{9,13},{13,9},{2,6},{6,2},{1... | collective-permute-start | bytes 196616 | tf_op jit(solution)/shard_map/ppermute | solution.py:44

commit v11 on v10

--- a/solution.py
+++ b/solution.py
@@ -4,7 +4,7 @@
 from jax.sharding import PartitionSpec as P
 
 SEQ = 256
-N_CHUNK = 2
+N_CHUNK = 4
 
 
 layer_eps = 1e-06

time: 129 us -> 150 us (1.16)
  starting transfers between devices: 19.5 us -> 39.9 us
    ppermute x4 -> x8, starting transfers between devices: 3.82 us -> 16.3 us  [_gather_rel(): lax.ppermute(jnp.stack([held[k] for k in keys]), axis, _pairs(n, flip))]
    ppermute x4 -> x8, starting transfers between devices: 6.53 us -> 14.3 us  [_scatter_rel(): lax.ppermute(jnp.stack([held[d] for d in sent]), axis, _pairs(n, flip))]
    ppermute x4 -> x8, waiting for transfers between devices: 22.1 us -> 27 us  [_gather_rel(): lax.ppermute(jnp.stack([held[k] for k in keys]), axis, _pairs(n, flip))]
    ppermute x4 -> x8, waiting for transfers between devices: 18.8 us -> 15.1 us  [_scatter_rel(): lax.ppermute(jnp.stack([held[d] for d in sent]), axis, _pairs(n, flip))]
  transfers between devices with their start and end apart: 20 -> 28, of which waited for: 16 -> 22; matrix products, arithmetic and copies ran while one was open for 17% -> 14% of each run, Pallas kernels for 0% -> 0%
where the time goes in v11:
time: 150 us; the launch traced here: 149 us
  waiting for transfers between devices  61.1 us (41%)
  matrix products  41.4 us (28%)
  starting transfers between devices  39.9 us (27%)
  other arithmetic  5.73 us (4%)
    ppermute x8, waiting for transfers between devices, _gather_rel(): lax.ppermute(jnp.stack([held[k] for k in keys]), axis, _pairs(n, flip))  27 us
    dot_general x4, matrix products, up_block(): jnp.dot(lhs, w, precision=lax.Precision.HIGH, preferred_element_type=jnp....  24 us
    dot_general x2, matrix products, down_pair(): jnp.dot(pair, w, precision=lax.Precision.HIGH, preferred_element_type=jnp...  17.4 us
    ppermute x8, starting transfers between devices, _gather_rel(): lax.ppermute(jnp.stack([held[k] for k in keys]), axis, _pairs(n, flip))  16.3 us
    ppermute x8, waiting for transfers between devices, _scatter_rel(): lax.ppermute(jnp.stack([held[d] for d in sent]), axis, _pairs(n, flip))  15.1 us
    ppermute x8, starting transfers between devices, _scatter_rel(): lax.ppermute(jnp.stack([held[d] for d in sent]), axis, _pairs(n, flip))  14.3 us
    ppermute x6, waiting for transfers between devices, _exchange_abs(): got.append(lax.ppermute(blocks[idx ^ d], axis, _pairs(n, d)))  7.82 us
    ppermute x1, waiting for transfers between devices, local(): lax.ppermute(jnp.stack([held[d] for d in sent]), 'row', _pairs(n_row, flip))  5.32 us
  transfers between devices with their start and end apart: 28, of which 22 were waited for; matrix products, arithmetic and copies ran while one was open for 14% of the time, Pallas kernels for 0%

profile of v11, /device:TPU:0, one launch (start us, length us, event | category | flops | bytes accessed | tf_op | source)
XLA Modules:
  0.0 149.4 jit_solution(15211674854157662645)
XLA Ops:
  0.0 1.1 reduce_sum.18
  1.1 1.2 multiply_reduce_fusion
  2.3 0.8 fusion.64
  3.2 1.1 multiply_add_fusion.1
  4.3 2.4 %collective-permute-start.2 = (f32[8,2048]{1,0:T(8,128)S(1)}, f32[8,2048]{1,0:T(8,128)S(1)}, u32[]{:S(2)}, u32[]{:S(2)}) collective-permute-start(f32[8,2048]{1,0:T(8,128)S(1)} %get-tuple-element.46), channel_id=1, source_target_pairs={{0,12},{4,8},{8,4},{12,0},{1,13},{5,9},{9,5},{13,1},{2,14},{6,10},... | collective-permute-start | bytes 196616 | tf_op jit(solution)/shard_map/ppermute | solution.py:44
  7.4 1.8 %collective-permute-done.2 = f32[8,2048]{1,0:T(8,128)S(1)} collective-permute-done((f32[8,2048]{1,0:T(8,128)S(1)}, f32[8,2048]{1,0:T(8,128)S(1)}, u32[]{:S(2)}, u32[]{:S(2)}) %collective-permute-start.2) | collective-permute-done | bytes 65568 | tf_op jit(solution)/shard_map/ppermute | solution.py:44
  9.2 2.2 %collective-permute-done.1 = f32[8,2048]{1,0:T(8,128)S(1)} collective-permute-done((f32[8,2048]{1,0:T(8,128)S(1)}, f32[8,2048]{1,0:T(8,128)S(1)}, u32[]{:S(2)}, u32[]{:S(2)}) %collective-permute-start.1) | collective-permute-done | bytes 65568 | tf_op jit(solution)/shard_map/ppermute | solution.py:44
  11.5 2.8 %collective-permute-start.3 = (f32[1,8,2048]{2,1,0:T(8,128)S(1)}, f32[1,8,2048]{2,1,0:T(8,128)S(1)}, u32[]{:S(2)}, u32[]{:S(2)}) collective-permute-start(f32[1,8,2048]{2,1,0:T(8,128)S(1)} %get-tuple-element.20), channel_id=1, source_target_pairs={{0,2},{1,3},{2,0},{3,1},{4,6},{5,7},{6,4},{7,5},{8,10},{9,11},{10,... | collective-permute-start | bytes 196616 | tf_op jit(solution)/shard_map/ppermute | solution.py:22
  14.3 3.8 %collective-permute-done.3 = f32[1,8,2048]{2,1,0:T(8,128)S(1)} collective-permute-done((f32[1,8,2048]{2,1,0:T(8,128)S(1)}, f32[1,8,2048]{2,1,0:T(8,128)S(1)}, u32[]{:S(2)}, u32[]{:S(2)}) %collective-permute-start.3) | collective-permute-done | bytes 65568 | tf_op jit(solution)/shard_map/ppermute | solution.py:22
  18.7 4.4 %collective-permute-done.4 = f32[2,8,2048]{2,1,0:T(8,128)S(1)} collective-permute-done((f32[2,8,2048]{2,1,0:T(8,128)S(1)}, f32[2,8,2048]{2,1,0:T(8,128)S(1)}, u32[]{:S(2)}, u32[]{:S(2)}) %collective-permute-start.4) | collective-permute-done | bytes 131104 | tf_op jit(solution)/shard_map/ppermute | solution.py:22
  23.2 2.5 %collective-permute-start.5 = (f32[1,8,2048]{2,1,0:T(8,128)S(1)}, f32[1,8,2048]{2,1,0:T(8,128)S(1)}, u32[]{:S(2)}, u32[]{:S(2)}) collective-permute-start(f32[1,8,2048]{2,1,0:T(8,128)S(1)} %get-tuple-element.18), channel_id=1, source_target_pairs={{0,2},{1,3},{2,0},{3,1},{4,6},{5,7},{6,4},{7,5},{8,10},{9,11},{10,... | collective-permute-start | bytes 196616 | tf_op jit(solution)/shard_map/ppermute | solution.py:22
  25.7 2.8 %collective-permute-done.5 = f32[1,8,2048]{2,1,0:T(8,128)S(1)} collective-permute-done((f32[1,8,2048]{2,1,0:T(8,128)S(1)}, f32[1,8,2048]{2,1,0:T(8,128)S(1)}, u32[]{:S(2)}, u32[]{:S(2)}) %collective-permute-start.5) | collective-permute-done | bytes 65568 | tf_op jit(solution)/shard_map/ppermute | solution.py:22
  28.5 1.3 collective-permute-start.6
  29.8 3.7 %collective-permute-done.6 = f32[2,8,2048]{2,1,0:T(8,128)S(1)} collective-permute-done((f32[2,8,2048]{2,1,0:T(8,128)S(1)}, f32[2,8,2048]{2,1,0:T(8,128)S(1)}, u32[]{:S(2)}, u32[]{:S(2)}) %collective-permute-start.6) | collective-permute-done | bytes 131104 | tf_op jit(solution)/shard_map/ppermute | solution.py:22
  33.5 2.7 %collective-permute-start.7 = (f32[1,8,2048]{2,1,0:T(8,128)S(1)}, f32[1,8,2048]{2,1,0:T(8,128)S(1)}, u32[]{:S(2)}, u32[]{:S(2)}) collective-permute-start(f32[1,8,2048]{2,1,0:T(8,128)S(1)} %get-tuple-element.16), channel_id=1, source_target_pairs={{0,2},{1,3},{2,0},{3,1},{4,6},{5,7},{6,4},{7,5},{8,10},{9,11},{10,... | collective-permute-start | bytes 196616 | tf_op jit(solution)/shard_map/ppermute | solution.py:22
  36.2 2.7 %collective-permute-done.7 = f32[1,8,2048]{2,1,0:T(8,128)S(1)} collective-permute-done((f32[1,8,2048]{2,1,0:T(8,128)S(1)}, f32[1,8,2048]{2,1,0:T(8,128)S(1)}, u32[]{:S(2)}, u32[]{:S(2)}) %collective-permute-start.7) | collective-permute-done | bytes 65568 | tf_op jit(solution)/shard_map/ppermute | solution.py:22
  38.9 1.6 %collective-permute-start.8 = (f32[2,8,2048]{2,1,0:T(8,128)S(1)}, f32[2,8,2048]{2,1,0:T(8,128)S(1)}, u32[]{:S(2)}, u32[]{:S(2)}) collective-permute-start(f32[2,8,2048]{2,1,0:T(8,128)S(1)} %pad_maximum_fusion.5), channel_id=1, source_target_pairs={{0,1},{1,0},{2,3},{3,2},{4,5},{5,4},{6,7},{7,6},{8,9},{9,8},{10,11... | collective-permute-start | bytes 393224 | tf_op jit(solution)/shard_map/ppermute | solution.py:22
  40.5 4.1 %collective-permute-done.8 = f32[2,8,2048]{2,1,0:T(8,128)S(1)} collective-permute-done((f32[2,8,2048]{2,1,0:T(8,128)S(1)}, f32[2,8,2048]{2,1,0:T(8,128)S(1)}, u32[]{:S(2)}, u32[]{:S(2)}) %collective-permute-start.8) | collective-permute-done | bytes 131104 | tf_op jit(solution)/shard_map/ppermute | solution.py:22
  44.7 2.6 %collective-permute-start.9 = (f32[1,8,2048]{2,1,0:T(8,128)S(1)}, f32[1,8,2048]{2,1,0:T(8,128)S(1)}, u32[]{:S(2)}, u32[]{:S(2)}) collective-permute-start(f32[1,8,2048]{2,1,0:T(8,128)S(1)} %get-tuple-element.14), channel_id=1, source_target_pairs={{0,2},{1,3},{2,0},{3,1},{4,6},{5,7},{6,4},{7,5},{8,10},{9,11},{10,... | collective-permute-start | bytes 196616 | tf_op jit(solution)/shard_map/ppermute | solution.py:22
  47.3 2.6 %collective-permute-done.9 = f32[1,8,2048]{2,1,0:T(8,128)S(1)} collective-permute-done((f32[1,8,2048]{2,1,0:T(8,128)S(1)}, f32[1,8,2048]{2,1,0:T(8,128)S(1)}, u32[]{:S(2)}, u32[]{:S(2)}) %collective-permute-start.9) | collective-permute-done | bytes 65568 | tf_op jit(solution)/shard_map/ppermute | solution.py:22
  49.9 2.1 %collective-permute-start.10 = (f32[2,8,2048]{2,1,0:T(8,128)S(1)}, f32[2,8,2048]{2,1,0:T(8,128)S(1)}, u32[]{:S(2)}, u32[]{:S(2)}) collective-permute-start(f32[2,8,2048]{2,1,0:T(8,128)S(1)} %pad_maximum_fusion.6), channel_id=1, source_target_pairs={{0,1},{1,0},{2,3},{3,2},{4,5},{5,4},{6,7},{7,6},{8,9},{9,8},{10,11... | collective-permute-start | bytes 393224 | tf_op jit(solution)/shard_map/ppermute | solution.py:22
  52.1 2.9 %collective-permute-done.10 = f32[2,8,2048]{2,1,0:T(8,128)S(1)} collective-permute-done((f32[2,8,2048]{2,1,0:T(8,128)S(1)}, f32[2,8,2048]{2,1,0:T(8,128)S(1)}, u32[]{:S(2)}, u32[]{:S(2)}) %collective-permute-start.10) | collective-permute-done | bytes 131104 | tf_op jit(solution)/shard_map/ppermute | solution.py:22
  55.1 5.9 %fusion.8 = f32[128,1024]{1,0:T(8,128)S(1)} fusion(f32[128,2048]{1,0:T(8,128)S(1)} %fusion.48, f32[2048,4096]{1,0:T(8,128)} %param.8, s32[]{:T(128)S(6)} %select_n.76), kind=kOutput, calls=%fused_computation.8 | convolution fusion | flops 1610612736 | bytes 9961476 | tf_op jit(solution)/shard_map/dot_general | solution.py:78
  61.1 5.9 %fusion.10 = f32[128,1024]{1,0:T(8,128)S(1)} fusion(f32[128,2048]{1,0:T(8,128)S(1)} %fusion.48, f32[2048,4096]{1,0:T(8,128)} %param.8, s32[]{:T(128)S(6)} %select_n.75), kind=kOutput, calls=%fused_computation.10 | convolution fusion | flops 1610612736 | bytes 9961476 | tf_op jit(solution)/shard_map/dot_general | solution.py:78
  67.2 6.0 %fusion.4 = f32[128,1024]{1,0:T(8,128)S(1)} fusion(f32[128,2048]{1,0:T(8,128)S(1)} %fusion.48, f32[2048,4096]{1,0:T(8,128)} %param.8, s32[]{:T(128)S(6)} %select_n.78), kind=kOutput, calls=%fused_computation.4 | convolution fusion | flops 1610612736 | bytes 9961476 | tf_op jit(solution)/shard_map/dot_general | solution.py:78
  73.7 1.8 %collective-permute-start.13 = (f32[1,128,1024]{2,1,0:T(8,128)S(1)}, f32[1,128,1024]{2,1,0:T(8,128)S(1)}, u32[]{:S(2)}, u32[]{:S(2)}) collective-permute-start(f32[1,128,1024]{2,1,0:T(8,128)S(1)} %bitcast.176), channel_id=1, source_target_pairs={{0,8},{4,12},{8,0},{12,4},{1,9},{5,13},{9,1},{13,5},{2,10},{6,14},... | collective-permute-start | bytes 1572872 | tf_op jit(solution)/shard_map/ppermute | solution.py:98
  76.1 6.1 %fusion.6 = f32[128,1024]{1,0:T(8,128)S(1)} fusion(f32[128,2048]{1,0:T(8,128)S(1)} %fusion.48, f32[2048,4096]{1,0:T(8,128)} %param.8, s32[]{:T(128)S(6)} %select_n.77), kind=kOutput, calls=%fused_computation.6 | convolution fusion | flops 1610612736 | bytes 9961476 | tf_op jit(solution)/shard_map/dot_general | solution.py:78
  82.3 5.3 %collective-permute-done.13 = f32[1,128,1024]{2,1,0:T(8,128)S(1)} collective-permute-done((f32[1,128,1024]{2,1,0:T(8,128)S(1)}, f32[1,128,1024]{2,1,0:T(8,128)S(1)}, u32[]{:S(2)}, u32[]{:S(2)}) %collective-permute-start.13) | collective-permute-done | bytes 524320 | tf_op jit(solution)/shard_map/ppermute | solution.py:98
  87.9 1.8 %collective-permute-start.14 = (f32[1,128,1024]{2,1,0:T(8,128)S(1)}, f32[1,128,1024]{2,1,0:T(8,128)S(1)}, u32[]{:S(2)}, u32[]{:S(2)}) collective-permute-start(f32[1,128,1024]{2,1,0:T(8,128)S(1)} %bitcast.171), channel_id=1, source_target_pairs={{0,8},{4,12},{8,0},{12,4},{1,9},{5,13},{9,1},{13,5},{2,10},{6,14},... | collective-permute-start | bytes 1572872 | tf_op jit(solution)/shard_map/ppermute | solution.py:107
  89.8 8.7 %fusion.2 = f32[128,2048]{1,0:T(8,128)S(1)} fusion(f32[4096,2048]{1,0:T(8,128)} %param.10, s32[]{:T(128)S(6)} %select_n.83, f32[128,1024]{1,0:T(8,128)S(1)} %collective-permute-done.15, f32[128,1024]{1,0:T(8,128)S(1)} %fusion.28, pred[]{:T(512)S(6)} %eq.6), kind=kOutput, calls=%fused_computation.2 | convolution fusion | flops 3222011904 | bytes 18874372 | tf_op jit(solution)/shard_map/dot_general | solution.py:118
  98.5 3.8 %collective-permute-done.14 = f32[1,128,1024]{2,1,0:T(8,128)S(1)} collective-permute-done((f32[1,128,1024]{2,1,0:T(8,128)S(1)}, f32[1,128,1024]{2,1,0:T(8,128)S(1)}, u32[]{:S(2)}, u32[]{:S(2)}) %collective-permute-start.14) | collective-permute-done | bytes 524320 | tf_op jit(solution)/shard_map/ppermute | solution.py:107
  102.3 1.9 %collective-permute-done.16 = f32[1,128,1024]{2,1,0:T(8,128)S(1)} collective-permute-done((f32[1,128,1024]{2,1,0:T(8,128)S(1)}, f32[1,128,1024]{2,1,0:T(8,128)S(1)}, u32[]{:S(2)}, u32[]{:S(2)}) %collective-permute-start.16) | collective-permute-done | bytes 524320 | tf_op jit(solution)/shard_map/ppermute | solution.py:126
  104.2 8.7 %fusion = f32[128,2048]{1,0:T(8,128)S(1)} fusion(f32[4096,2048]{1,0:T(8,128)} %param.10, s32[]{:T(128)S(6)} %select_n.86, f32[128,1024]{1,0:T(8,128)S(1)} %bitcast.175, f32[128,1024]{1,0:T(8,128)S(1)} %bitcast.174, pred[]{:T(512)S(6)} %eq.6), kind=kOutput, calls=%fused_computation | convolution fusion | flops 3222011904 | bytes 18874372 | tf_op jit(solution)/shard_map/dot_general | solution.py:118
  113.1 2.1 %collective-permute-start.17 = (f32[2,8,2048]{2,1,0:T(8,128)S(1)}, f32[2,8,2048]{2,1,0:T(8,128)S(1)}, u32[]{:S(2)}, u32[]{:S(2)}) collective-permute-start(f32[2,8,2048]{2,1,0:T(8,128)S(1)} %pad_maximum_fusion.7), channel_id=1, source_target_pairs={{0,1},{1,0},{2,3},{3,2},{4,5},{5,4},{6,7},{7,6},{8,9},{9,8},{10,11... | collective-permute-start | bytes 393224 | tf_op jit(solution)/shard_map/ppermute | solution.py:35
  115.2 3.8 %collective-permute-done.17 = f32[2,8,2048]{2,1,0:T(8,128)S(1)} collective-permute-done((f32[2,8,2048]{2,1,0:T(8,128)S(1)}, f32[2,8,2048]{2,1,0:T(8,128)S(1)}, u32[]{:S(2)}, u32[]{:S(2)}) %collective-permute-start.17) | collective-permute-done | bytes 131104 | tf_op jit(solution)/shard_map/ppermute | solution.py:35
  119.0 1.8 %collective-permute-start.19 = (f32[2,8,2048]{2,1,0:T(8,128)S(1)}, f32[2,8,2048]{2,1,0:T(8,128)S(1)}, u32[]{:S(2)}, u32[]{:S(2)}) collective-permute-start(f32[2,8,2048]{2,1,0:T(8,128)S(1)} %pad_maximum_fusion.8), channel_id=1, source_target_pairs={{0,1},{1,0},{2,3},{3,2},{4,5},{5,4},{6,7},{7,6},{8,9},{9,8},{10,11... | collective-permute-start | bytes 393224 | tf_op jit(solution)/shard_map/ppermute | solution.py:35
  121.2 1.8 %collective-permute-start.23 = (f32[2,8,2048]{2,1,0:T(8,128)S(1)}, f32[2,8,2048]{2,1,0:T(8,128)S(1)}, u32[]{:S(2)}, u32[]{:S(2)}) collective-permute-start(f32[2,8,2048]{2,1,0:T(8,128)S(1)} %pad_maximum_fusion.10), channel_id=1, source_target_pairs={{0,1},{1,0},{2,3},{3,2},{4,5},{5,4},{6,7},{7,6},{8,9},{9,8},{10,11... | collective-permute-start | bytes 393224 | tf_op jit(solution)/shard_map/ppermute | solution.py:35
  123.0 2.9 %collective-permute-start.18 = (f32[1,8,2048]{2,1,0:T(8,128)S(1)}, f32[1,8,2048]{2,1,0:T(8,128)S(1)}, u32[]{:S(2)}, u32[]{:S(2)}) collective-permute-start(f32[1,8,2048]{2,1,0:T(8,128)S(1)} %get-tuple-element.25), channel_id=1, source_target_pairs={{0,2},{1,3},{2,0},{3,1},{4,6},{5,7},{6,4},{7,5},{8,10},{9,11},{10,... | collective-permute-start | bytes 196616 | tf_op jit(solution)/shard_map/ppermute | solution.py:35
  125.9 4.1 %collective-permute-done.18 = f32[1,8,2048]{2,1,0:T(8,128)S(1)} collective-permute-done((f32[1,8,2048]{2,1,0:T(8,128)S(1)}, f32[1,8,2048]{2,1,0:T(8,128)S(1)}, u32[]{:S(2)}, u32[]{:S(2)}) %collective-permute-start.18) | collective-permute-done | bytes 65568 | tf_op jit(solution)/shard_map/ppermute | solution.py:35
  130.1 1.0 collective-permute-done.23
  131.2 2.4 %collective-permute-start.24 = (f32[1,8,2048]{2,1,0:T(8,128)S(1)}, f32[1,8,2048]{2,1,0:T(8,128)S(1)}, u32[]{:S(2)}, u32[]{:S(2)}) collective-permute-start(f32[1,8,2048]{2,1,0:T(8,128)S(1)} %get-tuple-element.22), channel_id=1, source_target_pairs={{0,2},{1,3},{2,0},{3,1},{4,6},{5,7},{6,4},{7,5},{8,10},{9,11},{10,... | collective-permute-start | bytes 196616 | tf_op jit(solution)/shard_map/ppermute | solution.py:35
  134.2 2.3 %collective-permute-start.20 = (f32[1,8,2048]{2,1,0:T(8,128)S(1)}, f32[1,8,2048]{2,1,0:T(8,128)S(1)}, u32[]{:S(2)}, u32[]{:S(2)}) collective-permute-start(f32[1,8,2048]{2,1,0:T(8,128)S(1)} %get-tuple-element.24), channel_id=1, source_target_pairs={{0,2},{1,3},{2,0},{3,1},{4,6},{5,7},{6,4},{7,5},{8,10},{9,11},{10,... | collective-permute-start | bytes 196616 | tf_op jit(solution)/shard_map/ppermute | solution.py:35
  136.5 4.0 %collective-permute-done.24 = f32[1,8,2048]{2,1,0:T(8,128)S(1)} collective-permute-done((f32[1,8,2048]{2,1,0:T(8,128)S(1)}, f32[1,8,2048]{2,1,0:T(8,128)S(1)}, u32[]{:S(2)}, u32[]{:S(2)}) %collective-permute-start.24) | collective-permute-done | bytes 65568 | tf_op jit(solution)/shard_map/ppermute | solution.py:35
  140.5 1.4 collective-permute-done.22
  142.8 1.8 %collective-permute-start.26 = (f32[8,2048]{1,0:T(8,128)S(1)}, f32[8,2048]{1,0:T(8,128)S(1)}, u32[]{:S(2)}, u32[]{:S(2)}) collective-permute-start(f32[8,2048]{1,0:T(8,128)S(1)} %get-tuple-element.43), channel_id=1, source_target_pairs={{0,8},{4,12},{8,0},{12,4},{1,9},{5,13},{9,1},{13,5},{2,10},{6,14},... | collective-permute-start | bytes 196616 | tf_op jit(solution)/shard_map/ppermute | solution.py:44
  144.7 2.2 %collective-permute-done.27 = f32[8,2048]{1,0:T(8,128)S(1)} collective-permute-done((f32[8,2048]{1,0:T(8,128)S(1)}, f32[8,2048]{1,0:T(8,128)S(1)}, u32[]{:S(2)}, u32[]{:S(2)}) %collective-permute-start.27) | collective-permute-done | bytes 65568 | tf_op jit(solution)/shard_map/ppermute | solution.py:44
  146.9 1.6 %collective-permute-done.26 = f32[8,2048]{1,0:T(8,128)S(1)} collective-permute-done((f32[8,2048]{1,0:T(8,128)S(1)}, f32[8,2048]{1,0:T(8,128)S(1)}, u32[]{:S(2)}, u32[]{:S(2)}) %collective-permute-start.26) | collective-permute-done | bytes 65568 | tf_op jit(solution)/shard_map/ppermute | solution.py:44
  148.6 0.8 multiply_add_fusion
  (64 shorter events, 5.5 us)
Async XLA Ops:
  4.3 4.9 %collective-permute-start.2 = (f32[8,2048]{1,0:T(8,128)S(1)}, f32[8,2048]{1,0:T(8,128)S(1)}, u32[]{:S(2)}, u32[]{:S(2)}) collective-permute-start(f32[8,2048]{1,0:T(8,128)S(1)} %get-tuple-element.46), channel_id=1, source_target_pairs={{0,12},{4,8},{8,4},{12,0},{1,13},{5,9},{9,5},{13,1},{2,14},{6,10},... | collective-permute-start | bytes 196616 | tf_op jit(solution)/shard_map/ppermute | solution.py:44
  6.7 4.7 %collective-permute-start.1 = (f32[8,2048]{1,0:T(8,128)S(1)}, f32[8,2048]{1,0:T(8,128)S(1)}, u32[]{:S(2)}, u32[]{:S(2)}) collective-permute-start(f32[8,2048]{1,0:T(8,128)S(1)} %get-tuple-element.47), channel_id=1, source_target_pairs={{0,8},{4,12},{8,0},{12,4},{1,9},{5,13},{9,1},{13,5},{2,10},{6,14},... | collective-permute-start | bytes 196616 | tf_op jit(solution)/shard_map/ppermute | solution.py:44
  7.4 4.0 %collective-permute-start = (f32[8,2048]{1,0:T(8,128)S(1)}, f32[8,2048]{1,0:T(8,128)S(1)}, u32[]{:S(2)}, u32[]{:S(2)}) collective-permute-start(f32[8,2048]{1,0:T(8,128)S(1)} %get-tuple-element.48), channel_id=1, source_target_pairs={{0,4},{4,0},{8,12},{12,8},{1,5},{5,1},{9,13},{13,9},{2,6},{6,2},{1... | collective-permute-start | bytes 196616 | tf_op jit(solution)/shard_map/ppermute | solution.py:44
  11.5 6.6 %collective-permute-start.3 = (f32[1,8,2048]{2,1,0:T(8,128)S(1)}, f32[1,8,2048]{2,1,0:T(8,128)S(1)}, u32[]{:S(2)}, u32[]{:S(2)}) collective-permute-start(f32[1,8,2048]{2,1,0:T(8,128)S(1)} %get-tuple-element.20), channel_id=1, source_target_pairs={{0,2},{1,3},{2,0},{3,1},{4,6},{5,7},{6,4},{7,5},{8,10},{9,11},{10,... | collective-permute-start | bytes 196616 | tf_op jit(solution)/shard_map/ppermute | solution.py:22
  18.1 5.0 %collective-permute-start.4 = (f32[2,8,2048]{2,1,0:T(8,128)S(1)}, f32[2,8,2048]{2,1,0:T(8,128)S(1)}, u32[]{:S(2)}, u32[]{:S(2)}) collective-permute-start(f32[2,8,2048]{2,1,0:T(8,128)S(1)} %pad_maximum_fusion.3), channel_id=1, source_target_pairs={{0,1},{1,0},{2,3},{3,2},{4,5},{5,4},{6,7},{7,6},{8,9},{9,8},{10,11... | collective-permute-start | bytes 393224 | tf_op jit(solution)/shard_map/ppermute | solution.py:22
  23.2 5.2 %collective-permute-start.5 = (f32[1,8,2048]{2,1,0:T(8,128)S(1)}, f32[1,8,2048]{2,1,0:T(8,128)S(1)}, u32[]{:S(2)}, u32[]{:S(2)}) collective-permute-start(f32[1,8,2048]{2,1,0:T(8,128)S(1)} %get-tuple-element.18), channel_id=1, source_target_pairs={{0,2},{1,3},{2,0},{3,1},{4,6},{5,7},{6,4},{7,5},{8,10},{9,11},{10,... | collective-permute-start | bytes 196616 | tf_op jit(solution)/shard_map/ppermute | solution.py:22
  28.5 5.0 %collective-permute-start.6 = (f32[2,8,2048]{2,1,0:T(8,128)S(1)}, f32[2,8,2048]{2,1,0:T(8,128)S(1)}, u32[]{:S(2)}, u32[]{:S(2)}) collective-permute-start(f32[2,8,2048]{2,1,0:T(8,128)S(1)} %pad_maximum_fusion.4), channel_id=1, source_target_pairs={{0,1},{1,0},{2,3},{3,2},{4,5},{5,4},{6,7},{7,6},{8,9},{9,8},{10,11... | collective-permute-start | bytes 393224 | tf_op jit(solution)/shard_map/ppermute | solution.py:22
  33.5 5.3 %collective-permute-start.7 = (f32[1,8,2048]{2,1,0:T(8,128)S(1)}, f32[1,8,2048]{2,1,0:T(8,128)S(1)}, u32[]{:S(2)}, u32[]{:S(2)}) collective-permute-start(f32[1,8,2048]{2,1,0:T(8,128)S(1)} %get-tuple-element.16), channel_id=1, source_target_pairs={{0,2},{1,3},{2,0},{3,1},{4,6},{5,7},{6,4},{7,5},{8,10},{9,11},{10,... | collective-permute-start | bytes 196616 | tf_op jit(solution)/shard_map/ppermute | solution.py:22
  38.9 5.7 %collective-permute-start.8 = (f32[2,8,2048]{2,1,0:T(8,128)S(1)}, f32[2,8,2048]{2,1,0:T(8,128)S(1)}, u32[]{:S(2)}, u32[]{:S(2)}) collective-permute-start(f32[2,8,2048]{2,1,0:T(8,128)S(1)} %pad_maximum_fusion.5), channel_id=1, source_target_pairs={{0,1},{1,0},{2,3},{3,2},{4,5},{5,4},{6,7},{7,6},{8,9},{9,8},{10,11... | collective-permute-start | bytes 393224 | tf_op jit(solution)/shard_map/ppermute | solution.py:22
  44.7 5.2 %collective-permute-start.9 = (f32[1,8,2048]{2,1,0:T(8,128)S(1)}, f32[1,8,2048]{2,1,0:T(8,128)S(1)}, u32[]{:S(2)}, u32[]{:S(2)}) collective-permute-start(f32[1,8,2048]{2,1,0:T(8,128)S(1)} %get-tuple-element.14), channel_id=1, source_target_pairs={{0,2},{1,3},{2,0},{3,1},{4,6},{5,7},{6,4},{7,5},{8,10},{9,11},{10,... | collective-permute-start | bytes 196616 | tf_op jit(solution)/shard_map/ppermute | solution.py:22
  49.9 5.1 %collective-permute-start.10 = (f32[2,8,2048]{2,1,0:T(8,128)S(1)}, f32[2,8,2048]{2,1,0:T(8,128)S(1)}, u32[]{:S(2)}, u32[]{:S(2)}) collective-permute-start(f32[2,8,2048]{2,1,0:T(8,128)S(1)} %pad_maximum_fusion.6), channel_id=1, source_target_pairs={{0,1},{1,0},{2,3},{3,2},{4,5},{5,4},{6,7},{7,6},{8,9},{9,8},{10,11... | collective-permute-start | bytes 393224 | tf_op jit(solution)/shard_map/ppermute | solution.py:22
  61.0 6.1 %collective-permute-start.11 = (f32[128,1024]{1,0:T(8,128)S(1)}, f32[128,1024]{1,0:T(8,128)S(1)}, u32[]{:S(2)}, u32[]{:S(2)}) collective-permute-start(f32[128,1024]{1,0:T(8,128)S(1)} %fusion.8), channel_id=1, source_target_pairs={{0,4},{4,0},{8,12},{12,8},{1,5},{5,1},{9,13},{13,9},{2,6},{6,2},{1... | collective-permute-start | bytes 1572872 | tf_op jit(solution)/shard_map/ppermute | solution.py:90
  67.1 81.4 %copy-start = (f32[8,8192]{1,0:T(8,128)S(1)}, f32[8,8192]{1,0:T(8,128)}, u32[]{:S(2)}) copy-start(f32[8,8192]{1,0:T(8,128)} %param.6) | copy-start | bytes 786436
  67.2 81.4 %copy-start.1 = (f32[8192]{0:T(1024)S(1)}, f32[8192]{0:T(1024)}, u32[]{:S(2)}) copy-start(f32[8192]{0:T(1024)} %param.11) | copy-start | bytes 98308
  73.2 9.1 %collective-permute-start.12 = (f32[128,1024]{1,0:T(8,128)S(1)}, f32[128,1024]{1,0:T(8,128)S(1)}, u32[]{:S(2)}, u32[]{:S(2)}) collective-permute-start(f32[128,1024]{1,0:T(8,128)S(1)} %fusion.4), channel_id=1, source_target_pairs={{0,4},{4,0},{8,12},{12,8},{1,5},{5,1},{9,13},{13,9},{2,6},{6,2},{1... | collective-permute-start | bytes 1572872 | tf_op jit(solution)/shard_map/ppermute | solution.py:90
  73.7 13.9 %collective-permute-start.13 = (f32[1,128,1024]{2,1,0:T(8,128)S(1)}, f32[1,128,1024]{2,1,0:T(8,128)S(1)}, u32[]{:S(2)}, u32[]{:S(2)}) collective-permute-start(f32[1,128,1024]{2,1,0:T(8,128)S(1)} %bitcast.176), channel_id=1, source_target_pairs={{0,8},{4,12},{8,0},{12,4},{1,9},{5,13},{9,1},{13,5},{2,10},{6,14},... | collective-permute-start | bytes 1572872 | tf_op jit(solution)/shard_map/ppermute | solution.py:98
  87.9 2.0 %collective-permute-start.15 = (f32[128,1024]{1,0:T(8,128)S(1)}, f32[128,1024]{1,0:T(8,128)S(1)}, u32[]{:S(2)}, u32[]{:S(2)}) collective-permute-start(f32[128,1024]{1,0:T(8,128)S(1)} %fusion.28), channel_id=1, source_target_pairs={{0,4},{4,0},{8,12},{12,8},{1,5},{5,1},{9,13},{13,9},{2,6},{6,2},{1... | collective-permute-start | bytes 1572872 | tf_op jit(solution)/shard_map/ppermute | solution.py:103
  87.9 14.3 %collective-permute-start.14 = (f32[1,128,1024]{2,1,0:T(8,128)S(1)}, f32[1,128,1024]{2,1,0:T(8,128)S(1)}, u32[]{:S(2)}, u32[]{:S(2)}) collective-permute-start(f32[1,128,1024]{2,1,0:T(8,128)S(1)} %bitcast.171), channel_id=1, source_target_pairs={{0,8},{4,12},{8,0},{12,4},{1,9},{5,13},{9,1},{13,5},{2,10},{6,14},... | collective-permute-start | bytes 1572872 | tf_op jit(solution)/shard_map/ppermute | solution.py:107
  102.3 1.9 %collective-permute-start.16 = (f32[1,128,1024]{2,1,0:T(8,128)S(1)}, f32[1,128,1024]{2,1,0:T(8,128)S(1)}, u32[]{:S(2)}, u32[]{:S(2)}) collective-permute-start(f32[1,128,1024]{2,1,0:T(8,128)S(1)} %collective-permute-done.14), channel_id=1, source_target_pairs={{0,4},{4,0},{8,12},{12,8},{1,5},{5,1},{9,13},{13,9},{2,6},{6,2},{1... | collective-permute-start | bytes 1572872 | tf_op jit(solution)/shard_map/ppermute | solution.py:126
  113.1 5.9 %collective-permute-start.17 = (f32[2,8,2048]{2,1,0:T(8,128)S(1)}, f32[2,8,2048]{2,1,0:T(8,128)S(1)}, u32[]{:S(2)}, u32[]{:S(2)}) collective-permute-start(f32[2,8,2048]{2,1,0:T(8,128)S(1)} %pad_maximum_fusion.7), channel_id=1, source_target_pairs={{0,1},{1,0},{2,3},{3,2},{4,5},{5,4},{6,7},{7,6},{8,9},{9,8},{10,11... | collective-permute-start | bytes 393224 | tf_op jit(solution)/shard_map/ppermute | solution.py:35
  119.0 11.1 %collective-permute-start.19 = (f32[2,8,2048]{2,1,0:T(8,128)S(1)}, f32[2,8,2048]{2,1,0:T(8,128)S(1)}, u32[]{:S(2)}, u32[]{:S(2)}) collective-permute-start(f32[2,8,2048]{2,1,0:T(8,128)S(1)} %pad_maximum_fusion.8), channel_id=1, source_target_pairs={{0,1},{1,0},{2,3},{3,2},{4,5},{5,4},{6,7},{7,6},{8,9},{9,8},{10,11... | collective-permute-start | bytes 393224 | tf_op jit(solution)/shard_map/ppermute | solution.py:35
  120.8 9.2 %collective-permute-start.21 = (f32[2,8,2048]{2,1,0:T(8,128)S(1)}, f32[2,8,2048]{2,1,0:T(8,128)S(1)}, u32[]{:S(2)}, u32[]{:S(2)}) collective-permute-start(f32[2,8,2048]{2,1,0:T(8,128)S(1)} %pad_maximum_fusion.9), channel_id=1, source_target_pairs={{0,1},{1,0},{2,3},{3,2},{4,5},{5,4},{6,7},{7,6},{8,9},{9,8},{10,11... | collective-permute-start | bytes 393224 | tf_op jit(solution)/shard_map/ppermute | solution.py:35
  121.2 9.9 %collective-permute-start.23 = (f32[2,8,2048]{2,1,0:T(8,128)S(1)}, f32[2,8,2048]{2,1,0:T(8,128)S(1)}, u32[]{:S(2)}, u32[]{:S(2)}) collective-permute-start(f32[2,8,2048]{2,1,0:T(8,128)S(1)} %pad_maximum_fusion.10), channel_id=1, source_target_pairs={{0,1},{1,0},{2,3},{3,2},{4,5},{5,4},{6,7},{7,6},{8,9},{9,8},{10,11... | collective-permute-start | bytes 393224 | tf_op jit(solution)/shard_map/ppermute | solution.py:35
  123.0 7.1 %collective-permute-start.18 = (f32[1,8,2048]{2,1,0:T(8,128)S(1)}, f32[1,8,2048]{2,1,0:T(8,128)S(1)}, u32[]{:S(2)}, u32[]{:S(2)}) collective-permute-start(f32[1,8,2048]{2,1,0:T(8,128)S(1)} %get-tuple-element.25), channel_id=1, source_target_pairs={{0,2},{1,3},{2,0},{3,1},{4,6},{5,7},{6,4},{7,5},{8,10},{9,11},{10,... | collective-permute-start | bytes 196616 | tf_op jit(solution)/shard_map/ppermute | solution.py:35
  131.2 9.3 %collective-permute-start.24 = (f32[1,8,2048]{2,1,0:T(8,128)S(1)}, f32[1,8,2048]{2,1,0:T(8,128)S(1)}, u32[]{:S(2)}, u32[]{:S(2)}) collective-permute-start(f32[1,8,2048]{2,1,0:T(8,128)S(1)} %get-tuple-element.22), channel_id=1, source_target_pairs={{0,2},{1,3},{2,0},{3,1},{4,6},{5,7},{6,4},{7,5},{8,10},{9,11},{10,... | collective-permute-start | bytes 196616 | tf_op jit(solution)/shard_map/ppermute | solution.py:35
  133.6 8.3 %collective-permute-start.22 = (f32[1,8,2048]{2,1,0:T(8,128)S(1)}, f32[1,8,2048]{2,1,0:T(8,128)S(1)}, u32[]{:S(2)}, u32[]{:S(2)}) collective-permute-start(f32[1,8,2048]{2,1,0:T(8,128)S(1)} %get-tuple-element.23), channel_id=1, source_target_pairs={{0,2},{1,3},{2,0},{3,1},{4,6},{5,7},{6,4},{7,5},{8,10},{9,11},{10,... | collective-permute-start | bytes 196616 | tf_op jit(solution)/shard_map/ppermute | solution.py:35
  134.2 8.4 %collective-permute-start.20 = (f32[1,8,2048]{2,1,0:T(8,128)S(1)}, f32[1,8,2048]{2,1,0:T(8,128)S(1)}, u32[]{:S(2)}, u32[]{:S(2)}) collective-permute-start(f32[1,8,2048]{2,1,0:T(8,128)S(1)} %get-tuple-element.24), channel_id=1, source_target_pairs={{0,2},{1,3},{2,0},{3,1},{4,6},{5,7},{6,4},{7,5},{8,10},{9,11},{10,... | collective-permute-start | bytes 196616 | tf_op jit(solution)/shard_map/ppermute | solution.py:35
  142.7 4.2 %collective-permute-start.27 = (f32[8,2048]{1,0:T(8,128)S(1)}, f32[8,2048]{1,0:T(8,128)S(1)}, u32[]{:S(2)}, u32[]{:S(2)}) collective-permute-start(f32[8,2048]{1,0:T(8,128)S(1)} %get-tuple-element.42), channel_id=1, source_target_pairs={{0,12},{4,8},{8,4},{12,0},{1,13},{5,9},{9,5},{13,1},{2,14},{6,10},... | collective-permute-start | bytes 196616 | tf_op jit(solution)/shard_map/ppermute | solution.py:44
  142.8 5.7 %collective-permute-start.26 = (f32[8,2048]{1,0:T(8,128)S(1)}, f32[8,2048]{1,0:T(8,128)S(1)}, u32[]{:S(2)}, u32[]{:S(2)}) collective-permute-start(f32[8,2048]{1,0:T(8,128)S(1)} %get-tuple-element.43), channel_id=1, source_target_pairs={{0,8},{4,12},{8,0},{12,4},{1,9},{5,13},{9,1},{13,5},{2,10},{6,14},... | collective-permute-start | bytes 196616 | tf_op jit(solution)/shard_map/ppermute | solution.py:44
  144.6 3.9 %collective-permute-start.25 = (f32[8,2048]{1,0:T(8,128)S(1)}, f32[8,2048]{1,0:T(8,128)S(1)}, u32[]{:S(2)}, u32[]{:S(2)}) collective-permute-start(f32[8,2048]{1,0:T(8,128)S(1)} %get-tuple-element.44), channel_id=1, source_target_pairs={{0,4},{4,0},{8,12},{12,8},{1,5},{5,1},{9,13},{13,9},{2,6},{6,2},{1... | collective-permute-start | bytes 196616 | tf_op jit(solution)/shard_map/ppermute | solution.py:44

commit v12 on v10

--- a/solution.py
+++ b/solution.py
@@ -81,16 +81,27 @@
     def low_bit(d):
         return (d & -d) if d else 2 * n_row
 
-    odd = sorted(range(1, n_row, 2), key=lambda d: low_bit(d ^ 1))
-    even = sorted(range(0, n_row, 2), key=low_bit)
-    recv = {}
+    core = r % 2
+
+    def up_pair(d, lhs):
+        w = lax.dynamic_slice_in_dim(up_weight, ((r ^ d) // 2) * 2 * quarter, 2 * quarter, 1)
+        both = lax.optimization_barrier(
+            jnp.dot(lhs, w, precision=lax.Precision.HIGH,
+                    preferred_element_type=jnp.float32))
+        mine = lax.dynamic_slice_in_dim(both, core * quarter, quarter, 1)
+        other = lax.dynamic_slice_in_dim(both, (1 - core) * quarter, quarter, 1)
+        return mine, other
+
     held = {}
     lhs = gathered
-    for d_odd, d_even in zip(odd, even):
-        recv[d_odd ^ 1] = lax.ppermute(
-            lax.optimization_barrier(up_block(d_odd, lhs)), "row", _pairs(n_row, 1))
-        held[d_even] = lax.optimization_barrier(up_block(d_even, lhs)) + recv[d_even]
-        if d_even == even[0]:
+    for i, d_even in enumerate(sorted(range(0, n_row, 2), key=low_bit)):
+        if d_even:
+            mine, other = up_pair(d_even, lhs)
+        else:
+            other = lax.optimization_barrier(up_block(1, lhs))
+            mine = lax.optimization_barrier(up_block(0, lhs))
+        held[d_even] = mine + lax.ppermute(other, "row", _pairs(n_row, 1))
+        if i == 0:
             lhs, held[d_even] = lax.optimization_barrier((lhs, held[d_even]))
     flip = 2
     while flip < n_row:
@@ -108,7 +119,6 @@
         for i, d in enumerate(mine):
             acts[d ^ flip] = got[i]
         flip *= 2
-    core = r % 2
 
     def down_pair(d):
         lo, hi = acts[d], acts[d ^ 1]

time: 129 us -> 128 us (level)
  matrix products: 41.2 us -> 38.3 us
  waiting for transfers between devices: 60.3 us -> 61.7 us
    dot_general x4 -> x2, matrix products: 23.8 us -> 11.9 us  [up_block(): jnp.dot(lhs, w, precision=lax.Precision.HIGH, preferred_element_type=jnp....]
    dot_general x0 -> x1, matrix products: none -> 8.88 us  [up_pair(): jnp.dot(lhs, w, precision=lax.Precision.HIGH, preferred_element_type=jnp....]
    ppermute x2, waiting for transfers between devices: 0.01 us -> 1.88 us  [local(): held[d_even] = mine + lax.ppermute(other, 'row', _pairs(n_row, 1))]
  transfers between devices with their start and end apart: 20 -> 20, of which waited for: 16 -> 17; matrix products, arithmetic and copies ran while one was open for 17% -> 12% of each run, Pallas kernels for 0% -> 0%
where the time goes in v12:
time: 128 us
  waiting for transfers between devices  61.7 us (48%)
  matrix products  38.3 us (30%)
  starting transfers between devices  19.9 us (16%)
  other arithmetic  6.75 us (5%)
    ppermute x4, waiting for transfers between devices, _gather_rel(): lax.ppermute(jnp.stack([held[k] for k in keys]), axis, _pairs(n, flip))  21.1 us
    ppermute x4, waiting for transfers between devices, _scatter_rel(): lax.ppermute(jnp.stack([held[d] for d in sent]), axis, _pairs(n, flip))  18.8 us
    dot_general x2, matrix products, down_pair(): jnp.dot(pair, w, precision=lax.Precision.HIGH, preferred_element_type=jnp...  17.5 us
    dot_general x2, matrix products, up_block(): jnp.dot(lhs, w, precision=lax.Precision.HIGH, preferred_element_type=jnp....  11.9 us
    dot_general x1, matrix products, up_pair(): jnp.dot(lhs, w, precision=lax.Precision.HIGH, preferred_element_type=jnp....  8.88 us
    ppermute x6, waiting for transfers between devices, _exchange_abs(): got.append(lax.ppermute(blocks[idx ^ d], axis, _pairs(n, d)))  8.2 us
    ppermute x4, starting transfers between devices, _scatter_rel(): lax.ppermute(jnp.stack([held[d] for d in sent]), axis, _pairs(n, flip))  6.4 us
    ppermute x1, waiting for transfers between devices, local(): lax.ppermute(jnp.stack([held[d] for d in sent]), 'row', _pairs(n_row, flip))  5.9 us
  transfers between devices with their start and end apart: 20, of which 17 were waited for; matrix products, arithmetic and copies ran while one was open for 12% of the time, Pallas kernels for 0%

profile of v12, /device:TPU:0, one launch (start us, length us, event | category | flops | bytes accessed | tf_op | source)
XLA Modules:
  0.0 128.0 jit_solution(13817228322810696663)
XLA Ops:
  0.0 0.8 fusion.51
  0.8 1.1 reduce_sum.18
  2.0 1.2 multiply_reduce_fusion
  3.2 1.1 multiply_add_fusion.1
  4.3 2.4 %collective-permute-start.2 = (f32[8,2048]{1,0:T(8,128)S(1)}, f32[8,2048]{1,0:T(8,128)S(1)}, u32[]{:S(2)}, u32[]{:S(2)}) collective-permute-start(f32[8,2048]{1,0:T(8,128)S(1)} %get-tuple-element.33), channel_id=1, source_target_pairs={{0,12},{4,8},{8,4},{12,0},{1,13},{5,9},{9,5},{13,1},{2,14},{6,10},... | collective-permute-start | bytes 196616 | tf_op jit(solution)/shard_map/ppermute | solution.py:44
  6.7 0.7 collective-permute-start
  7.5 1.8 %collective-permute-done.2 = f32[8,2048]{1,0:T(8,128)S(1)} collective-permute-done((f32[8,2048]{1,0:T(8,128)S(1)}, f32[8,2048]{1,0:T(8,128)S(1)}, u32[]{:S(2)}, u32[]{:S(2)}) %collective-permute-start.2) | collective-permute-done | bytes 65568 | tf_op jit(solution)/shard_map/ppermute | solution.py:44
  9.2 2.5 %collective-permute-done.1 = f32[8,2048]{1,0:T(8,128)S(1)} collective-permute-done((f32[8,2048]{1,0:T(8,128)S(1)}, f32[8,2048]{1,0:T(8,128)S(1)}, u32[]{:S(2)}, u32[]{:S(2)}) %collective-permute-start.1) | collective-permute-done | bytes 65568 | tf_op jit(solution)/shard_map/ppermute | solution.py:44
  11.8 2.7 %collective-permute-start.3 = (f32[1,16,2048]{2,1,0:T(8,128)S(1)}, f32[1,16,2048]{2,1,0:T(8,128)S(1)}, u32[]{:S(2)}, u32[]{:S(2)}) collective-permute-start(f32[1,16,2048]{2,1,0:T(8,128)S(1)} %fusion.43), channel_id=1, source_target_pairs={{0,2},{1,3},{2,0},{3,1},{4,6},{5,7},{6,4},{7,5},{8,10},{9,11},{10,... | collective-permute-start | bytes 393224 | tf_op jit(solution)/shard_map/ppermute | solution.py:22
  14.4 0.4 collective-permute-start.5
  14.8 9.1 %collective-permute-done.3 = f32[1,16,2048]{2,1,0:T(8,128)S(1)} collective-permute-done((f32[1,16,2048]{2,1,0:T(8,128)S(1)}, f32[1,16,2048]{2,1,0:T(8,128)S(1)}, u32[]{:S(2)}, u32[]{:S(2)}) %collective-permute-start.3) | collective-permute-done | bytes 131104 | tf_op jit(solution)/shard_map/ppermute | solution.py:22
  24.0 0.1 collective-permute-start.4
  24.1 1.6 %collective-permute-done.5 = f32[1,16,2048]{2,1,0:T(8,128)S(1)} collective-permute-done((f32[1,16,2048]{2,1,0:T(8,128)S(1)}, f32[1,16,2048]{2,1,0:T(8,128)S(1)}, u32[]{:S(2)}, u32[]{:S(2)}) %collective-permute-start.5) | collective-permute-done | bytes 131104 | tf_op jit(solution)/shard_map/ppermute | solution.py:22
  25.7 0.6 collective-permute-start.6
  26.3 6.9 %collective-permute-done.4 = f32[2,16,2048]{2,1,0:T(8,128)S(1)} collective-permute-done((f32[2,16,2048]{2,1,0:T(8,128)S(1)}, f32[2,16,2048]{2,1,0:T(8,128)S(1)}, u32[]{:S(2)}, u32[]{:S(2)}) %collective-permute-start.4) | collective-permute-done | bytes 262176 | tf_op jit(solution)/shard_map/ppermute | solution.py:22
  33.4 3.5 %collective-permute-done.6 = f32[2,16,2048]{2,1,0:T(8,128)S(1)} collective-permute-done((f32[2,16,2048]{2,1,0:T(8,128)S(1)}, f32[2,16,2048]{2,1,0:T(8,128)S(1)}, u32[]{:S(2)}, u32[]{:S(2)}) %collective-permute-start.6) | collective-permute-done | bytes 262176 | tf_op jit(solution)/shard_map/ppermute | solution.py:22
  36.9 8.9 %fusion.4 = f32[128,2048]{1,0:T(8,128)S(1)} fusion(f32[128,2048]{1,0:T(8,128)S(1)} %fusion.38, f32[2048,4096]{1,0:T(8,128)} %param.8, s32[]{:T(128)S(6)} %select_n.78), kind=kOutput, calls=%fused_computation.4 | convolution fusion | flops 3221225472 | bytes 18874372 | tf_op jit(solution)/shard_map/dot_general | solution.py:89
  45.8 0.1 collective-permute-start.7
  45.9 1.9 %collective-permute-done.7 = f32[128,1024]{1,0:T(8,128)S(1)} collective-permute-done((f32[128,1024]{1,0:T(8,128)S(1)}, f32[128,1024]{1,0:T(8,128)S(1)}, u32[]{:S(2)}, u32[]{:S(2)}) %collective-permute-start.7) | collective-permute-done | bytes 524320 | tf_op jit(solution)/shard_map/ppermute | solution.py:103
  47.9 6.0 %fusion.6 = f32[128,1024]{1,0:T(8,128)S(1)} fusion(f32[128,2048]{1,0:T(8,128)S(1)} %fusion.38, f32[2048,4096]{1,0:T(8,128)} %param.8, s32[]{:T(128)S(6)} %select_n.83), kind=kOutput, calls=%fused_computation.6 | convolution fusion | flops 1610612736 | bytes 9961476 | tf_op jit(solution)/shard_map/dot_general | solution.py:78
  53.9 0.2 collective-permute-start.8
  54.1 2.5 %collective-permute-start.9 = (f32[1,128,1024]{2,1,0:T(8,128)S(1)}, f32[1,128,1024]{2,1,0:T(8,128)}, u32[]{:S(2)}, u32[]{:S(2)}) collective-permute-start(f32[1,128,1024]{2,1,0:T(8,128)S(1)} %bitcast.115), channel_id=1, source_target_pairs={{0,8},{4,12},{8,0},{12,4},{1,9},{5,13},{9,1},{13,5},{2,10},{6,14},... | collective-permute-start | bytes 1572872 | tf_op jit(solution)/shard_map/ppermute | solution.py:109
  56.6 0.7 dynamic_slice.77
  57.3 5.9 %fusion.8 = f32[128,1024]{1,0:T(8,128)S(1)} fusion(f32[128,2048]{1,0:T(8,128)S(1)} %fusion.38, f32[2048,4096]{1,0:T(8,128)} %param.8, s32[]{:T(128)S(6)} %select_n.82), kind=kOutput, calls=%fused_computation.8 | convolution fusion | flops 1610612736 | bytes 9961476 | tf_op jit(solution)/shard_map/dot_general | solution.py:78
  63.2 5.9 %collective-permute-done.9 = f32[1,128,1024]{2,1,0:T(8,128)} collective-permute-done((f32[1,128,1024]{2,1,0:T(8,128)S(1)}, f32[1,128,1024]{2,1,0:T(8,128)}, u32[]{:S(2)}, u32[]{:S(2)}) %collective-permute-start.9) | collective-permute-done | bytes 524320 | tf_op jit(solution)/shard_map/ppermute | solution.py:109
  69.1 1.3 fusion.26
  70.4 0.1 collective-permute-start.11
  70.5 1.8 %collective-permute-start.10 = (f32[1,128,1024]{2,1,0:T(8,128)S(1)}, f32[1,128,1024]{2,1,0:T(8,128)S(1)}, u32[]{:S(2)}, u32[]{:S(2)}) collective-permute-start(f32[1,128,1024]{2,1,0:T(8,128)S(1)} %bitcast.110), channel_id=1, source_target_pairs={{0,8},{4,12},{8,0},{12,4},{1,9},{5,13},{9,1},{13,5},{2,10},{6,14},... | collective-permute-start | bytes 1572872 | tf_op jit(solution)/shard_map/ppermute | solution.py:118
  72.3 0.1 collective-permute-done.11
  72.4 8.7 %fusion.2 = f32[128,2048]{1,0:T(8,128)S(1)} fusion(f32[4096,2048]{1,0:T(8,128)} %param.10, s32[]{:T(128)S(6)} %select_n.87, f32[128,1024]{1,0:T(8,128)S(1)} %collective-permute-done.11, f32[128,1024]{1,0:T(8,128)S(1)} %fusion.26, pred[]{:T(512)S(6)} %eq.6), kind=kOutput, calls=%fused_computation.2 | convolution fusion | flops 3222011904 | bytes 18874372 | tf_op jit(solution)/shard_map/dot_general | solution.py:128
  81.1 3.7 %collective-permute-done.10 = f32[1,128,1024]{2,1,0:T(8,128)S(1)} collective-permute-done((f32[1,128,1024]{2,1,0:T(8,128)S(1)}, f32[1,128,1024]{2,1,0:T(8,128)S(1)}, u32[]{:S(2)}, u32[]{:S(2)}) %collective-permute-start.10) | collective-permute-done | bytes 524320 | tf_op jit(solution)/shard_map/ppermute | solution.py:118
  84.8 1.9 %collective-permute-done.12 = f32[1,128,1024]{2,1,0:T(8,128)S(1)} collective-permute-done((f32[1,128,1024]{2,1,0:T(8,128)S(1)}, f32[1,128,1024]{2,1,0:T(8,128)S(1)}, u32[]{:S(2)}, u32[]{:S(2)}) %collective-permute-start.12) | collective-permute-done | bytes 524320 | tf_op jit(solution)/shard_map/ppermute | solution.py:136
  86.7 8.8 %fusion = f32[128,2048]{1,0:T(8,128)S(1)} fusion(f32[4096,2048]{1,0:T(8,128)} %param.10, s32[]{:T(128)S(6)} %select_n.78, f32[128,1024]{1,0:T(8,128)S(1)} %bitcast.114, f32[128,1024]{1,0:T(8,128)S(1)} %bitcast.113, pred[]{:T(512)S(6)} %eq.6), kind=kOutput, calls=%fused_computation | convolution fusion | flops 3222011904 | bytes 18874372 | tf_op jit(solution)/shard_map/dot_general | solution.py:128
  95.5 0.1 add.168
  95.7 0.6 collective-permute-start.13
  96.4 7.8 %collective-permute-done.13 = f32[2,16,2048]{2,1,0:T(8,128)S(1)} collective-permute-done((f32[2,16,2048]{2,1,0:T(8,128)S(1)}, f32[2,16,2048]{2,1,0:T(8,128)S(1)}, u32[]{:S(2)}, u32[]{:S(2)}) %collective-permute-start.13) | collective-permute-done | bytes 262176 | tf_op jit(solution)/shard_map/ppermute | solution.py:35
  104.2 0.6 collective-permute-start.15
  104.8 3.5 %collective-permute-start.14 = (f32[1,16,2048]{2,1,0:T(8,128)S(1)}, f32[1,16,2048]{2,1,0:T(8,128)S(1)}, u32[]{:S(2)}, u32[]{:S(2)}) collective-permute-start(f32[1,16,2048]{2,1,0:T(8,128)S(1)} %get-tuple-element.15), channel_id=1, source_target_pairs={{0,2},{1,3},{2,0},{3,1},{4,6},{5,7},{6,4},{7,5},{8,10},{9,11},{10,... | collective-permute-start | bytes 393224 | tf_op jit(solution)/shard_map/ppermute | solution.py:35
  108.3 4.4 %collective-permute-done.14 = f32[1,16,2048]{2,1,0:T(8,128)S(1)} collective-permute-done((f32[1,16,2048]{2,1,0:T(8,128)S(1)}, f32[1,16,2048]{2,1,0:T(8,128)S(1)}, u32[]{:S(2)}, u32[]{:S(2)}) %collective-permute-start.14) | collective-permute-done | bytes 131104 | tf_op jit(solution)/shard_map/ppermute | solution.py:35
  112.7 1.9 %collective-permute-done.15 = f32[2,16,2048]{2,1,0:T(8,128)S(1)} collective-permute-done((f32[2,16,2048]{2,1,0:T(8,128)S(1)}, f32[2,16,2048]{2,1,0:T(8,128)S(1)}, u32[]{:S(2)}, u32[]{:S(2)}) %collective-permute-start.15) | collective-permute-done | bytes 262176 | tf_op jit(solution)/shard_map/ppermute | solution.py:35
  114.6 1.6 %collective-permute-start.16 = (f32[1,16,2048]{2,1,0:T(8,128)S(1)}, f32[1,16,2048]{2,1,0:T(8,128)S(1)}, u32[]{:S(2)}, u32[]{:S(2)}) collective-permute-start(f32[1,16,2048]{2,1,0:T(8,128)S(1)} %get-tuple-element.14), channel_id=1, source_target_pairs={{0,2},{1,3},{2,0},{3,1},{4,6},{5,7},{6,4},{7,5},{8,10},{9,11},{10,... | collective-permute-start | bytes 393224 | tf_op jit(solution)/shard_map/ppermute | solution.py:35
  116.3 4.8 %collective-permute-done.16 = f32[1,16,2048]{2,1,0:T(8,128)S(1)} collective-permute-done((f32[1,16,2048]{2,1,0:T(8,128)S(1)}, f32[1,16,2048]{2,1,0:T(8,128)S(1)}, u32[]{:S(2)}, u32[]{:S(2)}) %collective-permute-start.16) | collective-permute-done | bytes 131104 | tf_op jit(solution)/shard_map/ppermute | solution.py:35
  121.2 0.1 collective-permute-start.17
  121.2 1.8 %collective-permute-start.18 = (f32[8,2048]{1,0:T(8,128)S(1)}, f32[8,2048]{1,0:T(8,128)S(1)}, u32[]{:S(2)}, u32[]{:S(2)}) collective-permute-start(f32[8,2048]{1,0:T(8,128)S(1)} %get-tuple-element.26), channel_id=1, source_target_pairs={{0,8},{4,12},{8,0},{12,4},{1,9},{5,13},{9,1},{13,5},{2,10},{6,14},... | collective-permute-start | bytes 196616 | tf_op jit(solution)/shard_map/ppermute | solution.py:44
  123.0 0.1 collective-permute-start.19
  123.1 2.6 %collective-permute-done.18 = f32[8,2048]{1,0:T(8,128)S(1)} collective-permute-done((f32[8,2048]{1,0:T(8,128)S(1)}, f32[8,2048]{1,0:T(8,128)S(1)}, u32[]{:S(2)}, u32[]{:S(2)}) %collective-permute-start.18) | collective-permute-done | bytes 65568 | tf_op jit(solution)/shard_map/ppermute | solution.py:44
  125.7 1.3 %collective-permute-done.19 = f32[8,2048]{1,0:T(8,128)S(1)} collective-permute-done((f32[8,2048]{1,0:T(8,128)S(1)}, f32[8,2048]{1,0:T(8,128)S(1)}, u32[]{:S(2)}, u32[]{:S(2)}) %collective-permute-start.19) | collective-permute-done | bytes 65568 | tf_op jit(solution)/shard_map/ppermute | solution.py:44
  127.2 0.8 multiply_add_fusion
  (39 shorter events, 0.7 us)
Async XLA Ops:
  4.3 4.9 %collective-permute-start.2 = (f32[8,2048]{1,0:T(8,128)S(1)}, f32[8,2048]{1,0:T(8,128)S(1)}, u32[]{:S(2)}, u32[]{:S(2)}) collective-permute-start(f32[8,2048]{1,0:T(8,128)S(1)} %get-tuple-element.33), channel_id=1, source_target_pairs={{0,12},{4,8},{8,4},{12,0},{1,13},{5,9},{9,5},{13,1},{2,14},{6,10},... | collective-permute-start | bytes 196616 | tf_op jit(solution)/shard_map/ppermute | solution.py:44
  6.7 2.5 %collective-permute-start = (f32[8,2048]{1,0:T(8,128)S(1)}, f32[8,2048]{1,0:T(8,128)S(1)}, u32[]{:S(2)}, u32[]{:S(2)}) collective-permute-start(f32[8,2048]{1,0:T(8,128)S(1)} %get-tuple-element.35), channel_id=1, source_target_pairs={{0,4},{4,0},{8,12},{12,8},{1,5},{5,1},{9,13},{13,9},{2,6},{6,2},{1... | collective-permute-start | bytes 196616 | tf_op jit(solution)/shard_map/ppermute | solution.py:44
  7.4 4.3 %collective-permute-start.1 = (f32[8,2048]{1,0:T(8,128)S(1)}, f32[8,2048]{1,0:T(8,128)S(1)}, u32[]{:S(2)}, u32[]{:S(2)}) collective-permute-start(f32[8,2048]{1,0:T(8,128)S(1)} %get-tuple-element.34), channel_id=1, source_target_pairs={{0,8},{4,12},{8,0},{12,4},{1,9},{5,13},{9,1},{13,5},{2,10},{6,14},... | collective-permute-start | bytes 196616 | tf_op jit(solution)/shard_map/ppermute | solution.py:44
  11.8 12.2 %collective-permute-start.3 = (f32[1,16,2048]{2,1,0:T(8,128)S(1)}, f32[1,16,2048]{2,1,0:T(8,128)S(1)}, u32[]{:S(2)}, u32[]{:S(2)}) collective-permute-start(f32[1,16,2048]{2,1,0:T(8,128)S(1)} %fusion.43), channel_id=1, source_target_pairs={{0,2},{1,3},{2,0},{3,1},{4,6},{5,7},{6,4},{7,5},{8,10},{9,11},{10,... | collective-permute-start | bytes 393224 | tf_op jit(solution)/shard_map/ppermute | solution.py:22
  14.4 11.3 %collective-permute-start.5 = (f32[1,16,2048]{2,1,0:T(8,128)S(1)}, f32[1,16,2048]{2,1,0:T(8,128)S(1)}, u32[]{:S(2)}, u32[]{:S(2)}) collective-permute-start(f32[1,16,2048]{2,1,0:T(8,128)S(1)} %fusion.42), channel_id=1, source_target_pairs={{0,2},{1,3},{2,0},{3,1},{4,6},{5,7},{6,4},{7,5},{8,10},{9,11},{10,... | collective-permute-start | bytes 393224 | tf_op jit(solution)/shard_map/ppermute | solution.py:22
  24.0 9.3 %collective-permute-start.4 = (f32[2,16,2048]{2,1,0:T(8,128)S(1)}, f32[2,16,2048]{2,1,0:T(8,128)S(1)}, u32[]{:S(2)}, u32[]{:S(2)}) collective-permute-start(f32[2,16,2048]{2,1,0:T(8,128)S(1)} %pad_maximum_fusion.1), channel_id=1, source_target_pairs={{0,1},{1,0},{2,3},{3,2},{4,5},{5,4},{6,7},{7,6},{8,9},{9,8},{10,11... | collective-permute-start | bytes 786440 | tf_op jit(solution)/shard_map/ppermute | solution.py:22
  25.7 11.1 %collective-permute-start.6 = (f32[2,16,2048]{2,1,0:T(8,128)S(1)}, f32[2,16,2048]{2,1,0:T(8,128)S(1)}, u32[]{:S(2)}, u32[]{:S(2)}) collective-permute-start(f32[2,16,2048]{2,1,0:T(8,128)S(1)} %pad_maximum_fusion.2), channel_id=1, source_target_pairs={{0,1},{1,0},{2,3},{3,2},{4,5},{5,4},{6,7},{7,6},{8,9},{9,8},{10,11... | collective-permute-start | bytes 786440 | tf_op jit(solution)/shard_map/ppermute | solution.py:22
  45.8 2.0 %collective-permute-start.7 = (f32[128,1024]{1,0:T(8,128)S(1)}, f32[128,1024]{1,0:T(8,128)S(1)}, u32[]{:S(2)}, u32[]{:S(2)}) collective-permute-start(f32[128,1024]{1,0:T(8,128)S(1)} %constant_dynamic-slice_fusion.5), channel_id=1, source_target_pairs={{0,4},{4,0},{8,12},{12,8},{1,5},{5,1},{9,13},{13,9},{2,6},{6,2},{1... | collective-permute-start | bytes 1572872 | tf_op jit(solution)/shard_map/ppermute | solution.py:103
  47.9 79.3 %copy-start = (f32[8,8192]{1,0:T(8,128)S(1)}, f32[8,8192]{1,0:T(8,128)}, u32[]{:S(2)}) copy-start(f32[8,8192]{1,0:T(8,128)} %param.6) | copy-start | bytes 786436
  47.9 79.3 %copy-start.1 = (f32[8192]{0:T(1024)S(1)}, f32[8192]{0:T(1024)}, u32[]{:S(2)}) copy-start(f32[8192]{0:T(1024)} %param.11) | copy-start | bytes 98308
  53.9 9.3 %collective-permute-start.8 = (f32[128,1024]{1,0:T(8,128)S(1)}, f32[128,1024]{1,0:T(8,128)S(1)}, u32[]{:S(2)}, u32[]{:S(2)}) collective-permute-start(f32[128,1024]{1,0:T(8,128)S(1)} %fusion.6), channel_id=1, source_target_pairs={{0,4},{4,0},{8,12},{12,8},{1,5},{5,1},{9,13},{13,9},{2,6},{6,2},{1... | collective-permute-start | bytes 1572872 | tf_op jit(solution)/shard_map/ppermute | solution.py:103
  54.1 15.0 %collective-permute-start.9 = (f32[1,128,1024]{2,1,0:T(8,128)S(1)}, f32[1,128,1024]{2,1,0:T(8,128)}, u32[]{:S(2)}, u32[]{:S(2)}) collective-permute-start(f32[1,128,1024]{2,1,0:T(8,128)S(1)} %bitcast.115), channel_id=1, source_target_pairs={{0,8},{4,12},{8,0},{12,4},{1,9},{5,13},{9,1},{13,5},{2,10},{6,14},... | collective-permute-start | bytes 1572872 | tf_op jit(solution)/shard_map/ppermute | solution.py:109
  70.4 2.0 %collective-permute-start.11 = (f32[128,1024]{1,0:T(8,128)S(1)}, f32[128,1024]{1,0:T(8,128)S(1)}, u32[]{:S(2)}, u32[]{:S(2)}) collective-permute-start(f32[128,1024]{1,0:T(8,128)S(1)} %fusion.26), channel_id=1, source_target_pairs={{0,4},{4,0},{8,12},{12,8},{1,5},{5,1},{9,13},{13,9},{2,6},{6,2},{1... | collective-permute-start | bytes 1572872 | tf_op jit(solution)/shard_map/ppermute | solution.py:114
  70.5 14.3 %collective-permute-start.10 = (f32[1,128,1024]{2,1,0:T(8,128)S(1)}, f32[1,128,1024]{2,1,0:T(8,128)S(1)}, u32[]{:S(2)}, u32[]{:S(2)}) collective-permute-start(f32[1,128,1024]{2,1,0:T(8,128)S(1)} %bitcast.110), channel_id=1, source_target_pairs={{0,8},{4,12},{8,0},{12,4},{1,9},{5,13},{9,1},{13,5},{2,10},{6,14},... | collective-permute-start | bytes 1572872 | tf_op jit(solution)/shard_map/ppermute | solution.py:118
  84.8 1.9 %collective-permute-start.12 = (f32[1,128,1024]{2,1,0:T(8,128)S(1)}, f32[1,128,1024]{2,1,0:T(8,128)S(1)}, u32[]{:S(2)}, u32[]{:S(2)}) collective-permute-start(f32[1,128,1024]{2,1,0:T(8,128)S(1)} %collective-permute-done.10), channel_id=1, source_target_pairs={{0,4},{4,0},{8,12},{12,8},{1,5},{5,1},{9,13},{13,9},{2,6},{6,2},{1... | collective-permute-start | bytes 1572872 | tf_op jit(solution)/shard_map/ppermute | solution.py:136
  95.7 8.4 %collective-permute-start.13 = (f32[2,16,2048]{2,1,0:T(8,128)S(1)}, f32[2,16,2048]{2,1,0:T(8,128)S(1)}, u32[]{:S(2)}, u32[]{:S(2)}) collective-permute-start(f32[2,16,2048]{2,1,0:T(8,128)S(1)} %pad_maximum_fusion.3), channel_id=1, source_target_pairs={{0,1},{1,0},{2,3},{3,2},{4,5},{5,4},{6,7},{7,6},{8,9},{9,8},{10,11... | collective-permute-start | bytes 786440 | tf_op jit(solution)/shard_map/ppermute | solution.py:35
  104.2 10.4 %collective-permute-start.15 = (f32[2,16,2048]{2,1,0:T(8,128)S(1)}, f32[2,16,2048]{2,1,0:T(8,128)S(1)}, u32[]{:S(2)}, u32[]{:S(2)}) collective-permute-start(f32[2,16,2048]{2,1,0:T(8,128)S(1)} %pad_maximum_fusion.4), channel_id=1, source_target_pairs={{0,1},{1,0},{2,3},{3,2},{4,5},{5,4},{6,7},{7,6},{8,9},{9,8},{10,11... | collective-permute-start | bytes 786440 | tf_op jit(solution)/shard_map/ppermute | solution.py:35
  104.8 7.8 %collective-permute-start.14 = (f32[1,16,2048]{2,1,0:T(8,128)S(1)}, f32[1,16,2048]{2,1,0:T(8,128)S(1)}, u32[]{:S(2)}, u32[]{:S(2)}) collective-permute-start(f32[1,16,2048]{2,1,0:T(8,128)S(1)} %get-tuple-element.15), channel_id=1, source_target_pairs={{0,2},{1,3},{2,0},{3,1},{4,6},{5,7},{6,4},{7,5},{8,10},{9,11},{10,... | collective-permute-start | bytes 393224 | tf_op jit(solution)/shard_map/ppermute | solution.py:35
  114.6 6.4 %collective-permute-start.16 = (f32[1,16,2048]{2,1,0:T(8,128)S(1)}, f32[1,16,2048]{2,1,0:T(8,128)S(1)}, u32[]{:S(2)}, u32[]{:S(2)}) collective-permute-start(f32[1,16,2048]{2,1,0:T(8,128)S(1)} %get-tuple-element.14), channel_id=1, source_target_pairs={{0,2},{1,3},{2,0},{3,1},{4,6},{5,7},{6,4},{7,5},{8,10},{9,11},{10,... | collective-permute-start | bytes 393224 | tf_op jit(solution)/shard_map/ppermute | solution.py:35
  121.2 2.0 %collective-permute-start.17 = (f32[8,2048]{1,0:T(8,128)S(1)}, f32[8,2048]{1,0:T(8,128)S(1)}, u32[]{:S(2)}, u32[]{:S(2)}) collective-permute-start(f32[8,2048]{1,0:T(8,128)S(1)} %get-tuple-element.27), channel_id=1, source_target_pairs={{0,4},{4,0},{8,12},{12,8},{1,5},{5,1},{9,13},{13,9},{2,6},{6,2},{1... | collective-permute-start | bytes 196616 | tf_op jit(solution)/shard_map/ppermute | solution.py:44
  121.2 4.5 %collective-permute-start.18 = (f32[8,2048]{1,0:T(8,128)S(1)}, f32[8,2048]{1,0:T(8,128)S(1)}, u32[]{:S(2)}, u32[]{:S(2)}) collective-permute-start(f32[8,2048]{1,0:T(8,128)S(1)} %get-tuple-element.26), channel_id=1, source_target_pairs={{0,8},{4,12},{8,0},{12,4},{1,9},{5,13},{9,1},{13,5},{2,10},{6,14},... | collective-permute-start | bytes 196616 | tf_op jit(solution)/shard_map/ppermute | solution.py:44
  123.0 4.0 %collective-permute-start.19 = (f32[8,2048]{1,0:T(8,128)S(1)}, f32[8,2048]{1,0:T(8,128)S(1)}, u32[]{:S(2)}, u32[]{:S(2)}) collective-permute-start(f32[8,2048]{1,0:T(8,128)S(1)} %get-tuple-element.25), channel_id=1, source_target_pairs={{0,12},{4,8},{8,4},{12,0},{1,13},{5,9},{9,5},{13,1},{2,14},{6,10},... | collective-permute-start | bytes 196616 | tf_op jit(solution)/shard_map/ppermute | solution.py:44

commit v13 on v12

--- a/solution.py
+++ b/solution.py
@@ -2,6 +2,8 @@
 import jax.numpy as jnp
 from jax import lax
 from jax.sharding import PartitionSpec as P
+from jax.experimental import pallas as pl
+from jax.experimental.pallas import tpu as pltpu
 
 SEQ = 256
 N_CHUNK = 2
@@ -46,6 +48,26 @@
     return jnp.stack([rel[s ^ idx] for s in range(n)])
 
 
+def _norm_kernel(x_ref, o_ref):
+    x = x_ref[...]
+    average = jnp.mean(x, axis=1, keepdims=True)
+    centred = x - average
+    spread_sq = jnp.mean(centred * centred, axis=1, keepdims=True)
+    o_ref[...] = centred * lax.rsqrt(spread_sq + layer_eps)
+
+
+def _normalize(tokens):
+    rows, width = tokens.shape
+    return pl.pallas_call(
+        _norm_kernel,
+        out_shape=jax.ShapeDtypeStruct(tokens.shape, jnp.float32),
+        in_specs=[pl.BlockSpec(memory_space=pltpu.VMEM)],
+        out_specs=pl.BlockSpec(memory_space=pltpu.VMEM),
+        cost_estimate=pl.CostEstimate(flops=6 * rows * width, transcendentals=rows,
+                                      bytes_accessed=8 * rows * width),
+    )(tokens)
+
+
 def local(tokens, modulation, up_weight, up_bias, down_weight, down_bias):
     n_row = lax.axis_size("row")
     tok_dev = tokens.shape[0]
@@ -55,10 +77,7 @@
     shift_vec = own_mods[0]
     scale_vec = own_mods[1]
     gate_vec = own_mods[2]
-    average = jnp.mean(tokens, axis=1, keepdims=True)
-    centred = tokens - average
-    spread_sq = jnp.mean(centred * centred, axis=1, keepdims=True)
-    normed = centred * lax.rsqrt(spread_sq + layer_eps)
+    normed = _normalize(tokens)
     mixed = normed * (1.0 + scale_vec) + shift_vec
     r = lax.axis_index("row")
     d_blk = mixed.shape[1] // n_row

time: 128 us -> 128 us (level)
  other arithmetic: 6.75 us -> 4.34 us
  Pallas kernels: 0 us -> 1.97 us
    reduce_sum x2 -> x0, other arithmetic: 2.33 us -> none  [the longest x1 1.2 us: local(): spread_sq = jnp.mean(centred * centred, axis=1, keepdims=True)]
    pallas_call x0 -> x1, Pallas kernels: none -> 1.97 us  [_normalize(): pl.pallas_call(_norm_kernel, out_shape=jax.ShapeDtypeStruct(tokens.shape,...]
where the time goes in v13:
time: 128 us
  waiting for transfers between devices  61.7 us (48%)
  matrix products  38.3 us (30%)
  starting transfers between devices  19.9 us (16%)
  other arithmetic  4.34 us (3%)
  Pallas kernels  1.97 us (2%)
    ppermute x4, waiting for transfers between devices, _gather_rel(): lax.ppermute(jnp.stack([held[k] for k in keys]), axis, _pairs(n, flip))  21.1 us
    ppermute x4, waiting for transfers between devices, _scatter_rel(): lax.ppermute(jnp.stack([held[d] for d in sent]), axis, _pairs(n, flip))  18.8 us
    dot_general x2, matrix products, down_pair(): jnp.dot(pair, w, precision=lax.Precision.HIGH, preferred_element_type=jnp...  17.5 us
    dot_general x2, matrix products, up_block(): jnp.dot(lhs, w, precision=lax.Precision.HIGH, preferred_element_type=jnp....  11.9 us
    dot_general x1, matrix products, up_pair(): jnp.dot(lhs, w, precision=lax.Precision.HIGH, preferred_element_type=jnp....  8.88 us
    ppermute x6, waiting for transfers between devices, _exchange_abs(): got.append(lax.ppermute(blocks[idx ^ d], axis, _pairs(n, d)))  8.2 us
    ppermute x4, starting transfers between devices, _scatter_rel(): lax.ppermute(jnp.stack([held[d] for d in sent]), axis, _pairs(n, flip))  6.39 us
    ppermute x1, waiting for transfers between devices, local(): lax.ppermute(jnp.stack([held[d] for d in sent]), 'row', _pairs(n_row, flip))  5.9 us
  transfers between devices with their start and end apart: 20, of which 17 were waited for; matrix products, arithmetic and copies ran while one was open for 12% of the time, Pallas kernels for 0%

profile of v13, /device:TPU:0, one launch (start us, length us, event | category | flops | bytes accessed | tf_op | source)
XLA Modules:
  0.0 127.5 jit_solution(10255488084673725300)
XLA Ops:
  0.0 0.8 fusion.51
  0.8 2.0 %shard_map.64 = f32[8,8192]{1,0:T(8,128)} custom-call(f32[8,8192]{1,0:T(8,128)} %x_ref.1), custom_call_target="tpu_custom_call" | custom-call | flops 393216 | bytes 524288 | tf_op jit(solution)/shard_map/pallas_call | solution.py:61
  2.8 1.0 multiply_add_fusion.1
  3.8 2.4 %collective-permute-start.2 = (f32[8,2048]{1,0:T(8,128)S(1)}, f32[8,2048]{1,0:T(8,128)S(1)}, u32[]{:S(2)}, u32[]{:S(2)}) collective-permute-start(f32[8,2048]{1,0:T(8,128)S(1)} %get-tuple-element.33), channel_id=1, source_target_pairs={{0,12},{4,8},{8,4},{12,0},{1,13},{5,9},{9,5},{13,1},{2,14},{6,10},... | collective-permute-start | bytes 196616 | tf_op jit(solution)/shard_map/ppermute | solution.py:46
  6.3 0.7 collective-permute-start
  7.0 1.8 %collective-permute-done.2 = f32[8,2048]{1,0:T(8,128)S(1)} collective-permute-done((f32[8,2048]{1,0:T(8,128)S(1)}, f32[8,2048]{1,0:T(8,128)S(1)}, u32[]{:S(2)}, u32[]{:S(2)}) %collective-permute-start.2) | collective-permute-done | bytes 65568 | tf_op jit(solution)/shard_map/ppermute | solution.py:46
  8.8 2.5 %collective-permute-done.1 = f32[8,2048]{1,0:T(8,128)S(1)} collective-permute-done((f32[8,2048]{1,0:T(8,128)S(1)}, f32[8,2048]{1,0:T(8,128)S(1)}, u32[]{:S(2)}, u32[]{:S(2)}) %collective-permute-start.1) | collective-permute-done | bytes 65568 | tf_op jit(solution)/shard_map/ppermute | solution.py:46
  11.3 2.7 %collective-permute-start.3 = (f32[1,16,2048]{2,1,0:T(8,128)S(1)}, f32[1,16,2048]{2,1,0:T(8,128)S(1)}, u32[]{:S(2)}, u32[]{:S(2)}) collective-permute-start(f32[1,16,2048]{2,1,0:T(8,128)S(1)} %fusion.43), channel_id=1, source_target_pairs={{0,2},{1,3},{2,0},{3,1},{4,6},{5,7},{6,4},{7,5},{8,10},{9,11},{10,... | collective-permute-start | bytes 393224 | tf_op jit(solution)/shard_map/ppermute | solution.py:24
  14.0 0.4 collective-permute-start.5
  14.4 9.1 %collective-permute-done.3 = f32[1,16,2048]{2,1,0:T(8,128)S(1)} collective-permute-done((f32[1,16,2048]{2,1,0:T(8,128)S(1)}, f32[1,16,2048]{2,1,0:T(8,128)S(1)}, u32[]{:S(2)}, u32[]{:S(2)}) %collective-permute-start.3) | collective-permute-done | bytes 131104 | tf_op jit(solution)/shard_map/ppermute | solution.py:24
  23.5 0.1 collective-permute-start.4
  23.6 1.6 %collective-permute-done.5 = f32[1,16,2048]{2,1,0:T(8,128)S(1)} collective-permute-done((f32[1,16,2048]{2,1,0:T(8,128)S(1)}, f32[1,16,2048]{2,1,0:T(8,128)S(1)}, u32[]{:S(2)}, u32[]{:S(2)}) %collective-permute-start.5) | collective-permute-done | bytes 131104 | tf_op jit(solution)/shard_map/ppermute | solution.py:24
  25.2 0.6 collective-permute-start.6
  25.9 6.9 %collective-permute-done.4 = f32[2,16,2048]{2,1,0:T(8,128)S(1)} collective-permute-done((f32[2,16,2048]{2,1,0:T(8,128)S(1)}, f32[2,16,2048]{2,1,0:T(8,128)S(1)}, u32[]{:S(2)}, u32[]{:S(2)}) %collective-permute-start.4) | collective-permute-done | bytes 262176 | tf_op jit(solution)/shard_map/ppermute | solution.py:24
  32.9 3.5 %collective-permute-done.6 = f32[2,16,2048]{2,1,0:T(8,128)S(1)} collective-permute-done((f32[2,16,2048]{2,1,0:T(8,128)S(1)}, f32[2,16,2048]{2,1,0:T(8,128)S(1)}, u32[]{:S(2)}, u32[]{:S(2)}) %collective-permute-start.6) | collective-permute-done | bytes 262176 | tf_op jit(solution)/shard_map/ppermute | solution.py:24
  36.4 8.9 %fusion.4 = f32[128,2048]{1,0:T(8,128)S(1)} fusion(f32[128,2048]{1,0:T(8,128)S(1)} %fusion.38, f32[2048,4096]{1,0:T(8,128)} %param.8, s32[]{:T(128)S(6)} %select_n.78), kind=kOutput, calls=%fused_computation.4 | convolution fusion | flops 3221225472 | bytes 18874372 | tf_op jit(solution)/shard_map/dot_general | solution.py:108
  45.4 0.1 collective-permute-start.7
  45.4 1.9 %collective-permute-done.7 = f32[128,1024]{1,0:T(8,128)S(1)} collective-permute-done((f32[128,1024]{1,0:T(8,128)S(1)}, f32[128,1024]{1,0:T(8,128)S(1)}, u32[]{:S(2)}, u32[]{:S(2)}) %collective-permute-start.7) | collective-permute-done | bytes 524320 | tf_op jit(solution)/shard_map/ppermute | solution.py:122
  47.3 0.1 dynamic-slice_add_fusion
  47.4 6.0 %fusion.6 = f32[128,1024]{1,0:T(8,128)S(1)} fusion(f32[128,2048]{1,0:T(8,128)S(1)} %fusion.38, f32[2048,4096]{1,0:T(8,128)} %param.8, s32[]{:T(128)S(6)} %select_n.83), kind=kOutput, calls=%fused_computation.6 | convolution fusion | flops 1610612736 | bytes 9961476 | tf_op jit(solution)/shard_map/dot_general | solution.py:97
  53.4 0.2 collective-permute-start.8
  53.6 2.5 %collective-permute-start.9 = (f32[1,128,1024]{2,1,0:T(8,128)S(1)}, f32[1,128,1024]{2,1,0:T(8,128)}, u32[]{:S(2)}, u32[]{:S(2)}) collective-permute-start(f32[1,128,1024]{2,1,0:T(8,128)S(1)} %bitcast.115), channel_id=1, source_target_pairs={{0,8},{4,12},{8,0},{12,4},{1,9},{5,13},{9,1},{13,5},{2,10},{6,14},... | collective-permute-start | bytes 1572872 | tf_op jit(solution)/shard_map/ppermute | solution.py:128
  56.1 0.7 dynamic_slice.77
  56.8 5.9 %fusion.8 = f32[128,1024]{1,0:T(8,128)S(1)} fusion(f32[128,2048]{1,0:T(8,128)S(1)} %fusion.38, f32[2048,4096]{1,0:T(8,128)} %param.8, s32[]{:T(128)S(6)} %select_n.82), kind=kOutput, calls=%fused_computation.8 | convolution fusion | flops 1610612736 | bytes 9961476 | tf_op jit(solution)/shard_map/dot_general | solution.py:97
  62.8 5.9 %collective-permute-done.9 = f32[1,128,1024]{2,1,0:T(8,128)} collective-permute-done((f32[1,128,1024]{2,1,0:T(8,128)S(1)}, f32[1,128,1024]{2,1,0:T(8,128)}, u32[]{:S(2)}, u32[]{:S(2)}) %collective-permute-start.9) | collective-permute-done | bytes 524320 | tf_op jit(solution)/shard_map/ppermute | solution.py:128
  68.7 1.3 fusion.26
  69.9 0.1 collective-permute-start.11
  70.0 1.8 %collective-permute-start.10 = (f32[1,128,1024]{2,1,0:T(8,128)S(1)}, f32[1,128,1024]{2,1,0:T(8,128)S(1)}, u32[]{:S(2)}, u32[]{:S(2)}) collective-permute-start(f32[1,128,1024]{2,1,0:T(8,128)S(1)} %bitcast.110), channel_id=1, source_target_pairs={{0,8},{4,12},{8,0},{12,4},{1,9},{5,13},{9,1},{13,5},{2,10},{6,14},... | collective-permute-start | bytes 1572872 | tf_op jit(solution)/shard_map/ppermute | solution.py:137
  71.8 0.1 collective-permute-done.11
  71.9 8.7 %fusion.2 = f32[128,2048]{1,0:T(8,128)S(1)} fusion(f32[4096,2048]{1,0:T(8,128)} %param.10, s32[]{:T(128)S(6)} %select_n.87, f32[128,1024]{1,0:T(8,128)S(1)} %collective-permute-done.11, f32[128,1024]{1,0:T(8,128)S(1)} %fusion.26, pred[]{:T(512)S(6)} %eq.6), kind=kOutput, calls=%fused_computation.2 | convolution fusion | flops 3222011904 | bytes 18874372 | tf_op jit(solution)/shard_map/dot_general | solution.py:147
  80.6 3.7 %collective-permute-done.10 = f32[1,128,1024]{2,1,0:T(8,128)S(1)} collective-permute-done((f32[1,128,1024]{2,1,0:T(8,128)S(1)}, f32[1,128,1024]{2,1,0:T(8,128)S(1)}, u32[]{:S(2)}, u32[]{:S(2)}) %collective-permute-start.10) | collective-permute-done | bytes 524320 | tf_op jit(solution)/shard_map/ppermute | solution.py:137
  84.4 1.9 %collective-permute-done.12 = f32[1,128,1024]{2,1,0:T(8,128)S(1)} collective-permute-done((f32[1,128,1024]{2,1,0:T(8,128)S(1)}, f32[1,128,1024]{2,1,0:T(8,128)S(1)}, u32[]{:S(2)}, u32[]{:S(2)}) %collective-permute-start.12) | collective-permute-done | bytes 524320 | tf_op jit(solution)/shard_map/ppermute | solution.py:155
  86.3 8.8 %fusion = f32[128,2048]{1,0:T(8,128)S(1)} fusion(f32[4096,2048]{1,0:T(8,128)} %param.10, s32[]{:T(128)S(6)} %select_n.78, f32[128,1024]{1,0:T(8,128)S(1)} %bitcast.114, f32[128,1024]{1,0:T(8,128)S(1)} %bitcast.113, pred[]{:T(512)S(6)} %eq.6), kind=kOutput, calls=%fused_computation | convolution fusion | flops 3222011904 | bytes 18874372 | tf_op jit(solution)/shard_map/dot_general | solution.py:147
  95.1 0.1 add.159
  95.2 0.6 collective-permute-start.13
  95.9 7.8 %collective-permute-done.13 = f32[2,16,2048]{2,1,0:T(8,128)S(1)} collective-permute-done((f32[2,16,2048]{2,1,0:T(8,128)S(1)}, f32[2,16,2048]{2,1,0:T(8,128)S(1)}, u32[]{:S(2)}, u32[]{:S(2)}) %collective-permute-start.13) | collective-permute-done | bytes 262176 | tf_op jit(solution)/shard_map/ppermute | solution.py:37
  103.7 0.6 collective-permute-start.15
  104.4 3.5 %collective-permute-start.14 = (f32[1,16,2048]{2,1,0:T(8,128)S(1)}, f32[1,16,2048]{2,1,0:T(8,128)S(1)}, u32[]{:S(2)}, u32[]{:S(2)}) collective-permute-start(f32[1,16,2048]{2,1,0:T(8,128)S(1)} %get-tuple-element.15), channel_id=1, source_target_pairs={{0,2},{1,3},{2,0},{3,1},{4,6},{5,7},{6,4},{7,5},{8,10},{9,11},{10,... | collective-permute-start | bytes 393224 | tf_op jit(solution)/shard_map/ppermute | solution.py:37
  107.8 4.4 %collective-permute-done.14 = f32[1,16,2048]{2,1,0:T(8,128)S(1)} collective-permute-done((f32[1,16,2048]{2,1,0:T(8,128)S(1)}, f32[1,16,2048]{2,1,0:T(8,128)S(1)}, u32[]{:S(2)}, u32[]{:S(2)}) %collective-permute-start.14) | collective-permute-done | bytes 131104 | tf_op jit(solution)/shard_map/ppermute | solution.py:37
  112.2 1.9 %collective-permute-done.15 = f32[2,16,2048]{2,1,0:T(8,128)S(1)} collective-permute-done((f32[2,16,2048]{2,1,0:T(8,128)S(1)}, f32[2,16,2048]{2,1,0:T(8,128)S(1)}, u32[]{:S(2)}, u32[]{:S(2)}) %collective-permute-start.15) | collective-permute-done | bytes 262176 | tf_op jit(solution)/shard_map/ppermute | solution.py:37
  114.2 1.6 %collective-permute-start.16 = (f32[1,16,2048]{2,1,0:T(8,128)S(1)}, f32[1,16,2048]{2,1,0:T(8,128)S(1)}, u32[]{:S(2)}, u32[]{:S(2)}) collective-permute-start(f32[1,16,2048]{2,1,0:T(8,128)S(1)} %get-tuple-element.14), channel_id=1, source_target_pairs={{0,2},{1,3},{2,0},{3,1},{4,6},{5,7},{6,4},{7,5},{8,10},{9,11},{10,... | collective-permute-start | bytes 393224 | tf_op jit(solution)/shard_map/ppermute | solution.py:37
  115.8 4.8 %collective-permute-done.16 = f32[1,16,2048]{2,1,0:T(8,128)S(1)} collective-permute-done((f32[1,16,2048]{2,1,0:T(8,128)S(1)}, f32[1,16,2048]{2,1,0:T(8,128)S(1)}, u32[]{:S(2)}, u32[]{:S(2)}) %collective-permute-start.16) | collective-permute-done | bytes 131104 | tf_op jit(solution)/shard_map/ppermute | solution.py:37
  120.7 0.1 collective-permute-start.17
  120.8 1.8 %collective-permute-start.18 = (f32[8,2048]{1,0:T(8,128)S(1)}, f32[8,2048]{1,0:T(8,128)S(1)}, u32[]{:S(2)}, u32[]{:S(2)}) collective-permute-start(f32[8,2048]{1,0:T(8,128)S(1)} %get-tuple-element.26), channel_id=1, source_target_pairs={{0,8},{4,12},{8,0},{12,4},{1,9},{5,13},{9,1},{13,5},{2,10},{6,14},... | collective-permute-start | bytes 196616 | tf_op jit(solution)/shard_map/ppermute | solution.py:46
  122.6 0.1 collective-permute-start.19
  122.6 2.6 %collective-permute-done.18 = f32[8,2048]{1,0:T(8,128)S(1)} collective-permute-done((f32[8,2048]{1,0:T(8,128)S(1)}, f32[8,2048]{1,0:T(8,128)S(1)}, u32[]{:S(2)}, u32[]{:S(2)}) %collective-permute-start.18) | collective-permute-done | bytes 65568 | tf_op jit(solution)/shard_map/ppermute | solution.py:46
  125.3 1.3 %collective-permute-done.19 = f32[8,2048]{1,0:T(8,128)S(1)} collective-permute-done((f32[8,2048]{1,0:T(8,128)S(1)}, f32[8,2048]{1,0:T(8,128)S(1)}, u32[]{:S(2)}, u32[]{:S(2)}) %collective-permute-start.19) | collective-permute-done | bytes 65568 | tf_op jit(solution)/shard_map/ppermute | solution.py:46
  126.7 0.8 multiply_add_fusion
  (36 shorter events, 0.6 us)
Async XLA Ops:
  3.8 4.9 %collective-permute-start.2 = (f32[8,2048]{1,0:T(8,128)S(1)}, f32[8,2048]{1,0:T(8,128)S(1)}, u32[]{:S(2)}, u32[]{:S(2)}) collective-permute-start(f32[8,2048]{1,0:T(8,128)S(1)} %get-tuple-element.33), channel_id=1, source_target_pairs={{0,12},{4,8},{8,4},{12,0},{1,13},{5,9},{9,5},{13,1},{2,14},{6,10},... | collective-permute-start | bytes 196616 | tf_op jit(solution)/shard_map/ppermute | solution.py:46
  6.3 2.5 %collective-permute-start = (f32[8,2048]{1,0:T(8,128)S(1)}, f32[8,2048]{1,0:T(8,128)S(1)}, u32[]{:S(2)}, u32[]{:S(2)}) collective-permute-start(f32[8,2048]{1,0:T(8,128)S(1)} %get-tuple-element.35), channel_id=1, source_target_pairs={{0,4},{4,0},{8,12},{12,8},{1,5},{5,1},{9,13},{13,9},{2,6},{6,2},{1... | collective-permute-start | bytes 196616 | tf_op jit(solution)/shard_map/ppermute | solution.py:46
  6.9 4.3 %collective-permute-start.1 = (f32[8,2048]{1,0:T(8,128)S(1)}, f32[8,2048]{1,0:T(8,128)S(1)}, u32[]{:S(2)}, u32[]{:S(2)}) collective-permute-start(f32[8,2048]{1,0:T(8,128)S(1)} %get-tuple-element.34), channel_id=1, source_target_pairs={{0,8},{4,12},{8,0},{12,4},{1,9},{5,13},{9,1},{13,5},{2,10},{6,14},... | collective-permute-start | bytes 196616 | tf_op jit(solution)/shard_map/ppermute | solution.py:46
  11.3 12.2 %collective-permute-start.3 = (f32[1,16,2048]{2,1,0:T(8,128)S(1)}, f32[1,16,2048]{2,1,0:T(8,128)S(1)}, u32[]{:S(2)}, u32[]{:S(2)}) collective-permute-start(f32[1,16,2048]{2,1,0:T(8,128)S(1)} %fusion.43), channel_id=1, source_target_pairs={{0,2},{1,3},{2,0},{3,1},{4,6},{5,7},{6,4},{7,5},{8,10},{9,11},{10,... | collective-permute-start | bytes 393224 | tf_op jit(solution)/shard_map/ppermute | solution.py:24
  14.0 11.3 %collective-permute-start.5 = (f32[1,16,2048]{2,1,0:T(8,128)S(1)}, f32[1,16,2048]{2,1,0:T(8,128)S(1)}, u32[]{:S(2)}, u32[]{:S(2)}) collective-permute-start(f32[1,16,2048]{2,1,0:T(8,128)S(1)} %fusion.42), channel_id=1, source_target_pairs={{0,2},{1,3},{2,0},{3,1},{4,6},{5,7},{6,4},{7,5},{8,10},{9,11},{10,... | collective-permute-start | bytes 393224 | tf_op jit(solution)/shard_map/ppermute | solution.py:24
  23.5 9.3 %collective-permute-start.4 = (f32[2,16,2048]{2,1,0:T(8,128)S(1)}, f32[2,16,2048]{2,1,0:T(8,128)S(1)}, u32[]{:S(2)}, u32[]{:S(2)}) collective-permute-start(f32[2,16,2048]{2,1,0:T(8,128)S(1)} %pad_maximum_fusion.1), channel_id=1, source_target_pairs={{0,1},{1,0},{2,3},{3,2},{4,5},{5,4},{6,7},{7,6},{8,9},{9,8},{10,11... | collective-permute-start | bytes 786440 | tf_op jit(solution)/shard_map/ppermute | solution.py:24
  25.2 11.1 %collective-permute-start.6 = (f32[2,16,2048]{2,1,0:T(8,128)S(1)}, f32[2,16,2048]{2,1,0:T(8,128)S(1)}, u32[]{:S(2)}, u32[]{:S(2)}) collective-permute-start(f32[2,16,2048]{2,1,0:T(8,128)S(1)} %pad_maximum_fusion.2), channel_id=1, source_target_pairs={{0,1},{1,0},{2,3},{3,2},{4,5},{5,4},{6,7},{7,6},{8,9},{9,8},{10,11... | collective-permute-start | bytes 786440 | tf_op jit(solution)/shard_map/ppermute | solution.py:24
  45.4 2.0 %collective-permute-start.7 = (f32[128,1024]{1,0:T(8,128)S(1)}, f32[128,1024]{1,0:T(8,128)S(1)}, u32[]{:S(2)}, u32[]{:S(2)}) collective-permute-start(f32[128,1024]{1,0:T(8,128)S(1)} %constant_dynamic-slice_fusion.5), channel_id=1, source_target_pairs={{0,4},{4,0},{8,12},{12,8},{1,5},{5,1},{9,13},{13,9},{2,6},{6,2},{1... | collective-permute-start | bytes 1572872 | tf_op jit(solution)/shard_map/ppermute | solution.py:122
  47.4 79.3 %copy-start = (f32[8,8192]{1,0:T(8,128)S(1)}, f32[8,8192]{1,0:T(8,128)}, u32[]{:S(2)}) copy-start(f32[8,8192]{1,0:T(8,128)} %x_ref.1) | copy-start | bytes 786436
  47.4 79.3 %copy-start.1 = (f32[8192]{0:T(1024)S(1)}, f32[8192]{0:T(1024)}, u32[]{:S(2)}) copy-start(f32[8192]{0:T(1024)} %param.11) | copy-start | bytes 98308
  53.4 9.3 %collective-permute-start.8 = (f32[128,1024]{1,0:T(8,128)S(1)}, f32[128,1024]{1,0:T(8,128)S(1)}, u32[]{:S(2)}, u32[]{:S(2)}) collective-permute-start(f32[128,1024]{1,0:T(8,128)S(1)} %fusion.6), channel_id=1, source_target_pairs={{0,4},{4,0},{8,12},{12,8},{1,5},{5,1},{9,13},{13,9},{2,6},{6,2},{1... | collective-permute-start | bytes 1572872 | tf_op jit(solution)/shard_map/ppermute | solution.py:122
  53.6 15.0 %collective-permute-start.9 = (f32[1,128,1024]{2,1,0:T(8,128)S(1)}, f32[1,128,1024]{2,1,0:T(8,128)}, u32[]{:S(2)}, u32[]{:S(2)}) collective-permute-start(f32[1,128,1024]{2,1,0:T(8,128)S(1)} %bitcast.115), channel_id=1, source_target_pairs={{0,8},{4,12},{8,0},{12,4},{1,9},{5,13},{9,1},{13,5},{2,10},{6,14},... | collective-permute-start | bytes 1572872 | tf_op jit(solution)/shard_map/ppermute | solution.py:128
  69.9 2.0 %collective-permute-start.11 = (f32[128,1024]{1,0:T(8,128)S(1)}, f32[128,1024]{1,0:T(8,128)S(1)}, u32[]{:S(2)}, u32[]{:S(2)}) collective-permute-start(f32[128,1024]{1,0:T(8,128)S(1)} %fusion.26), channel_id=1, source_target_pairs={{0,4},{4,0},{8,12},{12,8},{1,5},{5,1},{9,13},{13,9},{2,6},{6,2},{1... | collective-permute-start | bytes 1572872 | tf_op jit(solution)/shard_map/ppermute | solution.py:133
  70.0 14.3 %collective-permute-start.10 = (f32[1,128,1024]{2,1,0:T(8,128)S(1)}, f32[1,128,1024]{2,1,0:T(8,128)S(1)}, u32[]{:S(2)}, u32[]{:S(2)}) collective-permute-start(f32[1,128,1024]{2,1,0:T(8,128)S(1)} %bitcast.110), channel_id=1, source_target_pairs={{0,8},{4,12},{8,0},{12,4},{1,9},{5,13},{9,1},{13,5},{2,10},{6,14},... | collective-permute-start | bytes 1572872 | tf_op jit(solution)/shard_map/ppermute | solution.py:137
  84.3 1.9 %collective-permute-start.12 = (f32[1,128,1024]{2,1,0:T(8,128)S(1)}, f32[1,128,1024]{2,1,0:T(8,128)S(1)}, u32[]{:S(2)}, u32[]{:S(2)}) collective-permute-start(f32[1,128,1024]{2,1,0:T(8,128)S(1)} %collective-permute-done.10), channel_id=1, source_target_pairs={{0,4},{4,0},{8,12},{12,8},{1,5},{5,1},{9,13},{13,9},{2,6},{6,2},{1... | collective-permute-start | bytes 1572872 | tf_op jit(solution)/shard_map/ppermute | solution.py:155
  95.2 8.4 %collective-permute-start.13 = (f32[2,16,2048]{2,1,0:T(8,128)S(1)}, f32[2,16,2048]{2,1,0:T(8,128)S(1)}, u32[]{:S(2)}, u32[]{:S(2)}) collective-permute-start(f32[2,16,2048]{2,1,0:T(8,128)S(1)} %pad_maximum_fusion.3), channel_id=1, source_target_pairs={{0,1},{1,0},{2,3},{3,2},{4,5},{5,4},{6,7},{7,6},{8,9},{9,8},{10,11... | collective-permute-start | bytes 786440 | tf_op jit(solution)/shard_map/ppermute | solution.py:37
  103.7 10.4 %collective-permute-start.15 = (f32[2,16,2048]{2,1,0:T(8,128)S(1)}, f32[2,16,2048]{2,1,0:T(8,128)S(1)}, u32[]{:S(2)}, u32[]{:S(2)}) collective-permute-start(f32[2,16,2048]{2,1,0:T(8,128)S(1)} %pad_maximum_fusion.4), channel_id=1, source_target_pairs={{0,1},{1,0},{2,3},{3,2},{4,5},{5,4},{6,7},{7,6},{8,9},{9,8},{10,11... | collective-permute-start | bytes 786440 | tf_op jit(solution)/shard_map/ppermute | solution.py:37
  104.4 7.8 %collective-permute-start.14 = (f32[1,16,2048]{2,1,0:T(8,128)S(1)}, f32[1,16,2048]{2,1,0:T(8,128)S(1)}, u32[]{:S(2)}, u32[]{:S(2)}) collective-permute-start(f32[1,16,2048]{2,1,0:T(8,128)S(1)} %get-tuple-element.15), channel_id=1, source_target_pairs={{0,2},{1,3},{2,0},{3,1},{4,6},{5,7},{6,4},{7,5},{8,10},{9,11},{10,... | collective-permute-start | bytes 393224 | tf_op jit(solution)/shard_map/ppermute | solution.py:37
  114.2 6.4 %collective-permute-start.16 = (f32[1,16,2048]{2,1,0:T(8,128)S(1)}, f32[1,16,2048]{2,1,0:T(8,128)S(1)}, u32[]{:S(2)}, u32[]{:S(2)}) collective-permute-start(f32[1,16,2048]{2,1,0:T(8,128)S(1)} %get-tuple-element.14), channel_id=1, source_target_pairs={{0,2},{1,3},{2,0},{3,1},{4,6},{5,7},{6,4},{7,5},{8,10},{9,11},{10,... | collective-permute-start | bytes 393224 | tf_op jit(solution)/shard_map/ppermute | solution.py:37
  120.7 2.0 %collective-permute-start.17 = (f32[8,2048]{1,0:T(8,128)S(1)}, f32[8,2048]{1,0:T(8,128)S(1)}, u32[]{:S(2)}, u32[]{:S(2)}) collective-permute-start(f32[8,2048]{1,0:T(8,128)S(1)} %get-tuple-element.27), channel_id=1, source_target_pairs={{0,4},{4,0},{8,12},{12,8},{1,5},{5,1},{9,13},{13,9},{2,6},{6,2},{1... | collective-permute-start | bytes 196616 | tf_op jit(solution)/shard_map/ppermute | solution.py:46
  120.8 4.5 %collective-permute-start.18 = (f32[8,2048]{1,0:T(8,128)S(1)}, f32[8,2048]{1,0:T(8,128)S(1)}, u32[]{:S(2)}, u32[]{:S(2)}) collective-permute-start(f32[8,2048]{1,0:T(8,128)S(1)} %get-tuple-element.26), channel_id=1, source_target_pairs={{0,8},{4,12},{8,0},{12,4},{1,9},{5,13},{9,1},{13,5},{2,10},{6,14},... | collective-permute-start | bytes 196616 | tf_op jit(solution)/shard_map/ppermute | solution.py:46
  122.6 4.0 %collective-permute-start.19 = (f32[8,2048]{1,0:T(8,128)S(1)}, f32[8,2048]{1,0:T(8,128)S(1)}, u32[]{:S(2)}, u32[]{:S(2)}) collective-permute-start(f32[8,2048]{1,0:T(8,128)S(1)} %get-tuple-element.25), channel_id=1, source_target_pairs={{0,12},{4,8},{8,4},{12,0},{1,13},{5,9},{9,5},{13,1},{2,14},{6,10},... | collective-permute-start | bytes 196616 | tf_op jit(solution)/shard_map/ppermute | solution.py:46

commit v14 on v13

--- a/solution.py
+++ b/solution.py
@@ -48,24 +48,25 @@
     return jnp.stack([rel[s ^ idx] for s in range(n)])
 
 
-def _norm_kernel(x_ref, o_ref):
+def _norm_kernel(x_ref, shift_ref, scale_ref, o_ref):
     x = x_ref[...]
     average = jnp.mean(x, axis=1, keepdims=True)
     centred = x - average
     spread_sq = jnp.mean(centred * centred, axis=1, keepdims=True)
-    o_ref[...] = centred * lax.rsqrt(spread_sq + layer_eps)
+    normed = centred * lax.rsqrt(spread_sq + layer_eps)
+    o_ref[...] = normed * (1.0 + scale_ref[...]) + shift_ref[...]
 
 
-def _normalize(tokens):
+def _normalize(tokens, shift, scale):
     rows, width = tokens.shape
     return pl.pallas_call(
         _norm_kernel,
         out_shape=jax.ShapeDtypeStruct(tokens.shape, jnp.float32),
-        in_specs=[pl.BlockSpec(memory_space=pltpu.VMEM)],
+        in_specs=[pl.BlockSpec(memory_space=pltpu.VMEM)] * 3,
         out_specs=pl.BlockSpec(memory_space=pltpu.VMEM),
         cost_estimate=pl.CostEstimate(flops=6 * rows * width, transcendentals=rows,
                                       bytes_accessed=8 * rows * width),
-    )(tokens)
+    )(tokens, shift, scale)
 
 
 def local(tokens, modulation, up_weight, up_bias, down_weight, down_bias):
@@ -74,11 +75,10 @@
     first_tok = (lax.axis_index("row") * lax.axis_size("col") + lax.axis_index("col")) * tok_dev
     sample = first_tok // SEQ
     own_mods = lax.dynamic_slice_in_dim(modulation, sample, 1, 1)[:, 0]
-    shift_vec = own_mods[0]
-    scale_vec = own_mods[1]
     gate_vec = own_mods[2]
-    normed = _normalize(tokens)
-    mixed = normed * (1.0 + scale_vec) + shift_vec
+    shift_row = lax.dynamic_slice_in_dim(modulation[0], sample, 1, 0)
+    scale_row = lax.dynamic_slice_in_dim(modulation[1], sample, 1, 0)
+    mixed = _normalize(tokens, shift_row, scale_row)
     r = lax.axis_index("row")
     d_blk = mixed.shape[1] // n_row
     sent_in = mixed.reshape(tok_dev, n_row, d_blk).swapaxes(0, 1)
@@ -119,6 +119,9 @@
         else:
             other = lax.optimization_barrier(up_block(1, lhs))
             mine = lax.optimization_barrier(up_block(0, lhs))
+        if not d_even:
+            bias_q = lax.dynamic_slice_in_dim(up_bias, r * quarter, quarter)
+            mine = lax.optimization_barrier(mine + bias_q[None, :])
         held[d_even] = mine + lax.ppermute(other, "row", _pairs(n_row, 1))
         if i == 0:
             lhs, held[d_even] = lax.optimization_barrier((lhs, held[d_even]))
@@ -128,8 +131,7 @@
         got = lax.ppermute(jnp.stack([held[d] for d in sent]), "row", _pairs(n_row, flip))
         held = {d ^ flip: held[d ^ flip] + got[i] for i, d in enumerate(sent)}
         flip *= 2
-    bias_q = lax.dynamic_slice_in_dim(up_bias, r * quarter, quarter)
-    acts = {0: jax.nn.gelu(held[0] + bias_q[None, :], approximate=True)}
+    acts = {0: jax.nn.gelu(held[0], approximate=True)}
     acts[1] = lax.ppermute(acts[0], "row", _pairs(n_row, 1))
     flip = 2
     while flip < n_row:

time: 128 us -> 128 us (level)
  local copies, waits for them, and re-layouts: 0.96 us -> 3.29 us
  other arithmetic: 4.34 us -> 2.55 us
    slice x0 -> x1, local copies, waits for them, and re-layouts: none -> 1.41 us  [local(): gate_vec = own_mods[2]]
where the time goes in v14:
time: 128 us
  waiting for transfers between devices  61.6 us (48%)
  matrix products  38.3 us (30%)
  starting transfers between devices  19.9 us (16%)
  local copies, waits for them, and re-layouts  3.29 us (3%)
  other arithmetic  2.55 us (2%)
  Pallas kernels  2.02 us (2%)
    ppermute x4, waiting for transfers between devices, _gather_rel(): lax.ppermute(jnp.stack([held[k] for k in keys]), axis, _pairs(n, flip))  21.1 us
    ppermute x4, waiting for transfers between devices, _scatter_rel(): lax.ppermute(jnp.stack([held[d] for d in sent]), axis, _pairs(n, flip))  18.8 us
    dot_general x2, matrix products, down_pair(): jnp.dot(pair, w, precision=lax.Precision.HIGH, preferred_element_type=jnp...  17.5 us
    dot_general x2, matrix products, up_block(): jnp.dot(lhs, w, precision=lax.Precision.HIGH, preferred_element_type=jnp....  11.9 us
    dot_general x1, matrix products, up_pair(): jnp.dot(lhs, w, precision=lax.Precision.HIGH, preferred_element_type=jnp....  8.88 us
    ppermute x6, waiting for transfers between devices, _exchange_abs(): got.append(lax.ppermute(blocks[idx ^ d], axis, _pairs(n, d)))  8.2 us
    ppermute x4, starting transfers between devices, _scatter_rel(): lax.ppermute(jnp.stack([held[d] for d in sent]), axis, _pairs(n, flip))  6.4 us
    ppermute x1, waiting for transfers between devices, local(): lax.ppermute(jnp.stack([held[d] for d in sent]), 'row', _pairs(n_row, flip))  5.85 us
  transfers between devices with their start and end apart: 20, of which 17 were waited for; matrix products, arithmetic and copies ran while one was open for 12% of the time, Pallas kernels for 0%

profile of v14, /device:TPU:0, one launch (start us, length us, event | category | flops | bytes accessed | tf_op | source)
XLA Modules:
  0.0 128.0 jit_solution(3859994895519309983)
XLA Ops:
  0.0 1.4 %fusion.50 = (f32[1,1,8192]{2,1,0:T(1,128)S(1)}, f32[1,8192]{1,0:T(1,128)}, f32[1,8192]{1,0:T(1,128)}) fusion(f32[3,1,8192]{2,1,0:T(1,128)} %param.7), kind=kLoop, calls=%fused_computation.102 | loop fusion | bytes 196608 | tf_op jit(solution)/shard_map/slice | solution.py:78
  1.4 2.0 %shard_map.64 = f32[8,8192]{1,0:T(8,128)} custom-call(f32[8,8192]{1,0:T(8,128)} %x_ref.1, f32[1,8192]{1,0:T(1,128)} %get-tuple-element.38.shift_ref, f32[1,8192]{1,0:T(1,128)} %get-tuple-element.37.scale_ref), custom_call_target="tpu_custom_call" | custom-call | flops 393216 | bytes 524288 | tf_op jit(solution)/shard_map/pallas_call | solution.py:62
  3.4 1.0 dynamic-slice_bitcast_fusion.6
  4.4 2.4 %collective-permute-start.2 = (f32[8,2048]{1,0:T(8,128)S(1)}, f32[8,2048]{1,0:T(8,128)S(1)}, u32[]{:S(2)}, u32[]{:S(2)}) collective-permute-start(f32[8,2048]{1,0:T(8,128)S(1)} %get-tuple-element.33), channel_id=1, source_target_pairs={{0,12},{4,8},{8,4},{12,0},{1,13},{5,9},{9,5},{13,1},{2,14},{6,10},... | collective-permute-start | bytes 196616 | tf_op jit(solution)/shard_map/ppermute | solution.py:46
  6.8 0.7 collective-permute-start
  7.5 1.8 %collective-permute-done.2 = f32[8,2048]{1,0:T(8,128)S(1)} collective-permute-done((f32[8,2048]{1,0:T(8,128)S(1)}, f32[8,2048]{1,0:T(8,128)S(1)}, u32[]{:S(2)}, u32[]{:S(2)}) %collective-permute-start.2) | collective-permute-done | bytes 65568 | tf_op jit(solution)/shard_map/ppermute | solution.py:46
  9.3 2.5 %collective-permute-done.1 = f32[8,2048]{1,0:T(8,128)S(1)} collective-permute-done((f32[8,2048]{1,0:T(8,128)S(1)}, f32[8,2048]{1,0:T(8,128)S(1)}, u32[]{:S(2)}, u32[]{:S(2)}) %collective-permute-start.1) | collective-permute-done | bytes 65568 | tf_op jit(solution)/shard_map/ppermute | solution.py:46
  11.8 2.7 %collective-permute-start.3 = (f32[1,16,2048]{2,1,0:T(8,128)S(1)}, f32[1,16,2048]{2,1,0:T(8,128)S(1)}, u32[]{:S(2)}, u32[]{:S(2)}) collective-permute-start(f32[1,16,2048]{2,1,0:T(8,128)S(1)} %fusion.42), channel_id=1, source_target_pairs={{0,2},{1,3},{2,0},{3,1},{4,6},{5,7},{6,4},{7,5},{8,10},{9,11},{10,... | collective-permute-start | bytes 393224 | tf_op jit(solution)/shard_map/ppermute | solution.py:24
  14.5 0.4 collective-permute-start.5
  14.9 9.1 %collective-permute-done.3 = f32[1,16,2048]{2,1,0:T(8,128)S(1)} collective-permute-done((f32[1,16,2048]{2,1,0:T(8,128)S(1)}, f32[1,16,2048]{2,1,0:T(8,128)S(1)}, u32[]{:S(2)}, u32[]{:S(2)}) %collective-permute-start.3) | collective-permute-done | bytes 131104 | tf_op jit(solution)/shard_map/ppermute | solution.py:24
  24.1 0.1 collective-permute-start.4
  24.2 1.6 %collective-permute-done.5 = f32[1,16,2048]{2,1,0:T(8,128)S(1)} collective-permute-done((f32[1,16,2048]{2,1,0:T(8,128)S(1)}, f32[1,16,2048]{2,1,0:T(8,128)S(1)}, u32[]{:S(2)}, u32[]{:S(2)}) %collective-permute-start.5) | collective-permute-done | bytes 131104 | tf_op jit(solution)/shard_map/ppermute | solution.py:24
  25.8 0.6 collective-permute-start.6
  26.4 6.9 %collective-permute-done.4 = f32[2,16,2048]{2,1,0:T(8,128)S(1)} collective-permute-done((f32[2,16,2048]{2,1,0:T(8,128)S(1)}, f32[2,16,2048]{2,1,0:T(8,128)S(1)}, u32[]{:S(2)}, u32[]{:S(2)}) %collective-permute-start.4) | collective-permute-done | bytes 262176 | tf_op jit(solution)/shard_map/ppermute | solution.py:24
  33.5 3.5 %collective-permute-done.6 = f32[2,16,2048]{2,1,0:T(8,128)S(1)} collective-permute-done((f32[2,16,2048]{2,1,0:T(8,128)S(1)}, f32[2,16,2048]{2,1,0:T(8,128)S(1)}, u32[]{:S(2)}, u32[]{:S(2)}) %collective-permute-start.6) | collective-permute-done | bytes 262176 | tf_op jit(solution)/shard_map/ppermute | solution.py:24
  37.0 8.9 %fusion.4 = f32[128,2048]{1,0:T(8,128)S(1)} fusion(f32[128,2048]{1,0:T(8,128)S(1)} %fusion.37, f32[2048,4096]{1,0:T(8,128)} %param.8, s32[]{:T(128)S(6)} %select_n.80), kind=kOutput, calls=%fused_computation.4 | convolution fusion | flops 3221225472 | bytes 18874372 | tf_op jit(solution)/shard_map/dot_general | solution.py:108
  45.9 0.1 collective-permute-start.7
  46.0 1.9 %collective-permute-done.7 = f32[128,1024]{1,0:T(8,128)S(1)} collective-permute-done((f32[128,1024]{1,0:T(8,128)S(1)}, f32[128,1024]{1,0:T(8,128)S(1)}, u32[]{:S(2)}, u32[]{:S(2)}) %collective-permute-start.7) | collective-permute-done | bytes 524320 | tf_op jit(solution)/shard_map/ppermute | solution.py:125
  47.9 0.1 dynamic-slice_add_fusion
  48.0 6.0 %fusion.6 = f32[128,1024]{1,0:T(8,128)S(1)} fusion(f32[128,2048]{1,0:T(8,128)S(1)} %fusion.37, f32[2048,4096]{1,0:T(8,128)} %param.8, s32[]{:T(128)S(6)} %select_n.85), kind=kOutput, calls=%fused_computation.6 | convolution fusion | flops 1610612736 | bytes 9961476 | tf_op jit(solution)/shard_map/dot_general | solution.py:97
  54.0 0.2 collective-permute-start.8
  54.2 2.5 %collective-permute-start.9 = (f32[1,128,1024]{2,1,0:T(8,128)S(1)}, f32[1,128,1024]{2,1,0:T(8,128)}, u32[]{:S(2)}, u32[]{:S(2)}) collective-permute-start(f32[1,128,1024]{2,1,0:T(8,128)S(1)} %bitcast.115), channel_id=1, source_target_pairs={{0,8},{4,12},{8,0},{12,4},{1,9},{5,13},{9,1},{13,5},{2,10},{6,14},... | collective-permute-start | bytes 1572872 | tf_op jit(solution)/shard_map/ppermute | solution.py:131
  56.7 0.7 dynamic_slice.78
  57.4 5.9 %fusion.8 = f32[128,1024]{1,0:T(8,128)S(1)} fusion(f32[128,2048]{1,0:T(8,128)S(1)} %fusion.37, f32[2048,4096]{1,0:T(8,128)} %param.8, s32[]{:T(128)S(6)} %select_n.84), kind=kOutput, calls=%fused_computation.8 | convolution fusion | flops 1610612736 | bytes 9961476 | tf_op jit(solution)/shard_map/dot_general | solution.py:97
  63.4 5.9 %collective-permute-done.9 = f32[1,128,1024]{2,1,0:T(8,128)} collective-permute-done((f32[1,128,1024]{2,1,0:T(8,128)S(1)}, f32[1,128,1024]{2,1,0:T(8,128)}, u32[]{:S(2)}, u32[]{:S(2)}) %collective-permute-start.9) | collective-permute-done | bytes 524320 | tf_op jit(solution)/shard_map/ppermute | solution.py:131
  69.2 1.2 fusion.26
  70.5 0.1 collective-permute-start.11
  70.6 1.8 %collective-permute-start.10 = (f32[1,128,1024]{2,1,0:T(8,128)S(1)}, f32[1,128,1024]{2,1,0:T(8,128)S(1)}, u32[]{:S(2)}, u32[]{:S(2)}) collective-permute-start(f32[1,128,1024]{2,1,0:T(8,128)S(1)} %bitcast.110), channel_id=1, source_target_pairs={{0,8},{4,12},{8,0},{12,4},{1,9},{5,13},{9,1},{13,5},{2,10},{6,14},... | collective-permute-start | bytes 1572872 | tf_op jit(solution)/shard_map/ppermute | solution.py:139
  72.4 0.1 collective-permute-done.11
  72.4 8.7 %fusion.2 = f32[128,2048]{1,0:T(8,128)S(1)} fusion(f32[4096,2048]{1,0:T(8,128)} %param.10, s32[]{:T(128)S(6)} %select_n.89, f32[128,1024]{1,0:T(8,128)S(1)} %collective-permute-done.11, f32[128,1024]{1,0:T(8,128)S(1)} %fusion.26, pred[]{:T(512)S(6)} %eq.6), kind=kOutput, calls=%fused_computation.2 | convolution fusion | flops 3222011904 | bytes 18874372 | tf_op jit(solution)/shard_map/dot_general | solution.py:149
  81.2 3.7 %collective-permute-done.10 = f32[1,128,1024]{2,1,0:T(8,128)S(1)} collective-permute-done((f32[1,128,1024]{2,1,0:T(8,128)S(1)}, f32[1,128,1024]{2,1,0:T(8,128)S(1)}, u32[]{:S(2)}, u32[]{:S(2)}) %collective-permute-start.10) | collective-permute-done | bytes 524320 | tf_op jit(solution)/shard_map/ppermute | solution.py:139
  84.9 1.9 %collective-permute-done.12 = f32[1,128,1024]{2,1,0:T(8,128)S(1)} collective-permute-done((f32[1,128,1024]{2,1,0:T(8,128)S(1)}, f32[1,128,1024]{2,1,0:T(8,128)S(1)}, u32[]{:S(2)}, u32[]{:S(2)}) %collective-permute-start.12) | collective-permute-done | bytes 524320 | tf_op jit(solution)/shard_map/ppermute | solution.py:157
  86.8 8.8 %fusion = f32[128,2048]{1,0:T(8,128)S(1)} fusion(f32[4096,2048]{1,0:T(8,128)} %param.10, s32[]{:T(128)S(6)} %select_n.80, f32[128,1024]{1,0:T(8,128)S(1)} %bitcast.114, f32[128,1024]{1,0:T(8,128)S(1)} %bitcast.113, pred[]{:T(512)S(6)} %eq.6), kind=kOutput, calls=%fused_computation | convolution fusion | flops 3222011904 | bytes 18874372 | tf_op jit(solution)/shard_map/dot_general | solution.py:149
  95.6 0.1 add.132
  95.8 0.6 collective-permute-start.13
  96.4 7.8 %collective-permute-done.13 = f32[2,16,2048]{2,1,0:T(8,128)S(1)} collective-permute-done((f32[2,16,2048]{2,1,0:T(8,128)S(1)}, f32[2,16,2048]{2,1,0:T(8,128)S(1)}, u32[]{:S(2)}, u32[]{:S(2)}) %collective-permute-start.13) | collective-permute-done | bytes 262176 | tf_op jit(solution)/shard_map/ppermute | solution.py:37
  104.3 0.6 collective-permute-start.15
  104.9 3.5 %collective-permute-start.14 = (f32[1,16,2048]{2,1,0:T(8,128)S(1)}, f32[1,16,2048]{2,1,0:T(8,128)S(1)}, u32[]{:S(2)}, u32[]{:S(2)}) collective-permute-start(f32[1,16,2048]{2,1,0:T(8,128)S(1)} %get-tuple-element.15), channel_id=1, source_target_pairs={{0,2},{1,3},{2,0},{3,1},{4,6},{5,7},{6,4},{7,5},{8,10},{9,11},{10,... | collective-permute-start | bytes 393224 | tf_op jit(solution)/shard_map/ppermute | solution.py:37
  108.4 4.4 %collective-permute-done.14 = f32[1,16,2048]{2,1,0:T(8,128)S(1)} collective-permute-done((f32[1,16,2048]{2,1,0:T(8,128)S(1)}, f32[1,16,2048]{2,1,0:T(8,128)S(1)}, u32[]{:S(2)}, u32[]{:S(2)}) %collective-permute-start.14) | collective-permute-done | bytes 131104 | tf_op jit(solution)/shard_map/ppermute | solution.py:37
  112.8 1.9 %collective-permute-done.15 = f32[2,16,2048]{2,1,0:T(8,128)S(1)} collective-permute-done((f32[2,16,2048]{2,1,0:T(8,128)S(1)}, f32[2,16,2048]{2,1,0:T(8,128)S(1)}, u32[]{:S(2)}, u32[]{:S(2)}) %collective-permute-start.15) | collective-permute-done | bytes 262176 | tf_op jit(solution)/shard_map/ppermute | solution.py:37
  114.7 1.6 %collective-permute-start.16 = (f32[1,16,2048]{2,1,0:T(8,128)S(1)}, f32[1,16,2048]{2,1,0:T(8,128)S(1)}, u32[]{:S(2)}, u32[]{:S(2)}) collective-permute-start(f32[1,16,2048]{2,1,0:T(8,128)S(1)} %get-tuple-element.14), channel_id=1, source_target_pairs={{0,2},{1,3},{2,0},{3,1},{4,6},{5,7},{6,4},{7,5},{8,10},{9,11},{10,... | collective-permute-start | bytes 393224 | tf_op jit(solution)/shard_map/ppermute | solution.py:37
  116.3 4.8 %collective-permute-done.16 = f32[1,16,2048]{2,1,0:T(8,128)S(1)} collective-permute-done((f32[1,16,2048]{2,1,0:T(8,128)S(1)}, f32[1,16,2048]{2,1,0:T(8,128)S(1)}, u32[]{:S(2)}, u32[]{:S(2)}) %collective-permute-start.16) | collective-permute-done | bytes 131104 | tf_op jit(solution)/shard_map/ppermute | solution.py:37
  121.2 0.1 collective-permute-start.17
  121.3 1.8 %collective-permute-start.18 = (f32[8,2048]{1,0:T(8,128)S(1)}, f32[8,2048]{1,0:T(8,128)S(1)}, u32[]{:S(2)}, u32[]{:S(2)}) collective-permute-start(f32[8,2048]{1,0:T(8,128)S(1)} %get-tuple-element.26), channel_id=1, source_target_pairs={{0,8},{4,12},{8,0},{12,4},{1,9},{5,13},{9,1},{13,5},{2,10},{6,14},... | collective-permute-start | bytes 196616 | tf_op jit(solution)/shard_map/ppermute | solution.py:46
  123.1 0.1 collective-permute-start.19
  123.2 2.6 %collective-permute-done.18 = f32[8,2048]{1,0:T(8,128)S(1)} collective-permute-done((f32[8,2048]{1,0:T(8,128)S(1)}, f32[8,2048]{1,0:T(8,128)S(1)}, u32[]{:S(2)}, u32[]{:S(2)}) %collective-permute-start.18) | collective-permute-done | bytes 65568 | tf_op jit(solution)/shard_map/ppermute | solution.py:46
  125.8 1.3 %collective-permute-done.19 = f32[8,2048]{1,0:T(8,128)S(1)} collective-permute-done((f32[8,2048]{1,0:T(8,128)S(1)}, f32[8,2048]{1,0:T(8,128)S(1)}, u32[]{:S(2)}, u32[]{:S(2)}) %collective-permute-start.19) | collective-permute-done | bytes 65568 | tf_op jit(solution)/shard_map/ppermute | solution.py:46
  127.3 0.8 multiply_add_fusion
  (36 shorter events, 0.6 us)
Async XLA Ops:
  4.4 4.9 %collective-permute-start.2 = (f32[8,2048]{1,0:T(8,128)S(1)}, f32[8,2048]{1,0:T(8,128)S(1)}, u32[]{:S(2)}, u32[]{:S(2)}) collective-permute-start(f32[8,2048]{1,0:T(8,128)S(1)} %get-tuple-element.33), channel_id=1, source_target_pairs={{0,12},{4,8},{8,4},{12,0},{1,13},{5,9},{9,5},{13,1},{2,14},{6,10},... | collective-permute-start | bytes 196616 | tf_op jit(solution)/shard_map/ppermute | solution.py:46
  6.8 2.5 %collective-permute-start = (f32[8,2048]{1,0:T(8,128)S(1)}, f32[8,2048]{1,0:T(8,128)S(1)}, u32[]{:S(2)}, u32[]{:S(2)}) collective-permute-start(f32[8,2048]{1,0:T(8,128)S(1)} %get-tuple-element.35), channel_id=1, source_target_pairs={{0,4},{4,0},{8,12},{12,8},{1,5},{5,1},{9,13},{13,9},{2,6},{6,2},{1... | collective-permute-start | bytes 196616 | tf_op jit(solution)/shard_map/ppermute | solution.py:46
  7.5 4.3 %collective-permute-start.1 = (f32[8,2048]{1,0:T(8,128)S(1)}, f32[8,2048]{1,0:T(8,128)S(1)}, u32[]{:S(2)}, u32[]{:S(2)}) collective-permute-start(f32[8,2048]{1,0:T(8,128)S(1)} %get-tuple-element.34), channel_id=1, source_target_pairs={{0,8},{4,12},{8,0},{12,4},{1,9},{5,13},{9,1},{13,5},{2,10},{6,14},... | collective-permute-start | bytes 196616 | tf_op jit(solution)/shard_map/ppermute | solution.py:46
  11.8 12.2 %collective-permute-start.3 = (f32[1,16,2048]{2,1,0:T(8,128)S(1)}, f32[1,16,2048]{2,1,0:T(8,128)S(1)}, u32[]{:S(2)}, u32[]{:S(2)}) collective-permute-start(f32[1,16,2048]{2,1,0:T(8,128)S(1)} %fusion.42), channel_id=1, source_target_pairs={{0,2},{1,3},{2,0},{3,1},{4,6},{5,7},{6,4},{7,5},{8,10},{9,11},{10,... | collective-permute-start | bytes 393224 | tf_op jit(solution)/shard_map/ppermute | solution.py:24
  14.5 11.3 %collective-permute-start.5 = (f32[1,16,2048]{2,1,0:T(8,128)S(1)}, f32[1,16,2048]{2,1,0:T(8,128)S(1)}, u32[]{:S(2)}, u32[]{:S(2)}) collective-permute-start(f32[1,16,2048]{2,1,0:T(8,128)S(1)} %fusion.41), channel_id=1, source_target_pairs={{0,2},{1,3},{2,0},{3,1},{4,6},{5,7},{6,4},{7,5},{8,10},{9,11},{10,... | collective-permute-start | bytes 393224 | tf_op jit(solution)/shard_map/ppermute | solution.py:24
  24.1 9.3 %collective-permute-start.4 = (f32[2,16,2048]{2,1,0:T(8,128)S(1)}, f32[2,16,2048]{2,1,0:T(8,128)S(1)}, u32[]{:S(2)}, u32[]{:S(2)}) collective-permute-start(f32[2,16,2048]{2,1,0:T(8,128)S(1)} %pad_maximum_fusion.1), channel_id=1, source_target_pairs={{0,1},{1,0},{2,3},{3,2},{4,5},{5,4},{6,7},{7,6},{8,9},{9,8},{10,11... | collective-permute-start | bytes 786440 | tf_op jit(solution)/shard_map/ppermute | solution.py:24
  25.8 11.1 %collective-permute-start.6 = (f32[2,16,2048]{2,1,0:T(8,128)S(1)}, f32[2,16,2048]{2,1,0:T(8,128)S(1)}, u32[]{:S(2)}, u32[]{:S(2)}) collective-permute-start(f32[2,16,2048]{2,1,0:T(8,128)S(1)} %pad_maximum_fusion.2), channel_id=1, source_target_pairs={{0,1},{1,0},{2,3},{3,2},{4,5},{5,4},{6,7},{7,6},{8,9},{9,8},{10,11... | collective-permute-start | bytes 786440 | tf_op jit(solution)/shard_map/ppermute | solution.py:24
  45.9 2.0 %collective-permute-start.7 = (f32[128,1024]{1,0:T(8,128)S(1)}, f32[128,1024]{1,0:T(8,128)S(1)}, u32[]{:S(2)}, u32[]{:S(2)}) collective-permute-start(f32[128,1024]{1,0:T(8,128)S(1)} %constant_dynamic-slice_fusion.5), channel_id=1, source_target_pairs={{0,4},{4,0},{8,12},{12,8},{1,5},{5,1},{9,13},{13,9},{2,6},{6,2},{1... | collective-permute-start | bytes 1572872 | tf_op jit(solution)/shard_map/ppermute | solution.py:125
  48.0 79.3 %copy-start = (f32[8,8192]{1,0:T(8,128)S(1)}, f32[8,8192]{1,0:T(8,128)}, u32[]{:S(2)}) copy-start(f32[8,8192]{1,0:T(8,128)} %x_ref.1) | copy-start | bytes 786436
  48.0 79.3 %copy-start.1 = (f32[8192]{0:T(1024)S(1)}, f32[8192]{0:T(1024)}, u32[]{:S(2)}) copy-start(f32[8192]{0:T(1024)} %param.11) | copy-start | bytes 98308
  54.0 9.4 %collective-permute-start.8 = (f32[128,1024]{1,0:T(8,128)S(1)}, f32[128,1024]{1,0:T(8,128)S(1)}, u32[]{:S(2)}, u32[]{:S(2)}) collective-permute-start(f32[128,1024]{1,0:T(8,128)S(1)} %fusion.6), channel_id=1, source_target_pairs={{0,4},{4,0},{8,12},{12,8},{1,5},{5,1},{9,13},{13,9},{2,6},{6,2},{1... | collective-permute-start | bytes 1572872 | tf_op jit(solution)/shard_map/ppermute | solution.py:125
  54.2 15.0 %collective-permute-start.9 = (f32[1,128,1024]{2,1,0:T(8,128)S(1)}, f32[1,128,1024]{2,1,0:T(8,128)}, u32[]{:S(2)}, u32[]{:S(2)}) collective-permute-start(f32[1,128,1024]{2,1,0:T(8,128)S(1)} %bitcast.115), channel_id=1, source_target_pairs={{0,8},{4,12},{8,0},{12,4},{1,9},{5,13},{9,1},{13,5},{2,10},{6,14},... | collective-permute-start | bytes 1572872 | tf_op jit(solution)/shard_map/ppermute | solution.py:131
  70.5 2.0 %collective-permute-start.11 = (f32[128,1024]{1,0:T(8,128)S(1)}, f32[128,1024]{1,0:T(8,128)S(1)}, u32[]{:S(2)}, u32[]{:S(2)}) collective-permute-start(f32[128,1024]{1,0:T(8,128)S(1)} %fusion.26), channel_id=1, source_target_pairs={{0,4},{4,0},{8,12},{12,8},{1,5},{5,1},{9,13},{13,9},{2,6},{6,2},{1... | collective-permute-start | bytes 1572872 | tf_op jit(solution)/shard_map/ppermute | solution.py:135
  70.6 14.3 %collective-permute-start.10 = (f32[1,128,1024]{2,1,0:T(8,128)S(1)}, f32[1,128,1024]{2,1,0:T(8,128)S(1)}, u32[]{:S(2)}, u32[]{:S(2)}) collective-permute-start(f32[1,128,1024]{2,1,0:T(8,128)S(1)} %bitcast.110), channel_id=1, source_target_pairs={{0,8},{4,12},{8,0},{12,4},{1,9},{5,13},{9,1},{13,5},{2,10},{6,14},... | collective-permute-start | bytes 1572872 | tf_op jit(solution)/shard_map/ppermute | solution.py:139
  84.9 1.9 %collective-permute-start.12 = (f32[1,128,1024]{2,1,0:T(8,128)S(1)}, f32[1,128,1024]{2,1,0:T(8,128)S(1)}, u32[]{:S(2)}, u32[]{:S(2)}) collective-permute-start(f32[1,128,1024]{2,1,0:T(8,128)S(1)} %collective-permute-done.10), channel_id=1, source_target_pairs={{0,4},{4,0},{8,12},{12,8},{1,5},{5,1},{9,13},{13,9},{2,6},{6,2},{1... | collective-permute-start | bytes 1572872 | tf_op jit(solution)/shard_map/ppermute | solution.py:157
  95.8 8.4 %collective-permute-start.13 = (f32[2,16,2048]{2,1,0:T(8,128)S(1)}, f32[2,16,2048]{2,1,0:T(8,128)S(1)}, u32[]{:S(2)}, u32[]{:S(2)}) collective-permute-start(f32[2,16,2048]{2,1,0:T(8,128)S(1)} %pad_maximum_fusion.3), channel_id=1, source_target_pairs={{0,1},{1,0},{2,3},{3,2},{4,5},{5,4},{6,7},{7,6},{8,9},{9,8},{10,11... | collective-permute-start | bytes 786440 | tf_op jit(solution)/shard_map/ppermute | solution.py:37
  104.3 10.4 %collective-permute-start.15 = (f32[2,16,2048]{2,1,0:T(8,128)S(1)}, f32[2,16,2048]{2,1,0:T(8,128)S(1)}, u32[]{:S(2)}, u32[]{:S(2)}) collective-permute-start(f32[2,16,2048]{2,1,0:T(8,128)S(1)} %pad_maximum_fusion.4), channel_id=1, source_target_pairs={{0,1},{1,0},{2,3},{3,2},{4,5},{5,4},{6,7},{7,6},{8,9},{9,8},{10,11... | collective-permute-start | bytes 786440 | tf_op jit(solution)/shard_map/ppermute | solution.py:37
  104.9 7.8 %collective-permute-start.14 = (f32[1,16,2048]{2,1,0:T(8,128)S(1)}, f32[1,16,2048]{2,1,0:T(8,128)S(1)}, u32[]{:S(2)}, u32[]{:S(2)}) collective-permute-start(f32[1,16,2048]{2,1,0:T(8,128)S(1)} %get-tuple-element.15), channel_id=1, source_target_pairs={{0,2},{1,3},{2,0},{3,1},{4,6},{5,7},{6,4},{7,5},{8,10},{9,11},{10,... | collective-permute-start | bytes 393224 | tf_op jit(solution)/shard_map/ppermute | solution.py:37
  114.7 6.4 %collective-permute-start.16 = (f32[1,16,2048]{2,1,0:T(8,128)S(1)}, f32[1,16,2048]{2,1,0:T(8,128)S(1)}, u32[]{:S(2)}, u32[]{:S(2)}) collective-permute-start(f32[1,16,2048]{2,1,0:T(8,128)S(1)} %get-tuple-element.14), channel_id=1, source_target_pairs={{0,2},{1,3},{2,0},{3,1},{4,6},{5,7},{6,4},{7,5},{8,10},{9,11},{10,... | collective-permute-start | bytes 393224 | tf_op jit(solution)/shard_map/ppermute | solution.py:37
  121.2 2.0 %collective-permute-start.17 = (f32[8,2048]{1,0:T(8,128)S(1)}, f32[8,2048]{1,0:T(8,128)S(1)}, u32[]{:S(2)}, u32[]{:S(2)}) collective-permute-start(f32[8,2048]{1,0:T(8,128)S(1)} %get-tuple-element.27), channel_id=1, source_target_pairs={{0,4},{4,0},{8,12},{12,8},{1,5},{5,1},{9,13},{13,9},{2,6},{6,2},{1... | collective-permute-start | bytes 196616 | tf_op jit(solution)/shard_map/ppermute | solution.py:46
  121.3 4.5 %collective-permute-start.18 = (f32[8,2048]{1,0:T(8,128)S(1)}, f32[8,2048]{1,0:T(8,128)S(1)}, u32[]{:S(2)}, u32[]{:S(2)}) collective-permute-start(f32[8,2048]{1,0:T(8,128)S(1)} %get-tuple-element.26), channel_id=1, source_target_pairs={{0,8},{4,12},{8,0},{12,4},{1,9},{5,13},{9,1},{13,5},{2,10},{6,14},... | collective-permute-start | bytes 196616 | tf_op jit(solution)/shard_map/ppermute | solution.py:46
  123.1 4.0 %collective-permute-start.19 = (f32[8,2048]{1,0:T(8,128)S(1)}, f32[8,2048]{1,0:T(8,128)S(1)}, u32[]{:S(2)}, u32[]{:S(2)}) collective-permute-start(f32[8,2048]{1,0:T(8,128)S(1)} %get-tuple-element.25), channel_id=1, source_target_pairs={{0,12},{4,8},{8,4},{12,0},{1,13},{5,9},{9,5},{13,1},{2,14},{6,10},... | collective-permute-start | bytes 196616 | tf_op jit(solution)/shard_map/ppermute | solution.py:46

commit v15 on v13

--- a/solution.py
+++ b/solution.py
@@ -120,8 +120,6 @@
             other = lax.optimization_barrier(up_block(1, lhs))
             mine = lax.optimization_barrier(up_block(0, lhs))
         held[d_even] = mine + lax.ppermute(other, "row", _pairs(n_row, 1))
-        if i == 0:
-            lhs, held[d_even] = lax.optimization_barrier((lhs, held[d_even]))
     flip = 2
     while flip < n_row:
         sent = [d for d in sorted(held) if d & flip]

time: 128 us -> 127 us (level)
  waiting for transfers between devices: 61.7 us -> 59.6 us
    ppermute x2, waiting for transfers between devices: 1.88 us -> 0.01 us  [local(): held[d_even] = mine + lax.ppermute(other, 'row', _pairs(n_row, 1))]
  transfers between devices with their start and end apart: 20 -> 20, of which waited for: 17 -> 16; matrix products, arithmetic and copies ran while one was open for 12% -> 18% of each run, Pallas kernels for 0% -> 0%
where the time goes in v15:
time: 127 us
  waiting for transfers between devices  59.6 us (47%)
  matrix products  38.2 us (30%)
  starting transfers between devices  20.2 us (16%)
  other arithmetic  5.14 us (4%)
  Pallas kernels  1.97 us (2%)
  local copies, waits for them, and re-layouts  1.76 us (1%)
    ppermute x4, waiting for transfers between devices, _gather_rel(): lax.ppermute(jnp.stack([held[k] for k in keys]), axis, _pairs(n, flip))  21.1 us
    ppermute x4, waiting for transfers between devices, _scatter_rel(): lax.ppermute(jnp.stack([held[d] for d in sent]), axis, _pairs(n, flip))  18.8 us
    dot_general x2, matrix products, down_pair(): jnp.dot(pair, w, precision=lax.Precision.HIGH, preferred_element_type=jnp...  17.4 us
    dot_general x2, matrix products, up_block(): jnp.dot(lhs, w, precision=lax.Precision.HIGH, preferred_element_type=jnp....  11.9 us
    dot_general x1, matrix products, up_pair(): jnp.dot(lhs, w, precision=lax.Precision.HIGH, preferred_element_type=jnp....  8.88 us
    ppermute x6, waiting for transfers between devices, _exchange_abs(): got.append(lax.ppermute(blocks[idx ^ d], axis, _pairs(n, d)))  8.2 us
    ppermute x4, starting transfers between devices, _scatter_rel(): lax.ppermute(jnp.stack([held[d] for d in sent]), axis, _pairs(n, flip))  6.4 us
    ppermute x1, waiting for transfers between devices, local(): lax.ppermute(jnp.stack([held[d] for d in sent]), 'row', _pairs(n_row, flip))  5.67 us
  transfers between devices with their start and end apart: 20, of which 16 were waited for; matrix products, arithmetic and copies ran while one was open for 18% of the time, Pallas kernels for 0%

profile of v15, /device:TPU:0, one launch (start us, length us, event | category | flops | bytes accessed | tf_op | source)
XLA Modules:
  0.0 127.1 jit_solution(2410050850962999792)
XLA Ops:
  0.0 0.8 fusion.51
  0.8 2.0 %shard_map.64 = f32[8,8192]{1,0:T(8,128)} custom-call(f32[8,8192]{1,0:T(8,128)} %x_ref.1), custom_call_target="tpu_custom_call" | custom-call | flops 393216 | bytes 524288 | tf_op jit(solution)/shard_map/pallas_call | solution.py:61
  2.8 1.0 multiply_add_fusion.1
  3.8 2.4 %collective-permute-start.2 = (f32[8,2048]{1,0:T(8,128)S(1)}, f32[8,2048]{1,0:T(8,128)S(1)}, u32[]{:S(2)}, u32[]{:S(2)}) collective-permute-start(f32[8,2048]{1,0:T(8,128)S(1)} %get-tuple-element.29), channel_id=1, source_target_pairs={{0,12},{4,8},{8,4},{12,0},{1,13},{5,9},{9,5},{13,1},{2,14},{6,10},... | collective-permute-start | bytes 196616 | tf_op jit(solution)/shard_map/ppermute | solution.py:46
  6.3 0.7 collective-permute-start
  6.9 0.0 collective-permute-start.1
  7.0 1.8 %collective-permute-done.2 = f32[8,2048]{1,0:T(8,128)S(1)} collective-permute-done((f32[8,2048]{1,0:T(8,128)S(1)}, f32[8,2048]{1,0:T(8,128)S(1)}, u32[]{:S(2)}, u32[]{:S(2)}) %collective-permute-start.2) | collective-permute-done | bytes 65568 | tf_op jit(solution)/shard_map/ppermute | solution.py:46
  8.8 2.5 %collective-permute-done.1 = f32[8,2048]{1,0:T(8,128)S(1)} collective-permute-done((f32[8,2048]{1,0:T(8,128)S(1)}, f32[8,2048]{1,0:T(8,128)S(1)}, u32[]{:S(2)}, u32[]{:S(2)}) %collective-permute-start.1) | collective-permute-done | bytes 65568 | tf_op jit(solution)/shard_map/ppermute | solution.py:46
  11.3 2.7 %collective-permute-start.3 = (f32[1,16,2048]{2,1,0:T(8,128)S(1)}, f32[1,16,2048]{2,1,0:T(8,128)S(1)}, u32[]{:S(2)}, u32[]{:S(2)}) collective-permute-start(f32[1,16,2048]{2,1,0:T(8,128)S(1)} %fusion.43), channel_id=1, source_target_pairs={{0,2},{1,3},{2,0},{3,1},{4,6},{5,7},{6,4},{7,5},{8,10},{9,11},{10,... | collective-permute-start | bytes 393224 | tf_op jit(solution)/shard_map/ppermute | solution.py:24
  14.0 0.4 collective-permute-start.5
  14.4 9.1 %collective-permute-done.3 = f32[1,16,2048]{2,1,0:T(8,128)S(1)} collective-permute-done((f32[1,16,2048]{2,1,0:T(8,128)S(1)}, f32[1,16,2048]{2,1,0:T(8,128)S(1)}, u32[]{:S(2)}, u32[]{:S(2)}) %collective-permute-start.3) | collective-permute-done | bytes 131104 | tf_op jit(solution)/shard_map/ppermute | solution.py:24
  23.5 0.1 collective-permute-start.4
  23.6 1.6 %collective-permute-done.5 = f32[1,16,2048]{2,1,0:T(8,128)S(1)} collective-permute-done((f32[1,16,2048]{2,1,0:T(8,128)S(1)}, f32[1,16,2048]{2,1,0:T(8,128)S(1)}, u32[]{:S(2)}, u32[]{:S(2)}) %collective-permute-start.5) | collective-permute-done | bytes 131104 | tf_op jit(solution)/shard_map/ppermute | solution.py:24
  25.2 0.6 collective-permute-start.6
  25.9 6.9 %collective-permute-done.4 = f32[2,16,2048]{2,1,0:T(8,128)S(1)} collective-permute-done((f32[2,16,2048]{2,1,0:T(8,128)S(1)}, f32[2,16,2048]{2,1,0:T(8,128)S(1)}, u32[]{:S(2)}, u32[]{:S(2)}) %collective-permute-start.4) | collective-permute-done | bytes 262176 | tf_op jit(solution)/shard_map/ppermute | solution.py:24
  32.9 3.5 %collective-permute-done.6 = f32[2,16,2048]{2,1,0:T(8,128)S(1)} collective-permute-done((f32[2,16,2048]{2,1,0:T(8,128)S(1)}, f32[2,16,2048]{2,1,0:T(8,128)S(1)}, u32[]{:S(2)}, u32[]{:S(2)}) %collective-permute-start.6) | collective-permute-done | bytes 262176 | tf_op jit(solution)/shard_map/ppermute | solution.py:24
  36.4 8.9 %fusion.4 = f32[128,2048]{1,0:T(8,128)S(1)} fusion(f32[128,2048]{1,0:T(8,128)S(1)} %fusion.38, f32[2048,4096]{1,0:T(8,128)} %param.8, s32[]{:T(128)S(6)} %select_n.80), kind=kOutput, calls=%fused_computation.4 | convolution fusion | flops 3221225472 | bytes 18874372 | tf_op jit(solution)/shard_map/dot_general | solution.py:108
  45.3 0.9 constant_dynamic-slice_fusion.5
  46.2 6.0 %fusion.6 = f32[128,1024]{1,0:T(8,128)S(1)} fusion(f32[128,2048]{1,0:T(8,128)S(1)} %fusion.38, f32[2048,4096]{1,0:T(8,128)} %param.8, s32[]{:T(128)S(6)} %select_n.78), kind=kOutput, calls=%fused_computation.6 | convolution fusion | flops 1610612736 | bytes 9961476 | tf_op jit(solution)/shard_map/dot_general | solution.py:97
  52.1 0.6 collective-permute-start.7
  52.7 0.9 add_bitcast_fusion
  53.6 2.5 %collective-permute-start.9 = (f32[1,128,1024]{2,1,0:T(8,128)}, f32[1,128,1024]{2,1,0:T(8,128)S(1)}, u32[]{:S(2)}, u32[]{:S(2)}) collective-permute-start(f32[1,128,1024]{2,1,0:T(8,128)} %add_bitcast_fusion), channel_id=1, source_target_pairs={{0,8},{4,12},{8,0},{12,4},{1,9},{5,13},{9,1},{13,5},{2,10},{6,14},... | collective-permute-start | bytes 1572872 | tf_op jit(solution)/shard_map/ppermute | solution.py:126
  56.1 0.7 dynamic_slice.77
  56.8 5.9 %fusion.8 = f32[128,1024]{1,0:T(8,128)S(1)} fusion(f32[128,2048]{1,0:T(8,128)S(1)} %fusion.38, f32[2048,4096]{1,0:T(8,128)} %param.8, s32[]{:T(128)S(6)} %select_n.77), kind=kOutput, calls=%fused_computation.8 | convolution fusion | flops 1610612736 | bytes 9961476 | tf_op jit(solution)/shard_map/dot_general | solution.py:97
  62.7 5.7 %collective-permute-done.9 = f32[1,128,1024]{2,1,0:T(8,128)S(1)} collective-permute-done((f32[1,128,1024]{2,1,0:T(8,128)}, f32[1,128,1024]{2,1,0:T(8,128)S(1)}, u32[]{:S(2)}, u32[]{:S(2)}) %collective-permute-start.9) | collective-permute-done | bytes 524320 | tf_op jit(solution)/shard_map/ppermute | solution.py:126
  68.4 1.3 fusion.26
  69.7 0.1 collective-permute-start.11
  69.7 1.8 %collective-permute-start.10 = (f32[1,128,1024]{2,1,0:T(8,128)S(1)}, f32[1,128,1024]{2,1,0:T(8,128)S(1)}, u32[]{:S(2)}, u32[]{:S(2)}) collective-permute-start(f32[1,128,1024]{2,1,0:T(8,128)S(1)} %bitcast.111), channel_id=1, source_target_pairs={{0,8},{4,12},{8,0},{12,4},{1,9},{5,13},{9,1},{13,5},{2,10},{6,14},... | collective-permute-start | bytes 1572872 | tf_op jit(solution)/shard_map/ppermute | solution.py:135
  71.6 0.1 collective-permute-done.11
  71.6 8.7 %fusion.2 = f32[128,2048]{1,0:T(8,128)S(1)} fusion(f32[4096,2048]{1,0:T(8,128)} %param.10, s32[]{:T(128)S(6)} %select_n.87, f32[128,1024]{1,0:T(8,128)S(1)} %collective-permute-done.11, f32[128,1024]{1,0:T(8,128)S(1)} %fusion.26, pred[]{:T(512)S(6)} %eq.6), kind=kOutput, calls=%fused_computation.2 | convolution fusion | flops 3222011904 | bytes 18874372 | tf_op jit(solution)/shard_map/dot_general | solution.py:145
  80.3 3.7 %collective-permute-done.10 = f32[1,128,1024]{2,1,0:T(8,128)S(1)} collective-permute-done((f32[1,128,1024]{2,1,0:T(8,128)S(1)}, f32[1,128,1024]{2,1,0:T(8,128)S(1)}, u32[]{:S(2)}, u32[]{:S(2)}) %collective-permute-start.10) | collective-permute-done | bytes 524320 | tf_op jit(solution)/shard_map/ppermute | solution.py:135
  84.1 1.9 %collective-permute-done.12 = f32[1,128,1024]{2,1,0:T(8,128)S(1)} collective-permute-done((f32[1,128,1024]{2,1,0:T(8,128)S(1)}, f32[1,128,1024]{2,1,0:T(8,128)S(1)}, u32[]{:S(2)}, u32[]{:S(2)}) %collective-permute-start.12) | collective-permute-done | bytes 524320 | tf_op jit(solution)/shard_map/ppermute | solution.py:153
  86.0 8.7 %fusion = f32[128,2048]{1,0:T(8,128)S(1)} fusion(f32[4096,2048]{1,0:T(8,128)} %param.10, s32[]{:T(128)S(6)} %select_n.80, f32[128,1024]{1,0:T(8,128)S(1)} %bitcast.115, f32[128,1024]{1,0:T(8,128)S(1)} %bitcast.114, pred[]{:T(512)S(6)} %eq.6), kind=kOutput, calls=%fused_computation | convolution fusion | flops 3222011904 | bytes 18874372 | tf_op jit(solution)/shard_map/dot_general | solution.py:145
  94.7 0.1 add.159
  94.9 0.6 collective-permute-start.13
  95.5 7.8 %collective-permute-done.13 = f32[2,16,2048]{2,1,0:T(8,128)S(1)} collective-permute-done((f32[2,16,2048]{2,1,0:T(8,128)S(1)}, f32[2,16,2048]{2,1,0:T(8,128)S(1)}, u32[]{:S(2)}, u32[]{:S(2)}) %collective-permute-start.13) | collective-permute-done | bytes 262176 | tf_op jit(solution)/shard_map/ppermute | solution.py:37
  103.4 0.6 collective-permute-start.15
  104.0 3.5 %collective-permute-start.14 = (f32[1,16,2048]{2,1,0:T(8,128)S(1)}, f32[1,16,2048]{2,1,0:T(8,128)S(1)}, u32[]{:S(2)}, u32[]{:S(2)}) collective-permute-start(f32[1,16,2048]{2,1,0:T(8,128)S(1)} %get-tuple-element.11), channel_id=1, source_target_pairs={{0,2},{1,3},{2,0},{3,1},{4,6},{5,7},{6,4},{7,5},{8,10},{9,11},{10,... | collective-permute-start | bytes 393224 | tf_op jit(solution)/shard_map/ppermute | solution.py:37
  107.5 4.4 %collective-permute-done.14 = f32[1,16,2048]{2,1,0:T(8,128)S(1)} collective-permute-done((f32[1,16,2048]{2,1,0:T(8,128)S(1)}, f32[1,16,2048]{2,1,0:T(8,128)S(1)}, u32[]{:S(2)}, u32[]{:S(2)}) %collective-permute-start.14) | collective-permute-done | bytes 131104 | tf_op jit(solution)/shard_map/ppermute | solution.py:37
  111.9 1.9 %collective-permute-done.15 = f32[2,16,2048]{2,1,0:T(8,128)S(1)} collective-permute-done((f32[2,16,2048]{2,1,0:T(8,128)S(1)}, f32[2,16,2048]{2,1,0:T(8,128)S(1)}, u32[]{:S(2)}, u32[]{:S(2)}) %collective-permute-start.15) | collective-permute-done | bytes 262176 | tf_op jit(solution)/shard_map/ppermute | solution.py:37
  113.8 1.6 %collective-permute-start.16 = (f32[1,16,2048]{2,1,0:T(8,128)S(1)}, f32[1,16,2048]{2,1,0:T(8,128)S(1)}, u32[]{:S(2)}, u32[]{:S(2)}) collective-permute-start(f32[1,16,2048]{2,1,0:T(8,128)S(1)} %get-tuple-element.10), channel_id=1, source_target_pairs={{0,2},{1,3},{2,0},{3,1},{4,6},{5,7},{6,4},{7,5},{8,10},{9,11},{10,... | collective-permute-start | bytes 393224 | tf_op jit(solution)/shard_map/ppermute | solution.py:37
  115.4 4.8 %collective-permute-done.16 = f32[1,16,2048]{2,1,0:T(8,128)S(1)} collective-permute-done((f32[1,16,2048]{2,1,0:T(8,128)S(1)}, f32[1,16,2048]{2,1,0:T(8,128)S(1)}, u32[]{:S(2)}, u32[]{:S(2)}) %collective-permute-start.16) | collective-permute-done | bytes 131104 | tf_op jit(solution)/shard_map/ppermute | solution.py:37
  120.3 0.1 collective-permute-start.17
  120.4 1.8 %collective-permute-start.18 = (f32[8,2048]{1,0:T(8,128)S(1)}, f32[8,2048]{1,0:T(8,128)S(1)}, u32[]{:S(2)}, u32[]{:S(2)}) collective-permute-start(f32[8,2048]{1,0:T(8,128)S(1)} %get-tuple-element.22), channel_id=1, source_target_pairs={{0,8},{4,12},{8,0},{12,4},{1,9},{5,13},{9,1},{13,5},{2,10},{6,14},... | collective-permute-start | bytes 196616 | tf_op jit(solution)/shard_map/ppermute | solution.py:46
  122.2 0.1 collective-permute-start.19
  122.3 2.6 %collective-permute-done.18 = f32[8,2048]{1,0:T(8,128)S(1)} collective-permute-done((f32[8,2048]{1,0:T(8,128)S(1)}, f32[8,2048]{1,0:T(8,128)S(1)}, u32[]{:S(2)}, u32[]{:S(2)}) %collective-permute-start.18) | collective-permute-done | bytes 65568 | tf_op jit(solution)/shard_map/ppermute | solution.py:46
  124.9 1.3 %collective-permute-done.19 = f32[8,2048]{1,0:T(8,128)S(1)} collective-permute-done((f32[8,2048]{1,0:T(8,128)S(1)}, f32[8,2048]{1,0:T(8,128)S(1)}, u32[]{:S(2)}, u32[]{:S(2)}) %collective-permute-start.19) | collective-permute-done | bytes 65568 | tf_op jit(solution)/shard_map/ppermute | solution.py:46
  126.4 0.8 multiply_add_fusion
  (36 shorter events, 0.5 us)
Async XLA Ops:
  3.8 4.9 %collective-permute-start.2 = (f32[8,2048]{1,0:T(8,128)S(1)}, f32[8,2048]{1,0:T(8,128)S(1)}, u32[]{:S(2)}, u32[]{:S(2)}) collective-permute-start(f32[8,2048]{1,0:T(8,128)S(1)} %get-tuple-element.29), channel_id=1, source_target_pairs={{0,12},{4,8},{8,4},{12,0},{1,13},{5,9},{9,5},{13,1},{2,14},{6,10},... | collective-permute-start | bytes 196616 | tf_op jit(solution)/shard_map/ppermute | solution.py:46
  6.3 2.5 %collective-permute-start = (f32[8,2048]{1,0:T(8,128)S(1)}, f32[8,2048]{1,0:T(8,128)S(1)}, u32[]{:S(2)}, u32[]{:S(2)}) collective-permute-start(f32[8,2048]{1,0:T(8,128)S(1)} %get-tuple-element.31), channel_id=1, source_target_pairs={{0,4},{4,0},{8,12},{12,8},{1,5},{5,1},{9,13},{13,9},{2,6},{6,2},{1... | collective-permute-start | bytes 196616 | tf_op jit(solution)/shard_map/ppermute | solution.py:46
  6.9 4.3 %collective-permute-start.1 = (f32[8,2048]{1,0:T(8,128)S(1)}, f32[8,2048]{1,0:T(8,128)S(1)}, u32[]{:S(2)}, u32[]{:S(2)}) collective-permute-start(f32[8,2048]{1,0:T(8,128)S(1)} %get-tuple-element.30), channel_id=1, source_target_pairs={{0,8},{4,12},{8,0},{12,4},{1,9},{5,13},{9,1},{13,5},{2,10},{6,14},... | collective-permute-start | bytes 196616 | tf_op jit(solution)/shard_map/ppermute | solution.py:46
  11.3 12.2 %collective-permute-start.3 = (f32[1,16,2048]{2,1,0:T(8,128)S(1)}, f32[1,16,2048]{2,1,0:T(8,128)S(1)}, u32[]{:S(2)}, u32[]{:S(2)}) collective-permute-start(f32[1,16,2048]{2,1,0:T(8,128)S(1)} %fusion.43), channel_id=1, source_target_pairs={{0,2},{1,3},{2,0},{3,1},{4,6},{5,7},{6,4},{7,5},{8,10},{9,11},{10,... | collective-permute-start | bytes 393224 | tf_op jit(solution)/shard_map/ppermute | solution.py:24
  14.0 11.3 %collective-permute-start.5 = (f32[1,16,2048]{2,1,0:T(8,128)S(1)}, f32[1,16,2048]{2,1,0:T(8,128)S(1)}, u32[]{:S(2)}, u32[]{:S(2)}) collective-permute-start(f32[1,16,2048]{2,1,0:T(8,128)S(1)} %fusion.42), channel_id=1, source_target_pairs={{0,2},{1,3},{2,0},{3,1},{4,6},{5,7},{6,4},{7,5},{8,10},{9,11},{10,... | collective-permute-start | bytes 393224 | tf_op jit(solution)/shard_map/ppermute | solution.py:24
  23.5 9.3 %collective-permute-start.4 = (f32[2,16,2048]{2,1,0:T(8,128)S(1)}, f32[2,16,2048]{2,1,0:T(8,128)S(1)}, u32[]{:S(2)}, u32[]{:S(2)}) collective-permute-start(f32[2,16,2048]{2,1,0:T(8,128)S(1)} %pad_maximum_fusion.1), channel_id=1, source_target_pairs={{0,1},{1,0},{2,3},{3,2},{4,5},{5,4},{6,7},{7,6},{8,9},{9,8},{10,11... | collective-permute-start | bytes 786440 | tf_op jit(solution)/shard_map/ppermute | solution.py:24
  25.2 11.1 %collective-permute-start.6 = (f32[2,16,2048]{2,1,0:T(8,128)S(1)}, f32[2,16,2048]{2,1,0:T(8,128)S(1)}, u32[]{:S(2)}, u32[]{:S(2)}) collective-permute-start(f32[2,16,2048]{2,1,0:T(8,128)S(1)} %pad_maximum_fusion.2), channel_id=1, source_target_pairs={{0,1},{1,0},{2,3},{3,2},{4,5},{5,4},{6,7},{7,6},{8,9},{9,8},{10,11... | collective-permute-start | bytes 786440 | tf_op jit(solution)/shard_map/ppermute | solution.py:24
  46.2 6.6 %collective-permute-start.8 = (f32[128,1024]{1,0:T(8,128)}, f32[128,1024]{1,0:T(8,128)S(1)}, u32[]{:S(2)}, u32[]{:S(2)}) collective-permute-start(f32[128,1024]{1,0:T(8,128)} %constant_dynamic-slice_fusion.5), channel_id=1, source_target_pairs={{0,4},{4,0},{8,12},{12,8},{1,5},{5,1},{9,13},{13,9},{2,6},{6,2},{1... | collective-permute-start | bytes 1572872 | tf_op jit(solution)/shard_map/ppermute | solution.py:122
  46.2 80.2 %copy-start = (f32[8,8192]{1,0:T(8,128)S(1)}, f32[8,8192]{1,0:T(8,128)}, u32[]{:S(2)}) copy-start(f32[8,8192]{1,0:T(8,128)} %x_ref.1) | copy-start | bytes 786436
  46.2 80.2 %copy-start.1 = (f32[8192]{0:T(1024)S(1)}, f32[8192]{0:T(1024)}, u32[]{:S(2)}) copy-start(f32[8192]{0:T(1024)} %param.11) | copy-start | bytes 98308
  52.1 10.6 %collective-permute-start.7 = (f32[128,1024]{1,0:T(8,128)S(1)}, f32[128,1024]{1,0:T(8,128)}, u32[]{:S(2)}, u32[]{:S(2)}) collective-permute-start(f32[128,1024]{1,0:T(8,128)S(1)} %fusion.6), channel_id=1, source_target_pairs={{0,4},{4,0},{8,12},{12,8},{1,5},{5,1},{9,13},{13,9},{2,6},{6,2},{1... | collective-permute-start | bytes 1572872 | tf_op jit(solution)/shard_map/ppermute | solution.py:122
  53.6 14.8 %collective-permute-start.9 = (f32[1,128,1024]{2,1,0:T(8,128)}, f32[1,128,1024]{2,1,0:T(8,128)S(1)}, u32[]{:S(2)}, u32[]{:S(2)}) collective-permute-start(f32[1,128,1024]{2,1,0:T(8,128)} %add_bitcast_fusion), channel_id=1, source_target_pairs={{0,8},{4,12},{8,0},{12,4},{1,9},{5,13},{9,1},{13,5},{2,10},{6,14},... | collective-permute-start | bytes 1572872 | tf_op jit(solution)/shard_map/ppermute | solution.py:126
  69.7 2.0 %collective-permute-start.11 = (f32[128,1024]{1,0:T(8,128)S(1)}, f32[128,1024]{1,0:T(8,128)S(1)}, u32[]{:S(2)}, u32[]{:S(2)}) collective-permute-start(f32[128,1024]{1,0:T(8,128)S(1)} %fusion.26), channel_id=1, source_target_pairs={{0,4},{4,0},{8,12},{12,8},{1,5},{5,1},{9,13},{13,9},{2,6},{6,2},{1... | collective-permute-start | bytes 1572872 | tf_op jit(solution)/shard_map/ppermute | solution.py:131
  69.7 14.3 %collective-permute-start.10 = (f32[1,128,1024]{2,1,0:T(8,128)S(1)}, f32[1,128,1024]{2,1,0:T(8,128)S(1)}, u32[]{:S(2)}, u32[]{:S(2)}) collective-permute-start(f32[1,128,1024]{2,1,0:T(8,128)S(1)} %bitcast.111), channel_id=1, source_target_pairs={{0,8},{4,12},{8,0},{12,4},{1,9},{5,13},{9,1},{13,5},{2,10},{6,14},... | collective-permute-start | bytes 1572872 | tf_op jit(solution)/shard_map/ppermute | solution.py:135
  84.1 1.9 %collective-permute-start.12 = (f32[1,128,1024]{2,1,0:T(8,128)S(1)}, f32[1,128,1024]{2,1,0:T(8,128)S(1)}, u32[]{:S(2)}, u32[]{:S(2)}) collective-permute-start(f32[1,128,1024]{2,1,0:T(8,128)S(1)} %collective-permute-done.10), channel_id=1, source_target_pairs={{0,4},{4,0},{8,12},{12,8},{1,5},{5,1},{9,13},{13,9},{2,6},{6,2},{1... | collective-permute-start | bytes 1572872 | tf_op jit(solution)/shard_map/ppermute | solution.py:153
  94.9 8.4 %collective-permute-start.13 = (f32[2,16,2048]{2,1,0:T(8,128)S(1)}, f32[2,16,2048]{2,1,0:T(8,128)S(1)}, u32[]{:S(2)}, u32[]{:S(2)}) collective-permute-start(f32[2,16,2048]{2,1,0:T(8,128)S(1)} %pad_maximum_fusion.3), channel_id=1, source_target_pairs={{0,1},{1,0},{2,3},{3,2},{4,5},{5,4},{6,7},{7,6},{8,9},{9,8},{10,11... | collective-permute-start | bytes 786440 | tf_op jit(solution)/shard_map/ppermute | solution.py:37
  103.4 10.4 %collective-permute-start.15 = (f32[2,16,2048]{2,1,0:T(8,128)S(1)}, f32[2,16,2048]{2,1,0:T(8,128)S(1)}, u32[]{:S(2)}, u32[]{:S(2)}) collective-permute-start(f32[2,16,2048]{2,1,0:T(8,128)S(1)} %pad_maximum_fusion.4), channel_id=1, source_target_pairs={{0,1},{1,0},{2,3},{3,2},{4,5},{5,4},{6,7},{7,6},{8,9},{9,8},{10,11... | collective-permute-start | bytes 786440 | tf_op jit(solution)/shard_map/ppermute | solution.py:37
  104.0 7.8 %collective-permute-start.14 = (f32[1,16,2048]{2,1,0:T(8,128)S(1)}, f32[1,16,2048]{2,1,0:T(8,128)S(1)}, u32[]{:S(2)}, u32[]{:S(2)}) collective-permute-start(f32[1,16,2048]{2,1,0:T(8,128)S(1)} %get-tuple-element.11), channel_id=1, source_target_pairs={{0,2},{1,3},{2,0},{3,1},{4,6},{5,7},{6,4},{7,5},{8,10},{9,11},{10,... | collective-permute-start | bytes 393224 | tf_op jit(solution)/shard_map/ppermute | solution.py:37
  113.8 6.4 %collective-permute-start.16 = (f32[1,16,2048]{2,1,0:T(8,128)S(1)}, f32[1,16,2048]{2,1,0:T(8,128)S(1)}, u32[]{:S(2)}, u32[]{:S(2)}) collective-permute-start(f32[1,16,2048]{2,1,0:T(8,128)S(1)} %get-tuple-element.10), channel_id=1, source_target_pairs={{0,2},{1,3},{2,0},{3,1},{4,6},{5,7},{6,4},{7,5},{8,10},{9,11},{10,... | collective-permute-start | bytes 393224 | tf_op jit(solution)/shard_map/ppermute | solution.py:37
  120.3 2.0 %collective-permute-start.17 = (f32[8,2048]{1,0:T(8,128)S(1)}, f32[8,2048]{1,0:T(8,128)S(1)}, u32[]{:S(2)}, u32[]{:S(2)}) collective-permute-start(f32[8,2048]{1,0:T(8,128)S(1)} %get-tuple-element.23), channel_id=1, source_target_pairs={{0,4},{4,0},{8,12},{12,8},{1,5},{5,1},{9,13},{13,9},{2,6},{6,2},{1... | collective-permute-start | bytes 196616 | tf_op jit(solution)/shard_map/ppermute | solution.py:46
  120.4 4.5 %collective-permute-start.18 = (f32[8,2048]{1,0:T(8,128)S(1)}, f32[8,2048]{1,0:T(8,128)S(1)}, u32[]{:S(2)}, u32[]{:S(2)}) collective-permute-start(f32[8,2048]{1,0:T(8,128)S(1)} %get-tuple-element.22), channel_id=1, source_target_pairs={{0,8},{4,12},{8,0},{12,4},{1,9},{5,13},{9,1},{13,5},{2,10},{6,14},... | collective-permute-start | bytes 196616 | tf_op jit(solution)/shard_map/ppermute | solution.py:46
  122.2 4.0 %collective-permute-start.19 = (f32[8,2048]{1,0:T(8,128)S(1)}, f32[8,2048]{1,0:T(8,128)S(1)}, u32[]{:S(2)}, u32[]{:S(2)}) collective-permute-start(f32[8,2048]{1,0:T(8,128)S(1)} %get-tuple-element.21), channel_id=1, source_target_pairs={{0,12},{4,8},{8,4},{12,0},{1,13},{5,9},{9,5},{13,1},{2,14},{6,10},... | collective-permute-start | bytes 196616 | tf_op jit(solution)/shard_map/ppermute | solution.py:46

commit v16 on v15

--- a/solution.py
+++ b/solution.py
@@ -107,8 +107,9 @@
         both = lax.optimization_barrier(
             jnp.dot(lhs, w, precision=lax.Precision.HIGH,
                     preferred_element_type=jnp.float32))
-        mine = lax.dynamic_slice_in_dim(both, core * quarter, quarter, 1)
-        other = lax.dynamic_slice_in_dim(both, (1 - core) * quarter, quarter, 1)
+        lo, hi = both[:, :quarter], both[:, quarter:]
+        mine = jnp.where(core == 0, lo, hi)
+        other = jnp.where(core == 0, hi, lo)
         return mine, other
 
     held = {}

time: 127 us -> 127 us (level)
  no operation moved by 1% of the time
where the time goes in v16:
time: 127 us
  waiting for transfers between devices  59.4 us (47%)
  matrix products  38.2 us (30%)
  starting transfers between devices  20.3 us (16%)
  other arithmetic  5.47 us (4%)
  Pallas kernels  1.97 us (2%)
    ppermute x4, waiting for transfers between devices, _gather_rel(): lax.ppermute(jnp.stack([held[k] for k in keys]), axis, _pairs(n, flip))  21.1 us
    ppermute x4, waiting for transfers between devices, _scatter_rel(): lax.ppermute(jnp.stack([held[d] for d in sent]), axis, _pairs(n, flip))  18.8 us
    dot_general x2, matrix products, down_pair(): jnp.dot(pair, w, precision=lax.Precision.HIGH, preferred_element_type=jnp...  17.4 us
    dot_general x2, matrix products, up_block(): jnp.dot(lhs, w, precision=lax.Precision.HIGH, preferred_element_type=jnp....  11.9 us
    dot_general x1, matrix products, up_pair(): jnp.dot(lhs, w, precision=lax.Precision.HIGH, preferred_element_type=jnp....  8.88 us
    ppermute x6, waiting for transfers between devices, _exchange_abs(): got.append(lax.ppermute(blocks[idx ^ d], axis, _pairs(n, d)))  8.2 us
    ppermute x4, starting transfers between devices, _scatter_rel(): lax.ppermute(jnp.stack([held[d] for d in sent]), axis, _pairs(n, flip))  6.39 us
    ppermute x1, waiting for transfers between devices, local(): lax.ppermute(jnp.stack([held[d] for d in sent]), 'row', _pairs(n_row, flip))  5.48 us
  transfers between devices with their start and end apart: 20, of which 16 were waited for; matrix products, arithmetic and copies ran while one was open for 18% of the time, Pallas kernels for 0%

profile of v16, /device:TPU:0, one launch (start us, length us, event | category | flops | bytes accessed | tf_op | source)
XLA Modules:
  0.0 126.6 jit_solution(2641409969511924479)
XLA Ops:
  0.0 0.8 fusion.51
  0.8 2.0 %shard_map.64 = f32[8,8192]{1,0:T(8,128)} custom-call(f32[8,8192]{1,0:T(8,128)} %x_ref.1), custom_call_target="tpu_custom_call" | custom-call | flops 393216 | bytes 524288 | tf_op jit(solution)/shard_map/pallas_call | solution.py:61
  2.8 1.0 multiply_add_fusion.1
  3.8 2.4 %collective-permute-start.2 = (f32[8,2048]{1,0:T(8,128)S(1)}, f32[8,2048]{1,0:T(8,128)S(1)}, u32[]{:S(2)}, u32[]{:S(2)}) collective-permute-start(f32[8,2048]{1,0:T(8,128)S(1)} %get-tuple-element.29), channel_id=1, source_target_pairs={{0,12},{4,8},{8,4},{12,0},{1,13},{5,9},{9,5},{13,1},{2,14},{6,10},... | collective-permute-start | bytes 196616 | tf_op jit(solution)/shard_map/ppermute | solution.py:46
  6.3 0.7 collective-permute-start
  7.0 1.8 %collective-permute-done.2 = f32[8,2048]{1,0:T(8,128)S(1)} collective-permute-done((f32[8,2048]{1,0:T(8,128)S(1)}, f32[8,2048]{1,0:T(8,128)S(1)}, u32[]{:S(2)}, u32[]{:S(2)}) %collective-permute-start.2) | collective-permute-done | bytes 65568 | tf_op jit(solution)/shard_map/ppermute | solution.py:46
  8.8 2.5 %collective-permute-done.1 = f32[8,2048]{1,0:T(8,128)S(1)} collective-permute-done((f32[8,2048]{1,0:T(8,128)S(1)}, f32[8,2048]{1,0:T(8,128)S(1)}, u32[]{:S(2)}, u32[]{:S(2)}) %collective-permute-start.1) | collective-permute-done | bytes 65568 | tf_op jit(solution)/shard_map/ppermute | solution.py:46
  11.3 2.7 %collective-permute-start.3 = (f32[1,16,2048]{2,1,0:T(8,128)S(1)}, f32[1,16,2048]{2,1,0:T(8,128)S(1)}, u32[]{:S(2)}, u32[]{:S(2)}) collective-permute-start(f32[1,16,2048]{2,1,0:T(8,128)S(1)} %fusion.43), channel_id=1, source_target_pairs={{0,2},{1,3},{2,0},{3,1},{4,6},{5,7},{6,4},{7,5},{8,10},{9,11},{10,... | collective-permute-start | bytes 393224 | tf_op jit(solution)/shard_map/ppermute | solution.py:24
  14.0 0.4 collective-permute-start.5
  14.4 9.1 %collective-permute-done.3 = f32[1,16,2048]{2,1,0:T(8,128)S(1)} collective-permute-done((f32[1,16,2048]{2,1,0:T(8,128)S(1)}, f32[1,16,2048]{2,1,0:T(8,128)S(1)}, u32[]{:S(2)}, u32[]{:S(2)}) %collective-permute-start.3) | collective-permute-done | bytes 131104 | tf_op jit(solution)/shard_map/ppermute | solution.py:24
  23.5 0.1 collective-permute-start.4
  23.6 1.6 %collective-permute-done.5 = f32[1,16,2048]{2,1,0:T(8,128)S(1)} collective-permute-done((f32[1,16,2048]{2,1,0:T(8,128)S(1)}, f32[1,16,2048]{2,1,0:T(8,128)S(1)}, u32[]{:S(2)}, u32[]{:S(2)}) %collective-permute-start.5) | collective-permute-done | bytes 131104 | tf_op jit(solution)/shard_map/ppermute | solution.py:24
  25.2 0.6 collective-permute-start.6
  25.9 6.9 %collective-permute-done.4 = f32[2,16,2048]{2,1,0:T(8,128)S(1)} collective-permute-done((f32[2,16,2048]{2,1,0:T(8,128)S(1)}, f32[2,16,2048]{2,1,0:T(8,128)S(1)}, u32[]{:S(2)}, u32[]{:S(2)}) %collective-permute-start.4) | collective-permute-done | bytes 262176 | tf_op jit(solution)/shard_map/ppermute | solution.py:24
  32.9 3.5 %collective-permute-done.6 = f32[2,16,2048]{2,1,0:T(8,128)S(1)} collective-permute-done((f32[2,16,2048]{2,1,0:T(8,128)S(1)}, f32[2,16,2048]{2,1,0:T(8,128)S(1)}, u32[]{:S(2)}, u32[]{:S(2)}) %collective-permute-start.6) | collective-permute-done | bytes 262176 | tf_op jit(solution)/shard_map/ppermute | solution.py:24
  36.4 8.9 %fusion.4 = f32[128,2048]{1,0:T(8,128)S(1)} fusion(f32[128,2048]{1,0:T(8,128)S(1)} %fusion.38, f32[2048,4096]{1,0:T(8,128)} %param.8, s32[]{:T(128)S(6)} %select_n.88), kind=kOutput, calls=%fused_computation.4 | convolution fusion | flops 3221225472 | bytes 18874372 | tf_op jit(solution)/shard_map/dot_general | solution.py:108
  45.3 0.1 slice_select_fusion
  45.4 0.1 collective-permute-start.8
  45.5 6.0 %fusion.6 = f32[128,1024]{1,0:T(8,128)S(1)} fusion(f32[128,2048]{1,0:T(8,128)S(1)} %fusion.38, f32[2048,4096]{1,0:T(8,128)} %param.8, s32[]{:T(128)S(6)} %select_n.84), kind=kOutput, calls=%fused_computation.6 | convolution fusion | flops 1610612736 | bytes 9961476 | tf_op jit(solution)/shard_map/dot_general | solution.py:97
  51.5 0.5 collective-permute-start.7
  52.0 1.1 add_bitcast_fusion
  53.1 2.5 %collective-permute-start.9 = (f32[1,128,1024]{2,1,0:T(8,128)S(1)}, f32[1,128,1024]{2,1,0:T(8,128)S(1)}, u32[]{:S(2)}, u32[]{:S(2)}) collective-permute-start(f32[1,128,1024]{2,1,0:T(8,128)S(1)} %add_bitcast_fusion), channel_id=1, source_target_pairs={{0,8},{4,12},{8,0},{12,4},{1,9},{5,13},{9,1},{13,5},{2,10},{6,14},... | collective-permute-start | bytes 1572872 | tf_op jit(solution)/shard_map/ppermute | solution.py:127
  55.7 0.7 dynamic_slice.69
  56.4 5.9 %fusion.8 = f32[128,1024]{1,0:T(8,128)S(1)} fusion(f32[128,2048]{1,0:T(8,128)S(1)} %fusion.38, f32[2048,4096]{1,0:T(8,128)} %param.8, s32[]{:T(128)S(6)} %select_n.83), kind=kOutput, calls=%fused_computation.8 | convolution fusion | flops 1610612736 | bytes 9961476 | tf_op jit(solution)/shard_map/dot_general | solution.py:97
  62.3 5.5 %collective-permute-done.9 = f32[1,128,1024]{2,1,0:T(8,128)S(1)} collective-permute-done((f32[1,128,1024]{2,1,0:T(8,128)S(1)}, f32[1,128,1024]{2,1,0:T(8,128)S(1)}, u32[]{:S(2)}, u32[]{:S(2)}) %collective-permute-start.9) | collective-permute-done | bytes 524320 | tf_op jit(solution)/shard_map/ppermute | solution.py:127
  67.8 1.3 %fusion.26 = f32[128,1024]{1,0:T(8,128)S(1)} fusion(f32[1,128,1024]{2,1,0:T(8,128)S(1)} %collective-permute-done.9, f32[128,1024]{1,0:T(8,128)S(1)} %fusion.8, f32[128,1024]{1,0:T(8,128)} %collective-permute-done.7, f32[1024]{0:T(1024)S(1)} %dynamic_slice.69), kind=kLoop, calls=%fused_computation.29 | loop fusion | flops 1441792 | bytes 2101248 | tf_op jit(solution)/shard_map/mul | solution.py:131
  69.1 0.1 collective-permute-start.11
  69.2 1.8 %collective-permute-start.10 = (f32[1,128,1024]{2,1,0:T(8,128)S(1)}, f32[1,128,1024]{2,1,0:T(8,128)S(1)}, u32[]{:S(2)}, u32[]{:S(2)}) collective-permute-start(f32[1,128,1024]{2,1,0:T(8,128)S(1)} %bitcast.111), channel_id=1, source_target_pairs={{0,8},{4,12},{8,0},{12,4},{1,9},{5,13},{9,1},{13,5},{2,10},{6,14},... | collective-permute-start | bytes 1572872 | tf_op jit(solution)/shard_map/ppermute | solution.py:136
  71.0 0.1 collective-permute-done.11
  71.1 8.7 %fusion.2 = f32[128,2048]{1,0:T(8,128)S(1)} fusion(f32[4096,2048]{1,0:T(8,128)} %param.10, s32[]{:T(128)S(6)} %select_n.94, f32[128,1024]{1,0:T(8,128)S(1)} %collective-permute-done.11, f32[128,1024]{1,0:T(8,128)S(1)} %fusion.26, pred[]{:T(512)S(6)} %eq.4), kind=kOutput, calls=%fused_computation.2 | convolution fusion | flops 3222011904 | bytes 18874372 | tf_op jit(solution)/shard_map/dot_general | solution.py:146
  79.8 3.7 %collective-permute-done.10 = f32[1,128,1024]{2,1,0:T(8,128)S(1)} collective-permute-done((f32[1,128,1024]{2,1,0:T(8,128)S(1)}, f32[1,128,1024]{2,1,0:T(8,128)S(1)}, u32[]{:S(2)}, u32[]{:S(2)}) %collective-permute-start.10) | collective-permute-done | bytes 524320 | tf_op jit(solution)/shard_map/ppermute | solution.py:136
  83.5 1.9 %collective-permute-done.12 = f32[1,128,1024]{2,1,0:T(8,128)S(1)} collective-permute-done((f32[1,128,1024]{2,1,0:T(8,128)S(1)}, f32[1,128,1024]{2,1,0:T(8,128)S(1)}, u32[]{:S(2)}, u32[]{:S(2)}) %collective-permute-start.12) | collective-permute-done | bytes 524320 | tf_op jit(solution)/shard_map/ppermute | solution.py:154
  85.4 8.7 %fusion = f32[128,2048]{1,0:T(8,128)S(1)} fusion(f32[4096,2048]{1,0:T(8,128)} %param.10, s32[]{:T(128)S(6)} %select_n.88, f32[128,1024]{1,0:T(8,128)S(1)} %bitcast.115, f32[128,1024]{1,0:T(8,128)S(1)} %bitcast.114, pred[]{:T(512)S(6)} %eq.4), kind=kOutput, calls=%fused_computation | convolution fusion | flops 3222011904 | bytes 18874372 | tf_op jit(solution)/shard_map/dot_general | solution.py:146
  94.1 0.1 add.151
  94.3 0.6 collective-permute-start.13
  94.9 7.8 %collective-permute-done.13 = f32[2,16,2048]{2,1,0:T(8,128)S(1)} collective-permute-done((f32[2,16,2048]{2,1,0:T(8,128)S(1)}, f32[2,16,2048]{2,1,0:T(8,128)S(1)}, u32[]{:S(2)}, u32[]{:S(2)}) %collective-permute-start.13) | collective-permute-done | bytes 262176 | tf_op jit(solution)/shard_map/ppermute | solution.py:37
  102.8 0.6 collective-permute-start.15
  103.4 3.5 %collective-permute-start.14 = (f32[1,16,2048]{2,1,0:T(8,128)S(1)}, f32[1,16,2048]{2,1,0:T(8,128)S(1)}, u32[]{:S(2)}, u32[]{:S(2)}) collective-permute-start(f32[1,16,2048]{2,1,0:T(8,128)S(1)} %get-tuple-element.11), channel_id=1, source_target_pairs={{0,2},{1,3},{2,0},{3,1},{4,6},{5,7},{6,4},{7,5},{8,10},{9,11},{10,... | collective-permute-start | bytes 393224 | tf_op jit(solution)/shard_map/ppermute | solution.py:37
  106.9 4.4 %collective-permute-done.14 = f32[1,16,2048]{2,1,0:T(8,128)S(1)} collective-permute-done((f32[1,16,2048]{2,1,0:T(8,128)S(1)}, f32[1,16,2048]{2,1,0:T(8,128)S(1)}, u32[]{:S(2)}, u32[]{:S(2)}) %collective-permute-start.14) | collective-permute-done | bytes 131104 | tf_op jit(solution)/shard_map/ppermute | solution.py:37
  111.3 1.9 %collective-permute-done.15 = f32[2,16,2048]{2,1,0:T(8,128)S(1)} collective-permute-done((f32[2,16,2048]{2,1,0:T(8,128)S(1)}, f32[2,16,2048]{2,1,0:T(8,128)S(1)}, u32[]{:S(2)}, u32[]{:S(2)}) %collective-permute-start.15) | collective-permute-done | bytes 262176 | tf_op jit(solution)/shard_map/ppermute | solution.py:37
  113.2 1.6 %collective-permute-start.16 = (f32[1,16,2048]{2,1,0:T(8,128)S(1)}, f32[1,16,2048]{2,1,0:T(8,128)S(1)}, u32[]{:S(2)}, u32[]{:S(2)}) collective-permute-start(f32[1,16,2048]{2,1,0:T(8,128)S(1)} %get-tuple-element.10), channel_id=1, source_target_pairs={{0,2},{1,3},{2,0},{3,1},{4,6},{5,7},{6,4},{7,5},{8,10},{9,11},{10,... | collective-permute-start | bytes 393224 | tf_op jit(solution)/shard_map/ppermute | solution.py:37
  114.8 4.8 %collective-permute-done.16 = f32[1,16,2048]{2,1,0:T(8,128)S(1)} collective-permute-done((f32[1,16,2048]{2,1,0:T(8,128)S(1)}, f32[1,16,2048]{2,1,0:T(8,128)S(1)}, u32[]{:S(2)}, u32[]{:S(2)}) %collective-permute-start.16) | collective-permute-done | bytes 131104 | tf_op jit(solution)/shard_map/ppermute | solution.py:37
  119.7 0.1 collective-permute-start.17
  119.8 1.8 %collective-permute-start.18 = (f32[8,2048]{1,0:T(8,128)S(1)}, f32[8,2048]{1,0:T(8,128)S(1)}, u32[]{:S(2)}, u32[]{:S(2)}) collective-permute-start(f32[8,2048]{1,0:T(8,128)S(1)} %get-tuple-element.22), channel_id=1, source_target_pairs={{0,8},{4,12},{8,0},{12,4},{1,9},{5,13},{9,1},{13,5},{2,10},{6,14},... | collective-permute-start | bytes 196616 | tf_op jit(solution)/shard_map/ppermute | solution.py:46
  121.6 0.1 collective-permute-start.19
  121.7 2.6 %collective-permute-done.18 = f32[8,2048]{1,0:T(8,128)S(1)} collective-permute-done((f32[8,2048]{1,0:T(8,128)S(1)}, f32[8,2048]{1,0:T(8,128)S(1)}, u32[]{:S(2)}, u32[]{:S(2)}) %collective-permute-start.18) | collective-permute-done | bytes 65568 | tf_op jit(solution)/shard_map/ppermute | solution.py:46
  124.3 1.3 %collective-permute-done.19 = f32[8,2048]{1,0:T(8,128)S(1)} collective-permute-done((f32[8,2048]{1,0:T(8,128)S(1)}, f32[8,2048]{1,0:T(8,128)S(1)}, u32[]{:S(2)}, u32[]{:S(2)}) %collective-permute-start.19) | collective-permute-done | bytes 65568 | tf_op jit(solution)/shard_map/ppermute | solution.py:46
  125.8 0.8 multiply_add_fusion
  (36 shorter events, 0.6 us)
Async XLA Ops:
  3.8 4.9 %collective-permute-start.2 = (f32[8,2048]{1,0:T(8,128)S(1)}, f32[8,2048]{1,0:T(8,128)S(1)}, u32[]{:S(2)}, u32[]{:S(2)}) collective-permute-start(f32[8,2048]{1,0:T(8,128)S(1)} %get-tuple-element.29), channel_id=1, source_target_pairs={{0,12},{4,8},{8,4},{12,0},{1,13},{5,9},{9,5},{13,1},{2,14},{6,10},... | collective-permute-start | bytes 196616 | tf_op jit(solution)/shard_map/ppermute | solution.py:46
  6.3 2.5 %collective-permute-start = (f32[8,2048]{1,0:T(8,128)S(1)}, f32[8,2048]{1,0:T(8,128)S(1)}, u32[]{:S(2)}, u32[]{:S(2)}) collective-permute-start(f32[8,2048]{1,0:T(8,128)S(1)} %get-tuple-element.31), channel_id=1, source_target_pairs={{0,4},{4,0},{8,12},{12,8},{1,5},{5,1},{9,13},{13,9},{2,6},{6,2},{1... | collective-permute-start | bytes 196616 | tf_op jit(solution)/shard_map/ppermute | solution.py:46
  6.9 4.3 %collective-permute-start.1 = (f32[8,2048]{1,0:T(8,128)S(1)}, f32[8,2048]{1,0:T(8,128)S(1)}, u32[]{:S(2)}, u32[]{:S(2)}) collective-permute-start(f32[8,2048]{1,0:T(8,128)S(1)} %get-tuple-element.30), channel_id=1, source_target_pairs={{0,8},{4,12},{8,0},{12,4},{1,9},{5,13},{9,1},{13,5},{2,10},{6,14},... | collective-permute-start | bytes 196616 | tf_op jit(solution)/shard_map/ppermute | solution.py:46
  11.3 12.2 %collective-permute-start.3 = (f32[1,16,2048]{2,1,0:T(8,128)S(1)}, f32[1,16,2048]{2,1,0:T(8,128)S(1)}, u32[]{:S(2)}, u32[]{:S(2)}) collective-permute-start(f32[1,16,2048]{2,1,0:T(8,128)S(1)} %fusion.43), channel_id=1, source_target_pairs={{0,2},{1,3},{2,0},{3,1},{4,6},{5,7},{6,4},{7,5},{8,10},{9,11},{10,... | collective-permute-start | bytes 393224 | tf_op jit(solution)/shard_map/ppermute | solution.py:24
  14.0 11.3 %collective-permute-start.5 = (f32[1,16,2048]{2,1,0:T(8,128)S(1)}, f32[1,16,2048]{2,1,0:T(8,128)S(1)}, u32[]{:S(2)}, u32[]{:S(2)}) collective-permute-start(f32[1,16,2048]{2,1,0:T(8,128)S(1)} %fusion.42), channel_id=1, source_target_pairs={{0,2},{1,3},{2,0},{3,1},{4,6},{5,7},{6,4},{7,5},{8,10},{9,11},{10,... | collective-permute-start | bytes 393224 | tf_op jit(solution)/shard_map/ppermute | solution.py:24
  23.5 9.3 %collective-permute-start.4 = (f32[2,16,2048]{2,1,0:T(8,128)S(1)}, f32[2,16,2048]{2,1,0:T(8,128)S(1)}, u32[]{:S(2)}, u32[]{:S(2)}) collective-permute-start(f32[2,16,2048]{2,1,0:T(8,128)S(1)} %pad_maximum_fusion.1), channel_id=1, source_target_pairs={{0,1},{1,0},{2,3},{3,2},{4,5},{5,4},{6,7},{7,6},{8,9},{9,8},{10,11... | collective-permute-start | bytes 786440 | tf_op jit(solution)/shard_map/ppermute | solution.py:24
  25.2 11.1 %collective-permute-start.6 = (f32[2,16,2048]{2,1,0:T(8,128)S(1)}, f32[2,16,2048]{2,1,0:T(8,128)S(1)}, u32[]{:S(2)}, u32[]{:S(2)}) collective-permute-start(f32[2,16,2048]{2,1,0:T(8,128)S(1)} %pad_maximum_fusion.2), channel_id=1, source_target_pairs={{0,1},{1,0},{2,3},{3,2},{4,5},{5,4},{6,7},{7,6},{8,9},{9,8},{10,11... | collective-permute-start | bytes 786440 | tf_op jit(solution)/shard_map/ppermute | solution.py:24
  45.4 6.6 %collective-permute-start.8 = (f32[128,1024]{1,0:T(8,128)S(1)}, f32[128,1024]{1,0:T(8,128)}, u32[]{:S(2)}, u32[]{:S(2)}) collective-permute-start(f32[128,1024]{1,0:T(8,128)S(1)} %slice_select_fusion), channel_id=1, source_target_pairs={{0,4},{4,0},{8,12},{12,8},{1,5},{5,1},{9,13},{13,9},{2,6},{6,2},{1... | collective-permute-start | bytes 1572872 | tf_op jit(solution)/shard_map/ppermute | solution.py:123
  45.5 80.3 %copy-start = (f32[8,8192]{1,0:T(8,128)S(1)}, f32[8,8192]{1,0:T(8,128)}, u32[]{:S(2)}) copy-start(f32[8,8192]{1,0:T(8,128)} %x_ref.1) | copy-start | bytes 786436
  45.5 80.3 %copy-start.1 = (f32[8192]{0:T(1024)S(1)}, f32[8192]{0:T(1024)}, u32[]{:S(2)}) copy-start(f32[8192]{0:T(1024)} %param.11) | copy-start | bytes 98308
  51.5 10.9 %collective-permute-start.7 = (f32[128,1024]{1,0:T(8,128)S(1)}, f32[128,1024]{1,0:T(8,128)}, u32[]{:S(2)}, u32[]{:S(2)}) collective-permute-start(f32[128,1024]{1,0:T(8,128)S(1)} %fusion.6), channel_id=1, source_target_pairs={{0,4},{4,0},{8,12},{12,8},{1,5},{5,1},{9,13},{13,9},{2,6},{6,2},{1... | collective-permute-start | bytes 1572872 | tf_op jit(solution)/shard_map/ppermute | solution.py:123
  53.1 14.7 %collective-permute-start.9 = (f32[1,128,1024]{2,1,0:T(8,128)S(1)}, f32[1,128,1024]{2,1,0:T(8,128)S(1)}, u32[]{:S(2)}, u32[]{:S(2)}) collective-permute-start(f32[1,128,1024]{2,1,0:T(8,128)S(1)} %add_bitcast_fusion), channel_id=1, source_target_pairs={{0,8},{4,12},{8,0},{12,4},{1,9},{5,13},{9,1},{13,5},{2,10},{6,14},... | collective-permute-start | bytes 1572872 | tf_op jit(solution)/shard_map/ppermute | solution.py:127
  69.1 2.0 %collective-permute-start.11 = (f32[128,1024]{1,0:T(8,128)S(1)}, f32[128,1024]{1,0:T(8,128)S(1)}, u32[]{:S(2)}, u32[]{:S(2)}) collective-permute-start(f32[128,1024]{1,0:T(8,128)S(1)} %fusion.26), channel_id=1, source_target_pairs={{0,4},{4,0},{8,12},{12,8},{1,5},{5,1},{9,13},{13,9},{2,6},{6,2},{1... | collective-permute-start | bytes 1572872 | tf_op jit(solution)/shard_map/ppermute | solution.py:132
  69.2 14.3 %collective-permute-start.10 = (f32[1,128,1024]{2,1,0:T(8,128)S(1)}, f32[1,128,1024]{2,1,0:T(8,128)S(1)}, u32[]{:S(2)}, u32[]{:S(2)}) collective-permute-start(f32[1,128,1024]{2,1,0:T(8,128)S(1)} %bitcast.111), channel_id=1, source_target_pairs={{0,8},{4,12},{8,0},{12,4},{1,9},{5,13},{9,1},{13,5},{2,10},{6,14},... | collective-permute-start | bytes 1572872 | tf_op jit(solution)/shard_map/ppermute | solution.py:136
  83.5 1.9 %collective-permute-start.12 = (f32[1,128,1024]{2,1,0:T(8,128)S(1)}, f32[1,128,1024]{2,1,0:T(8,128)S(1)}, u32[]{:S(2)}, u32[]{:S(2)}) collective-permute-start(f32[1,128,1024]{2,1,0:T(8,128)S(1)} %collective-permute-done.10), channel_id=1, source_target_pairs={{0,4},{4,0},{8,12},{12,8},{1,5},{5,1},{9,13},{13,9},{2,6},{6,2},{1... | collective-permute-start | bytes 1572872 | tf_op jit(solution)/shard_map/ppermute | solution.py:154
  94.3 8.4 %collective-permute-start.13 = (f32[2,16,2048]{2,1,0:T(8,128)S(1)}, f32[2,16,2048]{2,1,0:T(8,128)S(1)}, u32[]{:S(2)}, u32[]{:S(2)}) collective-permute-start(f32[2,16,2048]{2,1,0:T(8,128)S(1)} %pad_maximum_fusion.3), channel_id=1, source_target_pairs={{0,1},{1,0},{2,3},{3,2},{4,5},{5,4},{6,7},{7,6},{8,9},{9,8},{10,11... | collective-permute-start | bytes 786440 | tf_op jit(solution)/shard_map/ppermute | solution.py:37
  102.8 10.4 %collective-permute-start.15 = (f32[2,16,2048]{2,1,0:T(8,128)S(1)}, f32[2,16,2048]{2,1,0:T(8,128)S(1)}, u32[]{:S(2)}, u32[]{:S(2)}) collective-permute-start(f32[2,16,2048]{2,1,0:T(8,128)S(1)} %pad_maximum_fusion.4), channel_id=1, source_target_pairs={{0,1},{1,0},{2,3},{3,2},{4,5},{5,4},{6,7},{7,6},{8,9},{9,8},{10,11... | collective-permute-start | bytes 786440 | tf_op jit(solution)/shard_map/ppermute | solution.py:37
  103.4 7.8 %collective-permute-start.14 = (f32[1,16,2048]{2,1,0:T(8,128)S(1)}, f32[1,16,2048]{2,1,0:T(8,128)S(1)}, u32[]{:S(2)}, u32[]{:S(2)}) collective-permute-start(f32[1,16,2048]{2,1,0:T(8,128)S(1)} %get-tuple-element.11), channel_id=1, source_target_pairs={{0,2},{1,3},{2,0},{3,1},{4,6},{5,7},{6,4},{7,5},{8,10},{9,11},{10,... | collective-permute-start | bytes 393224 | tf_op jit(solution)/shard_map/ppermute | solution.py:37
  113.2 6.4 %collective-permute-start.16 = (f32[1,16,2048]{2,1,0:T(8,128)S(1)}, f32[1,16,2048]{2,1,0:T(8,128)S(1)}, u32[]{:S(2)}, u32[]{:S(2)}) collective-permute-start(f32[1,16,2048]{2,1,0:T(8,128)S(1)} %get-tuple-element.10), channel_id=1, source_target_pairs={{0,2},{1,3},{2,0},{3,1},{4,6},{5,7},{6,4},{7,5},{8,10},{9,11},{10,... | collective-permute-start | bytes 393224 | tf_op jit(solution)/shard_map/ppermute | solution.py:37
  119.7 2.0 %collective-permute-start.17 = (f32[8,2048]{1,0:T(8,128)S(1)}, f32[8,2048]{1,0:T(8,128)S(1)}, u32[]{:S(2)}, u32[]{:S(2)}) collective-permute-start(f32[8,2048]{1,0:T(8,128)S(1)} %get-tuple-element.23), channel_id=1, source_target_pairs={{0,4},{4,0},{8,12},{12,8},{1,5},{5,1},{9,13},{13,9},{2,6},{6,2},{1... | collective-permute-start | bytes 196616 | tf_op jit(solution)/shard_map/ppermute | solution.py:46
  119.8 4.5 %collective-permute-start.18 = (f32[8,2048]{1,0:T(8,128)S(1)}, f32[8,2048]{1,0:T(8,128)S(1)}, u32[]{:S(2)}, u32[]{:S(2)}) collective-permute-start(f32[8,2048]{1,0:T(8,128)S(1)} %get-tuple-element.22), channel_id=1, source_target_pairs={{0,8},{4,12},{8,0},{12,4},{1,9},{5,13},{9,1},{13,5},{2,10},{6,14},... | collective-permute-start | bytes 196616 | tf_op jit(solution)/shard_map/ppermute | solution.py:46
  121.6 4.0 %collective-permute-start.19 = (f32[8,2048]{1,0:T(8,128)S(1)}, f32[8,2048]{1,0:T(8,128)S(1)}, u32[]{:S(2)}, u32[]{:S(2)}) collective-permute-start(f32[8,2048]{1,0:T(8,128)S(1)} %get-tuple-element.21), channel_id=1, source_target_pairs={{0,12},{4,8},{8,4},{12,0},{1,13},{5,9},{9,5},{13,1},{2,14},{6,10},... | collective-permute-start | bytes 196616 | tf_op jit(solution)/shard_map/ppermute | solution.py:46

commit v17 on v16

--- a/solution.py
+++ b/solution.py
@@ -121,14 +121,16 @@
             other = lax.optimization_barrier(up_block(1, lhs))
             mine = lax.optimization_barrier(up_block(0, lhs))
         held[d_even] = mine + lax.ppermute(other, "row", _pairs(n_row, 1))
+        if not d_even:
+            bias_q = lax.dynamic_slice_in_dim(up_bias, r * quarter, quarter)
+            held[0] = lax.optimization_barrier(held[0] + bias_q[None, :])
     flip = 2
     while flip < n_row:
         sent = [d for d in sorted(held) if d & flip]
         got = lax.ppermute(jnp.stack([held[d] for d in sent]), "row", _pairs(n_row, flip))
         held = {d ^ flip: held[d ^ flip] + got[i] for i, d in enumerate(sent)}
         flip *= 2
-    bias_q = lax.dynamic_slice_in_dim(up_bias, r * quarter, quarter)
-    acts = {0: jax.nn.gelu(held[0] + bias_q[None, :], approximate=True)}
+    acts = {0: jax.nn.gelu(held[0], approximate=True)}
     acts[1] = lax.ppermute(acts[0], "row", _pairs(n_row, 1))
     flip = 2
     while flip < n_row:

time: 127 us -> 126 us (level)
  other arithmetic: 5.47 us -> 3.41 us
  waiting for transfers between devices: 59.4 us -> 60.8 us
  transfers between devices with their start and end apart: 20 -> 20, of which waited for: 16 -> 16; matrix products, arithmetic and copies ran while one was open for 18% -> 17% of each run, Pallas kernels for 0% -> 0%
where the time goes in v17:
time: 126 us; the launch traced here: 125 us
  waiting for transfers between devices  60.8 us (48%)
  matrix products  38.2 us (30%)
  starting transfers between devices  19.6 us (16%)
  other arithmetic  3.41 us (3%)
  Pallas kernels  1.96 us (2%)
    ppermute x4, waiting for transfers between devices, _gather_rel(): lax.ppermute(jnp.stack([held[k] for k in keys]), axis, _pairs(n, flip))  22.1 us
    ppermute x4, waiting for transfers between devices, _scatter_rel(): lax.ppermute(jnp.stack([held[d] for d in sent]), axis, _pairs(n, flip))  18.8 us
    dot_general x2, matrix products, down_pair(): jnp.dot(pair, w, precision=lax.Precision.HIGH, preferred_element_type=jnp...  17.4 us
    dot_general x2, matrix products, up_block(): jnp.dot(lhs, w, precision=lax.Precision.HIGH, preferred_element_type=jnp....  11.9 us
    dot_general x1, matrix products, up_pair(): jnp.dot(lhs, w, precision=lax.Precision.HIGH, preferred_element_type=jnp....  8.88 us
    ppermute x6, waiting for transfers between devices, _exchange_abs(): got.append(lax.ppermute(blocks[idx ^ d], axis, _pairs(n, d)))  7.93 us
    ppermute x4, starting transfers between devices, _scatter_rel(): lax.ppermute(jnp.stack([held[d] for d in sent]), axis, _pairs(n, flip))  6.53 us
    ppermute x1, waiting for transfers between devices, local(): lax.ppermute(jnp.stack([held[d] for d in sent]), 'row', _pairs(n_row, flip))  6.12 us
  transfers between devices with their start and end apart: 20, of which 16 were waited for; matrix products, arithmetic and copies ran while one was open for 17% of the time, Pallas kernels for 0%

profile of v17, /device:TPU:0, one launch (start us, length us, event | category | flops | bytes accessed | tf_op | source)
XLA Modules:
  0.0 125.2 jit_solution(1660167821301615824)
XLA Ops:
  0.0 2.0 %shard_map.64 = f32[8,8192]{1,0:T(8,128)} custom-call(f32[8,8192]{1,0:T(8,128)} %x_ref.1), custom_call_target="tpu_custom_call" | custom-call | flops 393216 | bytes 524288 | tf_op jit(solution)/shard_map/pallas_call | solution.py:61
  2.0 0.8 fusion.50
  2.8 1.0 multiply_add_fusion.1
  3.8 2.4 %collective-permute-start.2 = (f32[8,2048]{1,0:T(8,128)S(1)}, f32[8,2048]{1,0:T(8,128)S(1)}, u32[]{:S(2)}, u32[]{:S(2)}) collective-permute-start(f32[8,2048]{1,0:T(8,128)S(1)} %get-tuple-element.29), channel_id=1, source_target_pairs={{0,12},{4,8},{8,4},{12,0},{1,13},{5,9},{9,5},{13,1},{2,14},{6,10},... | collective-permute-start | bytes 196616 | tf_op jit(solution)/shard_map/ppermute | solution.py:46
  6.3 0.6 collective-permute-start.1
  7.0 1.8 %collective-permute-done.2 = f32[8,2048]{1,0:T(8,128)S(1)} collective-permute-done((f32[8,2048]{1,0:T(8,128)S(1)}, f32[8,2048]{1,0:T(8,128)S(1)}, u32[]{:S(2)}, u32[]{:S(2)}) %collective-permute-start.2) | collective-permute-done | bytes 65568 | tf_op jit(solution)/shard_map/ppermute | solution.py:46
  8.8 2.2 %collective-permute-done.1 = f32[8,2048]{1,0:T(8,128)S(1)} collective-permute-done((f32[8,2048]{1,0:T(8,128)S(1)}, f32[8,2048]{1,0:T(8,128)S(1)}, u32[]{:S(2)}, u32[]{:S(2)}) %collective-permute-start.1) | collective-permute-done | bytes 65568 | tf_op jit(solution)/shard_map/ppermute | solution.py:46
  11.0 2.8 %collective-permute-start.3 = (f32[1,16,2048]{2,1,0:T(8,128)S(1)}, f32[1,16,2048]{2,1,0:T(8,128)S(1)}, u32[]{:S(2)}, u32[]{:S(2)}) collective-permute-start(f32[1,16,2048]{2,1,0:T(8,128)S(1)} %fusion.42), channel_id=1, source_target_pairs={{0,2},{1,3},{2,0},{3,1},{4,6},{5,7},{6,4},{7,5},{8,10},{9,11},{10,... | collective-permute-start | bytes 393224 | tf_op jit(solution)/shard_map/ppermute | solution.py:24
  13.9 0.2 collective-permute-start.5
  14.1 9.9 %collective-permute-done.3 = f32[1,16,2048]{2,1,0:T(8,128)S(1)} collective-permute-done((f32[1,16,2048]{2,1,0:T(8,128)S(1)}, f32[1,16,2048]{2,1,0:T(8,128)S(1)}, u32[]{:S(2)}, u32[]{:S(2)}) %collective-permute-start.3) | collective-permute-done | bytes 131104 | tf_op jit(solution)/shard_map/ppermute | solution.py:24
  24.0 0.1 collective-permute-start.4
  24.1 1.9 %collective-permute-done.5 = f32[1,16,2048]{2,1,0:T(8,128)S(1)} collective-permute-done((f32[1,16,2048]{2,1,0:T(8,128)S(1)}, f32[1,16,2048]{2,1,0:T(8,128)S(1)}, u32[]{:S(2)}, u32[]{:S(2)}) %collective-permute-start.5) | collective-permute-done | bytes 131104 | tf_op jit(solution)/shard_map/ppermute | solution.py:24
  26.0 0.7 collective-permute-start.6
  26.7 6.6 %collective-permute-done.4 = f32[2,16,2048]{2,1,0:T(8,128)S(1)} collective-permute-done((f32[2,16,2048]{2,1,0:T(8,128)S(1)}, f32[2,16,2048]{2,1,0:T(8,128)S(1)}, u32[]{:S(2)}, u32[]{:S(2)}) %collective-permute-start.4) | collective-permute-done | bytes 262176 | tf_op jit(solution)/shard_map/ppermute | solution.py:24
  33.4 3.8 %collective-permute-done.6 = f32[2,16,2048]{2,1,0:T(8,128)S(1)} collective-permute-done((f32[2,16,2048]{2,1,0:T(8,128)S(1)}, f32[2,16,2048]{2,1,0:T(8,128)S(1)}, u32[]{:S(2)}, u32[]{:S(2)}) %collective-permute-start.6) | collective-permute-done | bytes 262176 | tf_op jit(solution)/shard_map/ppermute | solution.py:24
  37.2 8.9 %fusion.4 = f32[128,2048]{1,0:T(8,128)S(1)} fusion(f32[128,2048]{1,0:T(8,128)S(1)} %fusion.37, f32[2048,4096]{1,0:T(8,128)} %param.8, s32[]{:T(128)S(6)} %select_n.88), kind=kOutput, calls=%fused_computation.4 | convolution fusion | flops 3221225472 | bytes 18874372 | tf_op jit(solution)/shard_map/dot_general | solution.py:108
  46.2 0.1 collective-permute-start.8
  46.3 0.7 dynamic_slice.68
  47.0 5.9 %fusion.6 = f32[128,1024]{1,0:T(8,128)S(1)} fusion(f32[128,2048]{1,0:T(8,128)S(1)} %fusion.37, f32[2048,4096]{1,0:T(8,128)} %param.8, s32[]{:T(128)S(6)} %select_n.84), kind=kOutput, calls=%fused_computation.6 | convolution fusion | flops 1610612736 | bytes 9961476 | tf_op jit(solution)/shard_map/dot_general | solution.py:97
  52.9 0.5 collective-permute-start.7
  53.5 0.1 add_bitcast_fusion
  53.6 1.8 %collective-permute-start.9 = (f32[1,128,1024]{2,1,0:T(8,128)S(1)}, f32[1,128,1024]{2,1,0:T(8,128)S(1)}, u32[]{:S(2)}, u32[]{:S(2)}) collective-permute-start(f32[1,128,1024]{2,1,0:T(8,128)S(1)} %add_bitcast_fusion), channel_id=1, source_target_pairs={{0,8},{4,12},{8,0},{12,4},{1,9},{5,13},{9,1},{13,5},{2,10},{6,14},... | collective-permute-start | bytes 1572872 | tf_op jit(solution)/shard_map/ppermute | solution.py:130
  55.3 5.9 %fusion.8 = f32[128,1024]{1,0:T(8,128)S(1)} fusion(f32[128,2048]{1,0:T(8,128)S(1)} %fusion.37, f32[2048,4096]{1,0:T(8,128)} %param.8, s32[]{:T(128)S(6)} %select_n.83), kind=kOutput, calls=%fused_computation.8 | convolution fusion | flops 1610612736 | bytes 9961476 | tf_op jit(solution)/shard_map/dot_general | solution.py:97
  61.3 0.1 add_add_fusion
  61.4 6.1 %collective-permute-done.9 = f32[1,128,1024]{2,1,0:T(8,128)S(1)} collective-permute-done((f32[1,128,1024]{2,1,0:T(8,128)S(1)}, f32[1,128,1024]{2,1,0:T(8,128)S(1)}, u32[]{:S(2)}, u32[]{:S(2)}) %collective-permute-start.9) | collective-permute-done | bytes 524320 | tf_op jit(solution)/shard_map/ppermute | solution.py:130
  67.5 0.2 fusion.26
  67.7 0.1 collective-permute-start.11
  67.8 1.8 %collective-permute-start.10 = (f32[1,128,1024]{2,1,0:T(8,128)S(1)}, f32[1,128,1024]{2,1,0:T(8,128)S(1)}, u32[]{:S(2)}, u32[]{:S(2)}) collective-permute-start(f32[1,128,1024]{2,1,0:T(8,128)S(1)} %bitcast.109), channel_id=1, source_target_pairs={{0,8},{4,12},{8,0},{12,4},{1,9},{5,13},{9,1},{13,5},{2,10},{6,14},... | collective-permute-start | bytes 1572872 | tf_op jit(solution)/shard_map/ppermute | solution.py:138
  69.5 0.1 collective-permute-done.11
  69.7 8.7 %fusion.2 = f32[128,2048]{1,0:T(8,128)S(1)} fusion(f32[4096,2048]{1,0:T(8,128)} %param.10, s32[]{:T(128)S(6)} %select_n.94, f32[128,1024]{1,0:T(8,128)S(1)} %collective-permute-done.11, f32[128,1024]{1,0:T(8,128)S(1)} %fusion.26, pred[]{:T(512)S(6)} %eq.4), kind=kOutput, calls=%fused_computation.2 | convolution fusion | flops 3222011904 | bytes 18874372 | tf_op jit(solution)/shard_map/dot_general | solution.py:148
  78.4 3.7 %collective-permute-done.10 = f32[1,128,1024]{2,1,0:T(8,128)S(1)} collective-permute-done((f32[1,128,1024]{2,1,0:T(8,128)S(1)}, f32[1,128,1024]{2,1,0:T(8,128)S(1)}, u32[]{:S(2)}, u32[]{:S(2)}) %collective-permute-start.10) | collective-permute-done | bytes 524320 | tf_op jit(solution)/shard_map/ppermute | solution.py:138
  82.1 1.9 %collective-permute-done.12 = f32[1,128,1024]{2,1,0:T(8,128)S(1)} collective-permute-done((f32[1,128,1024]{2,1,0:T(8,128)S(1)}, f32[1,128,1024]{2,1,0:T(8,128)S(1)}, u32[]{:S(2)}, u32[]{:S(2)}) %collective-permute-start.12) | collective-permute-done | bytes 524320 | tf_op jit(solution)/shard_map/ppermute | solution.py:156
  84.0 8.7 %fusion = f32[128,2048]{1,0:T(8,128)S(1)} fusion(f32[4096,2048]{1,0:T(8,128)} %param.10, s32[]{:T(128)S(6)} %select_n.88, f32[128,1024]{1,0:T(8,128)S(1)} %bitcast.113, f32[128,1024]{1,0:T(8,128)S(1)} %bitcast.112, pred[]{:T(512)S(6)} %eq.4), kind=kOutput, calls=%fused_computation | convolution fusion | flops 3222011904 | bytes 18874372 | tf_op jit(solution)/shard_map/dot_general | solution.py:148
  92.7 0.1 add.151
  92.9 0.7 collective-permute-start.13
  93.6 7.7 %collective-permute-done.13 = f32[2,16,2048]{2,1,0:T(8,128)S(1)} collective-permute-done((f32[2,16,2048]{2,1,0:T(8,128)S(1)}, f32[2,16,2048]{2,1,0:T(8,128)S(1)}, u32[]{:S(2)}, u32[]{:S(2)}) %collective-permute-start.13) | collective-permute-done | bytes 262176 | tf_op jit(solution)/shard_map/ppermute | solution.py:37
  101.4 0.7 collective-permute-start.15
  102.0 3.5 %collective-permute-start.14 = (f32[1,16,2048]{2,1,0:T(8,128)S(1)}, f32[1,16,2048]{2,1,0:T(8,128)S(1)}, u32[]{:S(2)}, u32[]{:S(2)}) collective-permute-start(f32[1,16,2048]{2,1,0:T(8,128)S(1)} %get-tuple-element.11), channel_id=1, source_target_pairs={{0,2},{1,3},{2,0},{3,1},{4,6},{5,7},{6,4},{7,5},{8,10},{9,11},{10,... | collective-permute-start | bytes 393224 | tf_op jit(solution)/shard_map/ppermute | solution.py:37
  105.5 4.3 %collective-permute-done.14 = f32[1,16,2048]{2,1,0:T(8,128)S(1)} collective-permute-done((f32[1,16,2048]{2,1,0:T(8,128)S(1)}, f32[1,16,2048]{2,1,0:T(8,128)S(1)}, u32[]{:S(2)}, u32[]{:S(2)}) %collective-permute-start.14) | collective-permute-done | bytes 131104 | tf_op jit(solution)/shard_map/ppermute | solution.py:37
  109.9 1.9 %collective-permute-done.15 = f32[2,16,2048]{2,1,0:T(8,128)S(1)} collective-permute-done((f32[2,16,2048]{2,1,0:T(8,128)S(1)}, f32[2,16,2048]{2,1,0:T(8,128)S(1)}, u32[]{:S(2)}, u32[]{:S(2)}) %collective-permute-start.15) | collective-permute-done | bytes 262176 | tf_op jit(solution)/shard_map/ppermute | solution.py:37
  111.8 1.7 %collective-permute-start.16 = (f32[1,16,2048]{2,1,0:T(8,128)S(1)}, f32[1,16,2048]{2,1,0:T(8,128)S(1)}, u32[]{:S(2)}, u32[]{:S(2)}) collective-permute-start(f32[1,16,2048]{2,1,0:T(8,128)S(1)} %get-tuple-element.10), channel_id=1, source_target_pairs={{0,2},{1,3},{2,0},{3,1},{4,6},{5,7},{6,4},{7,5},{8,10},{9,11},{10,... | collective-permute-start | bytes 393224 | tf_op jit(solution)/shard_map/ppermute | solution.py:37
  113.5 4.8 %collective-permute-done.16 = f32[1,16,2048]{2,1,0:T(8,128)S(1)} collective-permute-done((f32[1,16,2048]{2,1,0:T(8,128)S(1)}, f32[1,16,2048]{2,1,0:T(8,128)S(1)}, u32[]{:S(2)}, u32[]{:S(2)}) %collective-permute-start.16) | collective-permute-done | bytes 131104 | tf_op jit(solution)/shard_map/ppermute | solution.py:37
  118.4 0.1 collective-permute-start.19
  118.5 1.7 %collective-permute-start.18 = (f32[8,2048]{1,0:T(8,128)S(1)}, f32[8,2048]{1,0:T(8,128)S(1)}, u32[]{:S(2)}, u32[]{:S(2)}) collective-permute-start(f32[8,2048]{1,0:T(8,128)S(1)} %get-tuple-element.22), channel_id=1, source_target_pairs={{0,8},{4,12},{8,0},{12,4},{1,9},{5,13},{9,1},{13,5},{2,10},{6,14},... | collective-permute-start | bytes 196616 | tf_op jit(solution)/shard_map/ppermute | solution.py:46
  120.2 0.2 collective-permute-start.17
  120.3 2.4 %collective-permute-done.19 = f32[8,2048]{1,0:T(8,128)S(1)} collective-permute-done((f32[8,2048]{1,0:T(8,128)S(1)}, f32[8,2048]{1,0:T(8,128)S(1)}, u32[]{:S(2)}, u32[]{:S(2)}) %collective-permute-start.19) | collective-permute-done | bytes 65568 | tf_op jit(solution)/shard_map/ppermute | solution.py:46
  122.7 1.6 %collective-permute-done.18 = f32[8,2048]{1,0:T(8,128)S(1)} collective-permute-done((f32[8,2048]{1,0:T(8,128)S(1)}, f32[8,2048]{1,0:T(8,128)S(1)}, u32[]{:S(2)}, u32[]{:S(2)}) %collective-permute-start.18) | collective-permute-done | bytes 65568 | tf_op jit(solution)/shard_map/ppermute | solution.py:46
  124.4 0.8 multiply_add_fusion
  (37 shorter events, 0.6 us)
Async XLA Ops:
  3.8 4.9 %collective-permute-start.2 = (f32[8,2048]{1,0:T(8,128)S(1)}, f32[8,2048]{1,0:T(8,128)S(1)}, u32[]{:S(2)}, u32[]{:S(2)}) collective-permute-start(f32[8,2048]{1,0:T(8,128)S(1)} %get-tuple-element.29), channel_id=1, source_target_pairs={{0,12},{4,8},{8,4},{12,0},{1,13},{5,9},{9,5},{13,1},{2,14},{6,10},... | collective-permute-start | bytes 196616 | tf_op jit(solution)/shard_map/ppermute | solution.py:46
  6.3 4.7 %collective-permute-start.1 = (f32[8,2048]{1,0:T(8,128)S(1)}, f32[8,2048]{1,0:T(8,128)S(1)}, u32[]{:S(2)}, u32[]{:S(2)}) collective-permute-start(f32[8,2048]{1,0:T(8,128)S(1)} %get-tuple-element.30), channel_id=1, source_target_pairs={{0,8},{4,12},{8,0},{12,4},{1,9},{5,13},{9,1},{13,5},{2,10},{6,14},... | collective-permute-start | bytes 196616 | tf_op jit(solution)/shard_map/ppermute | solution.py:46
  6.9 4.0 %collective-permute-start = (f32[8,2048]{1,0:T(8,128)S(1)}, f32[8,2048]{1,0:T(8,128)S(1)}, u32[]{:S(2)}, u32[]{:S(2)}) collective-permute-start(f32[8,2048]{1,0:T(8,128)S(1)} %get-tuple-element.31), channel_id=1, source_target_pairs={{0,4},{4,0},{8,12},{12,8},{1,5},{5,1},{9,13},{13,9},{2,6},{6,2},{1... | collective-permute-start | bytes 196616 | tf_op jit(solution)/shard_map/ppermute | solution.py:46
  11.0 12.9 %collective-permute-start.3 = (f32[1,16,2048]{2,1,0:T(8,128)S(1)}, f32[1,16,2048]{2,1,0:T(8,128)S(1)}, u32[]{:S(2)}, u32[]{:S(2)}) collective-permute-start(f32[1,16,2048]{2,1,0:T(8,128)S(1)} %fusion.42), channel_id=1, source_target_pairs={{0,2},{1,3},{2,0},{3,1},{4,6},{5,7},{6,4},{7,5},{8,10},{9,11},{10,... | collective-permute-start | bytes 393224 | tf_op jit(solution)/shard_map/ppermute | solution.py:24
  13.9 12.1 %collective-permute-start.5 = (f32[1,16,2048]{2,1,0:T(8,128)S(1)}, f32[1,16,2048]{2,1,0:T(8,128)S(1)}, u32[]{:S(2)}, u32[]{:S(2)}) collective-permute-start(f32[1,16,2048]{2,1,0:T(8,128)S(1)} %fusion.41), channel_id=1, source_target_pairs={{0,2},{1,3},{2,0},{3,1},{4,6},{5,7},{6,4},{7,5},{8,10},{9,11},{10,... | collective-permute-start | bytes 393224 | tf_op jit(solution)/shard_map/ppermute | solution.py:24
  24.0 9.3 %collective-permute-start.4 = (f32[2,16,2048]{2,1,0:T(8,128)S(1)}, f32[2,16,2048]{2,1,0:T(8,128)S(1)}, u32[]{:S(2)}, u32[]{:S(2)}) collective-permute-start(f32[2,16,2048]{2,1,0:T(8,128)S(1)} %pad_maximum_fusion.1), channel_id=1, source_target_pairs={{0,1},{1,0},{2,3},{3,2},{4,5},{5,4},{6,7},{7,6},{8,9},{9,8},{10,11... | collective-permute-start | bytes 786440 | tf_op jit(solution)/shard_map/ppermute | solution.py:24
  26.0 11.1 %collective-permute-start.6 = (f32[2,16,2048]{2,1,0:T(8,128)S(1)}, f32[2,16,2048]{2,1,0:T(8,128)S(1)}, u32[]{:S(2)}, u32[]{:S(2)}) collective-permute-start(f32[2,16,2048]{2,1,0:T(8,128)S(1)} %pad_maximum_fusion.2), channel_id=1, source_target_pairs={{0,1},{1,0},{2,3},{3,2},{4,5},{5,4},{6,7},{7,6},{8,9},{9,8},{10,11... | collective-permute-start | bytes 786440 | tf_op jit(solution)/shard_map/ppermute | solution.py:24
  46.2 7.3 %collective-permute-start.8 = (f32[128,1024]{1,0:T(8,128)S(1)}, f32[128,1024]{1,0:T(8,128)S(1)}, u32[]{:S(2)}, u32[]{:S(2)}) collective-permute-start(f32[128,1024]{1,0:T(8,128)S(1)} %slice_select_fusion), channel_id=1, source_target_pairs={{0,4},{4,0},{8,12},{12,8},{1,5},{5,1},{9,13},{13,9},{2,6},{6,2},{1... | collective-permute-start | bytes 1572872 | tf_op jit(solution)/shard_map/ppermute | solution.py:123
  52.9 71.5 %copy-start = (f32[8,8192]{1,0:T(8,128)S(1)}, f32[8,8192]{1,0:T(8,128)}, u32[]{:S(2)}) copy-start(f32[8,8192]{1,0:T(8,128)} %x_ref.1) | copy-start | bytes 786436
  52.9 71.5 %copy-start.1 = (f32[8192]{0:T(1024)S(1)}, f32[8192]{0:T(1024)}, u32[]{:S(2)}) copy-start(f32[8192]{0:T(1024)} %param.11) | copy-start | bytes 98308
  52.9 8.4 %collective-permute-start.7 = (f32[128,1024]{1,0:T(8,128)S(1)}, f32[128,1024]{1,0:T(8,128)S(1)}, u32[]{:S(2)}, u32[]{:S(2)}) collective-permute-start(f32[128,1024]{1,0:T(8,128)S(1)} %fusion.6), channel_id=1, source_target_pairs={{0,4},{4,0},{8,12},{12,8},{1,5},{5,1},{9,13},{13,9},{2,6},{6,2},{1... | collective-permute-start | bytes 1572872 | tf_op jit(solution)/shard_map/ppermute | solution.py:123
  53.6 13.9 %collective-permute-start.9 = (f32[1,128,1024]{2,1,0:T(8,128)S(1)}, f32[1,128,1024]{2,1,0:T(8,128)S(1)}, u32[]{:S(2)}, u32[]{:S(2)}) collective-permute-start(f32[1,128,1024]{2,1,0:T(8,128)S(1)} %add_bitcast_fusion), channel_id=1, source_target_pairs={{0,8},{4,12},{8,0},{12,4},{1,9},{5,13},{9,1},{13,5},{2,10},{6,14},... | collective-permute-start | bytes 1572872 | tf_op jit(solution)/shard_map/ppermute | solution.py:130
  67.7 2.0 %collective-permute-start.11 = (f32[128,1024]{1,0:T(8,128)S(1)}, f32[128,1024]{1,0:T(8,128)S(1)}, u32[]{:S(2)}, u32[]{:S(2)}) collective-permute-start(f32[128,1024]{1,0:T(8,128)S(1)} %fusion.26), channel_id=1, source_target_pairs={{0,4},{4,0},{8,12},{12,8},{1,5},{5,1},{9,13},{13,9},{2,6},{6,2},{1... | collective-permute-start | bytes 1572872 | tf_op jit(solution)/shard_map/ppermute | solution.py:134
  67.8 14.3 %collective-permute-start.10 = (f32[1,128,1024]{2,1,0:T(8,128)S(1)}, f32[1,128,1024]{2,1,0:T(8,128)S(1)}, u32[]{:S(2)}, u32[]{:S(2)}) collective-permute-start(f32[1,128,1024]{2,1,0:T(8,128)S(1)} %bitcast.109), channel_id=1, source_target_pairs={{0,8},{4,12},{8,0},{12,4},{1,9},{5,13},{9,1},{13,5},{2,10},{6,14},... | collective-permute-start | bytes 1572872 | tf_op jit(solution)/shard_map/ppermute | solution.py:138
  82.1 1.9 %collective-permute-start.12 = (f32[1,128,1024]{2,1,0:T(8,128)S(1)}, f32[1,128,1024]{2,1,0:T(8,128)S(1)}, u32[]{:S(2)}, u32[]{:S(2)}) collective-permute-start(f32[1,128,1024]{2,1,0:T(8,128)S(1)} %collective-permute-done.10), channel_id=1, source_target_pairs={{0,4},{4,0},{8,12},{12,8},{1,5},{5,1},{9,13},{13,9},{2,6},{6,2},{1... | collective-permute-start | bytes 1572872 | tf_op jit(solution)/shard_map/ppermute | solution.py:156
  92.9 8.4 %collective-permute-start.13 = (f32[2,16,2048]{2,1,0:T(8,128)S(1)}, f32[2,16,2048]{2,1,0:T(8,128)S(1)}, u32[]{:S(2)}, u32[]{:S(2)}) collective-permute-start(f32[2,16,2048]{2,1,0:T(8,128)S(1)} %pad_maximum_fusion.3), channel_id=1, source_target_pairs={{0,1},{1,0},{2,3},{3,2},{4,5},{5,4},{6,7},{7,6},{8,9},{9,8},{10,11... | collective-permute-start | bytes 786440 | tf_op jit(solution)/shard_map/ppermute | solution.py:37
  101.4 10.4 %collective-permute-start.15 = (f32[2,16,2048]{2,1,0:T(8,128)S(1)}, f32[2,16,2048]{2,1,0:T(8,128)S(1)}, u32[]{:S(2)}, u32[]{:S(2)}) collective-permute-start(f32[2,16,2048]{2,1,0:T(8,128)S(1)} %pad_maximum_fusion.4), channel_id=1, source_target_pairs={{0,1},{1,0},{2,3},{3,2},{4,5},{5,4},{6,7},{7,6},{8,9},{9,8},{10,11... | collective-permute-start | bytes 786440 | tf_op jit(solution)/shard_map/ppermute | solution.py:37
  102.0 7.8 %collective-permute-start.14 = (f32[1,16,2048]{2,1,0:T(8,128)S(1)}, f32[1,16,2048]{2,1,0:T(8,128)S(1)}, u32[]{:S(2)}, u32[]{:S(2)}) collective-permute-start(f32[1,16,2048]{2,1,0:T(8,128)S(1)} %get-tuple-element.11), channel_id=1, source_target_pairs={{0,2},{1,3},{2,0},{3,1},{4,6},{5,7},{6,4},{7,5},{8,10},{9,11},{10,... | collective-permute-start | bytes 393224 | tf_op jit(solution)/shard_map/ppermute | solution.py:37
  111.8 6.5 %collective-permute-start.16 = (f32[1,16,2048]{2,1,0:T(8,128)S(1)}, f32[1,16,2048]{2,1,0:T(8,128)S(1)}, u32[]{:S(2)}, u32[]{:S(2)}) collective-permute-start(f32[1,16,2048]{2,1,0:T(8,128)S(1)} %get-tuple-element.10), channel_id=1, source_target_pairs={{0,2},{1,3},{2,0},{3,1},{4,6},{5,7},{6,4},{7,5},{8,10},{9,11},{10,... | collective-permute-start | bytes 393224 | tf_op jit(solution)/shard_map/ppermute | solution.py:37
  118.4 4.3 %collective-permute-start.19 = (f32[8,2048]{1,0:T(8,128)S(1)}, f32[8,2048]{1,0:T(8,128)S(1)}, u32[]{:S(2)}, u32[]{:S(2)}) collective-permute-start(f32[8,2048]{1,0:T(8,128)S(1)} %get-tuple-element.21), channel_id=1, source_target_pairs={{0,12},{4,8},{8,4},{12,0},{1,13},{5,9},{9,5},{13,1},{2,14},{6,10},... | collective-permute-start | bytes 196616 | tf_op jit(solution)/shard_map/ppermute | solution.py:46
  118.5 5.8 %collective-permute-start.18 = (f32[8,2048]{1,0:T(8,128)S(1)}, f32[8,2048]{1,0:T(8,128)S(1)}, u32[]{:S(2)}, u32[]{:S(2)}) collective-permute-start(f32[8,2048]{1,0:T(8,128)S(1)} %get-tuple-element.22), channel_id=1, source_target_pairs={{0,8},{4,12},{8,0},{12,4},{1,9},{5,13},{9,1},{13,5},{2,10},{6,14},... | collective-permute-start | bytes 196616 | tf_op jit(solution)/shard_map/ppermute | solution.py:46
  120.2 4.1 %collective-permute-start.17 = (f32[8,2048]{1,0:T(8,128)S(1)}, f32[8,2048]{1,0:T(8,128)S(1)}, u32[]{:S(2)}, u32[]{:S(2)}) collective-permute-start(f32[8,2048]{1,0:T(8,128)S(1)} %get-tuple-element.23), channel_id=1, source_target_pairs={{0,4},{4,0},{8,12},{12,8},{1,5},{5,1},{9,13},{13,9},{2,6},{6,2},{1... | collective-permute-start | bytes 196616 | tf_op jit(solution)/shard_map/ppermute | solution.py:46

commit v18 on v17

--- a/solution.py
+++ b/solution.py
@@ -79,6 +79,7 @@
     gate_vec = own_mods[2]
     normed = _normalize(tokens)
     mixed = normed * (1.0 + scale_vec) + shift_vec
+    base = lax.optimization_barrier(tokens + gate_vec * down_bias)
     r = lax.axis_index("row")
     d_blk = mixed.shape[1] // n_row
     sent_in = mixed.reshape(tok_dev, n_row, d_blk).swapaxes(0, 1)
@@ -164,7 +165,7 @@
          for i in range(N_CHUNK)], axis=0)
     back = _exchange_abs(out_share.reshape(n_row, tok_dev, d_blk), "row", n_row, r)
     returned = back.swapaxes(0, 1).reshape(tok_dev, n_row * d_blk)
-    return tokens + gate_vec * (returned + down_bias)
+    return base + gate_vec * returned
 
 
 def solution(mesh):

time: 126 us -> 125 us (level)
  no operation moved by 1% of the time
where the time goes in v18:
time: 125 us
  waiting for transfers between devices  59.9 us (48%)
  matrix products  38.2 us (31%)
  starting transfers between devices  20.3 us (16%)
  other arithmetic  3.4 us (3%)
  Pallas kernels  1.97 us (2%)
    ppermute x4, waiting for transfers between devices, _gather_rel(): lax.ppermute(jnp.stack([held[k] for k in keys]), axis, _pairs(n, flip))  21.1 us
    ppermute x4, waiting for transfers between devices, _scatter_rel(): lax.ppermute(jnp.stack([held[d] for d in sent]), axis, _pairs(n, flip))  18.8 us
    dot_general x2, matrix products, down_pair(): jnp.dot(pair, w, precision=lax.Precision.HIGH, preferred_element_type=jnp...  17.4 us
    dot_general x2, matrix products, up_block(): jnp.dot(lhs, w, precision=lax.Precision.HIGH, preferred_element_type=jnp....  11.9 us
    dot_general x1, matrix products, up_pair(): jnp.dot(lhs, w, precision=lax.Precision.HIGH, preferred_element_type=jnp....  8.88 us
    ppermute x6, waiting for transfers between devices, _exchange_abs(): got.append(lax.ppermute(blocks[idx ^ d], axis, _pairs(n, d)))  8.16 us
    ppermute x4, starting transfers between devices, _scatter_rel(): lax.ppermute(jnp.stack([held[d] for d in sent]), axis, _pairs(n, flip))  6.39 us
    ppermute x1, waiting for transfers between devices, local(): lax.ppermute(jnp.stack([held[d] for d in sent]), 'row', _pairs(n_row, flip))  6.08 us
  transfers between devices with their start and end apart: 20, of which 16 were waited for; matrix products, arithmetic and copies ran while one was open for 17% of the time, Pallas kernels for 0%

profile of v18, /device:TPU:0, one launch (start us, length us, event | category | flops | bytes accessed | tf_op | source)
XLA Modules:
  0.0 125.1 jit_solution(10280685036646450416)
XLA Ops:
  0.0 0.8 slice_add_fusion
  0.8 2.0 %shard_map.64 = f32[8,8192]{1,0:T(8,128)} custom-call(f32[8,8192]{1,0:T(8,128)} %x_ref.1), custom_call_target="tpu_custom_call" | custom-call | flops 393216 | bytes 524288 | tf_op jit(solution)/shard_map/pallas_call | solution.py:61
  2.8 1.0 multiply_add_fusion.1
  3.8 2.4 %collective-permute-start.2 = (f32[8,2048]{1,0:T(8,128)S(1)}, f32[8,2048]{1,0:T(8,128)S(1)}, u32[]{:S(2)}, u32[]{:S(2)}) collective-permute-start(f32[8,2048]{1,0:T(8,128)S(1)} %get-tuple-element.29), channel_id=1, source_target_pairs={{0,12},{4,8},{8,4},{12,0},{1,13},{5,9},{9,5},{13,1},{2,14},{6,10},... | collective-permute-start | bytes 196616 | tf_op jit(solution)/shard_map/ppermute | solution.py:46
  6.3 0.7 collective-permute-start
  7.0 1.8 %collective-permute-done.2 = f32[8,2048]{1,0:T(8,128)S(1)} collective-permute-done((f32[8,2048]{1,0:T(8,128)S(1)}, f32[8,2048]{1,0:T(8,128)S(1)}, u32[]{:S(2)}, u32[]{:S(2)}) %collective-permute-start.2) | collective-permute-done | bytes 65568 | tf_op jit(solution)/shard_map/ppermute | solution.py:46
  8.8 2.5 %collective-permute-done.1 = f32[8,2048]{1,0:T(8,128)S(1)} collective-permute-done((f32[8,2048]{1,0:T(8,128)S(1)}, f32[8,2048]{1,0:T(8,128)S(1)}, u32[]{:S(2)}, u32[]{:S(2)}) %collective-permute-start.1) | collective-permute-done | bytes 65568 | tf_op jit(solution)/shard_map/ppermute | solution.py:46
  11.3 2.7 %collective-permute-start.3 = (f32[1,16,2048]{2,1,0:T(8,128)S(1)}, f32[1,16,2048]{2,1,0:T(8,128)S(1)}, u32[]{:S(2)}, u32[]{:S(2)}) collective-permute-start(f32[1,16,2048]{2,1,0:T(8,128)S(1)} %fusion.42), channel_id=1, source_target_pairs={{0,2},{1,3},{2,0},{3,1},{4,6},{5,7},{6,4},{7,5},{8,10},{9,11},{10,... | collective-permute-start | bytes 393224 | tf_op jit(solution)/shard_map/ppermute | solution.py:24
  14.0 0.4 collective-permute-start.5
  14.4 9.1 %collective-permute-done.3 = f32[1,16,2048]{2,1,0:T(8,128)S(1)} collective-permute-done((f32[1,16,2048]{2,1,0:T(8,128)S(1)}, f32[1,16,2048]{2,1,0:T(8,128)S(1)}, u32[]{:S(2)}, u32[]{:S(2)}) %collective-permute-start.3) | collective-permute-done | bytes 131104 | tf_op jit(solution)/shard_map/ppermute | solution.py:24
  23.5 0.1 collective-permute-start.4
  23.6 1.6 %collective-permute-done.5 = f32[1,16,2048]{2,1,0:T(8,128)S(1)} collective-permute-done((f32[1,16,2048]{2,1,0:T(8,128)S(1)}, f32[1,16,2048]{2,1,0:T(8,128)S(1)}, u32[]{:S(2)}, u32[]{:S(2)}) %collective-permute-start.5) | collective-permute-done | bytes 131104 | tf_op jit(solution)/shard_map/ppermute | solution.py:24
  25.2 0.6 collective-permute-start.6
  25.9 6.9 %collective-permute-done.4 = f32[2,16,2048]{2,1,0:T(8,128)S(1)} collective-permute-done((f32[2,16,2048]{2,1,0:T(8,128)S(1)}, f32[2,16,2048]{2,1,0:T(8,128)S(1)}, u32[]{:S(2)}, u32[]{:S(2)}) %collective-permute-start.4) | collective-permute-done | bytes 262176 | tf_op jit(solution)/shard_map/ppermute | solution.py:24
  32.9 3.5 %collective-permute-done.6 = f32[2,16,2048]{2,1,0:T(8,128)S(1)} collective-permute-done((f32[2,16,2048]{2,1,0:T(8,128)S(1)}, f32[2,16,2048]{2,1,0:T(8,128)S(1)}, u32[]{:S(2)}, u32[]{:S(2)}) %collective-permute-start.6) | collective-permute-done | bytes 262176 | tf_op jit(solution)/shard_map/ppermute | solution.py:24
  36.4 8.9 %fusion.4 = f32[128,2048]{1,0:T(8,128)S(1)} fusion(f32[128,2048]{1,0:T(8,128)S(1)} %fusion.37, f32[2048,4096]{1,0:T(8,128)} %param.8, s32[]{:T(128)S(6)} %select_n.88), kind=kOutput, calls=%fused_computation.4 | convolution fusion | flops 3221225472 | bytes 18874372 | tf_op jit(solution)/shard_map/dot_general | solution.py:109
  45.4 0.1 collective-permute-start.8
  45.5 0.7 dynamic_slice.68
  46.2 6.0 %fusion.6 = f32[128,1024]{1,0:T(8,128)S(1)} fusion(f32[128,2048]{1,0:T(8,128)S(1)} %fusion.37, f32[2048,4096]{1,0:T(8,128)} %param.8, s32[]{:T(128)S(6)} %select_n.84), kind=kOutput, calls=%fused_computation.6 | convolution fusion | flops 1610612736 | bytes 9961476 | tf_op jit(solution)/shard_map/dot_general | solution.py:98
  52.1 0.5 collective-permute-start.7
  52.7 0.1 add_bitcast_fusion
  52.8 2.5 %collective-permute-start.9 = (f32[1,128,1024]{2,1,0:T(8,128)S(1)}, f32[1,128,1024]{2,1,0:T(8,128)S(1)}, u32[]{:S(2)}, u32[]{:S(2)}) collective-permute-start(f32[1,128,1024]{2,1,0:T(8,128)S(1)} %add_bitcast_fusion), channel_id=1, source_target_pairs={{0,8},{4,12},{8,0},{12,4},{1,9},{5,13},{9,1},{13,5},{2,10},{6,14},... | collective-permute-start | bytes 1572872 | tf_op jit(solution)/shard_map/ppermute | solution.py:131
  55.3 5.9 %fusion.8 = f32[128,1024]{1,0:T(8,128)S(1)} fusion(f32[128,2048]{1,0:T(8,128)S(1)} %fusion.37, f32[2048,4096]{1,0:T(8,128)} %param.8, s32[]{:T(128)S(6)} %select_n.83), kind=kOutput, calls=%fused_computation.8 | convolution fusion | flops 1610612736 | bytes 9961476 | tf_op jit(solution)/shard_map/dot_general | solution.py:98
  61.3 0.1 add_add_fusion
  61.4 6.1 %collective-permute-done.9 = f32[1,128,1024]{2,1,0:T(8,128)S(1)} collective-permute-done((f32[1,128,1024]{2,1,0:T(8,128)S(1)}, f32[1,128,1024]{2,1,0:T(8,128)S(1)}, u32[]{:S(2)}, u32[]{:S(2)}) %collective-permute-start.9) | collective-permute-done | bytes 524320 | tf_op jit(solution)/shard_map/ppermute | solution.py:131
  67.5 0.2 fusion.26
  67.6 0.1 collective-permute-start.11
  67.7 1.8 %collective-permute-start.10 = (f32[1,128,1024]{2,1,0:T(8,128)S(1)}, f32[1,128,1024]{2,1,0:T(8,128)S(1)}, u32[]{:S(2)}, u32[]{:S(2)}) collective-permute-start(f32[1,128,1024]{2,1,0:T(8,128)S(1)} %bitcast.109), channel_id=1, source_target_pairs={{0,8},{4,12},{8,0},{12,4},{1,9},{5,13},{9,1},{13,5},{2,10},{6,14},... | collective-permute-start | bytes 1572872 | tf_op jit(solution)/shard_map/ppermute | solution.py:139
  69.5 0.1 collective-permute-done.11
  69.6 8.7 %fusion.2 = f32[128,2048]{1,0:T(8,128)S(1)} fusion(f32[4096,2048]{1,0:T(8,128)} %param.10, s32[]{:T(128)S(6)} %select_n.94, f32[128,1024]{1,0:T(8,128)S(1)} %collective-permute-done.11, f32[128,1024]{1,0:T(8,128)S(1)} %fusion.26, pred[]{:T(512)S(6)} %eq.4), kind=kOutput, calls=%fused_computation.2 | convolution fusion | flops 3222011904 | bytes 18874372 | tf_op jit(solution)/shard_map/dot_general | solution.py:149
  78.3 3.7 %collective-permute-done.10 = f32[1,128,1024]{2,1,0:T(8,128)S(1)} collective-permute-done((f32[1,128,1024]{2,1,0:T(8,128)S(1)}, f32[1,128,1024]{2,1,0:T(8,128)S(1)}, u32[]{:S(2)}, u32[]{:S(2)}) %collective-permute-start.10) | collective-permute-done | bytes 524320 | tf_op jit(solution)/shard_map/ppermute | solution.py:139
  82.1 1.9 %collective-permute-done.12 = f32[1,128,1024]{2,1,0:T(8,128)S(1)} collective-permute-done((f32[1,128,1024]{2,1,0:T(8,128)S(1)}, f32[1,128,1024]{2,1,0:T(8,128)S(1)}, u32[]{:S(2)}, u32[]{:S(2)}) %collective-permute-start.12) | collective-permute-done | bytes 524320 | tf_op jit(solution)/shard_map/ppermute | solution.py:157
  84.0 8.7 %fusion = f32[128,2048]{1,0:T(8,128)S(1)} fusion(f32[4096,2048]{1,0:T(8,128)} %param.10, s32[]{:T(128)S(6)} %select_n.88, f32[128,1024]{1,0:T(8,128)S(1)} %bitcast.113, f32[128,1024]{1,0:T(8,128)S(1)} %bitcast.112, pred[]{:T(512)S(6)} %eq.4), kind=kOutput, calls=%fused_computation | convolution fusion | flops 3222011904 | bytes 18874372 | tf_op jit(solution)/shard_map/dot_general | solution.py:149
  92.7 0.1 add.153
  92.9 0.6 collective-permute-start.13
  93.5 7.8 %collective-permute-done.13 = f32[2,16,2048]{2,1,0:T(8,128)S(1)} collective-permute-done((f32[2,16,2048]{2,1,0:T(8,128)S(1)}, f32[2,16,2048]{2,1,0:T(8,128)S(1)}, u32[]{:S(2)}, u32[]{:S(2)}) %collective-permute-start.13) | collective-permute-done | bytes 262176 | tf_op jit(solution)/shard_map/ppermute | solution.py:37
  101.3 0.6 collective-permute-start.15
  102.0 3.5 %collective-permute-start.14 = (f32[1,16,2048]{2,1,0:T(8,128)S(1)}, f32[1,16,2048]{2,1,0:T(8,128)S(1)}, u32[]{:S(2)}, u32[]{:S(2)}) collective-permute-start(f32[1,16,2048]{2,1,0:T(8,128)S(1)} %get-tuple-element.11), channel_id=1, source_target_pairs={{0,2},{1,3},{2,0},{3,1},{4,6},{5,7},{6,4},{7,5},{8,10},{9,11},{10,... | collective-permute-start | bytes 393224 | tf_op jit(solution)/shard_map/ppermute | solution.py:37
  105.4 4.4 %collective-permute-done.14 = f32[1,16,2048]{2,1,0:T(8,128)S(1)} collective-permute-done((f32[1,16,2048]{2,1,0:T(8,128)S(1)}, f32[1,16,2048]{2,1,0:T(8,128)S(1)}, u32[]{:S(2)}, u32[]{:S(2)}) %collective-permute-start.14) | collective-permute-done | bytes 131104 | tf_op jit(solution)/shard_map/ppermute | solution.py:37
  109.8 1.9 %collective-permute-done.15 = f32[2,16,2048]{2,1,0:T(8,128)S(1)} collective-permute-done((f32[2,16,2048]{2,1,0:T(8,128)S(1)}, f32[2,16,2048]{2,1,0:T(8,128)S(1)}, u32[]{:S(2)}, u32[]{:S(2)}) %collective-permute-start.15) | collective-permute-done | bytes 262176 | tf_op jit(solution)/shard_map/ppermute | solution.py:37
  111.8 1.6 %collective-permute-start.16 = (f32[1,16,2048]{2,1,0:T(8,128)S(1)}, f32[1,16,2048]{2,1,0:T(8,128)S(1)}, u32[]{:S(2)}, u32[]{:S(2)}) collective-permute-start(f32[1,16,2048]{2,1,0:T(8,128)S(1)} %get-tuple-element.10), channel_id=1, source_target_pairs={{0,2},{1,3},{2,0},{3,1},{4,6},{5,7},{6,4},{7,5},{8,10},{9,11},{10,... | collective-permute-start | bytes 393224 | tf_op jit(solution)/shard_map/ppermute | solution.py:37
  113.4 4.8 %collective-permute-done.16 = f32[1,16,2048]{2,1,0:T(8,128)S(1)} collective-permute-done((f32[1,16,2048]{2,1,0:T(8,128)S(1)}, f32[1,16,2048]{2,1,0:T(8,128)S(1)}, u32[]{:S(2)}, u32[]{:S(2)}) %collective-permute-start.16) | collective-permute-done | bytes 131104 | tf_op jit(solution)/shard_map/ppermute | solution.py:37
  118.3 0.1 collective-permute-start.17
  118.4 1.8 %collective-permute-start.18 = (f32[8,2048]{1,0:T(8,128)S(1)}, f32[8,2048]{1,0:T(8,128)S(1)}, u32[]{:S(2)}, u32[]{:S(2)}) collective-permute-start(f32[8,2048]{1,0:T(8,128)S(1)} %get-tuple-element.22), channel_id=1, source_target_pairs={{0,8},{4,12},{8,0},{12,4},{1,9},{5,13},{9,1},{13,5},{2,10},{6,14},... | collective-permute-start | bytes 196616 | tf_op jit(solution)/shard_map/ppermute | solution.py:46
  120.2 0.1 collective-permute-start.19
  120.3 2.6 %collective-permute-done.18 = f32[8,2048]{1,0:T(8,128)S(1)} collective-permute-done((f32[8,2048]{1,0:T(8,128)S(1)}, f32[8,2048]{1,0:T(8,128)S(1)}, u32[]{:S(2)}, u32[]{:S(2)}) %collective-permute-start.18) | collective-permute-done | bytes 65568 | tf_op jit(solution)/shard_map/ppermute | solution.py:46
  122.9 1.3 %collective-permute-done.19 = f32[8,2048]{1,0:T(8,128)S(1)} collective-permute-done((f32[8,2048]{1,0:T(8,128)S(1)}, f32[8,2048]{1,0:T(8,128)S(1)}, u32[]{:S(2)}, u32[]{:S(2)}) %collective-permute-start.19) | collective-permute-done | bytes 65568 | tf_op jit(solution)/shard_map/ppermute | solution.py:46
  124.3 0.8 multiply_add_fusion
  (39 shorter events, 0.6 us)
Async XLA Ops:
  3.8 4.9 %collective-permute-start.2 = (f32[8,2048]{1,0:T(8,128)S(1)}, f32[8,2048]{1,0:T(8,128)S(1)}, u32[]{:S(2)}, u32[]{:S(2)}) collective-permute-start(f32[8,2048]{1,0:T(8,128)S(1)} %get-tuple-element.29), channel_id=1, source_target_pairs={{0,12},{4,8},{8,4},{12,0},{1,13},{5,9},{9,5},{13,1},{2,14},{6,10},... | collective-permute-start | bytes 196616 | tf_op jit(solution)/shard_map/ppermute | solution.py:46
  6.3 2.5 %collective-permute-start = (f32[8,2048]{1,0:T(8,128)S(1)}, f32[8,2048]{1,0:T(8,128)S(1)}, u32[]{:S(2)}, u32[]{:S(2)}) collective-permute-start(f32[8,2048]{1,0:T(8,128)S(1)} %get-tuple-element.31), channel_id=1, source_target_pairs={{0,4},{4,0},{8,12},{12,8},{1,5},{5,1},{9,13},{13,9},{2,6},{6,2},{1... | collective-permute-start | bytes 196616 | tf_op jit(solution)/shard_map/ppermute | solution.py:46
  6.9 4.3 %collective-permute-start.1 = (f32[8,2048]{1,0:T(8,128)S(1)}, f32[8,2048]{1,0:T(8,128)S(1)}, u32[]{:S(2)}, u32[]{:S(2)}) collective-permute-start(f32[8,2048]{1,0:T(8,128)S(1)} %get-tuple-element.30), channel_id=1, source_target_pairs={{0,8},{4,12},{8,0},{12,4},{1,9},{5,13},{9,1},{13,5},{2,10},{6,14},... | collective-permute-start | bytes 196616 | tf_op jit(solution)/shard_map/ppermute | solution.py:46
  11.3 12.2 %collective-permute-start.3 = (f32[1,16,2048]{2,1,0:T(8,128)S(1)}, f32[1,16,2048]{2,1,0:T(8,128)S(1)}, u32[]{:S(2)}, u32[]{:S(2)}) collective-permute-start(f32[1,16,2048]{2,1,0:T(8,128)S(1)} %fusion.42), channel_id=1, source_target_pairs={{0,2},{1,3},{2,0},{3,1},{4,6},{5,7},{6,4},{7,5},{8,10},{9,11},{10,... | collective-permute-start | bytes 393224 | tf_op jit(solution)/shard_map/ppermute | solution.py:24
  14.0 11.3 %collective-permute-start.5 = (f32[1,16,2048]{2,1,0:T(8,128)S(1)}, f32[1,16,2048]{2,1,0:T(8,128)S(1)}, u32[]{:S(2)}, u32[]{:S(2)}) collective-permute-start(f32[1,16,2048]{2,1,0:T(8,128)S(1)} %fusion.41), channel_id=1, source_target_pairs={{0,2},{1,3},{2,0},{3,1},{4,6},{5,7},{6,4},{7,5},{8,10},{9,11},{10,... | collective-permute-start | bytes 393224 | tf_op jit(solution)/shard_map/ppermute | solution.py:24
  23.5 9.3 %collective-permute-start.4 = (f32[2,16,2048]{2,1,0:T(8,128)S(1)}, f32[2,16,2048]{2,1,0:T(8,128)S(1)}, u32[]{:S(2)}, u32[]{:S(2)}) collective-permute-start(f32[2,16,2048]{2,1,0:T(8,128)S(1)} %pad_maximum_fusion.1), channel_id=1, source_target_pairs={{0,1},{1,0},{2,3},{3,2},{4,5},{5,4},{6,7},{7,6},{8,9},{9,8},{10,11... | collective-permute-start | bytes 786440 | tf_op jit(solution)/shard_map/ppermute | solution.py:24
  25.2 11.1 %collective-permute-start.6 = (f32[2,16,2048]{2,1,0:T(8,128)S(1)}, f32[2,16,2048]{2,1,0:T(8,128)S(1)}, u32[]{:S(2)}, u32[]{:S(2)}) collective-permute-start(f32[2,16,2048]{2,1,0:T(8,128)S(1)} %pad_maximum_fusion.2), channel_id=1, source_target_pairs={{0,1},{1,0},{2,3},{3,2},{4,5},{5,4},{6,7},{7,6},{8,9},{9,8},{10,11... | collective-permute-start | bytes 786440 | tf_op jit(solution)/shard_map/ppermute | solution.py:24
  45.4 7.3 %collective-permute-start.8 = (f32[128,1024]{1,0:T(8,128)S(1)}, f32[128,1024]{1,0:T(8,128)S(1)}, u32[]{:S(2)}, u32[]{:S(2)}) collective-permute-start(f32[128,1024]{1,0:T(8,128)S(1)} %slice_select_fusion), channel_id=1, source_target_pairs={{0,4},{4,0},{8,12},{12,8},{1,5},{5,1},{9,13},{13,9},{2,6},{6,2},{1... | collective-permute-start | bytes 1572872 | tf_op jit(solution)/shard_map/ppermute | solution.py:124
  46.1 67.2 %copy-start.1 = (f32[8192]{0:T(1024)S(1)}, f32[8192]{0:T(1024)}, u32[]{:S(2)}) copy-start(f32[8192]{0:T(1024)} %param.11) | copy-start | bytes 98308
  46.1 74.1 %copy-start = (f32[8,8192]{1,0:T(8,128)S(1)}, f32[8,8192]{1,0:T(8,128)}, u32[]{:S(2)}) copy-start(f32[8,8192]{1,0:T(8,128)} %x_ref.1) | copy-start | bytes 786436
  52.1 9.1 %collective-permute-start.7 = (f32[128,1024]{1,0:T(8,128)S(1)}, f32[128,1024]{1,0:T(8,128)S(1)}, u32[]{:S(2)}, u32[]{:S(2)}) collective-permute-start(f32[128,1024]{1,0:T(8,128)S(1)} %fusion.6), channel_id=1, source_target_pairs={{0,4},{4,0},{8,12},{12,8},{1,5},{5,1},{9,13},{13,9},{2,6},{6,2},{1... | collective-permute-start | bytes 1572872 | tf_op jit(solution)/shard_map/ppermute | solution.py:124
  52.8 14.7 %collective-permute-start.9 = (f32[1,128,1024]{2,1,0:T(8,128)S(1)}, f32[1,128,1024]{2,1,0:T(8,128)S(1)}, u32[]{:S(2)}, u32[]{:S(2)}) collective-permute-start(f32[1,128,1024]{2,1,0:T(8,128)S(1)} %add_bitcast_fusion), channel_id=1, source_target_pairs={{0,8},{4,12},{8,0},{12,4},{1,9},{5,13},{9,1},{13,5},{2,10},{6,14},... | collective-permute-start | bytes 1572872 | tf_op jit(solution)/shard_map/ppermute | solution.py:131
  67.6 2.0 %collective-permute-start.11 = (f32[128,1024]{1,0:T(8,128)S(1)}, f32[128,1024]{1,0:T(8,128)S(1)}, u32[]{:S(2)}, u32[]{:S(2)}) collective-permute-start(f32[128,1024]{1,0:T(8,128)S(1)} %fusion.26), channel_id=1, source_target_pairs={{0,4},{4,0},{8,12},{12,8},{1,5},{5,1},{9,13},{13,9},{2,6},{6,2},{1... | collective-permute-start | bytes 1572872 | tf_op jit(solution)/shard_map/ppermute | solution.py:135
  67.7 14.3 %collective-permute-start.10 = (f32[1,128,1024]{2,1,0:T(8,128)S(1)}, f32[1,128,1024]{2,1,0:T(8,128)S(1)}, u32[]{:S(2)}, u32[]{:S(2)}) collective-permute-start(f32[1,128,1024]{2,1,0:T(8,128)S(1)} %bitcast.109), channel_id=1, source_target_pairs={{0,8},{4,12},{8,0},{12,4},{1,9},{5,13},{9,1},{13,5},{2,10},{6,14},... | collective-permute-start | bytes 1572872 | tf_op jit(solution)/shard_map/ppermute | solution.py:139
  82.1 1.9 %collective-permute-start.12 = (f32[1,128,1024]{2,1,0:T(8,128)S(1)}, f32[1,128,1024]{2,1,0:T(8,128)S(1)}, u32[]{:S(2)}, u32[]{:S(2)}) collective-permute-start(f32[1,128,1024]{2,1,0:T(8,128)S(1)} %collective-permute-done.10), channel_id=1, source_target_pairs={{0,4},{4,0},{8,12},{12,8},{1,5},{5,1},{9,13},{13,9},{2,6},{6,2},{1... | collective-permute-start | bytes 1572872 | tf_op jit(solution)/shard_map/ppermute | solution.py:157
  92.9 8.4 %collective-permute-start.13 = (f32[2,16,2048]{2,1,0:T(8,128)S(1)}, f32[2,16,2048]{2,1,0:T(8,128)S(1)}, u32[]{:S(2)}, u32[]{:S(2)}) collective-permute-start(f32[2,16,2048]{2,1,0:T(8,128)S(1)} %pad_maximum_fusion.3), channel_id=1, source_target_pairs={{0,1},{1,0},{2,3},{3,2},{4,5},{5,4},{6,7},{7,6},{8,9},{9,8},{10,11... | collective-permute-start | bytes 786440 | tf_op jit(solution)/shard_map/ppermute | solution.py:37
  101.3 10.4 %collective-permute-start.15 = (f32[2,16,2048]{2,1,0:T(8,128)S(1)}, f32[2,16,2048]{2,1,0:T(8,128)S(1)}, u32[]{:S(2)}, u32[]{:S(2)}) collective-permute-start(f32[2,16,2048]{2,1,0:T(8,128)S(1)} %pad_maximum_fusion.4), channel_id=1, source_target_pairs={{0,1},{1,0},{2,3},{3,2},{4,5},{5,4},{6,7},{7,6},{8,9},{9,8},{10,11... | collective-permute-start | bytes 786440 | tf_op jit(solution)/shard_map/ppermute | solution.py:37
  102.0 7.8 %collective-permute-start.14 = (f32[1,16,2048]{2,1,0:T(8,128)S(1)}, f32[1,16,2048]{2,1,0:T(8,128)S(1)}, u32[]{:S(2)}, u32[]{:S(2)}) collective-permute-start(f32[1,16,2048]{2,1,0:T(8,128)S(1)} %get-tuple-element.11), channel_id=1, source_target_pairs={{0,2},{1,3},{2,0},{3,1},{4,6},{5,7},{6,4},{7,5},{8,10},{9,11},{10,... | collective-permute-start | bytes 393224 | tf_op jit(solution)/shard_map/ppermute | solution.py:37
  111.8 6.4 %collective-permute-start.16 = (f32[1,16,2048]{2,1,0:T(8,128)S(1)}, f32[1,16,2048]{2,1,0:T(8,128)S(1)}, u32[]{:S(2)}, u32[]{:S(2)}) collective-permute-start(f32[1,16,2048]{2,1,0:T(8,128)S(1)} %get-tuple-element.10), channel_id=1, source_target_pairs={{0,2},{1,3},{2,0},{3,1},{4,6},{5,7},{6,4},{7,5},{8,10},{9,11},{10,... | collective-permute-start | bytes 393224 | tf_op jit(solution)/shard_map/ppermute | solution.py:37
  118.3 2.0 %collective-permute-start.17 = (f32[8,2048]{1,0:T(8,128)S(1)}, f32[8,2048]{1,0:T(8,128)S(1)}, u32[]{:S(2)}, u32[]{:S(2)}) collective-permute-start(f32[8,2048]{1,0:T(8,128)S(1)} %get-tuple-element.23), channel_id=1, source_target_pairs={{0,4},{4,0},{8,12},{12,8},{1,5},{5,1},{9,13},{13,9},{2,6},{6,2},{1... | collective-permute-start | bytes 196616 | tf_op jit(solution)/shard_map/ppermute | solution.py:46
  118.4 4.5 %collective-permute-start.18 = (f32[8,2048]{1,0:T(8,128)S(1)}, f32[8,2048]{1,0:T(8,128)S(1)}, u32[]{:S(2)}, u32[]{:S(2)}) collective-permute-start(f32[8,2048]{1,0:T(8,128)S(1)} %get-tuple-element.22), channel_id=1, source_target_pairs={{0,8},{4,12},{8,0},{12,4},{1,9},{5,13},{9,1},{13,5},{2,10},{6,14},... | collective-permute-start | bytes 196616 | tf_op jit(solution)/shard_map/ppermute | solution.py:46
  120.2 4.0 %collective-permute-start.19 = (f32[8,2048]{1,0:T(8,128)S(1)}, f32[8,2048]{1,0:T(8,128)S(1)}, u32[]{:S(2)}, u32[]{:S(2)}) collective-permute-start(f32[8,2048]{1,0:T(8,128)S(1)} %get-tuple-element.21), channel_id=1, source_target_pairs={{0,12},{4,8},{8,4},{12,0},{1,13},{5,9},{9,5},{13,1},{2,14},{6,10},... | collective-permute-start | bytes 196616 | tf_op jit(solution)/shard_map/ppermute | solution.py:46
